TPU v7x, 32 devices: a whole 2x2x4 slice. The times are simulated.
32 devices in a mesh: groups: 2 (over x), ctx: 16 (over z, y, core).
Axes of the slice: x: 2, y: 2, z: 4, core: 2. Of those that a mesh axis runs over, the one named last changes fastest.
Arguments:
- sem_queries: bfloat16 [8192, 1024], P(('groups', 'ctx')), parts along dimension 0, may hold values from -170 to 170
- sem_keys: bfloat16 [8192, 1024], P(('groups', 'ctx')), parts along dimension 0, may hold values from -7 to 7
- sem_values: bfloat16 [8192, 1024], P(('groups', 'ctx')), parts along dimension 0, may hold values from -6 to 6
- sem_inputs: bfloat16 [8192, 2048], P(('groups', 'ctx')), parts along dimension 0, may hold values from -80 to 80
- out_proj: bfloat16 [1024, 2048], P('ctx'), may hold values from -0.5 to 0.5
- norm_gain: float32 [2048], replicated, may hold values from 0.1 to 1.9
- key_proj: bfloat16 [2048, 1024], P('ctx'), may hold values from -0.125 to 0.125
- value_proj: bfloat16 [2048, 1024], P('ctx'), may hold values from -0.125 to 0.125
- slopes: float32 [8], replicated, may hold values from 1 to 16
- coarse_queries: bfloat16 [32768, 1024], P(('groups', 'ctx')), parts along dimension 0, may hold values from -400 to 400
- counts: int32 [32], P(('groups', 'ctx')), parts along dimension 0, may hold values from 512 to 1024, as said below
- band_bounds: int32 [128, 2], P(('groups', 'ctx')), parts along dimension 0, may hold values from 0 to 4096, as said below
Outputs:
- coarse_context: bfloat16 [32768, 1024], P(('groups', 'ctx')), parts along dimension 0
There are 2 independent parts, one for each index of `groups`. A program takes and returns all parts, laid end to end along the dimension named above; an argument that names none is the same for every part. Nothing has to cross between parts.
Inputs may be any that keep to these rules, and one draw needn't show every extreme that they name: `counts`: live coarse tokens of a ctx index fill its first slots; at least half of 1024; some index is full. `band_bounds`: a band of block n, held by ctx index c = n // 4, covers 512 // 2 to 512 rows and lies within the semantic rows of indices c - 1, c and c + 1; block 0 covers exactly 512.
All inputs are finite; a program needn't handle non-finite values.
Results may differ from a plain program's by a relative error of at most 0.0091.
Values may be sent and summed in bfloat16 or wider, within the bound.
No kernel may reach another device: no remote copies, remote signals or barrier semaphores. Data moves between devices by JAX's collectives and lax.ppermute only.
A program may use at most 128 MiB of HBM per device.

v0:
```python
import jax
import jax.numpy as jnp
from jax import lax
from jax.sharding import PartitionSpec as P

HEADS = 8
HEAD_DIM = 128
W = 512
BAND = 512
CB = 256


NEG_FILL = -1e30


def passed_along(array, axis, by):
    length = lax.axis_size(axis)
    pairs = [(i, i + by) for i in range(length) if 0 <= i + by < length]
    return lax.ppermute(array, axis, pairs)


def carried_in(array, axis, combine, identity):
    length, position = (lax.axis_size(axis), lax.axis_index(axis))
    everything = lax.all_gather(array, axis)
    start = jnp.broadcast_to(jnp.asarray(identity, array.dtype), array.shape)

    def step(k, before):
        reached = k < position
        new = combine(before, everything[k])
        return jnp.where(reached, new, before)

    return lax.fori_loop(0, length, step, start)


def with_halo(array, sides, width):
    for axis, dim in sides:
        size, length = (lax.axis_size(axis), array.shape[dim])
        up = [(i, (i + 1) % size) for i in range(size - 1)]
        down = [(j, i) for i, j in up]
        last = lax.slice_in_dim(array, length - width, length, axis=dim)
        first = lax.slice_in_dim(array, 0, width, axis=dim)
        before = lax.ppermute(last, axis, up)
        after = lax.ppermute(first, axis, down)
        array = jnp.concatenate([before, array, after], axis=dim)
    return array


def head_split(matrix):
    return matrix.reshape(matrix.shape[0], HEADS, HEAD_DIM)


def attend(queries, key_rows, value_rows, allowed, time_bias):
    scores = jnp.einsum(
        "qhd,khd->hqk",
        head_split(queries),
        head_split(key_rows),
        preferred_element_type=jnp.float32,
    ) * HEAD_DIM ** (-0.5)
    scores = jnp.where(allowed[None], scores + time_bias, NEG_FILL)
    largest = jnp.max(scores, axis=2, keepdims=True)
    exponent = jnp.exp(scores - largest)
    weights = (exponent / jnp.sum(exponent, axis=2, keepdims=True)).astype(jnp.bfloat16)
    blended = jnp.einsum(
        "hqk,khd->qhd", weights, head_split(value_rows), preferred_element_type=jnp.float32
    )
    return blended.reshape(queries.shape[0], -1)


def normalize(sem_stream, norm_gain):
    scaled = sem_stream * lax.rsqrt(
        jnp.mean(sem_stream * sem_stream, axis=1, keepdims=True) + 1e-05
    )
    return (scaled * norm_gain[None, :]).astype(jnp.bfloat16)


def cross_attend(
    queries, key_rows, value_rows, key_global, band_low, band_high, positions, slopes, live_rows
):
    timing = (positions // 2).astype(jnp.float32) * (2.0 / 3.0)
    distance = jnp.abs(timing[:, None] - key_global[None, :].astype(jnp.float32))
    time_bias = -slopes[:, None, None] * distance[None] / BAND
    inside = (key_global >= band_low) & (key_global < band_high)
    allowed = jnp.broadcast_to(inside[None, :], (queries.shape[0], key_global.shape[0]))
    blended = attend(queries, key_rows, value_rows, allowed, time_bias)
    return jnp.where(live_rows[:, None], blended, 0.0).astype(jnp.bfloat16)


def contract_rows(left_side, weight_piece):
    return jnp.dot(left_side, weight_piece, preferred_element_type=jnp.float32)


def add_counts(earlier_sum, later_sum):
    return earlier_sum + later_sum


def on_device(
    sem_queries,
    sem_keys,
    sem_values,
    sem_inputs,
    out_proj,
    norm_gain,
    key_proj,
    value_proj,
    slopes,
    coarse_queries,
    counts,
    band_bounds,
):
    rows_here = sem_queries.shape[0]
    device_index = lax.axis_index("ctx")
    own_pair = jnp.stack([sem_keys, sem_values])
    reach_shards = (W - 1 + rows_here - 1) // rows_here
    earlier = []
    for distance in range(1, reach_shards + 1):
        earlier.insert(0, passed_along(own_pair, "ctx", distance))
    window_pair = jnp.concatenate(earlier + [own_pair], axis=1)
    query_pos = jnp.arange(rows_here, dtype=jnp.int32)
    key_pos = jnp.arange(window_pair.shape[1], dtype=jnp.int32)
    key_lag = query_pos[:, None] + reach_shards * rows_here - key_pos[None, :]
    key_global = device_index * rows_here - reach_shards * rows_here + key_pos
    allowed = (key_lag >= 0) & (key_lag < W) & (key_global[None, :] >= 0)
    sem_att = attend(sem_queries, window_pair[0], window_pair[1], allowed, 0.0).astype(jnp.bfloat16)
    projected = contract_rows(sem_att, lax.all_gather(out_proj, "ctx", axis=0, tiled=True))
    sem_stream = sem_inputs.astype(jnp.float32) + projected
    normed = normalize(sem_stream, norm_gain)
    key_sum = contract_rows(normed, lax.all_gather(key_proj, "ctx", axis=0, tiled=True))
    value_sum = contract_rows(normed, lax.all_gather(value_proj, "ctx", axis=0, tiled=True))
    cross_keys = key_sum.astype(jnp.bfloat16)
    cross_values = value_sum.astype(jnp.bfloat16)
    stream_start = carried_in(counts, "ctx", add_counts, jnp.zeros_like(counts))[0]
    near_pair = with_halo(jnp.stack([cross_keys, cross_values]), (("ctx", 1),), rows_here)
    base_row = (device_index - 1) * rows_here
    live_count = counts[0]
    near_rows = near_pair.shape[1]
    block_total = band_bounds.shape[0]

    def coarse_block(block_index):
        band_low = band_bounds[block_index, 0]
        band_high = band_bounds[block_index, 1]
        first_key = jnp.minimum(band_low - base_row, near_rows - BAND)
        keys_block = lax.dynamic_slice_in_dim(near_pair, first_key, BAND, 1)
        key_global = base_row + first_key + jnp.arange(BAND, dtype=jnp.int32)
        row_local = block_index * CB + jnp.arange(CB, dtype=jnp.int32)
        queries = lax.dynamic_slice_in_dim(coarse_queries, block_index * CB, CB, 0)
        return cross_attend(
            queries,
            keys_block[0],
            keys_block[1],
            key_global,
            band_low,
            band_high,
            stream_start + row_local,
            slopes,
            row_local < live_count,
        )

    stacked = jax.vmap(coarse_block)(jnp.arange(block_total, dtype=jnp.int32))
    return stacked.reshape(coarse_queries.shape[0], coarse_queries.shape[1])


def solution(mesh):
    return jax.shard_map(
        on_device,
        mesh=mesh,
        in_specs=(
            P(("groups", "ctx"), None),
            P(("groups", "ctx"), None),
            P(("groups", "ctx"), None),
            P(("groups", "ctx"), None),
            P("ctx", None),
            P(),
            P("ctx", None),
            P("ctx", None),
            P(),
            P(("groups", "ctx"), None),
            P(("groups", "ctx")),
            P(("groups", "ctx"), None),
        ),
        out_specs=P(("groups", "ctx"), None),
        check_vma=False,
    )
```

profile of v0, /device:TPU:20, one launch (start us, length us, event | category | flops | bytes accessed | tf_op | source)
XLA Modules:
  0.0 286.4 jit_solution(17727069789186815152)
XLA Ops:
  6.6 0.7 all-gather.5.cloned.1.call-update
  7.3 0.7 all-gather.7.cloned.1.call-update
  8.1 0.7 all-gather.9.cloned.1.call-update
  8.8 1.2 copy.19
  10.0 1.2 copy.20
  11.4 3.4 %collective-permute-start = (bf16[2,256,1024]{1,2,0:T(8,128)(2,1)S(1)}, bf16[2,256,1024]{1,2,0:T(8,128)(2,1)}, u32[]{:S(2)}, u32[]{:S(2)}) collective-permute-start(bf16[2,256,1024]{1,2,0:T(8,128)(2,1)S(1)} %pad_maximum_fusion.1), channel_id=1, source_target_pairs={{0,2},{1,3},{2,4},{3,5},{4,6},{5,7},{6,8},{7,9},{8,10},{9,11},{10,... | collective-permute-start | bytes 3145736 | tf_op jit(solution)/shard_map/ppermute | solution.py:19
  16.1 0.8 dynamic-update-slice.4
  16.8 1.9 collective-permute-start.1
  18.7 36.6 %all-reduce.1 = s32[16]{0:T(128)S(1)} all-reduce(s32[16]{0:T(128)S(1)} %dynamic-update-slice.4), channel_id=2, replica_groups=mesh['groups'=2,'ctx'=16] {'ctx'}, use_global_device_ids=true, to_apply=%add.1 | all-reduce | flops 16 | bytes 128
  56.7 20.7 %while.15 = (s32[]{:T(128)}, s32[1]{0:T(128)}, s32[]{:T(128)}, s32[16,1]{0,1:T(1,128)S(1)}, s32[]{:T(128)}) while((s32[]{:T(128)}, s32[1]{0:T(128)}, s32[]{:T(128)}, s32[16,1]{0,1:T(1,128)S(1)}, s32[]{:T(128)}) %tuple.70), condition=%wide.region_4.5_spmd, body=%wide.region_3.4_spmd.sunk | while | flops 5 | bytes 107 | solution.py:32
  58.0 0.6 constant_dynamic-slice_fusion.6
  59.3 0.6 constant_dynamic-slice_fusion.6
  60.6 0.6 constant_dynamic-slice_fusion.6
  61.9 0.6 constant_dynamic-slice_fusion.6
  68.4 0.6 constant_dynamic-slice_fusion.6
  78.0 1.5 subtract_abs_fusion
  79.6 1.7 maximum_maximum_fusion
  81.4 1.0 fusion.35
  82.5 3.1 %fusion.66 = (f32[8,256]{1,0:T(8,128)S(1)}, f32[8,256,768]{1,2,0:T(8,128)S(1)}) fusion(f32[8,768,256]{2,1,0:T(8,128)S(1)} %fusion.35, pred[256,768]{0,1:T(8,128)(4,1)S(1)} %fusion.34), kind=kOutput, calls=%fused_computation.93 | output fusion | flops 9437951 | bytes 12787712 | tf_op jit(solution)/shard_map/sub | solution.py:61
  86.3 3.9 %multiply_reduce_fusion = (f32[256]{0:T(256)S(1)}, f32[256,2048]{1,0:T(8,128)S(1)}) fusion(bf16[256,1024]{0,1:T(8,128)(2,1)S(1)} %bitcast.109, bf16[1024,2048]{1,0:T(8,128)(2,1)} %all-gather.5.cloned.1.call-done, bf16[256,2048]{1,0:T(8,128)(2,1)} %param.17), kind=kOutput, calls=%fused_computation.38 | convolution fusion | flops 1075838720 | bytes 7865344 | tf_op jit(solution)/shard_map/dot_general | solution.py:89
  90.2 32.9 %all-gather.7.cloned.1.call-done = bf16[2048,1024]{1,0:T(8,128)(2,1)} async-done(((bf16[128,1024]{1,0:T(8,128)(2,1)}), bf16[2048,1024]{1,0:T(8,128)(2,1)}) %all-gather.7.cloned.1.call-update) | async-done | bytes 4194320 | tf_op jit(solution)/shard_map/all_gather | solution.py:127
  123.1 3.5 %fusion.29 = bf16[1,256,1024]{2,1,0:T(8,128)(2,1)S(1)} fusion(bf16[2048,1024]{1,0:T(8,128)(2,1)} %all-gather.7.cloned.1.call-done, f32[256,2048]{1,0:T(8,128)S(1)} %get-tuple-element.138, f32[2048]{0:T(1024)S(1)} %copy-done.9, f32[256]{0:T(256)S(1)} %add_rsqrt_fusion), kind=kOutput, calls=%fused_computation.44 | convolution fusion | flops 1075576832 | bytes 6824960 | tf_op jit(solution)/shard_map/dot_general | solution.py:89
  126.6 47.6 %all-gather.9.cloned.1.call-done = bf16[2048,1024]{1,0:T(8,128)(2,1)} async-done(((bf16[128,1024]{1,0:T(8,128)(2,1)}), bf16[2048,1024]{1,0:T(8,128)(2,1)}) %all-gather.9.cloned.1.call-update) | async-done | bytes 4194320 | tf_op jit(solution)/shard_map/all_gather | solution.py:128
  174.2 3.5 %fusion.30 = bf16[1,256,1024]{2,1,0:T(8,128)(2,1)S(1)} fusion(bf16[2048,1024]{1,0:T(8,128)(2,1)} %all-gather.9.cloned.1.call-done, f32[256,2048]{1,0:T(8,128)S(1)} %get-tuple-element.138, f32[2048]{0:T(1024)S(1)} %copy-done.9, f32[256]{0:T(256)S(1)} %add_rsqrt_fusion), kind=kOutput, calls=%fused_computation.45 | convolution fusion | flops 1075576832 | bytes 6824960 | tf_op jit(solution)/shard_map/dot_general | solution.py:89
  177.8 2.1 collective-permute-start.2
  180.0 3.6 %collective-permute-start.3 = (bf16[2,256,1024]{2,1,0:T(8,128)(2,1)S(1)}, bf16[2,256,1024]{2,1,0:T(8,128)(2,1)}, u32[]{:S(2)}, u32[]{:S(2)}) collective-permute-start(bf16[2,256,1024]{2,1,0:T(8,128)(2,1)S(1)} %pad_maximum_fusion.2), channel_id=1, source_target_pairs={{1,0},{2,1},{3,2},{4,3},{5,4},{6,5},{7,6},{8,7},{9,8},{10,9},{11,1... | collective-permute-start | bytes 3145736 | tf_op jit(solution)/shard_map/ppermute | solution.py:43
  183.7 12.5 %while.17 = (s32[]{:T(128)}, bf16[1024,1024]{1,0:T(8,128)(2,1)}, s32[4,2]{0,1:T(2,128)S(1)}, bf16[4,256,1024]{2,1,0:T(8,128)(2,1)}, s32[]{:T(128)}) while((s32[]{:T(128)}, bf16[1024,1024]{1,0:T(8,128)(2,1)}, s32[4,2]{0,1:T(2,128)S(1)}, bf16[4,256,1024]{2,1,0:T(8,128)(2,1)}, s32[]{:T(128)}) %tuple.61), condition=%wide.while_cond.1, body=%wide.while_body.1.sunk | while | flops 2 | bytes 1049689 | solution.py:145
  184.3 2.5 bitcast_dynamic-update-slice_fusion.5
  187.4 2.5 bitcast_dynamic-update-slice_fusion.5
  190.5 2.6 bitcast_dynamic-update-slice_fusion.5
  193.7 2.5 bitcast_dynamic-update-slice_fusion.5
  196.2 9.0 %collective-permute-done.2 = bf16[2,256,1024]{2,1,0:T(8,128)(2,1)S(1)} collective-permute-done((bf16[2,256,1024]{2,1,0:T(8,128)(2,1)S(1)}, bf16[2,256,1024]{2,1,0:T(8,128)(2,1)S(1)}, u32[]{:S(2)}, u32[]{:S(2)}) %collective-permute-start.2) | collective-permute-done | bytes 1048608 | tf_op jit(solution)/shard_map/ppermute | solution.py:42
  205.2 1.0 copy-done.7
  206.1 2.1 pad_maximum_fusion
  208.3 12.7 %while.16 = (s32[]{:T(128)}, bf16[2,768,1024]{2,1,0:T(8,128)(2,1)S(1)}, s32[4,3]{1,0:T(4,128)S(1)}, bf16[4,2,512,1024]{3,2,1,0:T(8,128)(2,1)}, s32[]{:T(128)}) while((s32[]{:T(128)}, bf16[2,768,1024]{2,1,0:T(8,128)(2,1)S(1)}, s32[4,3]{1,0:T(4,128)S(1)}, bf16[4,2,512,1024]{3,2,1,0:T(8,128)(2,1)}, s32[]{:T(128)}) %tuple.55), condition=%wide.while_cond, body=%wide.while_body.sunk | while | flops 2 | bytes 4195425 | solution.py:142
  208.9 2.6 bitcast_dynamic-update-slice_fusion.4
  212.1 2.5 bitcast_dynamic-update-slice_fusion.4
  215.2 2.6 bitcast_dynamic-update-slice_fusion.4
  218.4 2.6 bitcast_dynamic-update-slice_fusion.4
  221.0 11.5 %copy.26 = bf16[4,2,512,1024]{2,3,0,1:T(8,128)(2,1)} copy(bf16[4,2,512,1024]{3,2,1,0:T(8,128)(2,1)} %get-tuple-element.92) | data formatting | bytes 16777216 | tf_op jit(solution)/shard_map/vmap()/gather | solution.py:142
  232.5 4.9 %slice.14 = bf16[4,1,512,1024]{3,2,1,0:T(8,128)(2,1)} slice(bf16[4,2,512,1024]{3,2,1,0:T(8,128)(2,1)} %get-tuple-element.92), slice={[0:4], [1:2], [0:512], [0:1024]} | slice | bytes 8388608 | tf_op jit(solution)/shard_map/vmap()/slice | solution.py:149
  237.4 1.2 copy-done.3
  238.6 2.2 slice.48
  240.9 6.4 %copy.25 = bf16[4,1,512,1024]{2,3,0,1:T(8,128)(2,1)} copy(bf16[4,1,512,1024]{3,2,1,0:T(8,128)(2,1)} %slice.14) | data formatting | bytes 8388608 | tf_op jit(solution)/shard_map/vmap()/slice | solution.py:149
  247.2 8.7 %fusion.67 = f32[4,8,256]{2,1,0:T(8,128)S(1)} fusion(f32[4,256,512]{2,1,0:T(8,128)S(1)} %copy-done.4, f32[8]{0:T(128)S(1)} %neg.4, pred[4,512]{1,0:T(4,128)(4,1)S(1)} %fusion.45, bf16[4,512,8,128]{1,3,2,0:T(8,128)(2,1)} %bitcast.106, bf16[4,256,1024]{2,1,0:T(8,128)(2,1)} %get-tuple-element.100), kind=kOutput, calls=%fused_computation.94 | convolution fusion | flops 1103102464 | bytes 8423456 | tf_op jit(solution)/shard_map/vmap()/sub | solution.py:61
  255.9 19.1 %fusion.16 = bf16[4,256,8,128]{1,3,2,0:T(8,128)(2,1)} fusion(bf16[4,512,8,128]{1,3,2,0:T(8,128)(2,1)} %bitcast.108, f32[4,8,256]{2,1,0:T(8,128)S(1)} %fusion.67, f32[4,256,512]{2,1,0:T(8,128)S(1)} %copy-done.4, f32[8]{0:T(128)S(1)} %neg.4, pred[4,512]{1,0:T(4,128)(4,1)S(1)} %fusion.45, bf16[4,512,8,128]{1,3,2,0:T(8,128)(2,1)} %bitcast.107, ...), kind=kOutput, calls=%fused_computation.33 | convolution fusion | flops 2181046784 | bytes 14714912 | tf_op jit(solution)/shard_map/vmap(hqk,khd->qhd)/dot_general | solution.py:63
  275.0 3.1 %copy.29 = bf16[4,256,8,128]{3,2,1,0:T(8,128)(2,1)S(1)} copy(bf16[4,256,8,128]{1,3,2,0:T(8,128)(2,1)} %fusion.16) | data formatting | bytes 4194304 | tf_op jit(solution)/shard_map/vmap(hqk,khd->qhd)/transpose | solution.py:63
  278.2 1.7 fusion.11
  (85 shorter events, 15.7 us)
Async XLA Ops:
  6.5 74.9 %copy-start = (bf16[256,1024]{1,0:T(8,128)(2,1)S(1)}, bf16[256,1024]{1,0:T(8,128)(2,1)}, u32[]{:S(2)}) copy-start(bf16[256,1024]{1,0:T(8,128)(2,1)} %param.14) | copy-start | bytes 1572868
  6.5 8.9 %copy-start.11 = (u32[32]{0:T(128)S(1)}, u32[32]{0:T(128)}, u32[]{:S(2)}) copy-start(u32[32]{0:T(128)} %constant.166) | copy-start | bytes 388
  6.5 49.5 %copy-start.8 = (s32[4]{0:T(128)S(1)}, s32[4]{0:T(128)}, u32[]{:S(2)}) copy-start(s32[4]{0:T(128)} %constant.163) | copy-start | bytes 52
  6.5 48.8 %copy-start.2 = (s32[4,2]{0,1:T(2,128)S(1)}, s32[4,2]{0,1:T(2,128)}, u32[]{:S(2)}) copy-start(s32[4,2]{0,1:T(2,128)} %param.25) | copy-start | bytes 100
  6.5 79.7 %all-gather.5.cloned.1.call-start = ((), (), s32[]{:S(2)}) async-start(), calls=%async_computation | async-start | bytes 4456448 | tf_op jit(solution)/shard_map/all_gather | solution.py:124
  7.3 115.8 %all-gather.7.cloned.1.call-start = ((), (), s32[]{:S(2)}) async-start(), calls=%async_computation.1 | async-start | bytes 4456448 | tf_op jit(solution)/shard_map/all_gather | solution.py:127
  8.0 166.2 %all-gather.9.cloned.1.call-start = ((), (), s32[]{:S(2)}) async-start(), calls=%async_computation.2 | async-start | bytes 4456448 | tf_op jit(solution)/shard_map/all_gather | solution.py:128
  11.4 68.2 %collective-permute-start = (bf16[2,256,1024]{1,2,0:T(8,128)(2,1)S(1)}, bf16[2,256,1024]{1,2,0:T(8,128)(2,1)}, u32[]{:S(2)}, u32[]{:S(2)}) collective-permute-start(bf16[2,256,1024]{1,2,0:T(8,128)(2,1)S(1)} %pad_maximum_fusion.1), channel_id=1, source_target_pairs={{0,2},{1,3},{2,4},{3,5},{4,6},{5,7},{6,8},{7,9},{8,10},{9,11},{10,... | collective-permute-start | bytes 3145736 | tf_op jit(solution)/shard_map/ppermute | solution.py:19
  16.8 62.8 %collective-permute-start.1 = (bf16[2,256,1024]{1,2,0:T(8,128)(2,1)S(1)}, bf16[2,256,1024]{1,2,0:T(8,128)(2,1)}, u32[]{:S(2)}, u32[]{:S(2)}) collective-permute-start(bf16[2,256,1024]{1,2,0:T(8,128)(2,1)S(1)} %pad_maximum_fusion.1), channel_id=1, source_target_pairs={{0,1},{1,2},{2,3},{3,4},{4,5},{5,6},{6,7},{7,8},{8,9},{9,10},{10,1... | collective-permute-start | bytes 3145736 | tf_op jit(solution)/shard_map/ppermute | solution.py:19
  86.2 36.8 %copy-start.9 = (f32[2048]{0:T(1024)S(1)}, f32[2048]{0:T(1024)}, u32[]{:S(2)}) copy-start(f32[2048]{0:T(1024)} %param.19) | copy-start | bytes 24580
  126.6 51.2 %copy-start.5 = (bf16[1,256,1024]{2,1,0:T(8,128)(2,1)}, bf16[1,256,1024]{2,1,0:T(8,128)(2,1)S(1)}, u32[]{:S(2)}) copy-start(bf16[1,256,1024]{2,1,0:T(8,128)(2,1)S(1)} %fusion.29) | copy-start | bytes 1572868
  126.6 57.0 %copy-start.10 = (f32[8]{0:T(128)S(1)}, f32[8]{0:T(128)}, u32[]{:S(2)}) copy-start(f32[8]{0:T(128)} %param.22) | copy-start | bytes 100
  177.7 2.3 copy-start.6
  177.8 27.4 %collective-permute-start.2 = (bf16[2,256,1024]{2,1,0:T(8,128)(2,1)S(1)}, bf16[2,256,1024]{2,1,0:T(8,128)(2,1)S(1)}, u32[]{:S(2)}, u32[]{:S(2)}) collective-permute-start(bf16[2,256,1024]{2,1,0:T(8,128)(2,1)S(1)} %pad_maximum_fusion.2), channel_id=1, source_target_pairs={{0,1},{1,2},{2,3},{3,4},{4,5},{5,6},{6,7},{7,8},{8,9},{9,10},{10,1... | collective-permute-start | bytes 3145736 | tf_op jit(solution)/shard_map/ppermute | solution.py:42
  180.0 26.1 %collective-permute-start.3 = (bf16[2,256,1024]{2,1,0:T(8,128)(2,1)S(1)}, bf16[2,256,1024]{2,1,0:T(8,128)(2,1)}, u32[]{:S(2)}, u32[]{:S(2)}) collective-permute-start(bf16[2,256,1024]{2,1,0:T(8,128)(2,1)S(1)} %pad_maximum_fusion.2), channel_id=1, source_target_pairs={{1,0},{2,1},{3,2},{4,3},{5,4},{6,5},{7,6},{8,7},{9,8},{10,9},{11,1... | collective-permute-start | bytes 3145736 | tf_op jit(solution)/shard_map/ppermute | solution.py:43
  205.2 1.0 copy-start.7
  232.5 6.2 %copy-start.3 = (bf16[4,2,512,1024]{2,3,0,1:T(8,128)(2,1)S(1)}, bf16[4,2,512,1024]{2,3,0,1:T(8,128)(2,1)}, u32[]{:S(2)}) copy-start(bf16[4,2,512,1024]{2,3,0,1:T(8,128)(2,1)} %copy.26) | copy-start | bytes 25165828
  240.9 6.4 %copy-start.4 = (f32[4,256,512]{2,1,0:T(8,128)S(1)}, f32[4,256,512]{2,1,0:T(8,128)}, u32[]{:S(2)}) copy-start(f32[4,256,512]{2,1,0:T(8,128)} %subtract_abs_fusion) | copy-start | bytes 6291460
  255.9 24.0 %copy-start.1 = (bf16[256,1024]{1,0:T(8,128)(2,1)S(1)}, bf16[256,1024]{1,0:T(8,128)(2,1)}, u32[]{:S(2)}) copy-start(bf16[256,1024]{1,0:T(8,128)(2,1)} %param.14) | copy-start | bytes 1572868
Sparse Core Ops, SparseCore 0:
  9.5 62.1 all-gather.4
  73.9 49.1 all-gather.6
  125.3 48.8 all-gather.8
where the time goes:
time: 289 us; the launch traced here: 286 us
  waiting for transfers between devices  91.6 us (32%)
  local copies, waits for them, and re-layouts  71.4 us (25%)
  matrix products  40.3 us (14%)
  blocking collectives  36.6 us (13%)
  between operations  14.1 us (5%)
  starting transfers between devices  11.2 us (4%)
  other arithmetic  10.9 us (4%)
  loops' own time  10.4 us (4%)
    all_gather x1, waiting for transfers between devices, on_device(): lax.all_gather(value_proj, 'ctx', axis=0, tiled=True)  47.6 us
    unnamed x1, blocking collectives  36.6 us
    all_gather x1, waiting for transfers between devices, on_device(): lax.all_gather(key_proj, 'ctx', axis=0, tiled=True)  32.9 us
    gather x24, local copies, waits for them, and re-layouts  25.2 us
    dot_general x2, matrix products, attend(): jnp.einsum('hqk,khd->qhd', weights, head_split(value_rows), preferred_ele...  19.7 us
    gather x1, local copies, waits for them, and re-layouts, coarse_block(): keys_block = lax.dynamic_slice_in_dim(near_pair, first_key, BAND, 1)  11.5 us
    slice x2, local copies, waits for them, and re-layouts, coarse_block(): keys_block[1]  11.3 us
    dot_general x3, matrix products, contract_rows(): return jnp.dot(left_side, weight_piece, preferred_element_type=jnp.float32)  10.9 us
  transfers between devices with their start and end apart: 7, of which 3 were waited for; matrix products, arithmetic and copies ran while one was open for 15% of the time, Pallas kernels for 0%

commit v1 on v0

v1 whole, which is shorter than its diff:
```python
import functools

import jax
import jax.numpy as jnp
from jax import lax
from jax.experimental import pallas as pl
from jax.experimental.pallas import tpu as pltpu
from jax.sharding import PartitionSpec as P

HEADS = 8
HEAD_DIM = 128
W = 512
BAND = 512
CB = 256


NEG_FILL = -1e30


def passed_along(array, axis, by):
    length = lax.axis_size(axis)
    pairs = [(i, i + by) for i in range(length) if 0 <= i + by < length]
    return lax.ppermute(array, axis, pairs)


def with_halo(array, sides, width):
    for axis, dim in sides:
        size, length = (lax.axis_size(axis), array.shape[dim])
        up = [(i, (i + 1) % size) for i in range(size - 1)]
        down = [(j, i) for i, j in up]
        last = lax.slice_in_dim(array, length - width, length, axis=dim)
        first = lax.slice_in_dim(array, 0, width, axis=dim)
        before = lax.ppermute(last, axis, up)
        after = lax.ppermute(first, axis, down)
        array = jnp.concatenate([before, array, after], axis=dim)
    return array


def head_split(matrix):
    return matrix.reshape(matrix.shape[0], HEADS, HEAD_DIM)


def attend(queries, key_rows, value_rows, allowed, time_bias):
    scores = jnp.einsum(
        "qhd,khd->hqk",
        head_split(queries),
        head_split(key_rows),
        preferred_element_type=jnp.float32,
    ) * HEAD_DIM ** (-0.5)
    scores = jnp.where(allowed[None], scores + time_bias, NEG_FILL)
    largest = jnp.max(scores, axis=2, keepdims=True)
    exponent = jnp.exp(scores - largest)
    weights = (exponent / jnp.sum(exponent, axis=2, keepdims=True)).astype(jnp.bfloat16)
    blended = jnp.einsum(
        "hqk,khd->qhd", weights, head_split(value_rows), preferred_element_type=jnp.float32
    )
    return blended.reshape(queries.shape[0], -1)


def normalize(sem_stream, norm_gain):
    scaled = sem_stream * lax.rsqrt(
        jnp.mean(sem_stream * sem_stream, axis=1, keepdims=True) + 1e-05
    )
    return (scaled * norm_gain[None, :]).astype(jnp.bfloat16)


def contract_rows(left_side, weight_piece):
    return jnp.dot(left_side, weight_piece, preferred_element_type=jnp.float32)


def coarse_kernel(prm, slopes_ref, q_ref, k_ref, v_ref, o_ref, *, blocks, near_rows):
    n = pl.program_id(0)
    band_low = prm[2 * n]
    band_high = prm[2 * n + 1]
    stream_start = prm[2 * blocks]
    live_count = prm[2 * blocks + 1]
    base_row = prm[2 * blocks + 2]
    rows = n * CB + lax.broadcasted_iota(jnp.int32, (CB, 1), 0)
    timing = ((stream_start + rows) // 2).astype(jnp.float32) * (2.0 / 3.0)
    key_global = base_row + lax.broadcasted_iota(jnp.int32, (1, near_rows), 1)
    inside = (key_global >= band_low) & (key_global < band_high)
    distance = jnp.abs(timing - key_global.astype(jnp.float32))
    live_rows = rows < live_count
    for h in range(HEADS):
        cols = slice(h * HEAD_DIM, (h + 1) * HEAD_DIM)
        scores = lax.dot_general(
            q_ref[:, cols], k_ref[:, cols], (((1,), (1,)), ((), ())),
            preferred_element_type=jnp.float32,
        ) * HEAD_DIM ** (-0.5)
        time_bias = distance * (-slopes_ref[h] / BAND)
        scores = jnp.where(inside, scores + time_bias, NEG_FILL)
        largest = jnp.max(scores, axis=1, keepdims=True)
        exponent = jnp.exp(scores - largest)
        total = jnp.sum(exponent, axis=1, keepdims=True)
        weights = (exponent * (1.0 / total)).astype(jnp.bfloat16)
        blended = jnp.dot(weights, v_ref[:, cols], preferred_element_type=jnp.float32)
        o_ref[:, cols] = jnp.where(live_rows, blended, 0.0).astype(jnp.bfloat16)


def coarse_attention(coarse_queries, near_pair, params, slopes):
    slots, width = coarse_queries.shape
    blocks = slots // CB
    near_rows = near_pair.shape[1]
    kernel = functools.partial(coarse_kernel, blocks=blocks, near_rows=near_rows)
    grid_spec = pltpu.PrefetchScalarGridSpec(
        num_scalar_prefetch=1,
        grid=(blocks,),
        in_specs=[
            pl.BlockSpec(memory_space=pltpu.SMEM),
            pl.BlockSpec((CB, width), lambda n, prm: (n, 0)),
            pl.BlockSpec((None, near_rows, width), lambda n, prm: (0, 0, 0)),
            pl.BlockSpec((None, near_rows, width), lambda n, prm: (1, 0, 0)),
        ],
        out_specs=pl.BlockSpec((CB, width), lambda n, prm: (n, 0)),
    )
    return pl.pallas_call(
        kernel,
        grid_spec=grid_spec,
        out_shape=jax.ShapeDtypeStruct((slots, width), jnp.bfloat16),
        compiler_params=pltpu.CompilerParams(dimension_semantics=("arbitrary",)),
    )(params, slopes, coarse_queries, near_pair, near_pair)


def on_device(
    sem_queries,
    sem_keys,
    sem_values,
    sem_inputs,
    out_proj,
    norm_gain,
    key_proj,
    value_proj,
    slopes,
    coarse_queries,
    counts,
    band_bounds,
):
    rows_here = sem_queries.shape[0]
    device_index = lax.axis_index("ctx")
    ctx_size = lax.axis_size("ctx")
    full_out_proj = lax.all_gather(out_proj, "ctx", axis=0, tiled=True)
    cross_rows, cross_cols = key_proj.shape
    stacked_proj = jnp.stack([key_proj, value_proj])
    gathered_proj = lax.all_gather(stacked_proj, "ctx", axis=1, tiled=True)
    own_pair = jnp.stack([sem_keys, sem_values])
    reach_shards = (W - 1 + rows_here - 1) // rows_here
    earlier = []
    for distance in range(1, reach_shards + 1):
        earlier.insert(0, passed_along(own_pair, "ctx", distance))
    window_pair = jnp.concatenate(earlier + [own_pair], axis=1)
    query_pos = jnp.arange(rows_here, dtype=jnp.int32)
    key_pos = jnp.arange(window_pair.shape[1], dtype=jnp.int32)
    key_lag = query_pos[:, None] + reach_shards * rows_here - key_pos[None, :]
    key_global = device_index * rows_here - reach_shards * rows_here + key_pos
    allowed = (key_lag >= 0) & (key_lag < W) & (key_global[None, :] >= 0)
    sem_att = attend(sem_queries, window_pair[0], window_pair[1], allowed, 0.0).astype(jnp.bfloat16)
    projected = contract_rows(sem_att, full_out_proj)
    sem_stream = sem_inputs.astype(jnp.float32) + projected
    normed = normalize(sem_stream, norm_gain)
    key_sum = contract_rows(normed, gathered_proj[0])
    value_sum = contract_rows(normed, gathered_proj[1])
    cross_keys = key_sum.astype(jnp.bfloat16)
    cross_values = value_sum.astype(jnp.bfloat16)
    every_count = lax.all_gather(counts, "ctx", axis=0, tiled=True)
    earlier_index = jnp.arange(ctx_size, dtype=jnp.int32) < device_index
    stream_start = jnp.sum(jnp.where(earlier_index, every_count, 0)).astype(jnp.int32)
    near_pair = with_halo(jnp.stack([cross_keys, cross_values]), (("ctx", 1),), rows_here)
    base_row = (device_index - 1) * rows_here
    params = jnp.concatenate(
        [band_bounds.reshape(-1).astype(jnp.int32),
         jnp.stack([stream_start, counts[0], base_row]).astype(jnp.int32)]
    )
    return coarse_attention(coarse_queries, near_pair, params, slopes)


def solution(mesh):
    return jax.shard_map(
        on_device,
        mesh=mesh,
        in_specs=(
            P(("groups", "ctx"), None),
            P(("groups", "ctx"), None),
            P(("groups", "ctx"), None),
            P(("groups", "ctx"), None),
            P("ctx", None),
            P(),
            P("ctx", None),
            P("ctx", None),
            P(),
            P(("groups", "ctx"), None),
            P(("groups", "ctx")),
            P(("groups", "ctx"), None),
        ),
        out_specs=P(("groups", "ctx"), None),
        check_vma=False,
    )
```

time: 289 us -> 227 us (0.79)
  the two profiles are of different devices: /device:TPU:20 before, /device:TPU:0 now
where the time goes in v1:
time: 227 us; the launch traced here: 226 us
  waiting for transfers between devices  120 us (53%)
  blocking collectives  27.6 us (12%)
  Pallas kernels  22.4 us (10%)
  between operations  14.2 us (6%)
  starting transfers between devices  12.8 us (6%)
  other arithmetic  12.4 us (5%)
  matrix products  12.2 us (5%)
  local copies, waits for them, and re-layouts  5.23 us (2%)
    all_gather x1, waiting for transfers between devices, on_device(): gathered_proj = lax.all_gather(stacked_proj, 'ctx', axis=1, tiled=True)  71.2 us
    unnamed x1, blocking collectives  27.6 us
    all_gather x1, waiting for transfers between devices, on_device(): full_out_proj = lax.all_gather(out_proj, 'ctx', axis=0, tiled=True)  25 us
    ppermute x2, waiting for transfers between devices, passed_along(): return lax.ppermute(array, axis, pairs)  22.6 us
    pallas_call x1, Pallas kernels, coarse_attention(): pl.pallas_call(kernel, grid_spec=grid_spec, out_shape=jax.ShapeDtypeStruc...  22.4 us
    dot_general x3, matrix products, contract_rows(): return jnp.dot(left_side, weight_piece, preferred_element_type=jnp.float32)  10.5 us
    ppermute x2, starting transfers between devices, passed_along(): return lax.ppermute(array, axis, pairs)  8.37 us
    unnamed x18, local copies, waits for them, and re-layouts  4.94 us
  transfers between devices with their start and end apart: 6, of which 3 were waited for; matrix products, arithmetic and copies ran while one was open for 8% of the time, Pallas kernels for 0%

profile of v1, /device:TPU:0, one launch (start us, length us, event | category | flops | bytes accessed | tf_op | source)
XLA Modules:
  0.0 226.4 jit_solution(3093854944225406929)
XLA Ops:
  6.5 0.0 copy-start
  6.5 0.0 all-gather.3.cloned.1.call-start
  6.5 0.7 all-gather.3.cloned.1.call-update
  7.3 0.0 all-gather.5.cloned.1.call-start
  7.3 1.9 pad_maximum_fusion.3
  9.2 0.0 all-gather.5.cloned.1.call-update
  9.2 1.2 copy.18
  10.5 1.2 copy.19
  11.7 0.1 pad_maximum_fusion.1
  11.8 5.9 %collective-permute-start = (bf16[2,256,1024]{1,2,0:T(8,128)(2,1)S(1)}, bf16[2,256,1024]{1,2,0:T(8,128)(2,1)}, u32[]{:S(2)}, u32[]{:S(2)}) collective-permute-start(bf16[2,256,1024]{1,2,0:T(8,128)(2,1)S(1)} %pad_maximum_fusion.1), channel_id=1, source_target_pairs={{0,2},{1,3},{2,4},{3,5},{4,6},{5,7},{6,8},{7,9},{8,10},{9,11},{10,... | collective-permute-start | bytes 3145736 | tf_op jit(solution)/shard_map/ppermute | solution.py:23
  17.7 2.5 %collective-permute-start.1 = (bf16[2,256,1024]{1,2,0:T(8,128)(2,1)S(1)}, bf16[2,256,1024]{1,2,0:T(8,128)(2,1)}, u32[]{:S(2)}, u32[]{:S(2)}) collective-permute-start(bf16[2,256,1024]{1,2,0:T(8,128)(2,1)S(1)} %pad_maximum_fusion.1), channel_id=1, source_target_pairs={{0,1},{1,2},{2,3},{3,4},{4,5},{5,6},{6,7},{7,8},{8,9},{9,10},{10,1... | collective-permute-start | bytes 3145736 | tf_op jit(solution)/shard_map/ppermute | solution.py:23
  20.2 0.2 fusion.16
  20.4 22.6 %collective-permute-done = bf16[2,256,1024]{1,2,0:T(8,128)(2,1)} collective-permute-done((bf16[2,256,1024]{1,2,0:T(8,128)(2,1)S(1)}, bf16[2,256,1024]{1,2,0:T(8,128)(2,1)}, u32[]{:S(2)}, u32[]{:S(2)}) %collective-permute-start) | collective-permute-done | bytes 1048608 | tf_op jit(solution)/shard_map/ppermute | solution.py:23
  43.1 0.0 collective-permute-done.1
  43.1 2.1 maximum_maximum_fusion
  45.1 0.2 fusion.23
  45.4 0.0 copy-done
  45.4 1.0 fusion.17
  46.4 3.1 %fusion.24 = (f32[8,256]{1,0:T(8,128)S(1)}, f32[8,256,768]{1,2,0:T(8,128)S(1)}) fusion(f32[8,768,256]{2,1,0:T(8,128)S(1)} %fusion.17, pred[256,768]{0,1:T(8,128)(4,1)S(1)} %fusion.16), kind=kOutput, calls=%fused_computation.43 | output fusion | flops 9437951 | bytes 12787712 | tf_op jit(solution)/shard_map/sub | solution.py:52
  49.5 0.6 fusion.8
  50.1 25.0 %all-gather.3.cloned.1.call-done = bf16[1024,2048]{1,0:T(8,128)(2,1)} async-done(((bf16[64,2048]{1,0:T(8,128)(2,1)}), bf16[1024,2048]{1,0:T(8,128)(2,1)}) %all-gather.3.cloned.1.call-update) | async-done | bytes 4194320 | tf_op jit(solution)/shard_map/all_gather | solution.py:141
  75.1 0.0 copy-start.4
  75.1 3.9 %multiply_reduce_fusion = (f32[256]{0:T(256)S(1)}, f32[256,2048]{1,0:T(8,128)S(1)}) fusion(bf16[256,1024]{0,1:T(8,128)(2,1)S(1)} %bitcast.57, bf16[1024,2048]{1,0:T(8,128)(2,1)} %all-gather.3.cloned.1.call-done, bf16[256,2048]{1,0:T(8,128)(2,1)} %param.15), kind=kOutput, calls=%fused_computation.17 | convolution fusion | flops 1075838720 | bytes 7865344 | tf_op jit(solution)/shard_map/dot_general | solution.py:68
  79.0 0.0 copy-start.1
  79.0 71.2 %all-gather.5.cloned.1.call-done = bf16[2,2048,1024]{2,1,0:T(8,128)(2,1)} async-done(((bf16[2,128,1024]{2,1,0:T(8,128)(2,1)}), bf16[2,2048,1024]{2,1,0:T(8,128)(2,1)}) %all-gather.5.cloned.1.call-update) | async-done | bytes 8388624 | tf_op jit(solution)/shard_map/all_gather | solution.py:144
  150.2 0.0 copy-done.1
  150.2 0.0 copy-done.4
  150.2 0.0 copy-start.3
  150.2 3.6 %fusion.12 = bf16[1,256,1024]{2,1,0:T(8,128)(2,1)S(1)} fusion(bf16[2,2048,1024]{2,1,0:T(8,128)(2,1)} %all-gather.5.cloned.1.call-done, f32[256,2048]{1,0:T(8,128)S(1)} %get-tuple-element.10, f32[2048]{0:T(1024)S(1)} %copy-done.4, f32[256]{0:T(256)S(1)} %add_rsqrt_fusion), kind=kOutput, calls=%fused_computation.22 | convolution fusion | flops 1075576832 | bytes 6824960 | tf_op jit(solution)/shard_map/dot_general | solution.py:68
  153.9 1.0 copy-done.3
  154.9 0.0 copy-start.5
  154.9 3.0 %fusion.11 = bf16[1,256,1024]{2,1,0:T(8,128)(2,1)S(1)} fusion(bf16[2,2048,1024]{2,1,0:T(8,128)(2,1)S(1)} %copy-done.3, f32[256,2048]{1,0:T(8,128)} %copy-done.1, f32[2048]{0:T(1024)S(1)} %copy-done.4, f32[256]{0:T(256)S(1)} %add_rsqrt_fusion), kind=kOutput, calls=%fused_computation.21 | convolution fusion | flops 1075576832 | bytes 6824960 | tf_op jit(solution)/shard_map/dot_general | solution.py:68
  157.9 0.1 pad_maximum_fusion.2
  158.0 3.1 %collective-permute-start.2 = (bf16[2,256,1024]{2,1,0:T(8,128)(2,1)S(1)}, bf16[2,256,1024]{2,1,0:T(8,128)(2,1)}, u32[]{:S(2)}, u32[]{:S(2)}) collective-permute-start(bf16[2,256,1024]{2,1,0:T(8,128)(2,1)S(1)} %pad_maximum_fusion.2), channel_id=1, source_target_pairs={{0,1},{1,2},{2,3},{3,4},{4,5},{5,6},{6,7},{7,8},{8,9},{9,10},{10,1... | collective-permute-start | bytes 3145736 | tf_op jit(solution)/shard_map/ppermute | solution.py:33
  161.1 1.3 collective-permute-start.3
  163.1 0.0 copy-done.5
  163.1 0.6 dynamic-slice
  163.7 0.8 dynamic-update-slice
  164.4 27.6 %all-reduce = s32[16]{0:T(128)S(1)} all-reduce(s32[16]{0:T(128)S(1)} %dynamic-update-slice), channel_id=1, replica_groups=mesh['groups'=2,'ctx'=16] {'ctx'}, use_global_device_ids=true, to_apply=%add | all-reduce | flops 16 | bytes 128
  192.0 0.0 copy-done.2
  192.0 0.1 copy.17
  192.1 0.1 reshape.67
  192.2 0.6 fusion.20
  192.8 1.2 pad_add_fusion.prm
  194.0 0.0 collective-permute-done.2
  194.0 0.0 collective-permute-done.3
  194.0 3.1 %pad_maximum_fusion.k_ref.v_ref = bf16[2,768,1024]{2,1,0:T(8,128)(2,1)} fusion(bf16[2,256,1024]{2,1,0:T(8,128)(2,1)} %collective-permute-done.3, bf16[1,256,1024]{2,1,0:T(8,128)(2,1)S(1)} %fusion.11, bf16[1,256,1024]{2,1,0:T(8,128)(2,1)S(1)} %fusion.12, bf16[2,256,1024]{2,1,0:T(8,128)(2,1)} %collective-permute-done.2), kind=kLoop, calls=%fused_computation.10 | loop fusion | flops 12582912 | bytes 6291456 | tf_op jit(solution)/shard_map/concatenate | solution.py:35
  197.1 22.4 %shard_map.118 = bf16[1024,1024]{1,0:T(8,128)(2,1)} custom-call(s32[11]{0:T(128)} %pad_add_fusion.prm, f32[8]{0:T(128)} %slopes_ref.1, bf16[1024,1024]{1,0:T(8,128)(2,1)} %q_ref.1, bf16[2,768,1024]{2,1,0:T(8,128)(2,1)} %pad_maximum_fusion.k_ref.v_ref, bf16[2,768,1024]{2,1,0:T(8,128)(2,1)} %pad_maximum_fusion.k_ref.v_ref), custom_call_target="tpu_custom_call" | custom-call | tf_op jit(solution)/shard_map/pallas_call | solution.py:116
  (5 shorter events, 0.0 us)
Async XLA Ops:
  6.5 38.8 %copy-start = (bf16[256,1024]{1,0:T(8,128)(2,1)S(1)}, bf16[256,1024]{1,0:T(8,128)(2,1)}, u32[]{:S(2)}) copy-start(bf16[256,1024]{1,0:T(8,128)(2,1)} %param.12) | copy-start | bytes 1572868
  6.5 68.6 %all-gather.3.cloned.1.call-start = ((), (), s32[]{:S(2)}) async-start(), calls=%async_computation | async-start | bytes 4456448 | tf_op jit(solution)/shard_map/all_gather | solution.py:141
  7.3 143.0 %all-gather.5.cloned.1.call-start = ((), (), s32[]{:S(2)}) async-start(), calls=%async_computation.1 | async-start | bytes 8912896 | tf_op jit(solution)/shard_map/all_gather | solution.py:144
  11.8 31.2 %collective-permute-start = (bf16[2,256,1024]{1,2,0:T(8,128)(2,1)S(1)}, bf16[2,256,1024]{1,2,0:T(8,128)(2,1)}, u32[]{:S(2)}, u32[]{:S(2)}) collective-permute-start(bf16[2,256,1024]{1,2,0:T(8,128)(2,1)S(1)} %pad_maximum_fusion.1), channel_id=1, source_target_pairs={{0,2},{1,3},{2,4},{3,5},{4,6},{5,7},{6,8},{7,9},{8,10},{9,11},{10,... | collective-permute-start | bytes 3145736 | tf_op jit(solution)/shard_map/ppermute | solution.py:23
  17.7 25.4 %collective-permute-start.1 = (bf16[2,256,1024]{1,2,0:T(8,128)(2,1)S(1)}, bf16[2,256,1024]{1,2,0:T(8,128)(2,1)}, u32[]{:S(2)}, u32[]{:S(2)}) collective-permute-start(bf16[2,256,1024]{1,2,0:T(8,128)(2,1)S(1)} %pad_maximum_fusion.1), channel_id=1, source_target_pairs={{0,1},{1,2},{2,3},{3,4},{4,5},{5,6},{6,7},{7,8},{8,9},{9,10},{10,1... | collective-permute-start | bytes 3145736 | tf_op jit(solution)/shard_map/ppermute | solution.py:23
  75.1 75.1 %copy-start.4 = (f32[2048]{0:T(1024)S(1)}, f32[2048]{0:T(1024)}, u32[]{:S(2)}) copy-start(f32[2048]{0:T(1024)} %param.17) | copy-start | bytes 24580
  79.0 71.3 %copy-start.1 = (f32[256,2048]{1,0:T(8,128)}, f32[256,2048]{1,0:T(8,128)S(1)}, u32[]{:S(2)}) copy-start(f32[256,2048]{1,0:T(8,128)S(1)} %get-tuple-element.10) | copy-start | bytes 6291460
  150.2 4.6 %copy-start.3 = (bf16[2,2048,1024]{2,1,0:T(8,128)(2,1)S(1)}, bf16[2,2048,1024]{2,1,0:T(8,128)(2,1)}, u32[]{:S(2)}) copy-start(bf16[2,2048,1024]{2,1,0:T(8,128)(2,1)} %all-gather.5.cloned.1.call-done) | copy-start | bytes 25165828
  154.9 8.2 %copy-start.5 = (u32[32]{0:T(128)S(1)}, u32[32]{0:T(128)}, u32[]{:S(2)}) copy-start(u32[32]{0:T(128)} %constant.36) | copy-start | bytes 388
  154.9 37.1 %copy-start.2 = (s32[4,2]{0,1:T(2,128)S(1)}, s32[4,2]{0,1:T(2,128)}, u32[]{:S(2)}) copy-start(s32[4,2]{0,1:T(2,128)} %param.23) | copy-start | bytes 100
  158.0 36.0 %collective-permute-start.2 = (bf16[2,256,1024]{2,1,0:T(8,128)(2,1)S(1)}, bf16[2,256,1024]{2,1,0:T(8,128)(2,1)}, u32[]{:S(2)}, u32[]{:S(2)}) collective-permute-start(bf16[2,256,1024]{2,1,0:T(8,128)(2,1)S(1)} %pad_maximum_fusion.2), channel_id=1, source_target_pairs={{0,1},{1,2},{2,3},{3,4},{4,5},{5,6},{6,7},{7,8},{8,9},{9,10},{10,1... | collective-permute-start | bytes 3145736 | tf_op jit(solution)/shard_map/ppermute | solution.py:33
  161.1 32.9 %collective-permute-start.3 = (bf16[2,256,1024]{2,1,0:T(8,128)(2,1)S(1)}, bf16[2,256,1024]{2,1,0:T(8,128)(2,1)}, u32[]{:S(2)}, u32[]{:S(2)}) collective-permute-start(bf16[2,256,1024]{2,1,0:T(8,128)(2,1)S(1)} %pad_maximum_fusion.2), channel_id=1, source_target_pairs={{1,0},{2,1},{3,2},{4,3},{5,4},{6,5},{7,6},{8,7},{9,8},{10,9},{11,1... | collective-permute-start | bytes 3145736 | tf_op jit(solution)/shard_map/ppermute | solution.py:34
Sparse Core Ops, SparseCore 0:
  9.5 65.5 all-gather.2
  77.3 72.8 all-gather.4

commit v2 on v1

--- a/solution.py
+++ b/solution.py
@@ -139,6 +139,8 @@
     device_index = lax.axis_index("ctx")
     ctx_size = lax.axis_size("ctx")
     full_out_proj = lax.all_gather(out_proj, "ctx", axis=0, tiled=True)
+    every_count = lax.all_gather(counts, "ctx", axis=0, tiled=True)
+    every_count, sem_queries = lax.optimization_barrier((every_count, sem_queries))
     cross_rows, cross_cols = key_proj.shape
     stacked_proj = jnp.stack([key_proj, value_proj])
     gathered_proj = lax.all_gather(stacked_proj, "ctx", axis=1, tiled=True)
@@ -161,7 +163,6 @@
     value_sum = contract_rows(normed, gathered_proj[1])
     cross_keys = key_sum.astype(jnp.bfloat16)
     cross_values = value_sum.astype(jnp.bfloat16)
-    every_count = lax.all_gather(counts, "ctx", axis=0, tiled=True)
     earlier_index = jnp.arange(ctx_size, dtype=jnp.int32) < device_index
     stream_start = jnp.sum(jnp.where(earlier_index, every_count, 0)).astype(jnp.int32)
     near_pair = with_halo(jnp.stack([cross_keys, cross_values]), (("ctx", 1),), rows_here)

time: 227 us -> 217 us (0.956)
  the two profiles are of different devices: /device:TPU:0 before, /device:TPU:20 now
where the time goes in v2:
time: 217 us; the launch traced here: 215 us
  waiting for transfers between devices  99.7 us (46%)
  blocking collectives  37.3 us (17%)
  Pallas kernels  22.4 us (10%)
  between operations  14.2 us (7%)
  matrix products  12.7 us (6%)
  other arithmetic  11.9 us (5%)
  starting transfers between devices  11.1 us (5%)
  local copies, waits for them, and re-layouts  5.23 us (2%)
    all_gather x1, waiting for transfers between devices, on_device(): gathered_proj = lax.all_gather(stacked_proj, 'ctx', axis=1, tiled=True)  71.3 us
    optimization_barrier x1, blocking collectives, on_device(): lax.optimization_barrier((every_count, sem_queries))  37.3 us
    pallas_call x1, Pallas kernels, coarse_attention(): pl.pallas_call(kernel, grid_spec=grid_spec, out_shape=jax.ShapeDtypeStruc...  22.4 us
    ppermute x1, waiting for transfers between devices, with_halo(): before = lax.ppermute(last, axis, up)  19.6 us
    dot_general x3, matrix products, contract_rows(): return jnp.dot(left_side, weight_piece, preferred_element_type=jnp.float32)  10.5 us
    ppermute x2, waiting for transfers between devices, passed_along(): return lax.ppermute(array, axis, pairs)  7.26 us
    ppermute x2, starting transfers between devices, passed_along(): return lax.ppermute(array, axis, pairs)  5.35 us
    unnamed x18, local copies, waits for them, and re-layouts  4.94 us
  transfers between devices with their start and end apart: 6, of which 4 were waited for; matrix products, arithmetic and copies ran while one was open for 9% of the time, Pallas kernels for 0%

profile of v2, /device:TPU:20, one launch (start us, length us, event | category | flops | bytes accessed | tf_op | source)
XLA Modules:
  0.0 214.6 jit_solution(14680331633394160137)
XLA Ops:
  6.5 0.0 copy-start
  6.5 0.0 copy-start.5
  6.5 0.0 all-gather.3.cloned.1.call-start
  6.5 0.7 all-gather.3.cloned.1.call-update
  7.3 0.0 all-gather.5.cloned.1.call-start
  7.3 1.9 pad_maximum_fusion.3
  9.2 0.0 all-gather.5.cloned.1.call-update
  9.2 1.2 copy.17
  10.5 1.2 copy.18
  11.7 0.1 pad_maximum_fusion.1
  11.8 3.4 %collective-permute-start = (bf16[2,256,1024]{1,2,0:T(8,128)(2,1)S(1)}, bf16[2,256,1024]{1,2,0:T(8,128)(2,1)}, u32[]{:S(2)}, u32[]{:S(2)}) collective-permute-start(bf16[2,256,1024]{1,2,0:T(8,128)(2,1)S(1)} %pad_maximum_fusion.1), channel_id=1, source_target_pairs={{0,2},{1,3},{2,4},{3,5},{4,6},{5,7},{6,8},{7,9},{8,10},{9,11},{10,... | collective-permute-start | bytes 3145736 | tf_op jit(solution)/shard_map/ppermute | solution.py:23
  15.3 1.9 collective-permute-start.1
  17.9 0.0 copy-done.5
  17.9 0.6 dynamic-slice
  18.4 0.8 dynamic-update-slice
  19.2 37.3 %all-reduce = s32[16]{0:T(128)S(1)} all-reduce(s32[16]{0:T(128)S(1)} %dynamic-update-slice), channel_id=1, replica_groups=mesh['groups'=2,'ctx'=16] {'ctx'}, use_global_device_ids=true, to_apply=%add | all-reduce | flops 16 | bytes 128 | tf_op jit(solution)/shard_map/optimization_barrier | solution.py:143
  56.5 0.3 fusion.16
  56.8 0.0 collective-permute-done
  56.8 7.3 %collective-permute-done.1 = bf16[2,256,1024]{1,2,0:T(8,128)(2,1)} collective-permute-done((bf16[2,256,1024]{1,2,0:T(8,128)(2,1)S(1)}, bf16[2,256,1024]{1,2,0:T(8,128)(2,1)}, u32[]{:S(2)}, u32[]{:S(2)}) %collective-permute-start.1) | collective-permute-done | bytes 1048608 | tf_op jit(solution)/shard_map/ppermute | solution.py:23
  64.1 1.7 maximum_maximum_fusion
  65.7 0.2 fusion.23
  65.9 0.0 copy-done
  65.9 1.0 fusion.17
  66.9 2.9 %fusion.24 = (f32[8,256]{1,0:T(8,128)S(1)}, f32[8,256,768]{2,1,0:T(8,128)S(1)}) fusion(f32[8,256,768]{2,1,0:T(8,128)S(1)} %fusion.17, pred[256,768]{1,0:T(8,128)(4,1)S(1)} %fusion.16), kind=kOutput, calls=%fused_computation.43 | output fusion | flops 9437951 | bytes 12787712 | tf_op jit(solution)/shard_map/sub | solution.py:52
  69.8 1.3 fusion.8
  71.1 0.8 all-gather.3.cloned.1.call-done
  71.9 0.0 copy-start.4
  71.9 3.9 %multiply_reduce_fusion = (f32[256]{0:T(256)S(1)}, f32[256,2048]{1,0:T(8,128)S(1)}) fusion(bf16[256,1024]{0,1:T(8,128)(2,1)S(1)} %bitcast.46, bf16[1024,2048]{1,0:T(8,128)(2,1)} %all-gather.3.cloned.1.call-done, bf16[256,2048]{1,0:T(8,128)(2,1)} %param.15), kind=kOutput, calls=%fused_computation.17 | convolution fusion | flops 1075838720 | bytes 7865344 | tf_op jit(solution)/shard_map/dot_general | solution.py:68
  75.8 0.0 copy-start.1
  75.8 71.3 %all-gather.5.cloned.1.call-done = bf16[2,2048,1024]{2,1,0:T(8,128)(2,1)} async-done(((bf16[2,128,1024]{2,1,0:T(8,128)(2,1)}), bf16[2,2048,1024]{2,1,0:T(8,128)(2,1)}) %all-gather.5.cloned.1.call-update) | async-done | bytes 8388624 | tf_op jit(solution)/shard_map/all_gather | solution.py:146
  147.1 0.0 copy-done.1
  147.1 0.0 copy-done.4
  147.1 0.0 copy-start.3
  147.1 3.6 %fusion.12 = bf16[1,256,1024]{2,1,0:T(8,128)(2,1)S(1)} fusion(bf16[2,2048,1024]{2,1,0:T(8,128)(2,1)} %all-gather.5.cloned.1.call-done, f32[256,2048]{1,0:T(8,128)S(1)} %get-tuple-element.14, f32[2048]{0:T(1024)S(1)} %copy-done.4, f32[256]{0:T(256)S(1)} %add_rsqrt_fusion), kind=kOutput, calls=%fused_computation.22 | convolution fusion | flops 1075576832 | bytes 6824960 | tf_op jit(solution)/shard_map/dot_general | solution.py:68
  150.7 1.0 copy-done.3
  151.7 3.0 %fusion.11 = bf16[1,256,1024]{2,1,0:T(8,128)(2,1)S(1)} fusion(bf16[2,2048,1024]{2,1,0:T(8,128)(2,1)S(1)} %copy-done.3, f32[256,2048]{1,0:T(8,128)} %copy-done.1, f32[2048]{0:T(1024)S(1)} %copy-done.4, f32[256]{0:T(256)S(1)} %add_rsqrt_fusion), kind=kOutput, calls=%fused_computation.21 | convolution fusion | flops 1075576832 | bytes 6824960 | tf_op jit(solution)/shard_map/dot_general | solution.py:68
  154.7 0.1 pad_maximum_fusion.2
  154.8 2.2 %collective-permute-start.2 = (bf16[2,256,1024]{2,1,0:T(8,128)(2,1)S(1)}, bf16[2,256,1024]{2,1,0:T(8,128)(2,1)}, u32[]{:S(2)}, u32[]{:S(2)}) collective-permute-start(bf16[2,256,1024]{2,1,0:T(8,128)(2,1)S(1)} %pad_maximum_fusion.2), channel_id=1, source_target_pairs={{0,1},{1,2},{2,3},{3,4},{4,5},{5,6},{6,7},{7,8},{8,9},{9,10},{10,1... | collective-permute-start | bytes 3145736 | tf_op jit(solution)/shard_map/ppermute | solution.py:33
  157.0 3.6 %collective-permute-start.3 = (bf16[2,256,1024]{2,1,0:T(8,128)(2,1)S(1)}, bf16[2,256,1024]{2,1,0:T(8,128)(2,1)}, u32[]{:S(2)}, u32[]{:S(2)}) collective-permute-start(bf16[2,256,1024]{2,1,0:T(8,128)(2,1)S(1)} %pad_maximum_fusion.2), channel_id=1, source_target_pairs={{1,0},{2,1},{3,2},{4,3},{5,4},{6,5},{7,6},{8,7},{9,8},{10,9},{11,1... | collective-permute-start | bytes 3145736 | tf_op jit(solution)/shard_map/ppermute | solution.py:34
  160.6 0.0 copy-done.2
  160.6 0.1 copy.16
  160.7 0.1 reshape.67
  160.8 0.6 fusion.20
  161.4 1.2 pad_add_fusion.prm
  162.6 19.6 %collective-permute-done.2 = bf16[2,256,1024]{2,1,0:T(8,128)(2,1)} collective-permute-done((bf16[2,256,1024]{2,1,0:T(8,128)(2,1)S(1)}, bf16[2,256,1024]{2,1,0:T(8,128)(2,1)}, u32[]{:S(2)}, u32[]{:S(2)}) %collective-permute-start.2) | collective-permute-done | bytes 1048608 | tf_op jit(solution)/shard_map/ppermute | solution.py:33
  182.3 0.0 collective-permute-done.3
  182.3 3.1 %pad_maximum_fusion.k_ref.v_ref = bf16[2,768,1024]{2,1,0:T(8,128)(2,1)} fusion(bf16[2,256,1024]{2,1,0:T(8,128)(2,1)} %collective-permute-done.3, bf16[1,256,1024]{2,1,0:T(8,128)(2,1)S(1)} %fusion.11, bf16[1,256,1024]{2,1,0:T(8,128)(2,1)S(1)} %fusion.12, bf16[2,256,1024]{2,1,0:T(8,128)(2,1)} %collective-permute-done.2), kind=kLoop, calls=%fused_computation.10 | loop fusion | flops 12582912 | bytes 6291456 | tf_op jit(solution)/shard_map/concatenate | solution.py:35
  185.3 22.4 %shard_map.118 = bf16[1024,1024]{1,0:T(8,128)(2,1)} custom-call(s32[11]{0:T(128)} %pad_add_fusion.prm, f32[8]{0:T(128)} %slopes_ref.1, bf16[1024,1024]{1,0:T(8,128)(2,1)} %q_ref.1, bf16[2,768,1024]{2,1,0:T(8,128)(2,1)} %pad_maximum_fusion.k_ref.v_ref, bf16[2,768,1024]{2,1,0:T(8,128)(2,1)} %pad_maximum_fusion.k_ref.v_ref), custom_call_target="tpu_custom_call" | custom-call | tf_op jit(solution)/shard_map/pallas_call | solution.py:116
  (5 shorter events, 0.0 us)
Async XLA Ops:
  6.5 59.4 %copy-start = (bf16[256,1024]{1,0:T(8,128)(2,1)S(1)}, bf16[256,1024]{1,0:T(8,128)(2,1)}, u32[]{:S(2)}) copy-start(bf16[256,1024]{1,0:T(8,128)(2,1)} %param.12) | copy-start | bytes 1572868
  6.5 11.3 %copy-start.5 = (u32[32]{0:T(128)S(1)}, u32[32]{0:T(128)}, u32[]{:S(2)}) copy-start(u32[32]{0:T(128)} %constant.36) | copy-start | bytes 388
  6.5 65.4 %all-gather.3.cloned.1.call-start = ((), (), s32[]{:S(2)}) async-start(), calls=%async_computation | async-start | bytes 4456448 | tf_op jit(solution)/shard_map/all_gather | solution.py:141
  7.3 139.8 %all-gather.5.cloned.1.call-start = ((), (), s32[]{:S(2)}) async-start(), calls=%async_computation.1 | async-start | bytes 8912896 | tf_op jit(solution)/shard_map/all_gather | solution.py:146
  11.8 45.0 %collective-permute-start = (bf16[2,256,1024]{1,2,0:T(8,128)(2,1)S(1)}, bf16[2,256,1024]{1,2,0:T(8,128)(2,1)}, u32[]{:S(2)}, u32[]{:S(2)}) collective-permute-start(bf16[2,256,1024]{1,2,0:T(8,128)(2,1)S(1)} %pad_maximum_fusion.1), channel_id=1, source_target_pairs={{0,2},{1,3},{2,4},{3,5},{4,6},{5,7},{6,8},{7,9},{8,10},{9,11},{10,... | collective-permute-start | bytes 3145736 | tf_op jit(solution)/shard_map/ppermute | solution.py:23
  15.3 48.8 %collective-permute-start.1 = (bf16[2,256,1024]{1,2,0:T(8,128)(2,1)S(1)}, bf16[2,256,1024]{1,2,0:T(8,128)(2,1)}, u32[]{:S(2)}, u32[]{:S(2)}) collective-permute-start(bf16[2,256,1024]{1,2,0:T(8,128)(2,1)S(1)} %pad_maximum_fusion.1), channel_id=1, source_target_pairs={{0,1},{1,2},{2,3},{3,4},{4,5},{5,6},{6,7},{7,8},{8,9},{9,10},{10,1... | collective-permute-start | bytes 3145736 | tf_op jit(solution)/shard_map/ppermute | solution.py:23
  71.9 75.2 %copy-start.4 = (f32[2048]{0:T(1024)S(1)}, f32[2048]{0:T(1024)}, u32[]{:S(2)}) copy-start(f32[2048]{0:T(1024)} %param.17) | copy-start | bytes 24580
  75.8 71.3 %copy-start.1 = (f32[256,2048]{1,0:T(8,128)}, f32[256,2048]{1,0:T(8,128)S(1)}, u32[]{:S(2)}) copy-start(f32[256,2048]{1,0:T(8,128)S(1)} %get-tuple-element.14) | copy-start | bytes 6291460
  147.1 4.6 %copy-start.3 = (bf16[2,2048,1024]{2,1,0:T(8,128)(2,1)S(1)}, bf16[2,2048,1024]{2,1,0:T(8,128)(2,1)}, u32[]{:S(2)}) copy-start(bf16[2,2048,1024]{2,1,0:T(8,128)(2,1)} %all-gather.5.cloned.1.call-done) | copy-start | bytes 25165828
  151.7 8.9 %copy-start.2 = (s32[4,2]{0,1:T(2,128)S(1)}, s32[4,2]{0,1:T(2,128)}, u32[]{:S(2)}) copy-start(s32[4,2]{0,1:T(2,128)} %param.23) | copy-start | bytes 100
  154.8 27.5 %collective-permute-start.2 = (bf16[2,256,1024]{2,1,0:T(8,128)(2,1)S(1)}, bf16[2,256,1024]{2,1,0:T(8,128)(2,1)}, u32[]{:S(2)}, u32[]{:S(2)}) collective-permute-start(bf16[2,256,1024]{2,1,0:T(8,128)(2,1)S(1)} %pad_maximum_fusion.2), channel_id=1, source_target_pairs={{0,1},{1,2},{2,3},{3,4},{4,5},{5,6},{6,7},{7,8},{8,9},{9,10},{10,1... | collective-permute-start | bytes 3145736 | tf_op jit(solution)/shard_map/ppermute | solution.py:33
  157.0 25.3 %collective-permute-start.3 = (bf16[2,256,1024]{2,1,0:T(8,128)(2,1)S(1)}, bf16[2,256,1024]{2,1,0:T(8,128)(2,1)}, u32[]{:S(2)}, u32[]{:S(2)}) collective-permute-start(bf16[2,256,1024]{2,1,0:T(8,128)(2,1)S(1)} %pad_maximum_fusion.2), channel_id=1, source_target_pairs={{1,0},{2,1},{3,2},{4,3},{5,4},{6,5},{7,6},{8,7},{9,8},{10,9},{11,1... | collective-permute-start | bytes 3145736 | tf_op jit(solution)/shard_map/ppermute | solution.py:34
Sparse Core Ops, SparseCore 0:
  9.5 62.3 all-gather.2
  74.1 72.9 all-gather.4

commit v3 on v2

--- a/solution.py
+++ b/solution.py
@@ -141,9 +141,16 @@
     full_out_proj = lax.all_gather(out_proj, "ctx", axis=0, tiled=True)
     every_count = lax.all_gather(counts, "ctx", axis=0, tiled=True)
     every_count, sem_queries = lax.optimization_barrier((every_count, sem_queries))
-    cross_rows, cross_cols = key_proj.shape
-    stacked_proj = jnp.stack([key_proj, value_proj])
-    gathered_proj = lax.all_gather(stacked_proj, "ctx", axis=1, tiled=True)
+    group_size = lax.axis_size("groups")
+    shared = group_size % 2 == 0
+    if shared:
+        partners = [(i, i ^ 1) for i in range(group_size)]
+        key_side = lax.axis_index("groups") % 2 == 0
+        own_proj = jnp.where(key_side, key_proj, value_proj)
+        gathered_proj = lax.all_gather(own_proj, "ctx", axis=0, tiled=True)
+    else:
+        stacked_proj = jnp.stack([key_proj, value_proj])
+        gathered_proj = lax.all_gather(stacked_proj, "ctx", axis=1, tiled=True)
     own_pair = jnp.stack([sem_keys, sem_values])
     reach_shards = (W - 1 + rows_here - 1) // rows_here
     earlier = []
@@ -159,10 +166,17 @@
     projected = contract_rows(sem_att, full_out_proj)
     sem_stream = sem_inputs.astype(jnp.float32) + projected
     normed = normalize(sem_stream, norm_gain)
-    key_sum = contract_rows(normed, gathered_proj[0])
-    value_sum = contract_rows(normed, gathered_proj[1])
-    cross_keys = key_sum.astype(jnp.bfloat16)
-    cross_values = value_sum.astype(jnp.bfloat16)
+    if shared:
+        partner_normed = lax.ppermute(normed, "groups", partners)
+        both_streams = jnp.concatenate([normed, partner_normed], axis=0)
+        both_sums = contract_rows(both_streams, gathered_proj).astype(jnp.bfloat16)
+        own_sum = both_sums[:rows_here]
+        partner_sum = lax.ppermute(both_sums[rows_here:], "groups", partners)
+        cross_keys = jnp.where(key_side, own_sum, partner_sum)
+        cross_values = jnp.where(key_side, partner_sum, own_sum)
+    else:
+        cross_keys = contract_rows(normed, gathered_proj[0]).astype(jnp.bfloat16)
+        cross_values = contract_rows(normed, gathered_proj[1]).astype(jnp.bfloat16)
     earlier_index = jnp.arange(ctx_size, dtype=jnp.int32) < device_index
     stream_start = jnp.sum(jnp.where(earlier_index, every_count, 0)).astype(jnp.int32)
     near_pair = with_halo(jnp.stack([cross_keys, cross_values]), (("ctx", 1),), rows_here)

time: 217 us -> 205 us (0.945)
  waiting for transfers between devices: 99.7 us -> 85.4 us
  blocking collectives: 37.3 us -> 41.3 us
    all_gather x1, waiting for transfers between devices: 71.3 us -> 45.8 us  [on_device(): gathered_proj = lax.all_gather(own_proj, 'ctx', axis=0, tiled=True)]
    ppermute x1, waiting for transfers between devices: 0.01 us -> 19.1 us  [with_halo(): after = lax.ppermute(first, axis, down)]
    ppermute x1, waiting for transfers between devices: 19.6 us -> 2.01 us  [with_halo(): before = lax.ppermute(last, axis, up)]
    ppermute x0 -> x2, waiting for transfers between devices: none -> 12.6 us  [the longest x1 12.6 us: on_device(): partner_sum = lax.ppermute(both_sums[rows_here:], 'groups', partners)]
    ppermute x2, waiting for transfers between devices: 7.26 us -> 0.01 us  [passed_along(): return lax.ppermute(array, axis, pairs)]
    all_gather x1, waiting for transfers between devices: 0.77 us -> 5.17 us  [on_device(): full_out_proj = lax.all_gather(out_proj, 'ctx', axis=0, tiled=True)]
    optimization_barrier x1, blocking collectives: 37.3 us -> 41.3 us  [on_device(): lax.optimization_barrier((every_count, sem_queries))]
    ppermute x0 -> x2, starting transfers between devices: none -> 3.08 us  [the longest x1 1.55 us: on_device(): partner_normed = lax.ppermute(normed, 'groups', partners)]
  transfers between devices with their start and end apart: 6 -> 8, of which waited for: 4 -> 5; matrix products, arithmetic and copies ran while one was open for 9% -> 9% of each run, Pallas kernels for 0% -> 0%
where the time goes in v3:
time: 205 us; the launch traced here: 203 us
  waiting for transfers between devices  85.4 us (42%)
  blocking collectives  41.3 us (20%)
  Pallas kernels  22.4 us (11%)
  between operations  14.3 us (7%)
  starting transfers between devices  13 us (6%)
  other arithmetic  12.2 us (6%)
  matrix products  10.7 us (5%)
  local copies, waits for them, and re-layouts  4.18 us (2%)
    all_gather x1, waiting for transfers between devices, on_device(): gathered_proj = lax.all_gather(own_proj, 'ctx', axis=0, tiled=True)  45.8 us
    optimization_barrier x1, blocking collectives, on_device(): lax.optimization_barrier((every_count, sem_queries))  41.3 us
    pallas_call x1, Pallas kernels, coarse_attention(): pl.pallas_call(kernel, grid_spec=grid_spec, out_shape=jax.ShapeDtypeStruc...  22.4 us
    ppermute x1, waiting for transfers between devices, with_halo(): after = lax.ppermute(first, axis, down)  19.1 us
    ppermute x1, waiting for transfers between devices, on_device(): partner_sum = lax.ppermute(both_sums[rows_here:], 'groups', partners)  12.6 us
    dot_general x2, matrix products, contract_rows(): return jnp.dot(left_side, weight_piece, preferred_element_type=jnp.float32)  8.41 us
    ppermute x2, starting transfers between devices, passed_along(): return lax.ppermute(array, axis, pairs)  5.35 us
    all_gather x1, waiting for transfers between devices, on_device(): full_out_proj = lax.all_gather(out_proj, 'ctx', axis=0, tiled=True)  5.17 us
  transfers between devices with their start and end apart: 8, of which 5 were waited for; matrix products, arithmetic and copies ran while one was open for 9% of the time, Pallas kernels for 0%

profile of v3, /device:TPU:20, one launch (start us, length us, event | category | flops | bytes accessed | tf_op | source)
XLA Modules:
  0.0 203.4 jit_solution(5319256806052709769)
XLA Ops:
  6.5 0.0 copy-start
  6.5 0.0 all-gather.3.cloned.1.call-start
  6.5 0.7 all-gather.3.cloned.1.call-update
  7.3 0.0 all-gather.5.cloned.1.call-start
  7.3 1.7 broadcast_select_fusion
  9.0 0.0 all-gather.5.cloned.1.call-update
  9.0 1.2 copy.18
  10.3 1.2 copy.17
  11.5 0.1 pad_maximum_fusion.1
  11.6 1.9 collective-permute-start.1
  13.6 3.4 %collective-permute-start = (bf16[2,256,1024]{1,2,0:T(8,128)(2,1)S(1)}, bf16[2,256,1024]{1,2,0:T(8,128)(2,1)}, u32[]{:S(2)}, u32[]{:S(2)}) collective-permute-start(bf16[2,256,1024]{1,2,0:T(8,128)(2,1)S(1)} %pad_maximum_fusion.1), channel_id=1, source_target_pairs={{0,2},{1,3},{2,4},{3,5},{4,6},{5,7},{6,8},{7,9},{8,10},{9,11},{10,... | collective-permute-start | bytes 3145736 | tf_op jit(solution)/shard_map/ppermute | solution.py:23
  17.7 0.0 copy-done.4
  17.7 0.6 dynamic-slice
  18.3 0.7 dynamic-update-slice
  18.9 41.3 %all-reduce = s32[16]{0:T(128)S(1)} all-reduce(s32[16]{0:T(128)S(1)} %dynamic-update-slice), channel_id=1, replica_groups=mesh['groups'=2,'ctx'=16] {'ctx'}, use_global_device_ids=true, to_apply=%add | all-reduce | flops 16 | bytes 128 | tf_op jit(solution)/shard_map/optimization_barrier | solution.py:143
  60.2 0.3 fusion.17
  60.5 0.0 collective-permute-done.1
  60.5 0.0 collective-permute-done
  60.5 1.7 maximum_maximum_fusion
  62.2 0.2 fusion.25
  62.4 0.0 copy-done
  62.4 1.0 fusion.18
  63.4 2.9 %fusion.26 = (f32[8,256]{1,0:T(8,128)S(1)}, f32[8,256,768]{2,1,0:T(8,128)S(1)}) fusion(f32[8,256,768]{2,1,0:T(8,128)S(1)} %fusion.18, pred[256,768]{1,0:T(8,128)(4,1)S(1)} %fusion.17), kind=kOutput, calls=%fused_computation.43 | output fusion | flops 9437951 | bytes 12787712 | tf_op jit(solution)/shard_map/sub | solution.py:52
  66.3 0.0 copy-start.1
  66.3 1.3 fusion.13
  67.6 5.2 %all-gather.3.cloned.1.call-done = bf16[1024,2048]{1,0:T(8,128)(2,1)} async-done(((bf16[64,2048]{1,0:T(8,128)(2,1)}), bf16[1024,2048]{1,0:T(8,128)(2,1)}) %all-gather.3.cloned.1.call-update) | async-done | bytes 4194320 | tf_op jit(solution)/shard_map/all_gather | solution.py:141
  72.8 0.0 copy-done.1
  72.8 3.6 %multiply_reduce_fusion = (f32[256]{0:T(256)S(1)}, f32[256,2048]{1,0:T(8,128)S(1)}) fusion(bf16[256,1024]{0,1:T(8,128)(2,1)S(1)} %bitcast.31, bf16[1024,2048]{1,0:T(8,128)(2,1)} %all-gather.3.cloned.1.call-done, bf16[256,2048]{1,0:T(8,128)(2,1)S(1)} %copy-done.1), kind=kOutput, calls=%fused_computation.17 | convolution fusion | flops 1075838720 | bytes 7865344 | tf_op jit(solution)/shard_map/dot_general | solution.py:68
  76.4 0.2 multiply_convert_fusion
  76.6 1.5 collective-permute-start.2
  78.2 45.8 %all-gather.5.cloned.1.call-done = bf16[2048,1024]{1,0:T(8,128)(2,1)} async-done(((bf16[128,1024]{1,0:T(8,128)(2,1)}), bf16[2048,1024]{1,0:T(8,128)(2,1)}) %all-gather.5.cloned.1.call-update) | async-done | bytes 4194320 | tf_op jit(solution)/shard_map/all_gather | solution.py:150
  123.9 0.0 collective-permute-done.2
  123.9 4.8 %fusion.10 = bf16[512,1024]{1,0:T(8,128)(2,1)S(1)} fusion(bf16[2048,1024]{1,0:T(8,128)(2,1)} %all-gather.5.cloned.1.call-done, bf16[256,2048]{1,0:T(8,128)(2,1)} %collective-permute-done.2, bf16[256,2048]{1,0:T(8,128)(2,1)S(1)} %multiply_convert_fusion), kind=kOutput, calls=%fused_computation.18 | convolution fusion | flops 2152202240 | bytes 7340032 | tf_op jit(solution)/shard_map/dot_general | solution.py:68
  128.8 0.0 copy-start.3
  128.8 1.5 collective-permute-start.3
  130.4 12.6 %collective-permute-done.3 = bf16[256,1024]{1,0:T(8,128)(2,1)S(1)} collective-permute-done((bf16[256,1024]{1,0:T(8,128)(2,1)S(1)}, bf16[256,1024]{1,0:T(8,128)(2,1)S(1)}, u32[]{:S(2)}, u32[]{:S(2)}) %collective-permute-start.3) | collective-permute-done | bytes 524320 | tf_op jit(solution)/shard_map/ppermute | solution.py:174
  143.0 0.1 select_bitcast_fusion.1
  143.0 0.1 pad_maximum_fusion.2
  143.1 2.4 %collective-permute-start.5 = (bf16[2,256,1024]{2,1,0:T(8,128)(2,1)S(1)}, bf16[2,256,1024]{2,1,0:T(8,128)(2,1)}, u32[]{:S(2)}, u32[]{:S(2)}) collective-permute-start(bf16[2,256,1024]{2,1,0:T(8,128)(2,1)S(1)} %pad_maximum_fusion.2), channel_id=1, source_target_pairs={{1,0},{2,1},{3,2},{4,3},{5,4},{6,5},{7,6},{8,7},{9,8},{10,9},{11,1... | collective-permute-start | bytes 3145736 | tf_op jit(solution)/shard_map/ppermute | solution.py:34
  145.5 2.1 %collective-permute-start.4 = (bf16[2,256,1024]{2,1,0:T(8,128)(2,1)S(1)}, bf16[2,256,1024]{2,1,0:T(8,128)(2,1)}, u32[]{:S(2)}, u32[]{:S(2)}) collective-permute-start(bf16[2,256,1024]{2,1,0:T(8,128)(2,1)S(1)} %pad_maximum_fusion.2), channel_id=1, source_target_pairs={{0,1},{1,2},{2,3},{3,4},{4,5},{5,6},{6,7},{7,8},{8,9},{9,10},{10,1... | collective-permute-start | bytes 3145736 | tf_op jit(solution)/shard_map/ppermute | solution.py:33
  147.7 0.1 copy.16
  147.8 0.1 reshape.67
  147.9 0.7 fusion.21
  148.6 1.4 pad_add_fusion.prm
  149.9 19.1 %collective-permute-done.5 = bf16[2,256,1024]{2,1,0:T(8,128)(2,1)} collective-permute-done((bf16[2,256,1024]{2,1,0:T(8,128)(2,1)S(1)}, bf16[2,256,1024]{2,1,0:T(8,128)(2,1)}, u32[]{:S(2)}, u32[]{:S(2)}) %collective-permute-start.5) | collective-permute-done | bytes 1048608 | tf_op jit(solution)/shard_map/ppermute | solution.py:34
  169.1 2.0 collective-permute-done.4
  171.1 3.1 %pad_maximum_fusion.k_ref.v_ref = bf16[2,768,1024]{2,1,0:T(8,128)(2,1)} fusion(bf16[2,256,1024]{2,1,0:T(8,128)(2,1)} %collective-permute-done.5, bf16[1,256,1024]{2,1,0:T(8,128)(2,1)S(1)} %get-tuple-element.12, bf16[1,256,1024]{2,1,0:T(8,128)(2,1)S(1)} %get-tuple-element.11, bf16[2,256,1024]{2,1,0:T(8,128)(2,1)} %collective-permute-done.4), kind=kLoop, calls=%fused_computation.6 | loop fusion | flops 12582912 | bytes 6291456 | tf_op jit(solution)/shard_map/concatenate | solution.py:35
  174.2 22.4 %shard_map.118 = bf16[1024,1024]{1,0:T(8,128)(2,1)} custom-call(s32[11]{0:T(128)} %pad_add_fusion.prm, f32[8]{0:T(128)} %slopes_ref.1, bf16[1024,1024]{1,0:T(8,128)(2,1)} %q_ref.1, bf16[2,768,1024]{2,1,0:T(8,128)(2,1)} %pad_maximum_fusion.k_ref.v_ref, bf16[2,768,1024]{2,1,0:T(8,128)(2,1)} %pad_maximum_fusion.k_ref.v_ref), custom_call_target="tpu_custom_call" | custom-call | tf_op jit(solution)/shard_map/pallas_call | solution.py:116
  (9 shorter events, 0.1 us)
Async XLA Ops:
  6.5 55.9 %copy-start = (bf16[256,1024]{1,0:T(8,128)(2,1)S(1)}, bf16[256,1024]{1,0:T(8,128)(2,1)}, u32[]{:S(2)}) copy-start(bf16[256,1024]{1,0:T(8,128)(2,1)} %param.12) | copy-start | bytes 1572868
  6.5 11.1 %copy-start.4 = (u32[32]{0:T(128)S(1)}, u32[32]{0:T(128)}, u32[]{:S(2)}) copy-start(u32[32]{0:T(128)} %constant.53) | copy-start | bytes 388
  6.5 66.2 %all-gather.3.cloned.1.call-start = ((), (), s32[]{:S(2)}) async-start(), calls=%async_computation | async-start | bytes 4456448 | tf_op jit(solution)/shard_map/all_gather | solution.py:141
  7.3 116.7 %all-gather.5.cloned.1.call-start = ((), (), s32[]{:S(2)}) async-start(), calls=%async_computation.1 | async-start | bytes 4456448 | tf_op jit(solution)/shard_map/all_gather | solution.py:150
  11.6 48.8 %collective-permute-start.1 = (bf16[2,256,1024]{1,2,0:T(8,128)(2,1)S(1)}, bf16[2,256,1024]{1,2,0:T(8,128)(2,1)}, u32[]{:S(2)}, u32[]{:S(2)}) collective-permute-start(bf16[2,256,1024]{1,2,0:T(8,128)(2,1)S(1)} %pad_maximum_fusion.1), channel_id=1, source_target_pairs={{0,1},{1,2},{2,3},{3,4},{4,5},{5,6},{6,7},{7,8},{8,9},{9,10},{10,1... | collective-permute-start | bytes 3145736 | tf_op jit(solution)/shard_map/ppermute | solution.py:23
  13.6 46.9 %collective-permute-start = (bf16[2,256,1024]{1,2,0:T(8,128)(2,1)S(1)}, bf16[2,256,1024]{1,2,0:T(8,128)(2,1)}, u32[]{:S(2)}, u32[]{:S(2)}) collective-permute-start(bf16[2,256,1024]{1,2,0:T(8,128)(2,1)S(1)} %pad_maximum_fusion.1), channel_id=1, source_target_pairs={{0,2},{1,3},{2,4},{3,5},{4,6},{5,7},{6,8},{7,9},{8,10},{9,11},{10,... | collective-permute-start | bytes 3145736 | tf_op jit(solution)/shard_map/ppermute | solution.py:23
  66.3 6.5 %copy-start.1 = (bf16[256,2048]{1,0:T(8,128)(2,1)S(1)}, bf16[256,2048]{1,0:T(8,128)(2,1)}, u32[]{:S(2)}) copy-start(bf16[256,2048]{1,0:T(8,128)(2,1)} %param.15) | copy-start | bytes 3145732
  72.8 3.6 %copy-start.2 = (f32[2048]{0:T(1024)S(1)}, f32[2048]{0:T(1024)}, u32[]{:S(2)}) copy-start(f32[2048]{0:T(1024)} %param.17) | copy-start | bytes 24580
  76.6 47.3 %collective-permute-start.2 = (bf16[256,2048]{1,0:T(8,128)(2,1)S(1)}, bf16[256,2048]{1,0:T(8,128)(2,1)}, u32[]{:S(2)}, u32[]{:S(2)}) collective-permute-start(bf16[256,2048]{1,0:T(8,128)(2,1)S(1)} %multiply_convert_fusion), channel_id=1, source_target_pairs={{0,16},{16,0},{1,17},{17,1},{2,18},{18,2},{3,19},{19,3},{4,20},{20... | collective-permute-start | bytes 3145736 | tf_op jit(solution)/shard_map/ppermute | solution.py:170
  128.8 18.9 %copy-start.3 = (s32[4,2]{0,1:T(2,128)S(1)}, s32[4,2]{0,1:T(2,128)}, u32[]{:S(2)}) copy-start(s32[4,2]{0,1:T(2,128)} %param.23) | copy-start | bytes 100
  128.8 14.1 %collective-permute-start.3 = (bf16[256,1024]{1,0:T(8,128)(2,1)S(1)}, bf16[256,1024]{1,0:T(8,128)(2,1)S(1)}, u32[]{:S(2)}, u32[]{:S(2)}) collective-permute-start(bf16[256,1024]{1,0:T(8,128)(2,1)S(1)} %slice.19), channel_id=1, source_target_pairs={{0,16},{16,0},{1,17},{17,1},{2,18},{18,2},{3,19},{19,3},{4,20},{20... | collective-permute-start | bytes 1572872 | tf_op jit(solution)/shard_map/ppermute | solution.py:174
  143.1 25.9 %collective-permute-start.5 = (bf16[2,256,1024]{2,1,0:T(8,128)(2,1)S(1)}, bf16[2,256,1024]{2,1,0:T(8,128)(2,1)}, u32[]{:S(2)}, u32[]{:S(2)}) collective-permute-start(bf16[2,256,1024]{2,1,0:T(8,128)(2,1)S(1)} %pad_maximum_fusion.2), channel_id=1, source_target_pairs={{1,0},{2,1},{3,2},{4,3},{5,4},{6,5},{7,6},{8,7},{9,8},{10,9},{11,1... | collective-permute-start | bytes 3145736 | tf_op jit(solution)/shard_map/ppermute | solution.py:34
  145.5 25.5 %collective-permute-start.4 = (bf16[2,256,1024]{2,1,0:T(8,128)(2,1)S(1)}, bf16[2,256,1024]{2,1,0:T(8,128)(2,1)}, u32[]{:S(2)}, u32[]{:S(2)}) collective-permute-start(bf16[2,256,1024]{2,1,0:T(8,128)(2,1)S(1)} %pad_maximum_fusion.2), channel_id=1, source_target_pairs={{0,1},{1,2},{2,3},{3,4},{4,5},{5,6},{6,7},{7,8},{8,9},{9,10},{10,1... | collective-permute-start | bytes 3145736 | tf_op jit(solution)/shard_map/ppermute | solution.py:33
Sparse Core Ops, SparseCore 0:
  9.5 63.2 all-gather.2
  74.9 48.9 all-gather.4

commit v4 on v3

--- a/solution.py
+++ b/solution.py
@@ -139,8 +139,11 @@
     device_index = lax.axis_index("ctx")
     ctx_size = lax.axis_size("ctx")
     full_out_proj = lax.all_gather(out_proj, "ctx", axis=0, tiled=True)
-    every_count = lax.all_gather(counts, "ctx", axis=0, tiled=True)
-    every_count, sem_queries = lax.optimization_barrier((every_count, sem_queries))
+    running = counts
+    reach = 1
+    while reach < ctx_size:
+        running = running + passed_along(running, "ctx", reach)
+        reach *= 2
     group_size = lax.axis_size("groups")
     shared = group_size % 2 == 0
     if shared:
@@ -177,8 +180,7 @@
     else:
         cross_keys = contract_rows(normed, gathered_proj[0]).astype(jnp.bfloat16)
         cross_values = contract_rows(normed, gathered_proj[1]).astype(jnp.bfloat16)
-    earlier_index = jnp.arange(ctx_size, dtype=jnp.int32) < device_index
-    stream_start = jnp.sum(jnp.where(earlier_index, every_count, 0)).astype(jnp.int32)
+    stream_start = (running - counts)[0]
     near_pair = with_halo(jnp.stack([cross_keys, cross_values]), (("ctx", 1),), rows_here)
     base_row = (device_index - 1) * rows_here
     params = jnp.concatenate(

time: 205 us -> 226 us (1.10)
  waiting for transfers between devices: 85.4 us -> 137 us
  blocking collectives: 41.3 us -> 0 us
  starting transfers between devices: 13 us -> 24.1 us
  between operations: 14.3 us -> 16.8 us
    ppermute x2 -> x6, waiting for transfers between devices: 0.01 us -> 71.9 us  [passed_along(): return lax.ppermute(array, axis, pairs)]
    optimization_barrier x1 -> x0, blocking collectives: 41.3 us -> none  [on_device(): lax.optimization_barrier((every_count, sem_queries))]
    ppermute x1, waiting for transfers between devices: 19.1 us -> 0.01 us  [with_halo(): after = lax.ppermute(first, axis, down)]
    ppermute x2 -> x6, starting transfers between devices: 5.35 us -> 16.7 us  [passed_along(): return lax.ppermute(array, axis, pairs)]
  transfers between devices with their start and end apart: 8 -> 12, of which waited for: 5 -> 9; matrix products, arithmetic and copies ran while one was open for 9% -> 7% of each run, Pallas kernels for 0% -> 0%
where the time goes in v4:
time: 226 us; the launch traced here: 224 us
  waiting for transfers between devices  137 us (61%)
  starting transfers between devices  24.1 us (11%)
  Pallas kernels  22.4 us (10%)
  between operations  16.8 us (7%)
  other arithmetic  10.8 us (5%)
  matrix products  10.1 us (4%)
  local copies, waits for them, and re-layouts  2.93 us (1%)
    ppermute x6, waiting for transfers between devices, passed_along(): return lax.ppermute(array, axis, pairs)  71.9 us
    all_gather x1, waiting for transfers between devices, on_device(): gathered_proj = lax.all_gather(own_proj, 'ctx', axis=0, tiled=True)  45.8 us
    pallas_call x1, Pallas kernels, coarse_attention(): pl.pallas_call(kernel, grid_spec=grid_spec, out_shape=jax.ShapeDtypeStruc...  22.4 us
    ppermute x6, starting transfers between devices, passed_along(): return lax.ppermute(array, axis, pairs)  16.7 us
    ppermute x1, waiting for transfers between devices, on_device(): partner_sum = lax.ppermute(both_sums[rows_here:], 'groups', partners)  12.6 us
    dot_general x2, matrix products, contract_rows(): return jnp.dot(left_side, weight_piece, preferred_element_type=jnp.float32)  8.41 us
    all_gather x1, waiting for transfers between devices, on_device(): full_out_proj = lax.all_gather(out_proj, 'ctx', axis=0, tiled=True)  5.98 us
  transfers between devices with their start and end apart: 12, of which 9 were waited for; matrix products, arithmetic and copies ran while one was open for 7% of the time, Pallas kernels for 0%

profile of v4, /device:TPU:20, one launch (start us, length us, event | category | flops | bytes accessed | tf_op | source)
XLA Modules:
  0.0 224.2 jit_solution(4738770639186278177)
XLA Ops:
  6.5 0.0 copy-start
  6.5 0.7 all-gather.3.cloned.1.call-update
  7.3 0.0 all-gather.5.cloned.1.call-start
  7.3 1.7 broadcast_select_fusion
  9.0 0.0 all-gather.5.cloned.1.call-update
  9.0 1.2 copy.19
  10.3 1.2 copy.18
  11.5 0.1 pad_maximum_fusion.1
  11.6 1.9 collective-permute-start.5
  13.6 3.4 %collective-permute-start.4 = (bf16[2,256,1024]{1,2,0:T(8,128)(2,1)S(1)}, bf16[2,256,1024]{1,2,0:T(8,128)(2,1)}, u32[]{:S(2)}, u32[]{:S(2)}) collective-permute-start(bf16[2,256,1024]{1,2,0:T(8,128)(2,1)S(1)} %pad_maximum_fusion.1), channel_id=1, source_target_pairs={{0,2},{1,3},{2,4},{3,5},{4,6},{5,7},{6,8},{7,9},{8,10},{9,11},{10,... | collective-permute-start | bytes 3145736 | tf_op jit(solution)/shard_map/ppermute | solution.py:23
  17.0 0.2 fusion.17
  17.3 22.1 %collective-permute-done.5 = bf16[2,256,1024]{1,2,0:T(8,128)(2,1)} collective-permute-done((bf16[2,256,1024]{1,2,0:T(8,128)(2,1)S(1)}, bf16[2,256,1024]{1,2,0:T(8,128)(2,1)}, u32[]{:S(2)}, u32[]{:S(2)}) %collective-permute-start.5) | collective-permute-done | bytes 1048608 | tf_op jit(solution)/shard_map/ppermute | solution.py:23
  39.4 20.7 %collective-permute-done.4 = bf16[2,256,1024]{1,2,0:T(8,128)(2,1)} collective-permute-done((bf16[2,256,1024]{1,2,0:T(8,128)(2,1)S(1)}, bf16[2,256,1024]{1,2,0:T(8,128)(2,1)}, u32[]{:S(2)}, u32[]{:S(2)}) %collective-permute-start.4) | collective-permute-done | bytes 1048608 | tf_op jit(solution)/shard_map/ppermute | solution.py:23
  60.1 1.6 maximum_maximum_fusion
  61.7 0.2 fusion.24
  61.9 1.0 fusion.18
  63.0 3.1 %fusion.25 = (f32[8,256]{1,0:T(8,128)S(1)}, f32[8,256,768]{1,2,0:T(8,128)S(1)}) fusion(f32[8,768,256]{2,1,0:T(8,128)S(1)} %fusion.18, pred[256,768]{0,1:T(8,128)(4,1)S(1)} %fusion.17), kind=kOutput, calls=%fused_computation.41 | output fusion | flops 9437951 | bytes 12787712 | tf_op jit(solution)/shard_map/sub | solution.py:52
  66.1 0.0 copy-start.1
  66.1 0.6 fusion.13
  66.7 6.0 %all-gather.3.cloned.1.call-done = bf16[1024,2048]{1,0:T(8,128)(2,1)} async-done(((bf16[64,2048]{1,0:T(8,128)(2,1)}), bf16[1024,2048]{1,0:T(8,128)(2,1)}) %all-gather.3.cloned.1.call-update) | async-done | bytes 4194320 | tf_op jit(solution)/shard_map/all_gather | solution.py:141
  72.7 3.6 %multiply_reduce_fusion = (f32[256]{0:T(256)S(1)}, f32[256,2048]{1,0:T(8,128)S(1)}) fusion(bf16[256,1024]{0,1:T(8,128)(2,1)S(1)} %bitcast.40, bf16[1024,2048]{1,0:T(8,128)(2,1)} %all-gather.3.cloned.1.call-done, bf16[256,2048]{1,0:T(8,128)(2,1)S(1)} %copy-done.1), kind=kOutput, calls=%fused_computation.17 | convolution fusion | flops 1075838720 | bytes 7865344 | tf_op jit(solution)/shard_map/dot_general | solution.py:68
  76.3 0.2 multiply_convert_fusion
  76.5 1.5 collective-permute-start.6
  78.1 45.8 %all-gather.5.cloned.1.call-done = bf16[2048,1024]{1,0:T(8,128)(2,1)} async-done(((bf16[128,1024]{1,0:T(8,128)(2,1)}), bf16[2048,1024]{1,0:T(8,128)(2,1)}) %all-gather.5.cloned.1.call-update) | async-done | bytes 4194320 | tf_op jit(solution)/shard_map/all_gather | solution.py:153
  123.8 0.0 collective-permute-done.6
  123.8 4.8 %fusion.10 = bf16[512,1024]{1,0:T(8,128)(2,1)S(1)} fusion(bf16[2048,1024]{1,0:T(8,128)(2,1)} %all-gather.5.cloned.1.call-done, bf16[256,2048]{1,0:T(8,128)(2,1)} %collective-permute-done.6, bf16[256,2048]{1,0:T(8,128)(2,1)S(1)} %multiply_convert_fusion), kind=kOutput, calls=%fused_computation.18 | convolution fusion | flops 2152202240 | bytes 7340032 | tf_op jit(solution)/shard_map/dot_general | solution.py:68
  128.7 0.0 copy-start.3
  128.7 1.5 collective-permute-start.7
  130.3 12.6 %collective-permute-done.7 = bf16[256,1024]{1,0:T(8,128)(2,1)S(1)} collective-permute-done((bf16[256,1024]{1,0:T(8,128)(2,1)S(1)}, bf16[256,1024]{1,0:T(8,128)(2,1)S(1)}, u32[]{:S(2)}, u32[]{:S(2)}) %collective-permute-start.7) | collective-permute-done | bytes 524320 | tf_op jit(solution)/shard_map/ppermute | solution.py:177
  142.9 0.1 select_bitcast_fusion.1
  143.0 0.1 pad_maximum_fusion.2
  143.1 2.4 %collective-permute-start.9 = (bf16[2,256,1024]{2,1,0:T(8,128)(2,1)S(1)}, bf16[2,256,1024]{2,1,0:T(8,128)(2,1)}, u32[]{:S(2)}, u32[]{:S(2)}) collective-permute-start(bf16[2,256,1024]{2,1,0:T(8,128)(2,1)S(1)} %pad_maximum_fusion.2), channel_id=1, source_target_pairs={{1,0},{2,1},{3,2},{4,3},{5,4},{6,5},{7,6},{8,7},{9,8},{10,9},{11,1... | collective-permute-start | bytes 3145736 | tf_op jit(solution)/shard_map/ppermute | solution.py:34
  145.4 2.0 collective-permute-start.8
  147.4 3.4 %collective-permute-start = (s32[1]{0:T(128)}, s32[1]{0:T(128)}, u32[]{:S(2)}, u32[]{:S(2)}) collective-permute-start(s32[1]{0:T(128)} %param.22), channel_id=1, source_target_pairs={{0,1},{1,2},{2,3},{3,4},{4,5},{5,6},{6,7},{7,8},{8,9},{9,10},{10,1... | collective-permute-start | bytes 20 | tf_op jit(solution)/shard_map/ppermute | solution.py:23
  151.5 0.1 copy.17
  151.6 0.1 reshape.67
  151.7 19.4 %collective-permute-done = s32[1]{0:T(128)} collective-permute-done((s32[1]{0:T(128)}, s32[1]{0:T(128)}, u32[]{:S(2)}, u32[]{:S(2)}) %collective-permute-start) | collective-permute-done | bytes 36 | tf_op jit(solution)/shard_map/ppermute | solution.py:23
  171.7 3.2 %collective-permute-start.1 = (s32[1]{0:T(128)}, s32[1]{0:T(128)}, u32[]{:S(2)}, u32[]{:S(2)}) collective-permute-start(s32[1]{0:T(128)} %add.53), channel_id=1, source_target_pairs={{0,2},{1,3},{2,4},{3,5},{4,6},{5,7},{6,8},{7,9},{8,10},{9,11},{10,... | collective-permute-start | bytes 20 | tf_op jit(solution)/shard_map/ppermute | solution.py:23
  174.9 2.4 %collective-permute-done.1 = s32[1]{0:T(128)} collective-permute-done((s32[1]{0:T(128)}, s32[1]{0:T(128)}, u32[]{:S(2)}, u32[]{:S(2)}) %collective-permute-start.1) | collective-permute-done | bytes 36 | tf_op jit(solution)/shard_map/ppermute | solution.py:23
  177.9 3.2 %collective-permute-start.2 = (s32[1]{0:T(128)}, s32[1]{0:T(128)}, u32[]{:S(2)}, u32[]{:S(2)}) collective-permute-start(s32[1]{0:T(128)} %add.54), channel_id=1, source_target_pairs={{0,4},{1,5},{2,6},{3,7},{4,8},{5,9},{6,10},{7,11},{8,12},{9,13},{1... | collective-permute-start | bytes 20 | tf_op jit(solution)/shard_map/ppermute | solution.py:23
  181.1 2.4 %collective-permute-done.2 = s32[1]{0:T(128)} collective-permute-done((s32[1]{0:T(128)}, s32[1]{0:T(128)}, u32[]{:S(2)}, u32[]{:S(2)}) %collective-permute-start.2) | collective-permute-done | bytes 36 | tf_op jit(solution)/shard_map/ppermute | solution.py:23
  184.1 1.5 collective-permute-start.3
  185.6 5.0 %collective-permute-done.3 = s32[1]{0:T(128)} collective-permute-done((s32[1]{0:T(128)}, s32[1]{0:T(128)}, u32[]{:S(2)}, u32[]{:S(2)}) %collective-permute-start.3) | collective-permute-done | bytes 36 | tf_op jit(solution)/shard_map/ppermute | solution.py:23
  191.2 0.6 pad_add_fusion.prm
  191.8 0.0 collective-permute-done.9
  191.8 0.0 collective-permute-done.8
  191.8 3.1 %pad_maximum_fusion.k_ref.v_ref = bf16[2,768,1024]{2,1,0:T(8,128)(2,1)} fusion(bf16[2,256,1024]{2,1,0:T(8,128)(2,1)} %collective-permute-done.9, bf16[1,256,1024]{2,1,0:T(8,128)(2,1)S(1)} %get-tuple-element.8, bf16[1,256,1024]{2,1,0:T(8,128)(2,1)S(1)} %get-tuple-element.7, bf16[2,256,1024]{2,1,0:T(8,128)(2,1)} %collective-permute-done.8), kind=kLoop, calls=%fused_computation.6 | loop fusion | flops 12582912 | bytes 6291456 | tf_op jit(solution)/shard_map/concatenate | solution.py:35
  194.9 22.4 %shard_map.118 = bf16[1024,1024]{1,0:T(8,128)(2,1)} custom-call(s32[11]{0:T(128)} %pad_add_fusion.prm, f32[8]{0:T(128)} %slopes_ref.1, bf16[1024,1024]{1,0:T(8,128)(2,1)} %q_ref.1, bf16[2,768,1024]{2,1,0:T(8,128)(2,1)} %pad_maximum_fusion.k_ref.v_ref, bf16[2,768,1024]{2,1,0:T(8,128)(2,1)} %pad_maximum_fusion.k_ref.v_ref), custom_call_target="tpu_custom_call" | custom-call | tf_op jit(solution)/shard_map/pallas_call | solution.py:116
  (10 shorter events, 0.1 us)
Async XLA Ops:
  6.5 55.4 %copy-start = (bf16[256,1024]{1,0:T(8,128)(2,1)S(1)}, bf16[256,1024]{1,0:T(8,128)(2,1)}, u32[]{:S(2)}) copy-start(bf16[256,1024]{1,0:T(8,128)(2,1)} %param.12) | copy-start | bytes 1572868
  6.5 66.2 %all-gather.3.cloned.1.call-start = ((), (), s32[]{:S(2)}) async-start(), calls=%async_computation | async-start | bytes 4456448 | tf_op jit(solution)/shard_map/all_gather | solution.py:141
  7.3 116.6 %all-gather.5.cloned.1.call-start = ((), (), s32[]{:S(2)}) async-start(), calls=%async_computation.1 | async-start | bytes 4456448 | tf_op jit(solution)/shard_map/all_gather | solution.py:153
  11.6 27.8 %collective-permute-start.5 = (bf16[2,256,1024]{1,2,0:T(8,128)(2,1)S(1)}, bf16[2,256,1024]{1,2,0:T(8,128)(2,1)}, u32[]{:S(2)}, u32[]{:S(2)}) collective-permute-start(bf16[2,256,1024]{1,2,0:T(8,128)(2,1)S(1)} %pad_maximum_fusion.1), channel_id=1, source_target_pairs={{0,1},{1,2},{2,3},{3,4},{4,5},{5,6},{6,7},{7,8},{8,9},{9,10},{10,1... | collective-permute-start | bytes 3145736 | tf_op jit(solution)/shard_map/ppermute | solution.py:23
  13.6 46.5 %collective-permute-start.4 = (bf16[2,256,1024]{1,2,0:T(8,128)(2,1)S(1)}, bf16[2,256,1024]{1,2,0:T(8,128)(2,1)}, u32[]{:S(2)}, u32[]{:S(2)}) collective-permute-start(bf16[2,256,1024]{1,2,0:T(8,128)(2,1)S(1)} %pad_maximum_fusion.1), channel_id=1, source_target_pairs={{0,2},{1,3},{2,4},{3,5},{4,6},{5,7},{6,8},{7,9},{8,10},{9,11},{10,... | collective-permute-start | bytes 3145736 | tf_op jit(solution)/shard_map/ppermute | solution.py:23
  66.1 6.6 %copy-start.1 = (bf16[256,2048]{1,0:T(8,128)(2,1)S(1)}, bf16[256,2048]{1,0:T(8,128)(2,1)}, u32[]{:S(2)}) copy-start(bf16[256,2048]{1,0:T(8,128)(2,1)} %param.15) | copy-start | bytes 3145732
  72.7 3.6 %copy-start.2 = (f32[2048]{0:T(1024)S(1)}, f32[2048]{0:T(1024)}, u32[]{:S(2)}) copy-start(f32[2048]{0:T(1024)} %param.17) | copy-start | bytes 24580
  76.5 47.3 %collective-permute-start.6 = (bf16[256,2048]{1,0:T(8,128)(2,1)S(1)}, bf16[256,2048]{1,0:T(8,128)(2,1)}, u32[]{:S(2)}, u32[]{:S(2)}) collective-permute-start(bf16[256,2048]{1,0:T(8,128)(2,1)S(1)} %multiply_convert_fusion), channel_id=1, source_target_pairs={{0,16},{16,0},{1,17},{17,1},{2,18},{18,2},{3,19},{19,3},{4,20},{20... | collective-permute-start | bytes 3145736 | tf_op jit(solution)/shard_map/ppermute | solution.py:173
  128.7 22.8 %copy-start.3 = (s32[4,2]{0,1:T(2,128)S(1)}, s32[4,2]{0,1:T(2,128)}, u32[]{:S(2)}) copy-start(s32[4,2]{0,1:T(2,128)} %param.23) | copy-start | bytes 100
  128.7 14.1 %collective-permute-start.7 = (bf16[256,1024]{1,0:T(8,128)(2,1)S(1)}, bf16[256,1024]{1,0:T(8,128)(2,1)S(1)}, u32[]{:S(2)}, u32[]{:S(2)}) collective-permute-start(bf16[256,1024]{1,0:T(8,128)(2,1)S(1)} %slice.19), channel_id=1, source_target_pairs={{0,16},{16,0},{1,17},{17,1},{2,18},{18,2},{3,19},{19,3},{4,20},{20... | collective-permute-start | bytes 1572872 | tf_op jit(solution)/shard_map/ppermute | solution.py:177
  143.1 48.7 %collective-permute-start.9 = (bf16[2,256,1024]{2,1,0:T(8,128)(2,1)S(1)}, bf16[2,256,1024]{2,1,0:T(8,128)(2,1)}, u32[]{:S(2)}, u32[]{:S(2)}) collective-permute-start(bf16[2,256,1024]{2,1,0:T(8,128)(2,1)S(1)} %pad_maximum_fusion.2), channel_id=1, source_target_pairs={{1,0},{2,1},{3,2},{4,3},{5,4},{6,5},{7,6},{8,7},{9,8},{10,9},{11,1... | collective-permute-start | bytes 3145736 | tf_op jit(solution)/shard_map/ppermute | solution.py:34
  145.4 46.4 %collective-permute-start.8 = (bf16[2,256,1024]{2,1,0:T(8,128)(2,1)S(1)}, bf16[2,256,1024]{2,1,0:T(8,128)(2,1)}, u32[]{:S(2)}, u32[]{:S(2)}) collective-permute-start(bf16[2,256,1024]{2,1,0:T(8,128)(2,1)S(1)} %pad_maximum_fusion.2), channel_id=1, source_target_pairs={{0,1},{1,2},{2,3},{3,4},{4,5},{5,6},{6,7},{7,8},{8,9},{9,10},{10,1... | collective-permute-start | bytes 3145736 | tf_op jit(solution)/shard_map/ppermute | solution.py:33
  147.4 23.7 %collective-permute-start = (s32[1]{0:T(128)}, s32[1]{0:T(128)}, u32[]{:S(2)}, u32[]{:S(2)}) collective-permute-start(s32[1]{0:T(128)} %param.22), channel_id=1, source_target_pairs={{0,1},{1,2},{2,3},{3,4},{4,5},{5,6},{6,7},{7,8},{8,9},{9,10},{10,1... | collective-permute-start | bytes 20 | tf_op jit(solution)/shard_map/ppermute | solution.py:23
  171.7 5.6 %collective-permute-start.1 = (s32[1]{0:T(128)}, s32[1]{0:T(128)}, u32[]{:S(2)}, u32[]{:S(2)}) collective-permute-start(s32[1]{0:T(128)} %add.53), channel_id=1, source_target_pairs={{0,2},{1,3},{2,4},{3,5},{4,6},{5,7},{6,8},{7,9},{8,10},{9,11},{10,... | collective-permute-start | bytes 20 | tf_op jit(solution)/shard_map/ppermute | solution.py:23
  177.9 5.6 %collective-permute-start.2 = (s32[1]{0:T(128)}, s32[1]{0:T(128)}, u32[]{:S(2)}, u32[]{:S(2)}) collective-permute-start(s32[1]{0:T(128)} %add.54), channel_id=1, source_target_pairs={{0,4},{1,5},{2,6},{3,7},{4,8},{5,9},{6,10},{7,11},{8,12},{9,13},{1... | collective-permute-start | bytes 20 | tf_op jit(solution)/shard_map/ppermute | solution.py:23
  184.1 6.5 %collective-permute-start.3 = (s32[1]{0:T(128)}, s32[1]{0:T(128)}, u32[]{:S(2)}, u32[]{:S(2)}) collective-permute-start(s32[1]{0:T(128)} %add.55), channel_id=1, source_target_pairs={{0,8},{1,9},{2,10},{3,11},{4,12},{5,13},{6,14},{7,15},{16,24},{17,... | collective-permute-start | bytes 20 | tf_op jit(solution)/shard_map/ppermute | solution.py:23
Sparse Core Ops, SparseCore 0:
  9.5 63.1 all-gather.2
  74.8 48.9 all-gather.4

commit v5 on v4

--- a/solution.py
+++ b/solution.py
@@ -166,6 +166,7 @@
     key_global = device_index * rows_here - reach_shards * rows_here + key_pos
     allowed = (key_lag >= 0) & (key_lag < W) & (key_global[None, :] >= 0)
     sem_att = attend(sem_queries, window_pair[0], window_pair[1], allowed, 0.0).astype(jnp.bfloat16)
+    running, sem_att = lax.optimization_barrier((running, sem_att))
     projected = contract_rows(sem_att, full_out_proj)
     sem_stream = sem_inputs.astype(jnp.float32) + projected
     normed = normalize(sem_stream, norm_gain)

time: 226 us -> 205 us (0.907)
  waiting for transfers between devices: 137 us -> 99 us
  starting transfers between devices: 24.1 us -> 39.9 us
    all_gather x1, waiting for transfers between devices: 45.8 us -> 15.3 us  [on_device(): gathered_proj = lax.all_gather(own_proj, 'ctx', axis=0, tiled=True)]
    ppermute x6, waiting for transfers between devices: 71.9 us -> 48.8 us  [passed_along(): return lax.ppermute(array, axis, pairs)]
    ppermute x1, waiting for transfers between devices: 0.01 us -> 20.9 us  [with_halo(): before = lax.ppermute(last, axis, up)]
    ppermute x6, starting transfers between devices: 16.7 us -> 31 us  [passed_along(): return lax.ppermute(array, axis, pairs)]
    all_gather x1, waiting for transfers between devices: 5.98 us -> 0.02 us  [on_device(): full_out_proj = lax.all_gather(out_proj, 'ctx', axis=0, tiled=True)]
    ppermute x1, waiting for transfers between devices: 0.01 us -> 5.03 us  [on_device(): partner_normed = lax.ppermute(normed, 'groups', partners)]
    ppermute x1, waiting for transfers between devices: 12.6 us -> 8.21 us  [on_device(): partner_sum = lax.ppermute(both_sums[rows_here:], 'groups', partners)]
  transfers between devices with their start and end apart: 12 -> 12, of which waited for: 9 -> 7; matrix products, arithmetic and copies ran while one was open for 7% -> 8% of each run, Pallas kernels for 0% -> 0%
where the time goes in v5:
time: 205 us; the launch traced here: 202 us
  waiting for transfers between devices  99 us (48%)
  starting transfers between devices  39.9 us (19%)
  Pallas kernels  22.4 us (11%)
  between operations  17.1 us (8%)
  other arithmetic  10.9 us (5%)
  matrix products  9.76 us (5%)
  local copies, waits for them, and re-layouts  3.5 us (2%)
    ppermute x6, waiting for transfers between devices, passed_along(): return lax.ppermute(array, axis, pairs)  48.8 us
    ppermute x6, starting transfers between devices, passed_along(): return lax.ppermute(array, axis, pairs)  31 us
    pallas_call x1, Pallas kernels, coarse_attention(): pl.pallas_call(kernel, grid_spec=grid_spec, out_shape=jax.ShapeDtypeStruc...  22.4 us
    ppermute x1, waiting for transfers between devices, with_halo(): before = lax.ppermute(last, axis, up)  20.9 us
    all_gather x1, waiting for transfers between devices, on_device(): gathered_proj = lax.all_gather(own_proj, 'ctx', axis=0, tiled=True)  15.3 us
    ppermute x1, waiting for transfers between devices, on_device(): partner_sum = lax.ppermute(both_sums[rows_here:], 'groups', partners)  8.21 us
    dot_general x2, matrix products, contract_rows(): return jnp.dot(left_side, weight_piece, preferred_element_type=jnp.float32)  8.09 us
    ppermute x1, waiting for transfers between devices, on_device(): partner_normed = lax.ppermute(normed, 'groups', partners)  5.03 us
  transfers between devices with their start and end apart: 12, of which 7 were waited for; matrix products, arithmetic and copies ran while one was open for 8% of the time, Pallas kernels for 0%

profile of v5, /device:TPU:20, one launch (start us, length us, event | category | flops | bytes accessed | tf_op | source)
XLA Modules:
  0.0 202.4 jit_solution(13344823883710383138)
XLA Ops:
  6.5 0.7 all-gather.3.cloned.1.call-update
  7.3 0.0 all-gather.5.cloned.1.call-start
  7.3 1.7 broadcast_select_fusion
  9.0 0.0 all-gather.5.cloned.1.call-update
  9.0 1.2 copy.18
  10.3 1.2 copy.19
  11.5 0.1 pad_maximum_fusion.1
  11.6 3.4 %collective-permute-start.4 = (bf16[2,256,1024]{1,2,0:T(8,128)(2,1)S(1)}, bf16[2,256,1024]{1,2,0:T(8,128)(2,1)}, u32[]{:S(2)}, u32[]{:S(2)}) collective-permute-start(bf16[2,256,1024]{1,2,0:T(8,128)(2,1)S(1)} %pad_maximum_fusion.1), channel_id=1, source_target_pairs={{0,2},{1,3},{2,4},{3,5},{4,6},{5,7},{6,8},{7,9},{8,10},{9,11},{10,... | collective-permute-start | bytes 3145736 | tf_op jit(solution)/shard_map/ppermute | solution.py:23
  15.1 1.9 collective-permute-start.5
  17.0 3.5 %collective-permute-start = (s32[1]{0:T(128)}, s32[1]{0:T(128)}, u32[]{:S(2)}, u32[]{:S(2)}) collective-permute-start(s32[1]{0:T(128)} %param.22), channel_id=1, source_target_pairs={{0,1},{1,2},{2,3},{3,4},{4,5},{5,6},{6,7},{7,8},{8,9},{9,10},{10,1... | collective-permute-start | bytes 20 | tf_op jit(solution)/shard_map/ppermute | solution.py:23
  21.2 0.2 fusion.17
  21.5 42.4 %collective-permute-done = s32[1]{0:T(128)} collective-permute-done((s32[1]{0:T(128)}, s32[1]{0:T(128)}, u32[]{:S(2)}, u32[]{:S(2)}) %collective-permute-start) | collective-permute-done | bytes 36 | tf_op jit(solution)/shard_map/ppermute | solution.py:23
  64.5 16.8 %collective-permute-start.1 = (s32[1]{0:T(128)}, s32[1]{0:T(128)}, u32[]{:S(2)}, u32[]{:S(2)}) collective-permute-start(s32[1]{0:T(128)} %add.53), channel_id=1, source_target_pairs={{0,2},{1,3},{2,4},{3,5},{4,6},{5,7},{6,8},{7,9},{8,10},{9,11},{10,... | collective-permute-start | bytes 20 | tf_op jit(solution)/shard_map/ppermute | solution.py:23
  82.0 4.0 %collective-permute-start.2 = (s32[1]{0:T(128)}, s32[1]{0:T(128)}, u32[]{:S(2)}, u32[]{:S(2)}) collective-permute-start(s32[1]{0:T(128)} %add.54), channel_id=1, source_target_pairs={{0,4},{1,5},{2,6},{3,7},{4,8},{5,9},{6,10},{7,11},{8,12},{9,13},{1... | collective-permute-start | bytes 20 | tf_op jit(solution)/shard_map/ppermute | solution.py:23
  86.1 1.4 collective-permute-done.2
  88.1 1.3 collective-permute-start.3
  89.4 5.0 %collective-permute-done.3 = s32[1]{0:T(128)} collective-permute-done((s32[1]{0:T(128)}, s32[1]{0:T(128)}, u32[]{:S(2)}, u32[]{:S(2)}) %collective-permute-start.3) | collective-permute-done | bytes 36 | tf_op jit(solution)/shard_map/ppermute | solution.py:23
  95.1 0.0 collective-permute-done.4
  95.2 0.0 collective-permute-done.5
  95.2 1.7 maximum_maximum_fusion
  96.8 0.2 fusion.24
  97.1 1.0 fusion.18
  98.1 3.1 %fusion.25 = (f32[8,256]{1,0:T(8,128)S(1)}, f32[8,256,768]{1,2,0:T(8,128)S(1)}) fusion(f32[8,768,256]{2,1,0:T(8,128)S(1)} %fusion.18, pred[256,768]{0,1:T(8,128)(4,1)S(1)} %fusion.17), kind=kOutput, calls=%fused_computation.41 | output fusion | flops 9437951 | bytes 12787712 | tf_op jit(solution)/shard_map/sub | solution.py:52
  101.2 0.0 copy-start.1
  101.2 0.6 fusion.13
  101.8 0.0 copy-start.2
  101.9 0.0 all-gather.3.cloned.1.call-done
  101.9 0.6 copy-done.1
  102.4 3.6 %multiply_reduce_fusion = (f32[256]{0:T(256)S(1)}, f32[256,2048]{1,0:T(8,128)S(1)}) fusion(bf16[256,1024]{0,1:T(8,128)(2,1)S(1)} %bitcast.40, bf16[1024,2048]{1,0:T(8,128)(2,1)} %all-gather.3.cloned.1.call-done, bf16[256,2048]{1,0:T(8,128)(2,1)S(1)} %copy-done.1), kind=kOutput, calls=%fused_computation.17 | convolution fusion | flops 1075838720 | bytes 7865344 | tf_op jit(solution)/shard_map/dot_general | solution.py:68
  106.0 0.2 multiply_convert_fusion
  106.3 1.6 collective-permute-start.6
  107.8 15.3 %all-gather.5.cloned.1.call-done = bf16[2048,1024]{1,0:T(8,128)(2,1)} async-done(((bf16[128,1024]{1,0:T(8,128)(2,1)}), bf16[2048,1024]{1,0:T(8,128)(2,1)}) %all-gather.5.cloned.1.call-update) | async-done | bytes 4194320 | tf_op jit(solution)/shard_map/all_gather | solution.py:153
  123.1 5.0 %collective-permute-done.6 = bf16[256,2048]{1,0:T(8,128)(2,1)S(1)} collective-permute-done((bf16[256,2048]{1,0:T(8,128)(2,1)S(1)}, bf16[256,2048]{1,0:T(8,128)(2,1)S(1)}, u32[]{:S(2)}, u32[]{:S(2)}) %collective-permute-start.6) | collective-permute-done | bytes 1048608 | tf_op jit(solution)/shard_map/ppermute | solution.py:174
  128.1 4.5 %fusion.10 = bf16[512,1024]{1,0:T(8,128)(2,1)S(1)} fusion(bf16[2048,1024]{1,0:T(8,128)(2,1)} %all-gather.5.cloned.1.call-done, bf16[256,2048]{1,0:T(8,128)(2,1)S(1)} %collective-permute-done.6, bf16[256,2048]{1,0:T(8,128)(2,1)S(1)} %multiply_convert_fusion), kind=kOutput, calls=%fused_computation.18 | convolution fusion | flops 2152202240 | bytes 7340032 | tf_op jit(solution)/shard_map/dot_general | solution.py:68
  132.6 0.0 copy-start.3
  132.7 1.5 collective-permute-start.7
  134.2 8.2 %collective-permute-done.7 = bf16[256,1024]{1,0:T(8,128)(2,1)S(1)} collective-permute-done((bf16[256,1024]{1,0:T(8,128)(2,1)S(1)}, bf16[256,1024]{1,0:T(8,128)(2,1)S(1)}, u32[]{:S(2)}, u32[]{:S(2)}) %collective-permute-start.7) | collective-permute-done | bytes 524320 | tf_op jit(solution)/shard_map/ppermute | solution.py:178
  142.4 0.1 select_bitcast_fusion.1
  142.5 0.1 pad_maximum_fusion.2
  142.6 1.9 collective-permute-start.8
  144.6 3.8 %collective-permute-start.9 = (bf16[2,256,1024]{2,1,0:T(8,128)(2,1)S(1)}, bf16[2,256,1024]{2,1,0:T(8,128)(2,1)}, u32[]{:S(2)}, u32[]{:S(2)}) collective-permute-start(bf16[2,256,1024]{2,1,0:T(8,128)(2,1)S(1)} %pad_maximum_fusion.2), channel_id=1, source_target_pairs={{1,0},{2,1},{3,2},{4,3},{5,4},{6,5},{7,6},{8,7},{9,8},{10,9},{11,1... | collective-permute-start | bytes 3145736 | tf_op jit(solution)/shard_map/ppermute | solution.py:34
  148.4 0.1 copy.17
  148.5 0.1 reshape.67
  148.6 0.6 pad_add_fusion.prm
  149.1 20.9 %collective-permute-done.8 = bf16[2,256,1024]{2,1,0:T(8,128)(2,1)} collective-permute-done((bf16[2,256,1024]{2,1,0:T(8,128)(2,1)S(1)}, bf16[2,256,1024]{2,1,0:T(8,128)(2,1)}, u32[]{:S(2)}, u32[]{:S(2)}) %collective-permute-start.8) | collective-permute-done | bytes 1048608 | tf_op jit(solution)/shard_map/ppermute | solution.py:33
  170.1 0.0 collective-permute-done.9
  170.1 3.1 %pad_maximum_fusion.k_ref.v_ref = bf16[2,768,1024]{2,1,0:T(8,128)(2,1)} fusion(bf16[2,256,1024]{2,1,0:T(8,128)(2,1)} %collective-permute-done.9, bf16[1,256,1024]{2,1,0:T(8,128)(2,1)S(1)} %get-tuple-element.12, bf16[1,256,1024]{2,1,0:T(8,128)(2,1)S(1)} %get-tuple-element.11, bf16[2,256,1024]{2,1,0:T(8,128)(2,1)} %collective-permute-done.8), kind=kLoop, calls=%fused_computation.6 | loop fusion | flops 12582912 | bytes 6291456 | tf_op jit(solution)/shard_map/concatenate | solution.py:35
  173.2 22.4 %shard_map.118 = bf16[1024,1024]{1,0:T(8,128)(2,1)} custom-call(s32[11]{0:T(128)} %pad_add_fusion.prm, f32[8]{0:T(128)} %slopes_ref.1, bf16[1024,1024]{1,0:T(8,128)(2,1)} %q_ref.1, bf16[2,768,1024]{2,1,0:T(8,128)(2,1)} %pad_maximum_fusion.k_ref.v_ref, bf16[2,768,1024]{2,1,0:T(8,128)(2,1)} %pad_maximum_fusion.k_ref.v_ref), custom_call_target="tpu_custom_call" | custom-call | tf_op jit(solution)/shard_map/pallas_call | solution.py:116
  (10 shorter events, 0.1 us)
Async XLA Ops:
  6.5 90.5 %copy-start = (bf16[256,1024]{1,0:T(8,128)(2,1)S(1)}, bf16[256,1024]{1,0:T(8,128)(2,1)}, u32[]{:S(2)}) copy-start(bf16[256,1024]{1,0:T(8,128)(2,1)} %param.12) | copy-start | bytes 1572868
  6.5 95.3 %all-gather.3.cloned.1.call-start = ((), (), s32[]{:S(2)}) async-start(), calls=%async_computation | async-start | bytes 4456448 | tf_op jit(solution)/shard_map/all_gather | solution.py:141
  7.3 115.8 %all-gather.5.cloned.1.call-start = ((), (), s32[]{:S(2)}) async-start(), calls=%async_computation.1 | async-start | bytes 4456448 | tf_op jit(solution)/shard_map/all_gather | solution.py:153
  11.6 83.5 %collective-permute-start.4 = (bf16[2,256,1024]{1,2,0:T(8,128)(2,1)S(1)}, bf16[2,256,1024]{1,2,0:T(8,128)(2,1)}, u32[]{:S(2)}, u32[]{:S(2)}) collective-permute-start(bf16[2,256,1024]{1,2,0:T(8,128)(2,1)S(1)} %pad_maximum_fusion.1), channel_id=1, source_target_pairs={{0,2},{1,3},{2,4},{3,5},{4,6},{5,7},{6,8},{7,9},{8,10},{9,11},{10,... | collective-permute-start | bytes 3145736 | tf_op jit(solution)/shard_map/ppermute | solution.py:23
  15.1 80.1 %collective-permute-start.5 = (bf16[2,256,1024]{1,2,0:T(8,128)(2,1)S(1)}, bf16[2,256,1024]{1,2,0:T(8,128)(2,1)}, u32[]{:S(2)}, u32[]{:S(2)}) collective-permute-start(bf16[2,256,1024]{1,2,0:T(8,128)(2,1)S(1)} %pad_maximum_fusion.1), channel_id=1, source_target_pairs={{0,1},{1,2},{2,3},{3,4},{4,5},{5,6},{6,7},{7,8},{8,9},{9,10},{10,1... | collective-permute-start | bytes 3145736 | tf_op jit(solution)/shard_map/ppermute | solution.py:23
  17.0 46.8 %collective-permute-start = (s32[1]{0:T(128)}, s32[1]{0:T(128)}, u32[]{:S(2)}, u32[]{:S(2)}) collective-permute-start(s32[1]{0:T(128)} %param.22), channel_id=1, source_target_pairs={{0,1},{1,2},{2,3},{3,4},{4,5},{5,6},{6,7},{7,8},{8,9},{9,10},{10,1... | collective-permute-start | bytes 20 | tf_op jit(solution)/shard_map/ppermute | solution.py:23
  64.5 16.8 %collective-permute-start.1 = (s32[1]{0:T(128)}, s32[1]{0:T(128)}, u32[]{:S(2)}, u32[]{:S(2)}) collective-permute-start(s32[1]{0:T(128)} %add.53), channel_id=1, source_target_pairs={{0,2},{1,3},{2,4},{3,5},{4,6},{5,7},{6,8},{7,9},{8,10},{9,11},{10,... | collective-permute-start | bytes 20 | tf_op jit(solution)/shard_map/ppermute | solution.py:23
  82.0 5.4 %collective-permute-start.2 = (s32[1]{0:T(128)}, s32[1]{0:T(128)}, u32[]{:S(2)}, u32[]{:S(2)}) collective-permute-start(s32[1]{0:T(128)} %add.54), channel_id=1, source_target_pairs={{0,4},{1,5},{2,6},{3,7},{4,8},{5,9},{6,10},{7,11},{8,12},{9,13},{1... | collective-permute-start | bytes 20 | tf_op jit(solution)/shard_map/ppermute | solution.py:23
  88.1 6.3 %collective-permute-start.3 = (s32[1]{0:T(128)}, s32[1]{0:T(128)}, u32[]{:S(2)}, u32[]{:S(2)}) collective-permute-start(s32[1]{0:T(128)} %add.55), channel_id=1, source_target_pairs={{0,8},{1,9},{2,10},{3,11},{4,12},{5,13},{6,14},{7,15},{16,24},{17,... | collective-permute-start | bytes 20 | tf_op jit(solution)/shard_map/ppermute | solution.py:23
  101.2 1.3 copy-start.1
  101.8 4.2 %copy-start.2 = (f32[2048]{0:T(1024)S(1)}, f32[2048]{0:T(1024)}, u32[]{:S(2)}) copy-start(f32[2048]{0:T(1024)} %param.17) | copy-start | bytes 24580
  106.3 21.8 %collective-permute-start.6 = (bf16[256,2048]{1,0:T(8,128)(2,1)S(1)}, bf16[256,2048]{1,0:T(8,128)(2,1)S(1)}, u32[]{:S(2)}, u32[]{:S(2)}) collective-permute-start(bf16[256,2048]{1,0:T(8,128)(2,1)S(1)} %multiply_convert_fusion), channel_id=1, source_target_pairs={{0,16},{16,0},{1,17},{17,1},{2,18},{18,2},{3,19},{19,3},{4,20},{20... | collective-permute-start | bytes 3145736 | tf_op jit(solution)/shard_map/ppermute | solution.py:174
  132.6 15.7 %copy-start.3 = (s32[4,2]{0,1:T(2,128)S(1)}, s32[4,2]{0,1:T(2,128)}, u32[]{:S(2)}) copy-start(s32[4,2]{0,1:T(2,128)} %param.23) | copy-start | bytes 100
  132.7 9.7 %collective-permute-start.7 = (bf16[256,1024]{1,0:T(8,128)(2,1)S(1)}, bf16[256,1024]{1,0:T(8,128)(2,1)S(1)}, u32[]{:S(2)}, u32[]{:S(2)}) collective-permute-start(bf16[256,1024]{1,0:T(8,128)(2,1)S(1)} %slice.19), channel_id=1, source_target_pairs={{0,16},{16,0},{1,17},{17,1},{2,18},{18,2},{3,19},{19,3},{4,20},{20... | collective-permute-start | bytes 1572872 | tf_op jit(solution)/shard_map/ppermute | solution.py:178
  142.6 27.5 %collective-permute-start.8 = (bf16[2,256,1024]{2,1,0:T(8,128)(2,1)S(1)}, bf16[2,256,1024]{2,1,0:T(8,128)(2,1)}, u32[]{:S(2)}, u32[]{:S(2)}) collective-permute-start(bf16[2,256,1024]{2,1,0:T(8,128)(2,1)S(1)} %pad_maximum_fusion.2), channel_id=1, source_target_pairs={{0,1},{1,2},{2,3},{3,4},{4,5},{5,6},{6,7},{7,8},{8,9},{9,10},{10,1... | collective-permute-start | bytes 3145736 | tf_op jit(solution)/shard_map/ppermute | solution.py:33
  144.6 25.5 %collective-permute-start.9 = (bf16[2,256,1024]{2,1,0:T(8,128)(2,1)S(1)}, bf16[2,256,1024]{2,1,0:T(8,128)(2,1)}, u32[]{:S(2)}, u32[]{:S(2)}) collective-permute-start(bf16[2,256,1024]{2,1,0:T(8,128)(2,1)S(1)} %pad_maximum_fusion.2), channel_id=1, source_target_pairs={{1,0},{2,1},{3,2},{4,3},{5,4},{6,5},{7,6},{8,7},{9,8},{10,9},{11,1... | collective-permute-start | bytes 3145736 | tf_op jit(solution)/shard_map/ppermute | solution.py:34
Sparse Core Ops, SparseCore 0:
  9.5 62.1 all-gather.2
  73.9 49.1 all-gather.4

commit v6 on v5

--- a/solution.py
+++ b/solution.py
@@ -34,6 +34,17 @@
         after = lax.ppermute(first, axis, down)
         array = jnp.concatenate([before, array, after], axis=dim)
     return array
+
+
+def sent_to(array, group_flip, ctx_step):
+    groups, length = (lax.axis_size("groups"), lax.axis_size("ctx"))
+    pairs = [
+        (g * length + c, (g ^ group_flip) * length + c + ctx_step)
+        for g in range(groups)
+        for c in range(length)
+        if 0 <= c + ctx_step < length
+    ]
+    return lax.ppermute(array, ("groups", "ctx"), pairs)
 
 
 def head_split(matrix):
@@ -108,8 +119,8 @@
         in_specs=[
             pl.BlockSpec(memory_space=pltpu.SMEM),
             pl.BlockSpec((CB, width), lambda n, prm: (n, 0)),
-            pl.BlockSpec((None, near_rows, width), lambda n, prm: (0, 0, 0)),
-            pl.BlockSpec((None, near_rows, width), lambda n, prm: (1, 0, 0)),
+            pl.BlockSpec((None, near_rows, width), lambda n, prm: (prm[2 * blocks + 3], 0, 0)),
+            pl.BlockSpec((None, near_rows, width), lambda n, prm: (1 - prm[2 * blocks + 3], 0, 0)),
         ],
         out_specs=pl.BlockSpec((CB, width), lambda n, prm: (n, 0)),
     )
@@ -175,18 +186,23 @@
         both_streams = jnp.concatenate([normed, partner_normed], axis=0)
         both_sums = contract_rows(both_streams, gathered_proj).astype(jnp.bfloat16)
         own_sum = both_sums[:rows_here]
-        partner_sum = lax.ppermute(both_sums[rows_here:], "groups", partners)
-        cross_keys = jnp.where(key_side, own_sum, partner_sum)
-        cross_values = jnp.where(key_side, partner_sum, own_sum)
+        partner_part = both_sums[rows_here:]
+        mine_near = jnp.concatenate(
+            [sent_to(own_sum, 0, 1), own_sum, sent_to(own_sum, 0, -1)], axis=0)
+        other_near = jnp.concatenate(
+            [sent_to(partner_part, 1, 1), sent_to(partner_part, 1, 0), sent_to(partner_part, 1, -1)], axis=0)
+        near_pair = jnp.stack([mine_near, other_near])
+        key_slot = jnp.where(key_side, 0, 1)
     else:
         cross_keys = contract_rows(normed, gathered_proj[0]).astype(jnp.bfloat16)
         cross_values = contract_rows(normed, gathered_proj[1]).astype(jnp.bfloat16)
+        near_pair = with_halo(jnp.stack([cross_keys, cross_values]), (("ctx", 1),), rows_here)
+        key_slot = jnp.zeros((), jnp.int32)
     stream_start = (running - counts)[0]
-    near_pair = with_halo(jnp.stack([cross_keys, cross_values]), (("ctx", 1),), rows_here)
     base_row = (device_index - 1) * rows_here
     params = jnp.concatenate(
         [band_bounds.reshape(-1).astype(jnp.int32),
-         jnp.stack([stream_start, counts[0], base_row]).astype(jnp.int32)]
+         jnp.stack([stream_start, counts[0], base_row, key_slot]).astype(jnp.int32)]
     )
     return coarse_attention(coarse_queries, near_pair, params, slopes)
 

time: 205 us -> 207 us (level); the launches traced: 202 us -> 207 us
  starting transfers between devices: 39.9 us -> 45.6 us
  waiting for transfers between devices: 99 us -> 96.2 us
    ppermute x3 -> x5, starting transfers between devices: 7.28 us -> 12.8 us  [sent_to(): return lax.ppermute(array, ('groups', 'ctx'), pairs)]
    another operation x2 -> x3, other arithmetic: 0.17 us -> 4.25 us  [on_device(): near_pair = jnp.stack([mine_near, other_near])]
    concatenate x2 -> x0, other arithmetic: 3.66 us -> none  [the longest x1 3.1 us: with_halo(): array = jnp.concatenate([before, array, after], axis=dim)]
    ppermute x3 -> x5, waiting for transfers between devices: 29.2 us -> 27 us  [sent_to(): return lax.ppermute(array, ('groups', 'ctx'), pairs)]
  transfers between devices with their start and end apart: 12 -> 14, of which waited for: 7 -> 9; matrix products, arithmetic and copies ran while one was open for 8% -> 8% of each run, Pallas kernels for 0% -> 0%
where the time goes in v6:
time: 207 us
  waiting for transfers between devices  96.2 us (46%)
  starting transfers between devices  45.6 us (22%)
  Pallas kernels  22.5 us (11%)
  between operations  16.8 us (8%)
  other arithmetic  11.3 us (5%)
  matrix products  10.1 us (5%)
  local copies, waits for them, and re-layouts  4.31 us (2%)
    ppermute x6, waiting for transfers between devices, passed_along(): return lax.ppermute(array, axis, pairs)  48.6 us
    ppermute x6, starting transfers between devices, passed_along(): return lax.ppermute(array, axis, pairs)  31.2 us
    ppermute x5, waiting for transfers between devices, sent_to(): return lax.ppermute(array, ('groups', 'ctx'), pairs)  27 us
    pallas_call x1, Pallas kernels, coarse_attention(): pl.pallas_call(kernel, grid_spec=grid_spec, out_shape=jax.ShapeDtypeStruc...  22.5 us
    all_gather x1, waiting for transfers between devices, on_device(): gathered_proj = lax.all_gather(own_proj, 'ctx', axis=0, tiled=True)  15.4 us
    ppermute x5, starting transfers between devices, sent_to(): return lax.ppermute(array, ('groups', 'ctx'), pairs)  12.8 us
    dot_general x2, matrix products, contract_rows(): return jnp.dot(left_side, weight_piece, preferred_element_type=jnp.float32)  8.45 us
    ppermute x1, waiting for transfers between devices, on_device(): partner_normed = lax.ppermute(normed, 'groups', partners)  4.43 us
  transfers between devices with their start and end apart: 14, of which 9 were waited for; matrix products, arithmetic and copies ran while one was open for 8% of the time, Pallas kernels for 0%

profile of v6, /device:TPU:20, one launch (start us, length us, event | category | flops | bytes accessed | tf_op | source)
XLA Modules:
  0.0 206.7 jit_solution(13043123339623911124)
XLA Ops:
  6.5 0.7 all-gather.3.cloned.1.call-update
  7.3 0.0 all-gather.5.cloned.1.call-start
  7.3 1.7 broadcast_select_fusion
  9.0 0.0 all-gather.5.cloned.1.call-update
  9.0 1.2 copy.18
  10.3 1.2 copy.19
  11.5 0.1 pad_maximum_fusion.1
  11.6 3.4 %collective-permute-start.4 = (bf16[2,256,1024]{1,2,0:T(8,128)(2,1)S(1)}, bf16[2,256,1024]{1,2,0:T(8,128)(2,1)}, u32[]{:S(2)}, u32[]{:S(2)}) collective-permute-start(bf16[2,256,1024]{1,2,0:T(8,128)(2,1)S(1)} %pad_maximum_fusion.1), channel_id=1, source_target_pairs={{0,2},{1,3},{2,4},{3,5},{4,6},{5,7},{6,8},{7,9},{8,10},{9,11},{10,... | collective-permute-start | bytes 3145736 | tf_op jit(solution)/shard_map/ppermute | solution.py:23
  15.1 1.9 collective-permute-start.5
  17.0 3.5 %collective-permute-start = (s32[1]{0:T(128)}, s32[1]{0:T(128)}, u32[]{:S(2)}, u32[]{:S(2)}) collective-permute-start(s32[1]{0:T(128)} %param.22), channel_id=1, source_target_pairs={{0,1},{1,2},{2,3},{3,4},{4,5},{5,6},{6,7},{7,8},{8,9},{9,10},{10,1... | collective-permute-start | bytes 20 | tf_op jit(solution)/shard_map/ppermute | solution.py:23
  21.2 0.2 fusion.17
  21.5 42.4 %collective-permute-done = s32[1]{0:T(128)} collective-permute-done((s32[1]{0:T(128)}, s32[1]{0:T(128)}, u32[]{:S(2)}, u32[]{:S(2)}) %collective-permute-start) | collective-permute-done | bytes 36 | tf_op jit(solution)/shard_map/ppermute | solution.py:23
  64.4 16.8 %collective-permute-start.1 = (s32[1]{0:T(128)}, s32[1]{0:T(128)}, u32[]{:S(2)}, u32[]{:S(2)}) collective-permute-start(s32[1]{0:T(128)} %add.53), channel_id=1, source_target_pairs={{0,2},{1,3},{2,4},{3,5},{4,6},{5,7},{6,8},{7,9},{8,10},{9,11},{10,... | collective-permute-start | bytes 20 | tf_op jit(solution)/shard_map/ppermute | solution.py:23
  81.9 4.1 %collective-permute-start.2 = (s32[1]{0:T(128)}, s32[1]{0:T(128)}, u32[]{:S(2)}, u32[]{:S(2)}) collective-permute-start(s32[1]{0:T(128)} %add.54), channel_id=1, source_target_pairs={{0,4},{1,5},{2,6},{3,7},{4,8},{5,9},{6,10},{7,11},{8,12},{9,13},{1... | collective-permute-start | bytes 20 | tf_op jit(solution)/shard_map/ppermute | solution.py:23
  86.1 1.3 collective-permute-done.2
  88.0 1.3 collective-permute-start.3
  89.3 5.0 %collective-permute-done.3 = s32[1]{0:T(128)} collective-permute-done((s32[1]{0:T(128)}, s32[1]{0:T(128)}, u32[]{:S(2)}, u32[]{:S(2)}) %collective-permute-start.3) | collective-permute-done | bytes 36 | tf_op jit(solution)/shard_map/ppermute | solution.py:23
  94.9 1.7 maximum_maximum_fusion
  96.6 0.2 fusion.24
  96.8 1.0 fusion.18
  97.8 3.1 %fusion.26 = (f32[8,256]{1,0:T(8,128)S(1)}, f32[8,256,768]{1,2,0:T(8,128)S(1)}) fusion(f32[8,768,256]{2,1,0:T(8,128)S(1)} %fusion.18, pred[256,768]{0,1:T(8,128)(4,1)S(1)} %fusion.17), kind=kOutput, calls=%fused_computation.40 | output fusion | flops 9437951 | bytes 12787712 | tf_op jit(solution)/shard_map/sub | solution.py:63
  100.9 0.0 copy-start.1
  100.9 0.6 fusion.13
  101.6 0.0 all-gather.3.cloned.1.call-done
  101.6 0.7 copy-done.1
  102.3 3.6 %multiply_reduce_fusion = (f32[256]{0:T(256)S(1)}, f32[256,2048]{1,0:T(8,128)S(1)}) fusion(bf16[256,1024]{0,1:T(8,128)(2,1)S(1)} %bitcast.41, bf16[1024,2048]{1,0:T(8,128)(2,1)} %all-gather.3.cloned.1.call-done, bf16[256,2048]{1,0:T(8,128)(2,1)S(1)} %copy-done.1), kind=kOutput, calls=%fused_computation.17 | convolution fusion | flops 1075838720 | bytes 7865344 | tf_op jit(solution)/shard_map/dot_general | solution.py:79
  105.9 0.2 multiply_convert_fusion
  106.2 1.5 collective-permute-start.6
  107.7 15.4 %all-gather.5.cloned.1.call-done = bf16[2048,1024]{1,0:T(8,128)(2,1)} async-done(((bf16[128,1024]{1,0:T(8,128)(2,1)}), bf16[2048,1024]{1,0:T(8,128)(2,1)}) %all-gather.5.cloned.1.call-update) | async-done | bytes 4194320 | tf_op jit(solution)/shard_map/all_gather | solution.py:164
  123.1 4.4 %collective-permute-done.6 = bf16[256,2048]{1,0:T(8,128)(2,1)} collective-permute-done((bf16[256,2048]{1,0:T(8,128)(2,1)S(1)}, bf16[256,2048]{1,0:T(8,128)(2,1)}, u32[]{:S(2)}, u32[]{:S(2)}) %collective-permute-start.6) | collective-permute-done | bytes 1048608 | tf_op jit(solution)/shard_map/ppermute | solution.py:185
  127.5 4.9 %fusion.10 = bf16[512,1024]{1,0:T(8,128)(2,1)S(1)} fusion(bf16[2048,1024]{1,0:T(8,128)(2,1)} %all-gather.5.cloned.1.call-done, bf16[256,2048]{1,0:T(8,128)(2,1)} %collective-permute-done.6, bf16[256,2048]{1,0:T(8,128)(2,1)S(1)} %multiply_convert_fusion), kind=kOutput, calls=%fused_computation.20 | convolution fusion | flops 2152202240 | bytes 7340032 | tf_op jit(solution)/shard_map/dot_general | solution.py:79
  132.4 0.1 fusion.25
  132.5 1.9 collective-permute-start.7
  134.4 3.6 %collective-permute-start.8 = (bf16[256,1024]{1,0:T(8,128)(2,1)S(1)}, bf16[256,1024]{1,0:T(8,128)(2,1)}, u32[]{:S(2)}, u32[]{:S(2)}) collective-permute-start(bf16[256,1024]{1,0:T(8,128)(2,1)S(1)} %get-tuple-element.11), channel_id=1, source_target_pairs={{1,0},{2,1},{3,2},{4,3},{5,4},{6,5},{7,6},{8,7},{9,8},{10,9},{11,1... | collective-permute-start | bytes 1572872 | tf_op jit(solution)/shard_map/ppermute | solution.py:47
  138.1 1.5 collective-permute-start.10
  139.6 1.9 collective-permute-start.11
  141.5 3.8 %collective-permute-start.9 = (bf16[256,1024]{1,0:T(8,128)(2,1)S(1)}, bf16[256,1024]{1,0:T(8,128)(2,1)}, u32[]{:S(2)}, u32[]{:S(2)}) collective-permute-start(bf16[256,1024]{1,0:T(8,128)(2,1)S(1)} %get-tuple-element.12), channel_id=1, source_target_pairs={{0,17},{1,18},{2,19},{3,20},{4,21},{5,22},{6,23},{7,24},{8,25},{9,... | collective-permute-start | bytes 1572872 | tf_op jit(solution)/shard_map/ppermute | solution.py:47
  145.4 0.1 copy.17
  145.5 0.1 reshape.67
  145.5 0.7 concatenate.16.prm
  146.2 8.0 %collective-permute-done.7 = bf16[256,1024]{1,0:T(8,128)(2,1)S(1)} collective-permute-done((bf16[256,1024]{1,0:T(8,128)(2,1)S(1)}, bf16[256,1024]{1,0:T(8,128)(2,1)S(1)}, u32[]{:S(2)}, u32[]{:S(2)}) %collective-permute-start.7) | collective-permute-done | bytes 524320 | tf_op jit(solution)/shard_map/ppermute | solution.py:47
  154.2 1.2 maximum_bitcast_fusion
  155.4 3.2 %collective-permute-done.10 = bf16[256,1024]{1,0:T(8,128)(2,1)S(1)} collective-permute-done((bf16[256,1024]{1,0:T(8,128)(2,1)S(1)}, bf16[256,1024]{1,0:T(8,128)(2,1)S(1)}, u32[]{:S(2)}, u32[]{:S(2)}) %collective-permute-start.10) | collective-permute-done | bytes 524320 | tf_op jit(solution)/shard_map/ppermute | solution.py:47
  158.5 8.8 %collective-permute-done.11 = bf16[256,1024]{1,0:T(8,128)(2,1)S(1)} collective-permute-done((bf16[256,1024]{1,0:T(8,128)(2,1)S(1)}, bf16[256,1024]{1,0:T(8,128)(2,1)S(1)}, u32[]{:S(2)}, u32[]{:S(2)}) %collective-permute-start.11) | collective-permute-done | bytes 524320 | tf_op jit(solution)/shard_map/ppermute | solution.py:47
  167.3 7.1 %collective-permute-done.9 = bf16[256,1024]{1,0:T(8,128)(2,1)} collective-permute-done((bf16[256,1024]{1,0:T(8,128)(2,1)S(1)}, bf16[256,1024]{1,0:T(8,128)(2,1)}, u32[]{:S(2)}, u32[]{:S(2)}) %collective-permute-start.9) | collective-permute-done | bytes 524320 | tf_op jit(solution)/shard_map/ppermute | solution.py:47
  174.4 1.2 maximum_bitcast_fusion.1
  175.5 1.9 pad_maximum_fusion.k_ref.v_ref
  177.5 22.5 %shard_map.118 = bf16[1024,1024]{1,0:T(8,128)(2,1)} custom-call(s32[12]{0:T(128)} %concatenate.16.prm, f32[8]{0:T(128)} %slopes_ref.1, bf16[1024,1024]{1,0:T(8,128)(2,1)} %q_ref.1, bf16[2,768,1024]{2,1,0:T(8,128)(2,1)} %pad_maximum_fusion.k_ref.v_ref, bf16[2,768,1024]{2,1,0:T(8,128)(2,1)} %pad_maximum_fusion.k_ref.v_ref), custom_call_target="tpu_custom_call" | custom-call | tf_op jit(solution)/shard_map/pallas_call | solution.py:127
  (14 shorter events, 0.1 us)
Async XLA Ops:
  6.5 90.3 %copy-start = (bf16[256,1024]{1,0:T(8,128)(2,1)S(1)}, bf16[256,1024]{1,0:T(8,128)(2,1)}, u32[]{:S(2)}) copy-start(bf16[256,1024]{1,0:T(8,128)(2,1)} %param.12) | copy-start | bytes 1572868
  6.5 95.1 %all-gather.3.cloned.1.call-start = ((), (), s32[]{:S(2)}) async-start(), calls=%async_computation | async-start | bytes 4456448 | tf_op jit(solution)/shard_map/all_gather | solution.py:152
  7.3 115.8 %all-gather.5.cloned.1.call-start = ((), (), s32[]{:S(2)}) async-start(), calls=%async_computation.1 | async-start | bytes 4456448 | tf_op jit(solution)/shard_map/all_gather | solution.py:164
  11.6 83.3 %collective-permute-start.4 = (bf16[2,256,1024]{1,2,0:T(8,128)(2,1)S(1)}, bf16[2,256,1024]{1,2,0:T(8,128)(2,1)}, u32[]{:S(2)}, u32[]{:S(2)}) collective-permute-start(bf16[2,256,1024]{1,2,0:T(8,128)(2,1)S(1)} %pad_maximum_fusion.1), channel_id=1, source_target_pairs={{0,2},{1,3},{2,4},{3,5},{4,6},{5,7},{6,8},{7,9},{8,10},{9,11},{10,... | collective-permute-start | bytes 3145736 | tf_op jit(solution)/shard_map/ppermute | solution.py:23
  15.1 79.8 %collective-permute-start.5 = (bf16[2,256,1024]{1,2,0:T(8,128)(2,1)S(1)}, bf16[2,256,1024]{1,2,0:T(8,128)(2,1)}, u32[]{:S(2)}, u32[]{:S(2)}) collective-permute-start(bf16[2,256,1024]{1,2,0:T(8,128)(2,1)S(1)} %pad_maximum_fusion.1), channel_id=1, source_target_pairs={{0,1},{1,2},{2,3},{3,4},{4,5},{5,6},{6,7},{7,8},{8,9},{9,10},{10,1... | collective-permute-start | bytes 3145736 | tf_op jit(solution)/shard_map/ppermute | solution.py:23
  17.0 46.8 %collective-permute-start = (s32[1]{0:T(128)}, s32[1]{0:T(128)}, u32[]{:S(2)}, u32[]{:S(2)}) collective-permute-start(s32[1]{0:T(128)} %param.22), channel_id=1, source_target_pairs={{0,1},{1,2},{2,3},{3,4},{4,5},{5,6},{6,7},{7,8},{8,9},{9,10},{10,1... | collective-permute-start | bytes 20 | tf_op jit(solution)/shard_map/ppermute | solution.py:23
  64.4 16.8 %collective-permute-start.1 = (s32[1]{0:T(128)}, s32[1]{0:T(128)}, u32[]{:S(2)}, u32[]{:S(2)}) collective-permute-start(s32[1]{0:T(128)} %add.53), channel_id=1, source_target_pairs={{0,2},{1,3},{2,4},{3,5},{4,6},{5,7},{6,8},{7,9},{8,10},{9,11},{10,... | collective-permute-start | bytes 20 | tf_op jit(solution)/shard_map/ppermute | solution.py:23
  81.9 5.4 %collective-permute-start.2 = (s32[1]{0:T(128)}, s32[1]{0:T(128)}, u32[]{:S(2)}, u32[]{:S(2)}) collective-permute-start(s32[1]{0:T(128)} %add.54), channel_id=1, source_target_pairs={{0,4},{1,5},{2,6},{3,7},{4,8},{5,9},{6,10},{7,11},{8,12},{9,13},{1... | collective-permute-start | bytes 20 | tf_op jit(solution)/shard_map/ppermute | solution.py:23
  88.0 6.3 %collective-permute-start.3 = (s32[1]{0:T(128)}, s32[1]{0:T(128)}, u32[]{:S(2)}, u32[]{:S(2)}) collective-permute-start(s32[1]{0:T(128)} %add.55), channel_id=1, source_target_pairs={{0,8},{1,9},{2,10},{3,11},{4,12},{5,13},{6,14},{7,15},{16,24},{17,... | collective-permute-start | bytes 20 | tf_op jit(solution)/shard_map/ppermute | solution.py:23
  100.9 1.4 copy-start.1
  101.6 4.3 %copy-start.2 = (f32[2048]{0:T(1024)S(1)}, f32[2048]{0:T(1024)}, u32[]{:S(2)}) copy-start(f32[2048]{0:T(1024)} %param.17) | copy-start | bytes 24580
  106.1 39.2 %copy-start.3 = (s32[4,2]{0,1:T(2,128)S(1)}, s32[4,2]{0,1:T(2,128)}, u32[]{:S(2)}) copy-start(s32[4,2]{0,1:T(2,128)} %param.23) | copy-start | bytes 100
  106.2 21.4 %collective-permute-start.6 = (bf16[256,2048]{1,0:T(8,128)(2,1)S(1)}, bf16[256,2048]{1,0:T(8,128)(2,1)}, u32[]{:S(2)}, u32[]{:S(2)}) collective-permute-start(bf16[256,2048]{1,0:T(8,128)(2,1)S(1)} %multiply_convert_fusion), channel_id=1, source_target_pairs={{0,16},{16,0},{1,17},{17,1},{2,18},{18,2},{3,19},{19,3},{4,20},{20... | collective-permute-start | bytes 3145736 | tf_op jit(solution)/shard_map/ppermute | solution.py:185
  132.5 21.7 %collective-permute-start.7 = (bf16[256,1024]{1,0:T(8,128)(2,1)S(1)}, bf16[256,1024]{1,0:T(8,128)(2,1)S(1)}, u32[]{:S(2)}, u32[]{:S(2)}) collective-permute-start(bf16[256,1024]{1,0:T(8,128)(2,1)S(1)} %get-tuple-element.11), channel_id=1, source_target_pairs={{0,1},{1,2},{2,3},{3,4},{4,5},{5,6},{6,7},{7,8},{8,9},{9,10},{10,1... | collective-permute-start | bytes 1572872 | tf_op jit(solution)/shard_map/ppermute | solution.py:47
  134.4 19.8 %collective-permute-start.8 = (bf16[256,1024]{1,0:T(8,128)(2,1)S(1)}, bf16[256,1024]{1,0:T(8,128)(2,1)}, u32[]{:S(2)}, u32[]{:S(2)}) collective-permute-start(bf16[256,1024]{1,0:T(8,128)(2,1)S(1)} %get-tuple-element.11), channel_id=1, source_target_pairs={{1,0},{2,1},{3,2},{4,3},{5,4},{6,5},{7,6},{8,7},{9,8},{10,9},{11,1... | collective-permute-start | bytes 1572872 | tf_op jit(solution)/shard_map/ppermute | solution.py:47
  138.1 20.5 %collective-permute-start.10 = (bf16[256,1024]{1,0:T(8,128)(2,1)S(1)}, bf16[256,1024]{1,0:T(8,128)(2,1)S(1)}, u32[]{:S(2)}, u32[]{:S(2)}) collective-permute-start(bf16[256,1024]{1,0:T(8,128)(2,1)S(1)} %get-tuple-element.12), channel_id=1, source_target_pairs={{0,16},{1,17},{2,18},{3,19},{4,20},{5,21},{6,22},{7,23},{8,24},{9,... | collective-permute-start | bytes 1572872 | tf_op jit(solution)/shard_map/ppermute | solution.py:47
  139.6 27.7 %collective-permute-start.11 = (bf16[256,1024]{1,0:T(8,128)(2,1)S(1)}, bf16[256,1024]{1,0:T(8,128)(2,1)S(1)}, u32[]{:S(2)}, u32[]{:S(2)}) collective-permute-start(bf16[256,1024]{1,0:T(8,128)(2,1)S(1)} %get-tuple-element.12), channel_id=1, source_target_pairs={{1,16},{2,17},{3,18},{4,19},{5,20},{6,21},{7,22},{8,23},{9,24},{10... | collective-permute-start | bytes 1572872 | tf_op jit(solution)/shard_map/ppermute | solution.py:47
  141.5 32.9 %collective-permute-start.9 = (bf16[256,1024]{1,0:T(8,128)(2,1)S(1)}, bf16[256,1024]{1,0:T(8,128)(2,1)}, u32[]{:S(2)}, u32[]{:S(2)}) collective-permute-start(bf16[256,1024]{1,0:T(8,128)(2,1)S(1)} %get-tuple-element.12), channel_id=1, source_target_pairs={{0,17},{1,18},{2,19},{3,20},{4,21},{5,22},{6,23},{7,24},{8,25},{9,... | collective-permute-start | bytes 1572872 | tf_op jit(solution)/shard_map/ppermute | solution.py:47
Sparse Core Ops, SparseCore 0:
  9.5 62.1 all-gather.2
  73.9 49.1 all-gather.4

commit v7 on v6

--- a/solution.py
+++ b/solution.py
@@ -79,32 +79,34 @@
     return jnp.dot(left_side, weight_piece, preferred_element_type=jnp.float32)
 
 
-def coarse_kernel(prm, slopes_ref, q_ref, k_ref, v_ref, o_ref, *, blocks, near_rows):
+def coarse_kernel(prm, slopes_ref, q_ref, k_ref, v_ref, o_ref, *, blocks, near_rows, span):
     n = pl.program_id(0)
     band_low = prm[2 * n]
     band_high = prm[2 * n + 1]
     stream_start = prm[2 * blocks]
     live_count = prm[2 * blocks + 1]
     base_row = prm[2 * blocks + 2]
+    first_key = jnp.minimum(band_low - base_row, near_rows - BAND)
+    step = span - BAND
+    window = pl.multiple_of(jnp.clip(first_key // step * step, 0, near_rows - span), step)
     rows = n * CB + lax.broadcasted_iota(jnp.int32, (CB, 1), 0)
     timing = ((stream_start + rows) // 2).astype(jnp.float32) * (2.0 / 3.0)
-    key_global = base_row + lax.broadcasted_iota(jnp.int32, (1, near_rows), 1)
+    key_global = base_row + window + lax.broadcasted_iota(jnp.int32, (1, span), 1)
     inside = (key_global >= band_low) & (key_global < band_high)
-    distance = jnp.abs(timing - key_global.astype(jnp.float32))
+    distance = jnp.where(inside, jnp.abs(timing - key_global.astype(jnp.float32)), -NEG_FILL)
     live_rows = rows < live_count
     for h in range(HEADS):
         cols = slice(h * HEAD_DIM, (h + 1) * HEAD_DIM)
         scores = lax.dot_general(
-            q_ref[:, cols], k_ref[:, cols], (((1,), (1,)), ((), ())),
+            q_ref[:, cols], k_ref[pl.ds(window, span), cols], (((1,), (1,)), ((), ())),
             preferred_element_type=jnp.float32,
         ) * HEAD_DIM ** (-0.5)
-        time_bias = distance * (-slopes_ref[h] / BAND)
-        scores = jnp.where(inside, scores + time_bias, NEG_FILL)
+        scores = scores + distance * (-slopes_ref[h] / BAND)
         largest = jnp.max(scores, axis=1, keepdims=True)
         exponent = jnp.exp(scores - largest)
         total = jnp.sum(exponent, axis=1, keepdims=True)
         weights = (exponent * (1.0 / total)).astype(jnp.bfloat16)
-        blended = jnp.dot(weights, v_ref[:, cols], preferred_element_type=jnp.float32)
+        blended = jnp.dot(weights, v_ref[pl.ds(window, span), cols], preferred_element_type=jnp.float32)
         o_ref[:, cols] = jnp.where(live_rows, blended, 0.0).astype(jnp.bfloat16)
 
 
@@ -112,7 +114,7 @@
     slots, width = coarse_queries.shape
     blocks = slots // CB
     near_rows = near_pair.shape[1]
-    kernel = functools.partial(coarse_kernel, blocks=blocks, near_rows=near_rows)
+    kernel = functools.partial(coarse_kernel, blocks=blocks, near_rows=near_rows, span=BAND + 128)
     grid_spec = pltpu.PrefetchScalarGridSpec(
         num_scalar_prefetch=1,
         grid=(blocks,),

time: 207 us -> 207 us (level)
  no operation moved by 1% of the time
where the time goes in v7:
time: 207 us; the launch traced here: 206 us
  waiting for transfers between devices  96.2 us (46%)
  starting transfers between devices  45.6 us (22%)
  Pallas kernels  21.8 us (11%)
  between operations  16.8 us (8%)
  other arithmetic  11.3 us (5%)
  matrix products  10.1 us (5%)
  local copies, waits for them, and re-layouts  4.31 us (2%)
    ppermute x6, waiting for transfers between devices, passed_along(): return lax.ppermute(array, axis, pairs)  48.6 us
    ppermute x6, starting transfers between devices, passed_along(): return lax.ppermute(array, axis, pairs)  31.2 us
    ppermute x5, waiting for transfers between devices, sent_to(): return lax.ppermute(array, ('groups', 'ctx'), pairs)  27 us
    pallas_call x1, Pallas kernels, coarse_attention(): pl.pallas_call(kernel, grid_spec=grid_spec, out_shape=jax.ShapeDtypeStruc...  21.8 us
    all_gather x1, waiting for transfers between devices, on_device(): gathered_proj = lax.all_gather(own_proj, 'ctx', axis=0, tiled=True)  15.4 us
    ppermute x5, starting transfers between devices, sent_to(): return lax.ppermute(array, ('groups', 'ctx'), pairs)  12.8 us
    dot_general x2, matrix products, contract_rows(): return jnp.dot(left_side, weight_piece, preferred_element_type=jnp.float32)  8.45 us
    ppermute x1, waiting for transfers between devices, on_device(): partner_normed = lax.ppermute(normed, 'groups', partners)  4.43 us
  transfers between devices with their start and end apart: 14, of which 9 were waited for; matrix products, arithmetic and copies ran while one was open for 8% of the time, Pallas kernels for 0%

profile of v7, /device:TPU:20, one launch (start us, length us, event | category | flops | bytes accessed | tf_op | source)
XLA Modules:
  0.0 206.1 jit_solution(1901270993058928427)
XLA Ops:
  6.5 0.7 all-gather.3.cloned.1.call-update
  7.3 0.0 all-gather.5.cloned.1.call-start
  7.3 1.7 broadcast_select_fusion
  9.0 0.0 all-gather.5.cloned.1.call-update
  9.0 1.2 copy.18
  10.3 1.2 copy.19
  11.5 0.1 pad_maximum_fusion.1
  11.6 3.4 %collective-permute-start.4 = (bf16[2,256,1024]{1,2,0:T(8,128)(2,1)S(1)}, bf16[2,256,1024]{1,2,0:T(8,128)(2,1)}, u32[]{:S(2)}, u32[]{:S(2)}) collective-permute-start(bf16[2,256,1024]{1,2,0:T(8,128)(2,1)S(1)} %pad_maximum_fusion.1), channel_id=1, source_target_pairs={{0,2},{1,3},{2,4},{3,5},{4,6},{5,7},{6,8},{7,9},{8,10},{9,11},{10,... | collective-permute-start | bytes 3145736 | tf_op jit(solution)/shard_map/ppermute | solution.py:23
  15.1 1.9 collective-permute-start.5
  17.0 3.5 %collective-permute-start = (s32[1]{0:T(128)}, s32[1]{0:T(128)}, u32[]{:S(2)}, u32[]{:S(2)}) collective-permute-start(s32[1]{0:T(128)} %param.22), channel_id=1, source_target_pairs={{0,1},{1,2},{2,3},{3,4},{4,5},{5,6},{6,7},{7,8},{8,9},{9,10},{10,1... | collective-permute-start | bytes 20 | tf_op jit(solution)/shard_map/ppermute | solution.py:23
  21.2 0.2 fusion.17
  21.5 42.4 %collective-permute-done = s32[1]{0:T(128)} collective-permute-done((s32[1]{0:T(128)}, s32[1]{0:T(128)}, u32[]{:S(2)}, u32[]{:S(2)}) %collective-permute-start) | collective-permute-done | bytes 36 | tf_op jit(solution)/shard_map/ppermute | solution.py:23
  64.4 16.8 %collective-permute-start.1 = (s32[1]{0:T(128)}, s32[1]{0:T(128)}, u32[]{:S(2)}, u32[]{:S(2)}) collective-permute-start(s32[1]{0:T(128)} %add.53), channel_id=1, source_target_pairs={{0,2},{1,3},{2,4},{3,5},{4,6},{5,7},{6,8},{7,9},{8,10},{9,11},{10,... | collective-permute-start | bytes 20 | tf_op jit(solution)/shard_map/ppermute | solution.py:23
  81.9 4.1 %collective-permute-start.2 = (s32[1]{0:T(128)}, s32[1]{0:T(128)}, u32[]{:S(2)}, u32[]{:S(2)}) collective-permute-start(s32[1]{0:T(128)} %add.54), channel_id=1, source_target_pairs={{0,4},{1,5},{2,6},{3,7},{4,8},{5,9},{6,10},{7,11},{8,12},{9,13},{1... | collective-permute-start | bytes 20 | tf_op jit(solution)/shard_map/ppermute | solution.py:23
  86.1 1.3 collective-permute-done.2
  88.0 1.3 collective-permute-start.3
  89.3 5.0 %collective-permute-done.3 = s32[1]{0:T(128)} collective-permute-done((s32[1]{0:T(128)}, s32[1]{0:T(128)}, u32[]{:S(2)}, u32[]{:S(2)}) %collective-permute-start.3) | collective-permute-done | bytes 36 | tf_op jit(solution)/shard_map/ppermute | solution.py:23
  94.9 1.7 maximum_maximum_fusion
  96.6 0.2 fusion.24
  96.8 1.0 fusion.18
  97.8 3.1 %fusion.26 = (f32[8,256]{1,0:T(8,128)S(1)}, f32[8,256,768]{1,2,0:T(8,128)S(1)}) fusion(f32[8,768,256]{2,1,0:T(8,128)S(1)} %fusion.18, pred[256,768]{0,1:T(8,128)(4,1)S(1)} %fusion.17), kind=kOutput, calls=%fused_computation.40 | output fusion | flops 9437951 | bytes 12787712 | tf_op jit(solution)/shard_map/sub | solution.py:63
  100.9 0.0 copy-start.1
  100.9 0.6 fusion.13
  101.6 0.0 all-gather.3.cloned.1.call-done
  101.6 0.7 copy-done.1
  102.3 3.6 %multiply_reduce_fusion = (f32[256]{0:T(256)S(1)}, f32[256,2048]{1,0:T(8,128)S(1)}) fusion(bf16[256,1024]{0,1:T(8,128)(2,1)S(1)} %bitcast.41, bf16[1024,2048]{1,0:T(8,128)(2,1)} %all-gather.3.cloned.1.call-done, bf16[256,2048]{1,0:T(8,128)(2,1)S(1)} %copy-done.1), kind=kOutput, calls=%fused_computation.17 | convolution fusion | flops 1075838720 | bytes 7865344 | tf_op jit(solution)/shard_map/dot_general | solution.py:79
  105.9 0.2 multiply_convert_fusion
  106.2 1.5 collective-permute-start.6
  107.7 15.4 %all-gather.5.cloned.1.call-done = bf16[2048,1024]{1,0:T(8,128)(2,1)} async-done(((bf16[128,1024]{1,0:T(8,128)(2,1)}), bf16[2048,1024]{1,0:T(8,128)(2,1)}) %all-gather.5.cloned.1.call-update) | async-done | bytes 4194320 | tf_op jit(solution)/shard_map/all_gather | solution.py:166
  123.1 4.4 %collective-permute-done.6 = bf16[256,2048]{1,0:T(8,128)(2,1)} collective-permute-done((bf16[256,2048]{1,0:T(8,128)(2,1)S(1)}, bf16[256,2048]{1,0:T(8,128)(2,1)}, u32[]{:S(2)}, u32[]{:S(2)}) %collective-permute-start.6) | collective-permute-done | bytes 1048608 | tf_op jit(solution)/shard_map/ppermute | solution.py:187
  127.5 4.9 %fusion.10 = bf16[512,1024]{1,0:T(8,128)(2,1)S(1)} fusion(bf16[2048,1024]{1,0:T(8,128)(2,1)} %all-gather.5.cloned.1.call-done, bf16[256,2048]{1,0:T(8,128)(2,1)} %collective-permute-done.6, bf16[256,2048]{1,0:T(8,128)(2,1)S(1)} %multiply_convert_fusion), kind=kOutput, calls=%fused_computation.20 | convolution fusion | flops 2152202240 | bytes 7340032 | tf_op jit(solution)/shard_map/dot_general | solution.py:79
  132.4 0.1 fusion.25
  132.5 1.9 collective-permute-start.7
  134.4 3.6 %collective-permute-start.8 = (bf16[256,1024]{1,0:T(8,128)(2,1)S(1)}, bf16[256,1024]{1,0:T(8,128)(2,1)}, u32[]{:S(2)}, u32[]{:S(2)}) collective-permute-start(bf16[256,1024]{1,0:T(8,128)(2,1)S(1)} %get-tuple-element.11), channel_id=1, source_target_pairs={{1,0},{2,1},{3,2},{4,3},{5,4},{6,5},{7,6},{8,7},{9,8},{10,9},{11,1... | collective-permute-start | bytes 1572872 | tf_op jit(solution)/shard_map/ppermute | solution.py:47
  138.1 1.5 collective-permute-start.10
  139.6 1.9 collective-permute-start.11
  141.5 3.8 %collective-permute-start.9 = (bf16[256,1024]{1,0:T(8,128)(2,1)S(1)}, bf16[256,1024]{1,0:T(8,128)(2,1)}, u32[]{:S(2)}, u32[]{:S(2)}) collective-permute-start(bf16[256,1024]{1,0:T(8,128)(2,1)S(1)} %get-tuple-element.12), channel_id=1, source_target_pairs={{0,17},{1,18},{2,19},{3,20},{4,21},{5,22},{6,23},{7,24},{8,25},{9,... | collective-permute-start | bytes 1572872 | tf_op jit(solution)/shard_map/ppermute | solution.py:47
  145.4 0.1 copy.17
  145.5 0.1 reshape.67
  145.5 0.7 concatenate.16.prm
  146.2 8.0 %collective-permute-done.7 = bf16[256,1024]{1,0:T(8,128)(2,1)S(1)} collective-permute-done((bf16[256,1024]{1,0:T(8,128)(2,1)S(1)}, bf16[256,1024]{1,0:T(8,128)(2,1)S(1)}, u32[]{:S(2)}, u32[]{:S(2)}) %collective-permute-start.7) | collective-permute-done | bytes 524320 | tf_op jit(solution)/shard_map/ppermute | solution.py:47
  154.2 1.2 maximum_bitcast_fusion
  155.4 3.2 %collective-permute-done.10 = bf16[256,1024]{1,0:T(8,128)(2,1)S(1)} collective-permute-done((bf16[256,1024]{1,0:T(8,128)(2,1)S(1)}, bf16[256,1024]{1,0:T(8,128)(2,1)S(1)}, u32[]{:S(2)}, u32[]{:S(2)}) %collective-permute-start.10) | collective-permute-done | bytes 524320 | tf_op jit(solution)/shard_map/ppermute | solution.py:47
  158.5 8.8 %collective-permute-done.11 = bf16[256,1024]{1,0:T(8,128)(2,1)S(1)} collective-permute-done((bf16[256,1024]{1,0:T(8,128)(2,1)S(1)}, bf16[256,1024]{1,0:T(8,128)(2,1)S(1)}, u32[]{:S(2)}, u32[]{:S(2)}) %collective-permute-start.11) | collective-permute-done | bytes 524320 | tf_op jit(solution)/shard_map/ppermute | solution.py:47
  167.3 7.1 %collective-permute-done.9 = bf16[256,1024]{1,0:T(8,128)(2,1)} collective-permute-done((bf16[256,1024]{1,0:T(8,128)(2,1)S(1)}, bf16[256,1024]{1,0:T(8,128)(2,1)}, u32[]{:S(2)}, u32[]{:S(2)}) %collective-permute-start.9) | collective-permute-done | bytes 524320 | tf_op jit(solution)/shard_map/ppermute | solution.py:47
  174.4 1.2 maximum_bitcast_fusion.1
  175.5 1.9 pad_maximum_fusion.k_ref.v_ref
  177.5 21.8 %shard_map.118 = bf16[1024,1024]{1,0:T(8,128)(2,1)} custom-call(s32[12]{0:T(128)} %concatenate.16.prm, f32[8]{0:T(128)} %slopes_ref.1, bf16[1024,1024]{1,0:T(8,128)(2,1)} %q_ref.1, bf16[2,768,1024]{2,1,0:T(8,128)(2,1)} %pad_maximum_fusion.k_ref.v_ref, bf16[2,768,1024]{2,1,0:T(8,128)(2,1)} %pad_maximum_fusion.k_ref.v_ref), custom_call_target="tpu_custom_call" | custom-call | tf_op jit(solution)/shard_map/pallas_call | solution.py:129
  (14 shorter events, 0.1 us)
Async XLA Ops:
  6.5 90.3 %copy-start = (bf16[256,1024]{1,0:T(8,128)(2,1)S(1)}, bf16[256,1024]{1,0:T(8,128)(2,1)}, u32[]{:S(2)}) copy-start(bf16[256,1024]{1,0:T(8,128)(2,1)} %param.12) | copy-start | bytes 1572868
  6.5 95.1 %all-gather.3.cloned.1.call-start = ((), (), s32[]{:S(2)}) async-start(), calls=%async_computation | async-start | bytes 4456448 | tf_op jit(solution)/shard_map/all_gather | solution.py:154
  7.3 115.8 %all-gather.5.cloned.1.call-start = ((), (), s32[]{:S(2)}) async-start(), calls=%async_computation.1 | async-start | bytes 4456448 | tf_op jit(solution)/shard_map/all_gather | solution.py:166
  11.6 83.3 %collective-permute-start.4 = (bf16[2,256,1024]{1,2,0:T(8,128)(2,1)S(1)}, bf16[2,256,1024]{1,2,0:T(8,128)(2,1)}, u32[]{:S(2)}, u32[]{:S(2)}) collective-permute-start(bf16[2,256,1024]{1,2,0:T(8,128)(2,1)S(1)} %pad_maximum_fusion.1), channel_id=1, source_target_pairs={{0,2},{1,3},{2,4},{3,5},{4,6},{5,7},{6,8},{7,9},{8,10},{9,11},{10,... | collective-permute-start | bytes 3145736 | tf_op jit(solution)/shard_map/ppermute | solution.py:23
  15.1 79.8 %collective-permute-start.5 = (bf16[2,256,1024]{1,2,0:T(8,128)(2,1)S(1)}, bf16[2,256,1024]{1,2,0:T(8,128)(2,1)}, u32[]{:S(2)}, u32[]{:S(2)}) collective-permute-start(bf16[2,256,1024]{1,2,0:T(8,128)(2,1)S(1)} %pad_maximum_fusion.1), channel_id=1, source_target_pairs={{0,1},{1,2},{2,3},{3,4},{4,5},{5,6},{6,7},{7,8},{8,9},{9,10},{10,1... | collective-permute-start | bytes 3145736 | tf_op jit(solution)/shard_map/ppermute | solution.py:23
  17.0 46.8 %collective-permute-start = (s32[1]{0:T(128)}, s32[1]{0:T(128)}, u32[]{:S(2)}, u32[]{:S(2)}) collective-permute-start(s32[1]{0:T(128)} %param.22), channel_id=1, source_target_pairs={{0,1},{1,2},{2,3},{3,4},{4,5},{5,6},{6,7},{7,8},{8,9},{9,10},{10,1... | collective-permute-start | bytes 20 | tf_op jit(solution)/shard_map/ppermute | solution.py:23
  64.4 16.8 %collective-permute-start.1 = (s32[1]{0:T(128)}, s32[1]{0:T(128)}, u32[]{:S(2)}, u32[]{:S(2)}) collective-permute-start(s32[1]{0:T(128)} %add.53), channel_id=1, source_target_pairs={{0,2},{1,3},{2,4},{3,5},{4,6},{5,7},{6,8},{7,9},{8,10},{9,11},{10,... | collective-permute-start | bytes 20 | tf_op jit(solution)/shard_map/ppermute | solution.py:23
  81.9 5.4 %collective-permute-start.2 = (s32[1]{0:T(128)}, s32[1]{0:T(128)}, u32[]{:S(2)}, u32[]{:S(2)}) collective-permute-start(s32[1]{0:T(128)} %add.54), channel_id=1, source_target_pairs={{0,4},{1,5},{2,6},{3,7},{4,8},{5,9},{6,10},{7,11},{8,12},{9,13},{1... | collective-permute-start | bytes 20 | tf_op jit(solution)/shard_map/ppermute | solution.py:23
  88.0 6.3 %collective-permute-start.3 = (s32[1]{0:T(128)}, s32[1]{0:T(128)}, u32[]{:S(2)}, u32[]{:S(2)}) collective-permute-start(s32[1]{0:T(128)} %add.55), channel_id=1, source_target_pairs={{0,8},{1,9},{2,10},{3,11},{4,12},{5,13},{6,14},{7,15},{16,24},{17,... | collective-permute-start | bytes 20 | tf_op jit(solution)/shard_map/ppermute | solution.py:23
  100.9 1.4 copy-start.1
  101.6 4.3 %copy-start.2 = (f32[2048]{0:T(1024)S(1)}, f32[2048]{0:T(1024)}, u32[]{:S(2)}) copy-start(f32[2048]{0:T(1024)} %param.17) | copy-start | bytes 24580
  106.1 39.2 %copy-start.3 = (s32[4,2]{0,1:T(2,128)S(1)}, s32[4,2]{0,1:T(2,128)}, u32[]{:S(2)}) copy-start(s32[4,2]{0,1:T(2,128)} %param.23) | copy-start | bytes 100
  106.2 21.4 %collective-permute-start.6 = (bf16[256,2048]{1,0:T(8,128)(2,1)S(1)}, bf16[256,2048]{1,0:T(8,128)(2,1)}, u32[]{:S(2)}, u32[]{:S(2)}) collective-permute-start(bf16[256,2048]{1,0:T(8,128)(2,1)S(1)} %multiply_convert_fusion), channel_id=1, source_target_pairs={{0,16},{16,0},{1,17},{17,1},{2,18},{18,2},{3,19},{19,3},{4,20},{20... | collective-permute-start | bytes 3145736 | tf_op jit(solution)/shard_map/ppermute | solution.py:187
  132.5 21.7 %collective-permute-start.7 = (bf16[256,1024]{1,0:T(8,128)(2,1)S(1)}, bf16[256,1024]{1,0:T(8,128)(2,1)S(1)}, u32[]{:S(2)}, u32[]{:S(2)}) collective-permute-start(bf16[256,1024]{1,0:T(8,128)(2,1)S(1)} %get-tuple-element.11), channel_id=1, source_target_pairs={{0,1},{1,2},{2,3},{3,4},{4,5},{5,6},{6,7},{7,8},{8,9},{9,10},{10,1... | collective-permute-start | bytes 1572872 | tf_op jit(solution)/shard_map/ppermute | solution.py:47
  134.4 19.8 %collective-permute-start.8 = (bf16[256,1024]{1,0:T(8,128)(2,1)S(1)}, bf16[256,1024]{1,0:T(8,128)(2,1)}, u32[]{:S(2)}, u32[]{:S(2)}) collective-permute-start(bf16[256,1024]{1,0:T(8,128)(2,1)S(1)} %get-tuple-element.11), channel_id=1, source_target_pairs={{1,0},{2,1},{3,2},{4,3},{5,4},{6,5},{7,6},{8,7},{9,8},{10,9},{11,1... | collective-permute-start | bytes 1572872 | tf_op jit(solution)/shard_map/ppermute | solution.py:47
  138.1 20.5 %collective-permute-start.10 = (bf16[256,1024]{1,0:T(8,128)(2,1)S(1)}, bf16[256,1024]{1,0:T(8,128)(2,1)S(1)}, u32[]{:S(2)}, u32[]{:S(2)}) collective-permute-start(bf16[256,1024]{1,0:T(8,128)(2,1)S(1)} %get-tuple-element.12), channel_id=1, source_target_pairs={{0,16},{1,17},{2,18},{3,19},{4,20},{5,21},{6,22},{7,23},{8,24},{9,... | collective-permute-start | bytes 1572872 | tf_op jit(solution)/shard_map/ppermute | solution.py:47
  139.6 27.7 %collective-permute-start.11 = (bf16[256,1024]{1,0:T(8,128)(2,1)S(1)}, bf16[256,1024]{1,0:T(8,128)(2,1)S(1)}, u32[]{:S(2)}, u32[]{:S(2)}) collective-permute-start(bf16[256,1024]{1,0:T(8,128)(2,1)S(1)} %get-tuple-element.12), channel_id=1, source_target_pairs={{1,16},{2,17},{3,18},{4,19},{5,20},{6,21},{7,22},{8,23},{9,24},{10... | collective-permute-start | bytes 1572872 | tf_op jit(solution)/shard_map/ppermute | solution.py:47
  141.5 32.9 %collective-permute-start.9 = (bf16[256,1024]{1,0:T(8,128)(2,1)S(1)}, bf16[256,1024]{1,0:T(8,128)(2,1)}, u32[]{:S(2)}, u32[]{:S(2)}) collective-permute-start(bf16[256,1024]{1,0:T(8,128)(2,1)S(1)} %get-tuple-element.12), channel_id=1, source_target_pairs={{0,17},{1,18},{2,19},{3,20},{4,21},{5,22},{6,23},{7,24},{8,25},{9,... | collective-permute-start | bytes 1572872 | tf_op jit(solution)/shard_map/ppermute | solution.py:47
Sparse Core Ops, SparseCore 0:
  9.5 62.1 all-gather.2
  73.9 49.1 all-gather.4

commit v8 on v7

--- a/solution.py
+++ b/solution.py
@@ -79,7 +79,7 @@
     return jnp.dot(left_side, weight_piece, preferred_element_type=jnp.float32)
 
 
-def coarse_kernel(prm, slopes_ref, q_ref, k_ref, v_ref, o_ref, *, blocks, near_rows, span):
+def coarse_kernel(prm, slopes_ref, q_ref, k_ref, v_ref, o_ref, *, blocks, near_rows, span, first_head, heads):
     n = pl.program_id(0)
     band_low = prm[2 * n]
     band_high = prm[2 * n + 1]
@@ -95,13 +95,13 @@
     inside = (key_global >= band_low) & (key_global < band_high)
     distance = jnp.where(inside, jnp.abs(timing - key_global.astype(jnp.float32)), -NEG_FILL)
     live_rows = rows < live_count
-    for h in range(HEADS):
+    for h in range(heads):
         cols = slice(h * HEAD_DIM, (h + 1) * HEAD_DIM)
         scores = lax.dot_general(
             q_ref[:, cols], k_ref[pl.ds(window, span), cols], (((1,), (1,)), ((), ())),
             preferred_element_type=jnp.float32,
         ) * HEAD_DIM ** (-0.5)
-        scores = scores + distance * (-slopes_ref[h] / BAND)
+        scores = scores + distance * (-slopes_ref[first_head + h] / BAND)
         largest = jnp.max(scores, axis=1, keepdims=True)
         exponent = jnp.exp(scores - largest)
         total = jnp.sum(exponent, axis=1, keepdims=True)
@@ -110,17 +110,21 @@
         o_ref[:, cols] = jnp.where(live_rows, blended, 0.0).astype(jnp.bfloat16)
 
 
-def coarse_attention(coarse_queries, near_pair, params, slopes):
-    slots, width = coarse_queries.shape
+def coarse_attention(coarse_queries, near_pair, params, slopes, first_head, heads):
+    slots = coarse_queries.shape[0]
     blocks = slots // CB
-    near_rows = near_pair.shape[1]
-    kernel = functools.partial(coarse_kernel, blocks=blocks, near_rows=near_rows, span=BAND + 128)
+    near_rows, width = near_pair.shape[1:]
+    kernel = functools.partial(
+        coarse_kernel, blocks=blocks, near_rows=near_rows, span=BAND + 128,
+        first_head=first_head, heads=heads,
+    )
+    column_block = first_head // heads
     grid_spec = pltpu.PrefetchScalarGridSpec(
         num_scalar_prefetch=1,
         grid=(blocks,),
         in_specs=[
             pl.BlockSpec(memory_space=pltpu.SMEM),
-            pl.BlockSpec((CB, width), lambda n, prm: (n, 0)),
+            pl.BlockSpec((CB, width), lambda n, prm: (n, column_block)),
             pl.BlockSpec((None, near_rows, width), lambda n, prm: (prm[2 * blocks + 3], 0, 0)),
             pl.BlockSpec((None, near_rows, width), lambda n, prm: (1 - prm[2 * blocks + 3], 0, 0)),
         ],
@@ -187,18 +191,24 @@
         partner_normed = lax.ppermute(normed, "groups", partners)
         both_streams = jnp.concatenate([normed, partner_normed], axis=0)
         both_sums = contract_rows(both_streams, gathered_proj).astype(jnp.bfloat16)
-        own_sum = both_sums[:rows_here]
-        partner_part = both_sums[rows_here:]
-        mine_near = jnp.concatenate(
-            [sent_to(own_sum, 0, 1), own_sum, sent_to(own_sum, 0, -1)], axis=0)
-        other_near = jnp.concatenate(
-            [sent_to(partner_part, 1, 1), sent_to(partner_part, 1, 0), sent_to(partner_part, 1, -1)], axis=0)
-        near_pair = jnp.stack([mine_near, other_near])
+        pieces = []
+        half = both_sums.shape[1] // 2
+        for part in range(2):
+            piece = both_sums[:, part * half:(part + 1) * half]
+            if pieces:
+                _, piece = lax.optimization_barrier((pieces[-1], piece))
+            own_sum = piece[:rows_here]
+            partner_part = piece[rows_here:]
+            mine_near = jnp.concatenate(
+                [sent_to(own_sum, 0, 1), own_sum, sent_to(own_sum, 0, -1)], axis=0)
+            other_near = jnp.concatenate(
+                [sent_to(partner_part, 1, 1), sent_to(partner_part, 1, 0), sent_to(partner_part, 1, -1)], axis=0)
+            pieces.append(jnp.stack([mine_near, other_near]))
         key_slot = jnp.where(key_side, 0, 1)
     else:
         cross_keys = contract_rows(normed, gathered_proj[0]).astype(jnp.bfloat16)
         cross_values = contract_rows(normed, gathered_proj[1]).astype(jnp.bfloat16)
-        near_pair = with_halo(jnp.stack([cross_keys, cross_values]), (("ctx", 1),), rows_here)
+        pieces = [with_halo(jnp.stack([cross_keys, cross_values]), (("ctx", 1),), rows_here)]
         key_slot = jnp.zeros((), jnp.int32)
     stream_start = (running - counts)[0]
     base_row = (device_index - 1) * rows_here
@@ -206,7 +216,12 @@
         [band_bounds.reshape(-1).astype(jnp.int32),
          jnp.stack([stream_start, counts[0], base_row, key_slot]).astype(jnp.int32)]
     )
-    return coarse_attention(coarse_queries, near_pair, params, slopes)
+    heads = HEADS // len(pieces)
+    outputs = [
+        coarse_attention(coarse_queries, piece, params, slopes, part * heads, heads)
+        for part, piece in enumerate(pieces)
+    ]
+    return jnp.concatenate(outputs, axis=1)
 
 
 def solution(mesh):

time: 207 us -> 209 us (level)
  waiting for transfers between devices: 96.2 us -> 81 us
  starting transfers between devices: 45.6 us -> 58.7 us
  Pallas kernels: 21.8 us -> 25.1 us
    ppermute x5 -> x10, waiting for transfers between devices: 27 us -> 12.1 us  [sent_to(): return lax.ppermute(array, ('groups', 'ctx'), pairs)]
    ppermute x5 -> x10, starting transfers between devices: 12.8 us -> 26.1 us  [sent_to(): return lax.ppermute(array, ('groups', 'ctx'), pairs)]
    pallas_call x1 -> x2, Pallas kernels: 21.8 us -> 25.1 us  [coarse_attention(): pl.pallas_call(kernel, grid_spec=grid_spec, out_shape=jax.ShapeDtypeStruc...]
    concatenate x0 -> x1, other arithmetic: none -> 2.81 us  [on_device(): return jnp.concatenate(outputs, axis=1)]
    another operation x3 -> x6, other arithmetic: 4.25 us -> 2.77 us  [on_device(): pieces.append(jnp.stack([mine_near, other_near]))]
  transfers between devices with their start and end apart: 14 -> 19, of which waited for: 9 -> 8; matrix products, arithmetic and copies ran while one was open for 8% -> 7% of each run, Pallas kernels for 0% -> 6%
where the time goes in v8:
time: 209 us; the launch traced here: 208 us
  waiting for transfers between devices  81 us (39%)
  starting transfers between devices  58.7 us (28%)
  Pallas kernels  25.1 us (12%)
  between operations  17.2 us (8%)
  other arithmetic  12.6 us (6%)
  matrix products  9.78 us (5%)
  local copies, waits for them, and re-layouts  3.33 us (2%)
    ppermute x6, waiting for transfers between devices, passed_along(): return lax.ppermute(array, axis, pairs)  49.1 us
    ppermute x6, starting transfers between devices, passed_along(): return lax.ppermute(array, axis, pairs)  31 us
    ppermute x10, starting transfers between devices, sent_to(): return lax.ppermute(array, ('groups', 'ctx'), pairs)  26.1 us
    pallas_call x2, Pallas kernels, coarse_attention(): pl.pallas_call(kernel, grid_spec=grid_spec, out_shape=jax.ShapeDtypeStruc...  25.1 us
    all_gather x1, waiting for transfers between devices, on_device(): gathered_proj = lax.all_gather(own_proj, 'ctx', axis=0, tiled=True)  15.8 us
    ppermute x10, waiting for transfers between devices, sent_to(): return lax.ppermute(array, ('groups', 'ctx'), pairs)  12.1 us
    dot_general x2, matrix products, contract_rows(): return jnp.dot(left_side, weight_piece, preferred_element_type=jnp.float32)  8.11 us
  transfers between devices with their start and end apart: 19, of which 8 were waited for; matrix products, arithmetic and copies ran while one was open for 7% of the time, Pallas kernels for 6%

profile of v8, /device:TPU:20, one launch (start us, length us, event | category | flops | bytes accessed | tf_op | source)
XLA Modules:
  0.0 207.6 jit_solution(5355166850488627766)
XLA Ops:
  6.5 0.7 all-gather.3.cloned.1.call-update
  7.3 1.7 broadcast_select_fusion
  9.0 1.2 copy.18
  10.3 0.2 copy.19
  10.5 0.1 pad_maximum_fusion.3
  10.6 3.4 %collective-permute-start.4 = (bf16[2,256,1024]{1,2,0:T(8,128)(2,1)S(1)}, bf16[2,256,1024]{1,2,0:T(8,128)(2,1)}, u32[]{:S(2)}, u32[]{:S(2)}) collective-permute-start(bf16[2,256,1024]{1,2,0:T(8,128)(2,1)S(1)} %pad_maximum_fusion.3), channel_id=1, source_target_pairs={{0,2},{1,3},{2,4},{3,5},{4,6},{5,7},{6,8},{7,9},{8,10},{9,11},{10,... | collective-permute-start | bytes 3145736 | tf_op jit(solution)/shard_map/ppermute | solution.py:23
  14.0 1.9 collective-permute-start.5
  16.0 3.5 %collective-permute-start = (s32[1]{0:T(128)}, s32[1]{0:T(128)}, u32[]{:S(2)}, u32[]{:S(2)}) collective-permute-start(s32[1]{0:T(128)} %param.22), channel_id=1, source_target_pairs={{0,1},{1,2},{2,3},{3,4},{4,5},{5,6},{6,7},{7,8},{8,9},{9,10},{10,1... | collective-permute-start | bytes 20 | tf_op jit(solution)/shard_map/ppermute | solution.py:23
  20.2 0.2 fusion.17
  20.4 42.4 %collective-permute-done = s32[1]{0:T(128)} collective-permute-done((s32[1]{0:T(128)}, s32[1]{0:T(128)}, u32[]{:S(2)}, u32[]{:S(2)}) %collective-permute-start) | collective-permute-done | bytes 36 | tf_op jit(solution)/shard_map/ppermute | solution.py:23
  63.5 16.8 %collective-permute-start.1 = (s32[1]{0:T(128)}, s32[1]{0:T(128)}, u32[]{:S(2)}, u32[]{:S(2)}) collective-permute-start(s32[1]{0:T(128)} %add.53), channel_id=1, source_target_pairs={{0,2},{1,3},{2,4},{3,5},{4,6},{5,7},{6,8},{7,9},{8,10},{9,11},{10,... | collective-permute-start | bytes 20 | tf_op jit(solution)/shard_map/ppermute | solution.py:23
  81.0 4.0 %collective-permute-start.2 = (s32[1]{0:T(128)}, s32[1]{0:T(128)}, u32[]{:S(2)}, u32[]{:S(2)}) collective-permute-start(s32[1]{0:T(128)} %add.54), channel_id=1, source_target_pairs={{0,4},{1,5},{2,6},{3,7},{4,8},{5,9},{6,10},{7,11},{8,12},{9,13},{1... | collective-permute-start | bytes 20 | tf_op jit(solution)/shard_map/ppermute | solution.py:23
  85.0 1.8 collective-permute-done.2
  87.4 1.3 collective-permute-start.3
  88.7 5.0 %collective-permute-done.3 = s32[1]{0:T(128)} collective-permute-done((s32[1]{0:T(128)}, s32[1]{0:T(128)}, u32[]{:S(2)}, u32[]{:S(2)}) %collective-permute-start.3) | collective-permute-done | bytes 36 | tf_op jit(solution)/shard_map/ppermute | solution.py:23
  94.4 1.7 maximum_maximum_fusion
  96.1 0.2 fusion.24
  96.3 1.0 fusion.18
  97.3 3.1 %fusion.27 = (f32[8,256]{1,0:T(8,128)S(1)}, f32[8,256,768]{1,2,0:T(8,128)S(1)}) fusion(f32[8,768,256]{2,1,0:T(8,128)S(1)} %fusion.18, pred[256,768]{0,1:T(8,128)(4,1)S(1)} %fusion.17), kind=kOutput, calls=%fused_computation.45 | output fusion | flops 9437951 | bytes 12787712 | tf_op jit(solution)/shard_map/sub | solution.py:63
  100.4 0.6 fusion.13
  101.1 0.7 copy-done.2
  101.9 3.6 %multiply_reduce_fusion = (f32[256]{0:T(256)S(1)}, f32[256,2048]{1,0:T(8,128)S(1)}) fusion(bf16[256,1024]{0,1:T(8,128)(2,1)S(1)} %bitcast.45, bf16[1024,2048]{1,0:T(8,128)(2,1)} %all-gather.3.cloned.1.call-done, bf16[256,2048]{1,0:T(8,128)(2,1)S(1)} %copy-done.2), kind=kOutput, calls=%fused_computation.17 | convolution fusion | flops 1075838720 | bytes 7865344 | tf_op jit(solution)/shard_map/dot_general | solution.py:79
  105.5 0.2 multiply_convert_fusion
  105.7 1.6 collective-permute-start.6
  107.3 15.8 %all-gather.5.cloned.1.call-done = bf16[2048,1024]{1,0:T(8,128)(2,1)} async-done(((bf16[128,1024]{1,0:T(8,128)(2,1)}), bf16[2048,1024]{1,0:T(8,128)(2,1)}) %all-gather.5.cloned.1.call-update) | async-done | bytes 4194320 | tf_op jit(solution)/shard_map/all_gather | solution.py:170
  123.1 3.2 %collective-permute-done.6 = bf16[256,2048]{1,0:T(8,128)(2,1)S(1)} collective-permute-done((bf16[256,2048]{1,0:T(8,128)(2,1)S(1)}, bf16[256,2048]{1,0:T(8,128)(2,1)S(1)}, u32[]{:S(2)}, u32[]{:S(2)}) %collective-permute-start.6) | collective-permute-done | bytes 1048608 | tf_op jit(solution)/shard_map/ppermute | solution.py:191
  126.2 4.5 %fusion.10 = bf16[512,1024]{1,0:T(8,128)(2,1)S(1)} fusion(bf16[2048,1024]{1,0:T(8,128)(2,1)} %all-gather.5.cloned.1.call-done, bf16[256,2048]{1,0:T(8,128)(2,1)S(1)} %collective-permute-done.6, bf16[256,2048]{1,0:T(8,128)(2,1)S(1)} %multiply_convert_fusion), kind=kOutput, calls=%fused_computation.20 | convolution fusion | flops 2152202240 | bytes 7340032 | tf_op jit(solution)/shard_map/dot_general | solution.py:79
  130.8 1.9 collective-permute-start.7
  132.8 3.6 %collective-permute-start.8 = (bf16[256,512]{1,0:T(8,128)(2,1)S(1)}, bf16[256,512]{1,0:T(8,128)(2,1)S(1)}, u32[]{:S(2)}, u32[]{:S(2)}) collective-permute-start(bf16[256,512]{1,0:T(8,128)(2,1)S(1)} %get-tuple-element.13), channel_id=1, source_target_pairs={{1,0},{2,1},{3,2},{4,3},{5,4},{6,5},{7,6},{8,7},{9,8},{10,9},{11,1... | collective-permute-start | bytes 786440 | tf_op jit(solution)/shard_map/ppermute | solution.py:47
  136.4 1.6 collective-permute-start.10
  138.0 1.9 collective-permute-start.11
  139.9 3.6 %collective-permute-start.9 = (bf16[256,512]{1,0:T(8,128)(2,1)S(1)}, bf16[256,512]{1,0:T(8,128)(2,1)S(1)}, u32[]{:S(2)}, u32[]{:S(2)}) collective-permute-start(bf16[256,512]{1,0:T(8,128)(2,1)S(1)} %get-tuple-element.14), channel_id=1, source_target_pairs={{0,17},{1,18},{2,19},{3,20},{4,21},{5,22},{6,23},{7,24},{8,25},{9,... | collective-permute-start | bytes 786440 | tf_op jit(solution)/shard_map/ppermute | solution.py:47
  143.7 2.0 collective-permute-done.10
  145.7 6.3 %collective-permute-done.11 = bf16[256,512]{1,0:T(8,128)(2,1)S(1)} collective-permute-done((bf16[256,512]{1,0:T(8,128)(2,1)S(1)}, bf16[256,512]{1,0:T(8,128)(2,1)S(1)}, u32[]{:S(2)}, u32[]{:S(2)}) %collective-permute-start.11) | collective-permute-done | bytes 262176 | tf_op jit(solution)/shard_map/ppermute | solution.py:47
  152.0 3.8 %collective-permute-done.9 = bf16[256,512]{1,0:T(8,128)(2,1)S(1)} collective-permute-done((bf16[256,512]{1,0:T(8,128)(2,1)S(1)}, bf16[256,512]{1,0:T(8,128)(2,1)S(1)}, u32[]{:S(2)}, u32[]{:S(2)}) %collective-permute-start.9) | collective-permute-done | bytes 262176 | tf_op jit(solution)/shard_map/ppermute | solution.py:47
  155.8 1.3 pad_maximum_fusion.1.k_ref.v_ref
  157.1 2.0 collective-permute-start.12
  159.2 3.5 %collective-permute-start.13 = (bf16[256,512]{1,0:T(8,128)(2,1)S(1)}, bf16[256,512]{1,0:T(8,128)(2,1)S(1)}, u32[]{:S(2)}, u32[]{:S(2)}) collective-permute-start(bf16[256,512]{1,0:T(8,128)(2,1)S(1)} %get-tuple-element.15), channel_id=1, source_target_pairs={{1,0},{2,1},{3,2},{4,3},{5,4},{6,5},{7,6},{8,7},{9,8},{10,9},{11,1... | collective-permute-start | bytes 786440 | tf_op jit(solution)/shard_map/ppermute | solution.py:47
  162.7 1.9 collective-permute-start.14
  164.7 1.6 collective-permute-start.15
  166.2 4.4 %collective-permute-start.16 = (bf16[256,512]{1,0:T(8,128)(2,1)S(1)}, bf16[256,512]{1,0:T(8,128)(2,1)S(1)}, u32[]{:S(2)}, u32[]{:S(2)}) collective-permute-start(bf16[256,512]{1,0:T(8,128)(2,1)S(1)} %get-tuple-element.16), channel_id=1, source_target_pairs={{1,16},{2,17},{3,18},{4,19},{5,20},{6,21},{7,22},{8,23},{9,24},{10... | collective-permute-start | bytes 786440 | tf_op jit(solution)/shard_map/ppermute | solution.py:47
  170.7 0.1 copy.17
  170.8 0.1 reshape.67
  170.8 0.6 concatenate.25.prm
  171.5 12.4 %shard_map.118 = bf16[1024,512]{1,0:T(8,128)(2,1)} custom-call(s32[12]{0:T(128)} %concatenate.25.prm, f32[8]{0:T(128)} %slopes_ref.3, bf16[1024,1024]{1,0:T(8,128)(2,1)} %q_ref.3, bf16[2,768,512]{2,1,0:T(8,128)(2,1)} %pad_maximum_fusion.1.k_ref.v_ref, bf16[2,768,512]{2,1,0:T(8,128)(2,1)} %pad_maximum_fusion.1.k_ref.v_ref), custom_call_target="tpu_custom_call" | custom-call | tf_op jit(solution)/shard_map/pallas_call | solution.py:133
  184.1 1.3 pad_maximum_fusion.2.k_ref.v_ref
  185.4 12.6 %shard_map.119 = bf16[1024,512]{1,0:T(8,128)(2,1)} custom-call(s32[12]{0:T(128)} %concatenate.25.prm, f32[8]{0:T(128)} %slopes_ref.3, bf16[1024,1024]{1,0:T(8,128)(2,1)} %q_ref.3, bf16[2,768,512]{2,1,0:T(8,128)(2,1)} %pad_maximum_fusion.2.k_ref.v_ref, bf16[2,768,512]{2,1,0:T(8,128)(2,1)} %pad_maximum_fusion.2.k_ref.v_ref), custom_call_target="tpu_custom_call" | custom-call | tf_op jit(solution)/shard_map/pallas_call | solution.py:133
  198.0 2.8 %pad_maximum_fusion = bf16[1024,1024]{1,0:T(8,128)(2,1)} fusion(bf16[1024,512]{1,0:T(8,128)(2,1)} %shard_map.119, bf16[1024,512]{1,0:T(8,128)(2,1)S(1)} %copy-done.1), kind=kLoop, calls=%fused_computation.15 | loop fusion | flops 4194304 | bytes 4194304 | tf_op jit(solution)/shard_map/concatenate | solution.py:224
  (35 shorter events, 0.5 us)
Async XLA Ops:
  6.5 89.8 %copy-start = (bf16[256,1024]{1,0:T(8,128)(2,1)S(1)}, bf16[256,1024]{1,0:T(8,128)(2,1)}, u32[]{:S(2)}) copy-start(bf16[256,1024]{1,0:T(8,128)(2,1)} %param.12) | copy-start | bytes 1572868
  6.5 3.7 %copy-start.3 = (bf16[256,1024]{1,0:T(8,128)(2,1)S(1)}, bf16[256,1024]{1,0:T(8,128)(2,1)}, u32[]{:S(2)}) copy-start(bf16[256,1024]{1,0:T(8,128)(2,1)} %param.14) | copy-start | bytes 1572868
  6.5 94.6 %all-gather.3.cloned.1.call-start = ((), (), s32[]{:S(2)}) async-start(), calls=%async_computation | async-start | bytes 4456448 | tf_op jit(solution)/shard_map/all_gather | solution.py:158
  7.3 115.8 %all-gather.5.cloned.1.call-start = ((), (), s32[]{:S(2)}) async-start(), calls=%async_computation.1 | async-start | bytes 4456448 | tf_op jit(solution)/shard_map/all_gather | solution.py:170
  10.6 83.8 %collective-permute-start.4 = (bf16[2,256,1024]{1,2,0:T(8,128)(2,1)S(1)}, bf16[2,256,1024]{1,2,0:T(8,128)(2,1)}, u32[]{:S(2)}, u32[]{:S(2)}) collective-permute-start(bf16[2,256,1024]{1,2,0:T(8,128)(2,1)S(1)} %pad_maximum_fusion.3), channel_id=1, source_target_pairs={{0,2},{1,3},{2,4},{3,5},{4,6},{5,7},{6,8},{7,9},{8,10},{9,11},{10,... | collective-permute-start | bytes 3145736 | tf_op jit(solution)/shard_map/ppermute | solution.py:23
  14.0 80.4 %collective-permute-start.5 = (bf16[2,256,1024]{1,2,0:T(8,128)(2,1)S(1)}, bf16[2,256,1024]{1,2,0:T(8,128)(2,1)}, u32[]{:S(2)}, u32[]{:S(2)}) collective-permute-start(bf16[2,256,1024]{1,2,0:T(8,128)(2,1)S(1)} %pad_maximum_fusion.3), channel_id=1, source_target_pairs={{0,1},{1,2},{2,3},{3,4},{4,5},{5,6},{6,7},{7,8},{8,9},{9,10},{10,1... | collective-permute-start | bytes 3145736 | tf_op jit(solution)/shard_map/ppermute | solution.py:23
  16.0 46.8 %collective-permute-start = (s32[1]{0:T(128)}, s32[1]{0:T(128)}, u32[]{:S(2)}, u32[]{:S(2)}) collective-permute-start(s32[1]{0:T(128)} %param.22), channel_id=1, source_target_pairs={{0,1},{1,2},{2,3},{3,4},{4,5},{5,6},{6,7},{7,8},{8,9},{9,10},{10,1... | collective-permute-start | bytes 20 | tf_op jit(solution)/shard_map/ppermute | solution.py:23
  63.5 16.8 %collective-permute-start.1 = (s32[1]{0:T(128)}, s32[1]{0:T(128)}, u32[]{:S(2)}, u32[]{:S(2)}) collective-permute-start(s32[1]{0:T(128)} %add.53), channel_id=1, source_target_pairs={{0,2},{1,3},{2,4},{3,5},{4,6},{5,7},{6,8},{7,9},{8,10},{9,11},{10,... | collective-permute-start | bytes 20 | tf_op jit(solution)/shard_map/ppermute | solution.py:23
  81.0 5.7 %collective-permute-start.2 = (s32[1]{0:T(128)}, s32[1]{0:T(128)}, u32[]{:S(2)}, u32[]{:S(2)}) collective-permute-start(s32[1]{0:T(128)} %add.54), channel_id=1, source_target_pairs={{0,4},{1,5},{2,6},{3,7},{4,8},{5,9},{6,10},{7,11},{8,12},{9,13},{1... | collective-permute-start | bytes 20 | tf_op jit(solution)/shard_map/ppermute | solution.py:23
  87.4 6.3 %collective-permute-start.3 = (s32[1]{0:T(128)}, s32[1]{0:T(128)}, u32[]{:S(2)}, u32[]{:S(2)}) collective-permute-start(s32[1]{0:T(128)} %add.55), channel_id=1, source_target_pairs={{0,8},{1,9},{2,10},{3,11},{4,12},{5,13},{6,14},{7,15},{16,24},{17,... | collective-permute-start | bytes 20 | tf_op jit(solution)/shard_map/ppermute | solution.py:23
  100.4 1.4 copy-start.2
  101.1 4.4 %copy-start.4 = (f32[2048]{0:T(1024)S(1)}, f32[2048]{0:T(1024)}, u32[]{:S(2)}) copy-start(f32[2048]{0:T(1024)} %param.17) | copy-start | bytes 24580
  105.7 20.5 %collective-permute-start.6 = (bf16[256,2048]{1,0:T(8,128)(2,1)S(1)}, bf16[256,2048]{1,0:T(8,128)(2,1)S(1)}, u32[]{:S(2)}, u32[]{:S(2)}) collective-permute-start(bf16[256,2048]{1,0:T(8,128)(2,1)S(1)} %multiply_convert_fusion), channel_id=1, source_target_pairs={{0,16},{16,0},{1,17},{17,1},{2,18},{18,2},{3,19},{19,3},{4,20},{20... | collective-permute-start | bytes 3145736 | tf_op jit(solution)/shard_map/ppermute | solution.py:191
  130.8 12.7 %collective-permute-start.7 = (bf16[256,512]{1,0:T(8,128)(2,1)S(1)}, bf16[256,512]{1,0:T(8,128)(2,1)S(1)}, u32[]{:S(2)}, u32[]{:S(2)}) collective-permute-start(bf16[256,512]{1,0:T(8,128)(2,1)S(1)} %get-tuple-element.13), channel_id=1, source_target_pairs={{0,1},{1,2},{2,3},{3,4},{4,5},{5,6},{6,7},{7,8},{8,9},{9,10},{10,1... | collective-permute-start | bytes 786440 | tf_op jit(solution)/shard_map/ppermute | solution.py:47
  132.8 10.8 %collective-permute-start.8 = (bf16[256,512]{1,0:T(8,128)(2,1)S(1)}, bf16[256,512]{1,0:T(8,128)(2,1)S(1)}, u32[]{:S(2)}, u32[]{:S(2)}) collective-permute-start(bf16[256,512]{1,0:T(8,128)(2,1)S(1)} %get-tuple-element.13), channel_id=1, source_target_pairs={{1,0},{2,1},{3,2},{4,3},{5,4},{6,5},{7,6},{8,7},{9,8},{10,9},{11,1... | collective-permute-start | bytes 786440 | tf_op jit(solution)/shard_map/ppermute | solution.py:47
  136.4 9.2 %collective-permute-start.10 = (bf16[256,512]{1,0:T(8,128)(2,1)S(1)}, bf16[256,512]{1,0:T(8,128)(2,1)S(1)}, u32[]{:S(2)}, u32[]{:S(2)}) collective-permute-start(bf16[256,512]{1,0:T(8,128)(2,1)S(1)} %get-tuple-element.14), channel_id=1, source_target_pairs={{0,16},{1,17},{2,18},{3,19},{4,20},{5,21},{6,22},{7,23},{8,24},{9,... | collective-permute-start | bytes 786440 | tf_op jit(solution)/shard_map/ppermute | solution.py:47
  138.0 14.0 %collective-permute-start.11 = (bf16[256,512]{1,0:T(8,128)(2,1)S(1)}, bf16[256,512]{1,0:T(8,128)(2,1)S(1)}, u32[]{:S(2)}, u32[]{:S(2)}) collective-permute-start(bf16[256,512]{1,0:T(8,128)(2,1)S(1)} %get-tuple-element.14), channel_id=1, source_target_pairs={{1,16},{2,17},{3,18},{4,19},{5,20},{6,21},{7,22},{8,23},{9,24},{10... | collective-permute-start | bytes 786440 | tf_op jit(solution)/shard_map/ppermute | solution.py:47
  139.9 15.9 %collective-permute-start.9 = (bf16[256,512]{1,0:T(8,128)(2,1)S(1)}, bf16[256,512]{1,0:T(8,128)(2,1)S(1)}, u32[]{:S(2)}, u32[]{:S(2)}) collective-permute-start(bf16[256,512]{1,0:T(8,128)(2,1)S(1)} %get-tuple-element.14), channel_id=1, source_target_pairs={{0,17},{1,18},{2,19},{3,20},{4,21},{5,22},{6,23},{7,24},{8,25},{9,... | collective-permute-start | bytes 786440 | tf_op jit(solution)/shard_map/ppermute | solution.py:47
  155.8 14.8 %copy-start.5 = (s32[4,2]{0,1:T(2,128)S(1)}, s32[4,2]{0,1:T(2,128)}, u32[]{:S(2)}) copy-start(s32[4,2]{0,1:T(2,128)} %param.23) | copy-start | bytes 100
  157.1 26.8 %collective-permute-start.12 = (bf16[256,512]{1,0:T(8,128)(2,1)S(1)}, bf16[256,512]{1,0:T(8,128)(2,1)S(1)}, u32[]{:S(2)}, u32[]{:S(2)}) collective-permute-start(bf16[256,512]{1,0:T(8,128)(2,1)S(1)} %get-tuple-element.15), channel_id=1, source_target_pairs={{0,1},{1,2},{2,3},{3,4},{4,5},{5,6},{6,7},{7,8},{8,9},{9,10},{10,1... | collective-permute-start | bytes 786440 | tf_op jit(solution)/shard_map/ppermute | solution.py:47
  159.2 24.7 %collective-permute-start.13 = (bf16[256,512]{1,0:T(8,128)(2,1)S(1)}, bf16[256,512]{1,0:T(8,128)(2,1)S(1)}, u32[]{:S(2)}, u32[]{:S(2)}) collective-permute-start(bf16[256,512]{1,0:T(8,128)(2,1)S(1)} %get-tuple-element.15), channel_id=1, source_target_pairs={{1,0},{2,1},{3,2},{4,3},{5,4},{6,5},{7,6},{8,7},{9,8},{10,9},{11,1... | collective-permute-start | bytes 786440 | tf_op jit(solution)/shard_map/ppermute | solution.py:47
  162.7 21.3 %collective-permute-start.14 = (bf16[256,512]{1,0:T(8,128)(2,1)S(1)}, bf16[256,512]{1,0:T(8,128)(2,1)S(1)}, u32[]{:S(2)}, u32[]{:S(2)}) collective-permute-start(bf16[256,512]{1,0:T(8,128)(2,1)S(1)} %get-tuple-element.16), channel_id=1, source_target_pairs={{0,17},{1,18},{2,19},{3,20},{4,21},{5,22},{6,23},{7,24},{8,25},{9,... | collective-permute-start | bytes 786440 | tf_op jit(solution)/shard_map/ppermute | solution.py:47
  164.7 19.4 %collective-permute-start.15 = (bf16[256,512]{1,0:T(8,128)(2,1)S(1)}, bf16[256,512]{1,0:T(8,128)(2,1)S(1)}, u32[]{:S(2)}, u32[]{:S(2)}) collective-permute-start(bf16[256,512]{1,0:T(8,128)(2,1)S(1)} %get-tuple-element.16), channel_id=1, source_target_pairs={{0,16},{1,17},{2,18},{3,19},{4,20},{5,21},{6,22},{7,23},{8,24},{9,... | collective-permute-start | bytes 786440 | tf_op jit(solution)/shard_map/ppermute | solution.py:47
  166.2 17.8 %collective-permute-start.16 = (bf16[256,512]{1,0:T(8,128)(2,1)S(1)}, bf16[256,512]{1,0:T(8,128)(2,1)S(1)}, u32[]{:S(2)}, u32[]{:S(2)}) collective-permute-start(bf16[256,512]{1,0:T(8,128)(2,1)S(1)} %get-tuple-element.16), channel_id=1, source_target_pairs={{1,16},{2,17},{3,18},{4,19},{5,20},{6,21},{7,22},{8,23},{9,24},{10... | collective-permute-start | bytes 786440 | tf_op jit(solution)/shard_map/ppermute | solution.py:47
  185.4 12.6 %copy-start.1 = (bf16[1024,512]{1,0:T(8,128)(2,1)S(1)}, bf16[1024,512]{1,0:T(8,128)(2,1)}, u32[]{:S(2)}) copy-start(bf16[1024,512]{1,0:T(8,128)(2,1)} %shard_map.118) | copy-start | bytes 3145732
Sparse Core Ops, SparseCore 0:
  9.5 62.0 all-gather.2
  73.7 49.2 all-gather.4

commit v9 on v7

--- a/solution.py
+++ b/solution.py
@@ -89,24 +89,27 @@
     first_key = jnp.minimum(band_low - base_row, near_rows - BAND)
     step = span - BAND
     window = pl.multiple_of(jnp.clip(first_key // step * step, 0, near_rows - span), step)
-    rows = n * CB + lax.broadcasted_iota(jnp.int32, (CB, 1), 0)
+    rows = n * CB + lax.broadcasted_iota(jnp.int32, (1, CB), 1)
     timing = ((stream_start + rows) // 2).astype(jnp.float32) * (2.0 / 3.0)
-    key_global = base_row + window + lax.broadcasted_iota(jnp.int32, (1, span), 1)
+    key_global = base_row + window + lax.broadcasted_iota(jnp.int32, (span, 1), 0)
     inside = (key_global >= band_low) & (key_global < band_high)
     distance = jnp.where(inside, jnp.abs(timing - key_global.astype(jnp.float32)), -NEG_FILL)
-    live_rows = rows < live_count
+    live_rows = n * CB + lax.broadcasted_iota(jnp.int32, (CB, 1), 0) < live_count
     for h in range(HEADS):
         cols = slice(h * HEAD_DIM, (h + 1) * HEAD_DIM)
         scores = lax.dot_general(
-            q_ref[:, cols], k_ref[pl.ds(window, span), cols], (((1,), (1,)), ((), ())),
+            k_ref[pl.ds(window, span), cols], q_ref[:, cols], (((1,), (1,)), ((), ())),
             preferred_element_type=jnp.float32,
         ) * HEAD_DIM ** (-0.5)
         scores = scores + distance * (-slopes_ref[h] / BAND)
-        largest = jnp.max(scores, axis=1, keepdims=True)
+        largest = jnp.max(scores, axis=0, keepdims=True)
         exponent = jnp.exp(scores - largest)
-        total = jnp.sum(exponent, axis=1, keepdims=True)
+        total = jnp.sum(exponent, axis=0, keepdims=True)
         weights = (exponent * (1.0 / total)).astype(jnp.bfloat16)
-        blended = jnp.dot(weights, v_ref[pl.ds(window, span), cols], preferred_element_type=jnp.float32)
+        blended = lax.dot_general(
+            weights, v_ref[pl.ds(window, span), cols], (((0,), (0,)), ((), ())),
+            preferred_element_type=jnp.float32,
+        )
         o_ref[:, cols] = jnp.where(live_rows, blended, 0.0).astype(jnp.bfloat16)
 
 

time: 207 us -> 202 us (0.976)
  Pallas kernels: 21.8 us -> 16.6 us
    pallas_call x1, Pallas kernels: 21.8 us -> 16.6 us  [coarse_attention(): pl.pallas_call(kernel, grid_spec=grid_spec, out_shape=jax.ShapeDtypeStruc...]
where the time goes in v9:
time: 202 us; the launch traced here: 201 us
  waiting for transfers between devices  96.2 us (48%)
  starting transfers between devices  45.6 us (23%)
  between operations  16.8 us (8%)
  Pallas kernels  16.6 us (8%)
  other arithmetic  11.3 us (6%)
  matrix products  10.1 us (5%)
  local copies, waits for them, and re-layouts  4.31 us (2%)
    ppermute x6, waiting for transfers between devices, passed_along(): return lax.ppermute(array, axis, pairs)  48.6 us
    ppermute x6, starting transfers between devices, passed_along(): return lax.ppermute(array, axis, pairs)  31.2 us
    ppermute x5, waiting for transfers between devices, sent_to(): return lax.ppermute(array, ('groups', 'ctx'), pairs)  27 us
    pallas_call x1, Pallas kernels, coarse_attention(): pl.pallas_call(kernel, grid_spec=grid_spec, out_shape=jax.ShapeDtypeStruc...  16.6 us
    all_gather x1, waiting for transfers between devices, on_device(): gathered_proj = lax.all_gather(own_proj, 'ctx', axis=0, tiled=True)  15.4 us
    ppermute x5, starting transfers between devices, sent_to(): return lax.ppermute(array, ('groups', 'ctx'), pairs)  12.8 us
    dot_general x2, matrix products, contract_rows(): return jnp.dot(left_side, weight_piece, preferred_element_type=jnp.float32)  8.45 us
    ppermute x1, waiting for transfers between devices, on_device(): partner_normed = lax.ppermute(normed, 'groups', partners)  4.43 us
  transfers between devices with their start and end apart: 14, of which 9 were waited for; matrix products, arithmetic and copies ran while one was open for 8% of the time, Pallas kernels for 0%

profile of v9, /device:TPU:20, one launch (start us, length us, event | category | flops | bytes accessed | tf_op | source)
XLA Modules:
  0.0 200.9 jit_solution(11475313720977054730)
XLA Ops:
  6.5 0.7 all-gather.3.cloned.1.call-update
  7.3 0.0 all-gather.5.cloned.1.call-start
  7.3 1.7 broadcast_select_fusion
  9.0 0.0 all-gather.5.cloned.1.call-update
  9.0 1.2 copy.18
  10.3 1.2 copy.19
  11.5 0.1 pad_maximum_fusion.1
  11.6 3.4 %collective-permute-start.4 = (bf16[2,256,1024]{1,2,0:T(8,128)(2,1)S(1)}, bf16[2,256,1024]{1,2,0:T(8,128)(2,1)}, u32[]{:S(2)}, u32[]{:S(2)}) collective-permute-start(bf16[2,256,1024]{1,2,0:T(8,128)(2,1)S(1)} %pad_maximum_fusion.1), channel_id=1, source_target_pairs={{0,2},{1,3},{2,4},{3,5},{4,6},{5,7},{6,8},{7,9},{8,10},{9,11},{10,... | collective-permute-start | bytes 3145736 | tf_op jit(solution)/shard_map/ppermute | solution.py:23
  15.1 1.9 collective-permute-start.5
  17.0 3.5 %collective-permute-start = (s32[1]{0:T(128)}, s32[1]{0:T(128)}, u32[]{:S(2)}, u32[]{:S(2)}) collective-permute-start(s32[1]{0:T(128)} %param.22), channel_id=1, source_target_pairs={{0,1},{1,2},{2,3},{3,4},{4,5},{5,6},{6,7},{7,8},{8,9},{9,10},{10,1... | collective-permute-start | bytes 20 | tf_op jit(solution)/shard_map/ppermute | solution.py:23
  21.2 0.2 fusion.17
  21.5 42.4 %collective-permute-done = s32[1]{0:T(128)} collective-permute-done((s32[1]{0:T(128)}, s32[1]{0:T(128)}, u32[]{:S(2)}, u32[]{:S(2)}) %collective-permute-start) | collective-permute-done | bytes 36 | tf_op jit(solution)/shard_map/ppermute | solution.py:23
  64.4 16.8 %collective-permute-start.1 = (s32[1]{0:T(128)}, s32[1]{0:T(128)}, u32[]{:S(2)}, u32[]{:S(2)}) collective-permute-start(s32[1]{0:T(128)} %add.53), channel_id=1, source_target_pairs={{0,2},{1,3},{2,4},{3,5},{4,6},{5,7},{6,8},{7,9},{8,10},{9,11},{10,... | collective-permute-start | bytes 20 | tf_op jit(solution)/shard_map/ppermute | solution.py:23
  81.9 4.1 %collective-permute-start.2 = (s32[1]{0:T(128)}, s32[1]{0:T(128)}, u32[]{:S(2)}, u32[]{:S(2)}) collective-permute-start(s32[1]{0:T(128)} %add.54), channel_id=1, source_target_pairs={{0,4},{1,5},{2,6},{3,7},{4,8},{5,9},{6,10},{7,11},{8,12},{9,13},{1... | collective-permute-start | bytes 20 | tf_op jit(solution)/shard_map/ppermute | solution.py:23
  86.1 1.3 collective-permute-done.2
  88.0 1.3 collective-permute-start.3
  89.3 5.0 %collective-permute-done.3 = s32[1]{0:T(128)} collective-permute-done((s32[1]{0:T(128)}, s32[1]{0:T(128)}, u32[]{:S(2)}, u32[]{:S(2)}) %collective-permute-start.3) | collective-permute-done | bytes 36 | tf_op jit(solution)/shard_map/ppermute | solution.py:23
  94.9 1.7 maximum_maximum_fusion
  96.6 0.2 fusion.24
  96.8 1.0 fusion.18
  97.8 3.1 %fusion.26 = (f32[8,256]{1,0:T(8,128)S(1)}, f32[8,256,768]{1,2,0:T(8,128)S(1)}) fusion(f32[8,768,256]{2,1,0:T(8,128)S(1)} %fusion.18, pred[256,768]{0,1:T(8,128)(4,1)S(1)} %fusion.17), kind=kOutput, calls=%fused_computation.40 | output fusion | flops 9437951 | bytes 12787712 | tf_op jit(solution)/shard_map/sub | solution.py:63
  100.9 0.0 copy-start.1
  100.9 0.6 fusion.13
  101.6 0.0 all-gather.3.cloned.1.call-done
  101.6 0.7 copy-done.1
  102.3 3.6 %multiply_reduce_fusion = (f32[256]{0:T(256)S(1)}, f32[256,2048]{1,0:T(8,128)S(1)}) fusion(bf16[256,1024]{0,1:T(8,128)(2,1)S(1)} %bitcast.41, bf16[1024,2048]{1,0:T(8,128)(2,1)} %all-gather.3.cloned.1.call-done, bf16[256,2048]{1,0:T(8,128)(2,1)S(1)} %copy-done.1), kind=kOutput, calls=%fused_computation.17 | convolution fusion | flops 1075838720 | bytes 7865344 | tf_op jit(solution)/shard_map/dot_general | solution.py:79
  105.9 0.2 multiply_convert_fusion
  106.2 1.5 collective-permute-start.6
  107.7 15.4 %all-gather.5.cloned.1.call-done = bf16[2048,1024]{1,0:T(8,128)(2,1)} async-done(((bf16[128,1024]{1,0:T(8,128)(2,1)}), bf16[2048,1024]{1,0:T(8,128)(2,1)}) %all-gather.5.cloned.1.call-update) | async-done | bytes 4194320 | tf_op jit(solution)/shard_map/all_gather | solution.py:169
  123.1 4.4 %collective-permute-done.6 = bf16[256,2048]{1,0:T(8,128)(2,1)} collective-permute-done((bf16[256,2048]{1,0:T(8,128)(2,1)S(1)}, bf16[256,2048]{1,0:T(8,128)(2,1)}, u32[]{:S(2)}, u32[]{:S(2)}) %collective-permute-start.6) | collective-permute-done | bytes 1048608 | tf_op jit(solution)/shard_map/ppermute | solution.py:190
  127.5 4.9 %fusion.10 = bf16[512,1024]{1,0:T(8,128)(2,1)S(1)} fusion(bf16[2048,1024]{1,0:T(8,128)(2,1)} %all-gather.5.cloned.1.call-done, bf16[256,2048]{1,0:T(8,128)(2,1)} %collective-permute-done.6, bf16[256,2048]{1,0:T(8,128)(2,1)S(1)} %multiply_convert_fusion), kind=kOutput, calls=%fused_computation.20 | convolution fusion | flops 2152202240 | bytes 7340032 | tf_op jit(solution)/shard_map/dot_general | solution.py:79
  132.4 0.1 fusion.25
  132.5 1.9 collective-permute-start.7
  134.4 3.6 %collective-permute-start.8 = (bf16[256,1024]{1,0:T(8,128)(2,1)S(1)}, bf16[256,1024]{1,0:T(8,128)(2,1)}, u32[]{:S(2)}, u32[]{:S(2)}) collective-permute-start(bf16[256,1024]{1,0:T(8,128)(2,1)S(1)} %get-tuple-element.11), channel_id=1, source_target_pairs={{1,0},{2,1},{3,2},{4,3},{5,4},{6,5},{7,6},{8,7},{9,8},{10,9},{11,1... | collective-permute-start | bytes 1572872 | tf_op jit(solution)/shard_map/ppermute | solution.py:47
  138.1 1.5 collective-permute-start.10
  139.6 1.9 collective-permute-start.11
  141.5 3.8 %collective-permute-start.9 = (bf16[256,1024]{1,0:T(8,128)(2,1)S(1)}, bf16[256,1024]{1,0:T(8,128)(2,1)}, u32[]{:S(2)}, u32[]{:S(2)}) collective-permute-start(bf16[256,1024]{1,0:T(8,128)(2,1)S(1)} %get-tuple-element.12), channel_id=1, source_target_pairs={{0,17},{1,18},{2,19},{3,20},{4,21},{5,22},{6,23},{7,24},{8,25},{9,... | collective-permute-start | bytes 1572872 | tf_op jit(solution)/shard_map/ppermute | solution.py:47
  145.4 0.1 copy.17
  145.5 0.1 reshape.67
  145.5 0.7 concatenate.16.prm
  146.2 8.0 %collective-permute-done.7 = bf16[256,1024]{1,0:T(8,128)(2,1)S(1)} collective-permute-done((bf16[256,1024]{1,0:T(8,128)(2,1)S(1)}, bf16[256,1024]{1,0:T(8,128)(2,1)S(1)}, u32[]{:S(2)}, u32[]{:S(2)}) %collective-permute-start.7) | collective-permute-done | bytes 524320 | tf_op jit(solution)/shard_map/ppermute | solution.py:47
  154.2 1.2 maximum_bitcast_fusion
  155.4 3.2 %collective-permute-done.10 = bf16[256,1024]{1,0:T(8,128)(2,1)S(1)} collective-permute-done((bf16[256,1024]{1,0:T(8,128)(2,1)S(1)}, bf16[256,1024]{1,0:T(8,128)(2,1)S(1)}, u32[]{:S(2)}, u32[]{:S(2)}) %collective-permute-start.10) | collective-permute-done | bytes 524320 | tf_op jit(solution)/shard_map/ppermute | solution.py:47
  158.5 8.8 %collective-permute-done.11 = bf16[256,1024]{1,0:T(8,128)(2,1)S(1)} collective-permute-done((bf16[256,1024]{1,0:T(8,128)(2,1)S(1)}, bf16[256,1024]{1,0:T(8,128)(2,1)S(1)}, u32[]{:S(2)}, u32[]{:S(2)}) %collective-permute-start.11) | collective-permute-done | bytes 524320 | tf_op jit(solution)/shard_map/ppermute | solution.py:47
  167.3 7.1 %collective-permute-done.9 = bf16[256,1024]{1,0:T(8,128)(2,1)} collective-permute-done((bf16[256,1024]{1,0:T(8,128)(2,1)S(1)}, bf16[256,1024]{1,0:T(8,128)(2,1)}, u32[]{:S(2)}, u32[]{:S(2)}) %collective-permute-start.9) | collective-permute-done | bytes 524320 | tf_op jit(solution)/shard_map/ppermute | solution.py:47
  174.4 1.2 maximum_bitcast_fusion.1
  175.5 1.9 pad_maximum_fusion.k_ref.v_ref
  177.5 16.6 %shard_map.118 = bf16[1024,1024]{1,0:T(8,128)(2,1)} custom-call(s32[12]{0:T(128)} %concatenate.16.prm, f32[8]{0:T(128)} %slopes_ref.1, bf16[1024,1024]{1,0:T(8,128)(2,1)} %q_ref.1, bf16[2,768,1024]{2,1,0:T(8,128)(2,1)} %pad_maximum_fusion.k_ref.v_ref, bf16[2,768,1024]{2,1,0:T(8,128)(2,1)} %pad_maximum_fusion.k_ref.v_ref), custom_call_target="tpu_custom_call" | custom-call | tf_op jit(solution)/shard_map/pallas_call | solution.py:132
  (14 shorter events, 0.1 us)
Async XLA Ops:
  6.5 90.3 %copy-start = (bf16[256,1024]{1,0:T(8,128)(2,1)S(1)}, bf16[256,1024]{1,0:T(8,128)(2,1)}, u32[]{:S(2)}) copy-start(bf16[256,1024]{1,0:T(8,128)(2,1)} %param.12) | copy-start | bytes 1572868
  6.5 95.1 %all-gather.3.cloned.1.call-start = ((), (), s32[]{:S(2)}) async-start(), calls=%async_computation | async-start | bytes 4456448 | tf_op jit(solution)/shard_map/all_gather | solution.py:157
  7.3 115.8 %all-gather.5.cloned.1.call-start = ((), (), s32[]{:S(2)}) async-start(), calls=%async_computation.1 | async-start | bytes 4456448 | tf_op jit(solution)/shard_map/all_gather | solution.py:169
  11.6 83.3 %collective-permute-start.4 = (bf16[2,256,1024]{1,2,0:T(8,128)(2,1)S(1)}, bf16[2,256,1024]{1,2,0:T(8,128)(2,1)}, u32[]{:S(2)}, u32[]{:S(2)}) collective-permute-start(bf16[2,256,1024]{1,2,0:T(8,128)(2,1)S(1)} %pad_maximum_fusion.1), channel_id=1, source_target_pairs={{0,2},{1,3},{2,4},{3,5},{4,6},{5,7},{6,8},{7,9},{8,10},{9,11},{10,... | collective-permute-start | bytes 3145736 | tf_op jit(solution)/shard_map/ppermute | solution.py:23
  15.1 79.8 %collective-permute-start.5 = (bf16[2,256,1024]{1,2,0:T(8,128)(2,1)S(1)}, bf16[2,256,1024]{1,2,0:T(8,128)(2,1)}, u32[]{:S(2)}, u32[]{:S(2)}) collective-permute-start(bf16[2,256,1024]{1,2,0:T(8,128)(2,1)S(1)} %pad_maximum_fusion.1), channel_id=1, source_target_pairs={{0,1},{1,2},{2,3},{3,4},{4,5},{5,6},{6,7},{7,8},{8,9},{9,10},{10,1... | collective-permute-start | bytes 3145736 | tf_op jit(solution)/shard_map/ppermute | solution.py:23
  17.0 46.8 %collective-permute-start = (s32[1]{0:T(128)}, s32[1]{0:T(128)}, u32[]{:S(2)}, u32[]{:S(2)}) collective-permute-start(s32[1]{0:T(128)} %param.22), channel_id=1, source_target_pairs={{0,1},{1,2},{2,3},{3,4},{4,5},{5,6},{6,7},{7,8},{8,9},{9,10},{10,1... | collective-permute-start | bytes 20 | tf_op jit(solution)/shard_map/ppermute | solution.py:23
  64.4 16.8 %collective-permute-start.1 = (s32[1]{0:T(128)}, s32[1]{0:T(128)}, u32[]{:S(2)}, u32[]{:S(2)}) collective-permute-start(s32[1]{0:T(128)} %add.53), channel_id=1, source_target_pairs={{0,2},{1,3},{2,4},{3,5},{4,6},{5,7},{6,8},{7,9},{8,10},{9,11},{10,... | collective-permute-start | bytes 20 | tf_op jit(solution)/shard_map/ppermute | solution.py:23
  81.9 5.4 %collective-permute-start.2 = (s32[1]{0:T(128)}, s32[1]{0:T(128)}, u32[]{:S(2)}, u32[]{:S(2)}) collective-permute-start(s32[1]{0:T(128)} %add.54), channel_id=1, source_target_pairs={{0,4},{1,5},{2,6},{3,7},{4,8},{5,9},{6,10},{7,11},{8,12},{9,13},{1... | collective-permute-start | bytes 20 | tf_op jit(solution)/shard_map/ppermute | solution.py:23
  88.0 6.3 %collective-permute-start.3 = (s32[1]{0:T(128)}, s32[1]{0:T(128)}, u32[]{:S(2)}, u32[]{:S(2)}) collective-permute-start(s32[1]{0:T(128)} %add.55), channel_id=1, source_target_pairs={{0,8},{1,9},{2,10},{3,11},{4,12},{5,13},{6,14},{7,15},{16,24},{17,... | collective-permute-start | bytes 20 | tf_op jit(solution)/shard_map/ppermute | solution.py:23
  100.9 1.4 copy-start.1
  101.6 4.3 %copy-start.2 = (f32[2048]{0:T(1024)S(1)}, f32[2048]{0:T(1024)}, u32[]{:S(2)}) copy-start(f32[2048]{0:T(1024)} %param.17) | copy-start | bytes 24580
  106.1 39.2 %copy-start.3 = (s32[4,2]{0,1:T(2,128)S(1)}, s32[4,2]{0,1:T(2,128)}, u32[]{:S(2)}) copy-start(s32[4,2]{0,1:T(2,128)} %param.23) | copy-start | bytes 100
  106.2 21.4 %collective-permute-start.6 = (bf16[256,2048]{1,0:T(8,128)(2,1)S(1)}, bf16[256,2048]{1,0:T(8,128)(2,1)}, u32[]{:S(2)}, u32[]{:S(2)}) collective-permute-start(bf16[256,2048]{1,0:T(8,128)(2,1)S(1)} %multiply_convert_fusion), channel_id=1, source_target_pairs={{0,16},{16,0},{1,17},{17,1},{2,18},{18,2},{3,19},{19,3},{4,20},{20... | collective-permute-start | bytes 3145736 | tf_op jit(solution)/shard_map/ppermute | solution.py:190
  132.5 21.7 %collective-permute-start.7 = (bf16[256,1024]{1,0:T(8,128)(2,1)S(1)}, bf16[256,1024]{1,0:T(8,128)(2,1)S(1)}, u32[]{:S(2)}, u32[]{:S(2)}) collective-permute-start(bf16[256,1024]{1,0:T(8,128)(2,1)S(1)} %get-tuple-element.11), channel_id=1, source_target_pairs={{0,1},{1,2},{2,3},{3,4},{4,5},{5,6},{6,7},{7,8},{8,9},{9,10},{10,1... | collective-permute-start | bytes 1572872 | tf_op jit(solution)/shard_map/ppermute | solution.py:47
  134.4 19.8 %collective-permute-start.8 = (bf16[256,1024]{1,0:T(8,128)(2,1)S(1)}, bf16[256,1024]{1,0:T(8,128)(2,1)}, u32[]{:S(2)}, u32[]{:S(2)}) collective-permute-start(bf16[256,1024]{1,0:T(8,128)(2,1)S(1)} %get-tuple-element.11), channel_id=1, source_target_pairs={{1,0},{2,1},{3,2},{4,3},{5,4},{6,5},{7,6},{8,7},{9,8},{10,9},{11,1... | collective-permute-start | bytes 1572872 | tf_op jit(solution)/shard_map/ppermute | solution.py:47
  138.1 20.5 %collective-permute-start.10 = (bf16[256,1024]{1,0:T(8,128)(2,1)S(1)}, bf16[256,1024]{1,0:T(8,128)(2,1)S(1)}, u32[]{:S(2)}, u32[]{:S(2)}) collective-permute-start(bf16[256,1024]{1,0:T(8,128)(2,1)S(1)} %get-tuple-element.12), channel_id=1, source_target_pairs={{0,16},{1,17},{2,18},{3,19},{4,20},{5,21},{6,22},{7,23},{8,24},{9,... | collective-permute-start | bytes 1572872 | tf_op jit(solution)/shard_map/ppermute | solution.py:47
  139.6 27.7 %collective-permute-start.11 = (bf16[256,1024]{1,0:T(8,128)(2,1)S(1)}, bf16[256,1024]{1,0:T(8,128)(2,1)S(1)}, u32[]{:S(2)}, u32[]{:S(2)}) collective-permute-start(bf16[256,1024]{1,0:T(8,128)(2,1)S(1)} %get-tuple-element.12), channel_id=1, source_target_pairs={{1,16},{2,17},{3,18},{4,19},{5,20},{6,21},{7,22},{8,23},{9,24},{10... | collective-permute-start | bytes 1572872 | tf_op jit(solution)/shard_map/ppermute | solution.py:47
  141.5 32.9 %collective-permute-start.9 = (bf16[256,1024]{1,0:T(8,128)(2,1)S(1)}, bf16[256,1024]{1,0:T(8,128)(2,1)}, u32[]{:S(2)}, u32[]{:S(2)}) collective-permute-start(bf16[256,1024]{1,0:T(8,128)(2,1)S(1)} %get-tuple-element.12), channel_id=1, source_target_pairs={{0,17},{1,18},{2,19},{3,20},{4,21},{5,22},{6,23},{7,24},{8,25},{9,... | collective-permute-start | bytes 1572872 | tf_op jit(solution)/shard_map/ppermute | solution.py:47
Sparse Core Ops, SparseCore 0:
  9.5 62.1 all-gather.2
  73.9 49.1 all-gather.4

commit v10 on v9

--- a/solution.py
+++ b/solution.py
@@ -188,15 +188,12 @@
     normed = normalize(sem_stream, norm_gain)
     if shared:
         partner_normed = lax.ppermute(normed, "groups", partners)
-        both_streams = jnp.concatenate([normed, partner_normed], axis=0)
-        both_sums = contract_rows(both_streams, gathered_proj).astype(jnp.bfloat16)
-        own_sum = both_sums[:rows_here]
-        partner_part = both_sums[rows_here:]
-        mine_near = jnp.concatenate(
-            [sent_to(own_sum, 0, 1), own_sum, sent_to(own_sum, 0, -1)], axis=0)
-        other_near = jnp.concatenate(
-            [sent_to(partner_part, 1, 1), sent_to(partner_part, 1, 0), sent_to(partner_part, 1, -1)], axis=0)
-        near_pair = jnp.stack([mine_near, other_near])
+        partner_part = contract_rows(partner_normed, gathered_proj).astype(jnp.bfloat16)
+        other_pieces = [sent_to(partner_part, 1, 1), sent_to(partner_part, 1, 0), sent_to(partner_part, 1, -1)]
+        own_sum = contract_rows(normed, gathered_proj).astype(jnp.bfloat16)
+        mine_pieces = [sent_to(own_sum, 0, 1), own_sum, sent_to(own_sum, 0, -1)]
+        near_pair = jnp.concatenate(mine_pieces + other_pieces, axis=0).reshape(
+            2, 3 * rows_here, own_sum.shape[1])
         key_slot = jnp.where(key_side, 0, 1)
     else:
         cross_keys = contract_rows(normed, gathered_proj[0]).astype(jnp.bfloat16)

time: 202 us -> 202 us (level); the launches traced: 201 us -> 198 us
  waiting for transfers between devices: 96.2 us -> 89.8 us
  local copies, waits for them, and re-layouts: 4.31 us -> 9.3 us
  other arithmetic: 11.3 us -> 7.02 us
    ppermute x1, waiting for transfers between devices: 4.43 us -> 0.01 us  [on_device(): partner_normed = lax.ppermute(normed, 'groups', partners)]
    another operation x3 -> x0, other arithmetic: 4.25 us -> none  [on_device(): near_pair = jnp.stack([mine_near, other_near])]
    unnamed x11 -> x18, local copies, waits for them, and re-layouts: 3.27 us -> 7.49 us
    dot_general x2 -> x3, matrix products: 8.45 us -> 10.5 us  [contract_rows(): return jnp.dot(left_side, weight_piece, preferred_element_type=jnp.float32)]
    ppermute x5, waiting for transfers between devices: 27 us -> 24.9 us  [sent_to(): return lax.ppermute(array, ('groups', 'ctx'), pairs)]
  transfers between devices with their start and end apart: 14 -> 14, of which waited for: 9 -> 9; matrix products, arithmetic and copies ran while one was open for 8% -> 14% of each run, Pallas kernels for 0% -> 0%
where the time goes in v10:
time: 202 us; the launch traced here: 198 us
  waiting for transfers between devices  89.8 us (44%)
  starting transfers between devices  46.2 us (23%)
  between operations  16.8 us (8%)
  Pallas kernels  16.6 us (8%)
  matrix products  12.1 us (6%)
  local copies, waits for them, and re-layouts  9.3 us (5%)
  other arithmetic  7.02 us (3%)
    ppermute x6, waiting for transfers between devices, passed_along(): return lax.ppermute(array, axis, pairs)  48.6 us
    ppermute x6, starting transfers between devices, passed_along(): return lax.ppermute(array, axis, pairs)  31.2 us
    ppermute x5, waiting for transfers between devices, sent_to(): return lax.ppermute(array, ('groups', 'ctx'), pairs)  24.9 us
    pallas_call x1, Pallas kernels, coarse_attention(): pl.pallas_call(kernel, grid_spec=grid_spec, out_shape=jax.ShapeDtypeStruc...  16.6 us
    all_gather x1, waiting for transfers between devices, on_device(): gathered_proj = lax.all_gather(own_proj, 'ctx', axis=0, tiled=True)  15.4 us
    ppermute x5, starting transfers between devices, sent_to(): return lax.ppermute(array, ('groups', 'ctx'), pairs)  13.4 us
    dot_general x3, matrix products, contract_rows(): return jnp.dot(left_side, weight_piece, preferred_element_type=jnp.float32)  10.5 us
    unnamed x18, local copies, waits for them, and re-layouts  7.49 us
  transfers between devices with their start and end apart: 14, of which 9 were waited for; matrix products, arithmetic and copies ran while one was open for 14% of the time, Pallas kernels for 0%

profile of v10, /device:TPU:20, one launch (start us, length us, event | category | flops | bytes accessed | tf_op | source)
XLA Modules:
  0.0 197.8 jit_solution(6647664754171729919)
XLA Ops:
  6.5 0.7 all-gather.3.cloned.1.call-update
  7.3 0.0 all-gather.5.cloned.1.call-start
  7.3 1.7 broadcast_select_fusion
  9.0 1.2 copy.18
  10.3 1.2 copy.19
  11.5 0.1 pad_maximum_fusion
  11.6 3.4 %collective-permute-start.4 = (bf16[2,256,1024]{1,2,0:T(8,128)(2,1)S(1)}, bf16[2,256,1024]{1,2,0:T(8,128)(2,1)}, u32[]{:S(2)}, u32[]{:S(2)}) collective-permute-start(bf16[2,256,1024]{1,2,0:T(8,128)(2,1)S(1)} %pad_maximum_fusion), channel_id=1, source_target_pairs={{0,2},{1,3},{2,4},{3,5},{4,6},{5,7},{6,8},{7,9},{8,10},{9,11},{10,... | collective-permute-start | bytes 3145736 | tf_op jit(solution)/shard_map/ppermute | solution.py:23
  15.1 1.9 collective-permute-start.5
  17.0 3.5 %collective-permute-start = (s32[1]{0:T(128)}, s32[1]{0:T(128)}, u32[]{:S(2)}, u32[]{:S(2)}) collective-permute-start(s32[1]{0:T(128)} %param.22), channel_id=1, source_target_pairs={{0,1},{1,2},{2,3},{3,4},{4,5},{5,6},{6,7},{7,8},{8,9},{9,10},{10,1... | collective-permute-start | bytes 20 | tf_op jit(solution)/shard_map/ppermute | solution.py:23
  21.2 0.2 fusion.10
  21.5 42.4 %collective-permute-done = s32[1]{0:T(128)} collective-permute-done((s32[1]{0:T(128)}, s32[1]{0:T(128)}, u32[]{:S(2)}, u32[]{:S(2)}) %collective-permute-start) | collective-permute-done | bytes 36 | tf_op jit(solution)/shard_map/ppermute | solution.py:23
  64.4 16.8 %collective-permute-start.1 = (s32[1]{0:T(128)}, s32[1]{0:T(128)}, u32[]{:S(2)}, u32[]{:S(2)}) collective-permute-start(s32[1]{0:T(128)} %add.53), channel_id=1, source_target_pairs={{0,2},{1,3},{2,4},{3,5},{4,6},{5,7},{6,8},{7,9},{8,10},{9,11},{10,... | collective-permute-start | bytes 20 | tf_op jit(solution)/shard_map/ppermute | solution.py:23
  81.9 4.1 %collective-permute-start.2 = (s32[1]{0:T(128)}, s32[1]{0:T(128)}, u32[]{:S(2)}, u32[]{:S(2)}) collective-permute-start(s32[1]{0:T(128)} %add.54), channel_id=1, source_target_pairs={{0,4},{1,5},{2,6},{3,7},{4,8},{5,9},{6,10},{7,11},{8,12},{9,13},{1... | collective-permute-start | bytes 20 | tf_op jit(solution)/shard_map/ppermute | solution.py:23
  86.1 1.3 collective-permute-done.2
  88.0 1.3 collective-permute-start.3
  89.3 5.0 %collective-permute-done.3 = s32[1]{0:T(128)} collective-permute-done((s32[1]{0:T(128)}, s32[1]{0:T(128)}, u32[]{:S(2)}, u32[]{:S(2)}) %collective-permute-start.3) | collective-permute-done | bytes 36 | tf_op jit(solution)/shard_map/ppermute | solution.py:23
  94.9 1.7 maximum_maximum_fusion
  96.6 0.2 fusion.16
  96.8 1.0 fusion.11
  97.8 3.1 %fusion.17 = (f32[8,256]{1,0:T(8,128)S(1)}, f32[8,256,768]{1,2,0:T(8,128)S(1)}) fusion(f32[8,768,256]{2,1,0:T(8,128)S(1)} %fusion.11, pred[256,768]{0,1:T(8,128)(4,1)S(1)} %fusion.10), kind=kOutput, calls=%fused_computation.38 | output fusion | flops 9437951 | bytes 12787712 | tf_op jit(solution)/shard_map/sub | solution.py:63
  100.9 0.6 fusion.6
  101.6 0.7 copy-done.1
  102.3 3.6 %multiply_reduce_fusion = (f32[256]{0:T(256)S(1)}, f32[256,2048]{1,0:T(8,128)S(1)}) fusion(bf16[256,1024]{0,1:T(8,128)(2,1)S(1)} %bitcast.41, bf16[1024,2048]{1,0:T(8,128)(2,1)} %all-gather.3.cloned.1.call-done, bf16[256,2048]{1,0:T(8,128)(2,1)S(1)} %copy-done.1), kind=kOutput, calls=%fused_computation.12 | convolution fusion | flops 1075838720 | bytes 7865344 | tf_op jit(solution)/shard_map/dot_general | solution.py:79
  105.9 0.2 multiply_convert_fusion
  106.1 1.5 collective-permute-start.8
  107.7 15.4 %all-gather.5.cloned.1.call-done = bf16[2048,1024]{1,0:T(8,128)(2,1)} async-done(((bf16[128,1024]{1,0:T(8,128)(2,1)}), bf16[2048,1024]{1,0:T(8,128)(2,1)}) %all-gather.5.cloned.1.call-update) | async-done | bytes 4194320 | tf_op jit(solution)/shard_map/all_gather | solution.py:169
  123.1 3.6 %convolution_convert_fusion.1 = bf16[256,1024]{1,0:T(8,128)(2,1)S(1)} fusion(bf16[256,2048]{1,0:T(8,128)(2,1)S(1)} %multiply_convert_fusion, bf16[2048,1024]{1,0:T(8,128)(2,1)} %all-gather.5.cloned.1.call-done), kind=kOutput, calls=%fused_computation.15 | convolution fusion | flops 1074003968 | bytes 5767168 | tf_op jit(solution)/shard_map/dot_general | solution.py:79
  126.7 2.1 %collective-permute-start.6 = (bf16[256,1024]{1,0:T(8,128)(2,1)S(1)}, bf16[256,1024]{1,0:T(8,128)(2,1)S(1)}, u32[]{:S(2)}, u32[]{:S(2)}) collective-permute-start(bf16[256,1024]{1,0:T(8,128)(2,1)S(1)} %convolution_convert_fusion.1), channel_id=1, source_target_pairs={{0,1},{1,2},{2,3},{3,4},{4,5},{5,6},{6,7},{7,8},{8,9},{9,10},{10,1... | collective-permute-start | bytes 1572872 | tf_op jit(solution)/shard_map/ppermute | solution.py:47
  128.9 3.4 %collective-permute-start.7 = (bf16[256,1024]{1,0:T(8,128)(2,1)S(1)}, bf16[256,1024]{1,0:T(8,128)(2,1)S(1)}, u32[]{:S(2)}, u32[]{:S(2)}) collective-permute-start(bf16[256,1024]{1,0:T(8,128)(2,1)S(1)} %convolution_convert_fusion.1), channel_id=1, source_target_pairs={{1,0},{2,1},{3,2},{4,3},{5,4},{6,5},{7,6},{8,7},{9,8},{10,9},{11,1... | collective-permute-start | bytes 1572872 | tf_op jit(solution)/shard_map/ppermute | solution.py:47
  132.3 3.3 %convolution_convert_fusion = bf16[256,1024]{1,0:T(8,128)(2,1)} fusion(bf16[256,2048]{1,0:T(8,128)(2,1)} %collective-permute-done.8, bf16[2048,1024]{1,0:T(8,128)(2,1)S(1)} %copy-done.4), kind=kOutput, calls=%fused_computation.14 | convolution fusion | flops 1074003968 | bytes 5767168 | tf_op jit(solution)/shard_map/dot_general | solution.py:79
  135.6 2.8 %collective-permute-start.9 = (bf16[256,1024]{1,0:T(8,128)(2,1)}, bf16[256,1024]{1,0:T(8,128)(2,1)S(1)}, u32[]{:S(2)}, u32[]{:S(2)}) collective-permute-start(bf16[256,1024]{1,0:T(8,128)(2,1)} %convolution_convert_fusion), channel_id=1, source_target_pairs={{0,17},{1,18},{2,19},{3,20},{4,21},{5,22},{6,23},{7,24},{8,25},{9,... | collective-permute-start | bytes 1572872 | tf_op jit(solution)/shard_map/ppermute | solution.py:47
  138.5 0.6 collective-permute-start.10
  139.1 0.1 copy.17
  139.2 0.1 reshape.70
  139.3 0.7 concatenate.10.prm
  140.0 4.4 %collective-permute-start.11 = (bf16[256,1024]{1,0:T(8,128)(2,1)}, bf16[256,1024]{1,0:T(8,128)(2,1)S(1)}, u32[]{:S(2)}, u32[]{:S(2)}) collective-permute-start(bf16[256,1024]{1,0:T(8,128)(2,1)} %convolution_convert_fusion), channel_id=1, source_target_pairs={{1,16},{2,17},{3,18},{4,19},{5,20},{6,21},{7,22},{8,23},{9,24},{10... | collective-permute-start | bytes 1572872 | tf_op jit(solution)/shard_map/ppermute | solution.py:47
  144.4 0.6 collective-permute-done.6
  145.0 0.8 constant_dynamic-update-slice_fusion.5
  145.8 0.8 constant_dynamic-update-slice_fusion.4
  146.6 1.8 collective-permute-done.7
  148.4 0.9 constant_dynamic-update-slice_fusion.3
  149.3 8.2 %collective-permute-done.9 = bf16[256,1024]{1,0:T(8,128)(2,1)S(1)} collective-permute-done((bf16[256,1024]{1,0:T(8,128)(2,1)}, bf16[256,1024]{1,0:T(8,128)(2,1)S(1)}, u32[]{:S(2)}, u32[]{:S(2)}) %collective-permute-start.9) | collective-permute-done | bytes 524320 | tf_op jit(solution)/shard_map/ppermute | solution.py:47
  157.5 0.9 constant_dynamic-update-slice_fusion.2
  158.4 7.7 %collective-permute-done.10 = bf16[256,1024]{1,0:T(8,128)(2,1)S(1)} collective-permute-done((bf16[256,1024]{1,0:T(8,128)(2,1)}, bf16[256,1024]{1,0:T(8,128)(2,1)S(1)}, u32[]{:S(2)}, u32[]{:S(2)}) %collective-permute-start.10) | collective-permute-done | bytes 524320 | tf_op jit(solution)/shard_map/ppermute | solution.py:47
  166.0 0.8 constant_dynamic-update-slice_fusion.1
  166.9 6.7 %collective-permute-done.11 = bf16[256,1024]{1,0:T(8,128)(2,1)S(1)} collective-permute-done((bf16[256,1024]{1,0:T(8,128)(2,1)}, bf16[256,1024]{1,0:T(8,128)(2,1)S(1)}, u32[]{:S(2)}, u32[]{:S(2)}) %collective-permute-start.11) | collective-permute-done | bytes 524320 | tf_op jit(solution)/shard_map/ppermute | solution.py:47
  173.5 0.8 constant_dynamic-update-slice_fusion
  174.4 16.6 %shard_map.118 = bf16[1024,1024]{1,0:T(8,128)(2,1)} custom-call(s32[12]{0:T(128)} %concatenate.10.prm, f32[8]{0:T(128)} %slopes_ref.1, bf16[1024,1024]{1,0:T(8,128)(2,1)} %q_ref.1, bf16[2,768,1024]{2,1,0:T(8,128)(2,1)} %bitcast.9.k_ref.v_ref, bf16[2,768,1024]{2,1,0:T(8,128)(2,1)} %bitcast.9.k_ref.v_ref), custom_call_target="tpu_custom_call" | custom-call | tf_op jit(solution)/shard_map/pallas_call | solution.py:132
  (19 shorter events, 0.1 us)
Async XLA Ops:
  6.5 90.3 %copy-start = (bf16[256,1024]{1,0:T(8,128)(2,1)S(1)}, bf16[256,1024]{1,0:T(8,128)(2,1)}, u32[]{:S(2)}) copy-start(bf16[256,1024]{1,0:T(8,128)(2,1)} %param.12) | copy-start | bytes 1572868
  6.5 95.1 %all-gather.3.cloned.1.call-start = ((), (), s32[]{:S(2)}) async-start(), calls=%async_computation | async-start | bytes 4456448 | tf_op jit(solution)/shard_map/all_gather | solution.py:157
  7.3 115.8 %all-gather.5.cloned.1.call-start = ((), (), s32[]{:S(2)}) async-start(), calls=%async_computation.1 | async-start | bytes 4456448 | tf_op jit(solution)/shard_map/all_gather | solution.py:169
  11.6 83.3 %collective-permute-start.4 = (bf16[2,256,1024]{1,2,0:T(8,128)(2,1)S(1)}, bf16[2,256,1024]{1,2,0:T(8,128)(2,1)}, u32[]{:S(2)}, u32[]{:S(2)}) collective-permute-start(bf16[2,256,1024]{1,2,0:T(8,128)(2,1)S(1)} %pad_maximum_fusion), channel_id=1, source_target_pairs={{0,2},{1,3},{2,4},{3,5},{4,6},{5,7},{6,8},{7,9},{8,10},{9,11},{10,... | collective-permute-start | bytes 3145736 | tf_op jit(solution)/shard_map/ppermute | solution.py:23
  15.1 79.8 %collective-permute-start.5 = (bf16[2,256,1024]{1,2,0:T(8,128)(2,1)S(1)}, bf16[2,256,1024]{1,2,0:T(8,128)(2,1)}, u32[]{:S(2)}, u32[]{:S(2)}) collective-permute-start(bf16[2,256,1024]{1,2,0:T(8,128)(2,1)S(1)} %pad_maximum_fusion), channel_id=1, source_target_pairs={{0,1},{1,2},{2,3},{3,4},{4,5},{5,6},{6,7},{7,8},{8,9},{9,10},{10,1... | collective-permute-start | bytes 3145736 | tf_op jit(solution)/shard_map/ppermute | solution.py:23
  17.0 46.8 %collective-permute-start = (s32[1]{0:T(128)}, s32[1]{0:T(128)}, u32[]{:S(2)}, u32[]{:S(2)}) collective-permute-start(s32[1]{0:T(128)} %param.22), channel_id=1, source_target_pairs={{0,1},{1,2},{2,3},{3,4},{4,5},{5,6},{6,7},{7,8},{8,9},{9,10},{10,1... | collective-permute-start | bytes 20 | tf_op jit(solution)/shard_map/ppermute | solution.py:23
  64.4 16.8 %collective-permute-start.1 = (s32[1]{0:T(128)}, s32[1]{0:T(128)}, u32[]{:S(2)}, u32[]{:S(2)}) collective-permute-start(s32[1]{0:T(128)} %add.53), channel_id=1, source_target_pairs={{0,2},{1,3},{2,4},{3,5},{4,6},{5,7},{6,8},{7,9},{8,10},{9,11},{10,... | collective-permute-start | bytes 20 | tf_op jit(solution)/shard_map/ppermute | solution.py:23
  81.9 5.4 %collective-permute-start.2 = (s32[1]{0:T(128)}, s32[1]{0:T(128)}, u32[]{:S(2)}, u32[]{:S(2)}) collective-permute-start(s32[1]{0:T(128)} %add.54), channel_id=1, source_target_pairs={{0,4},{1,5},{2,6},{3,7},{4,8},{5,9},{6,10},{7,11},{8,12},{9,13},{1... | collective-permute-start | bytes 20 | tf_op jit(solution)/shard_map/ppermute | solution.py:23
  88.0 6.3 %collective-permute-start.3 = (s32[1]{0:T(128)}, s32[1]{0:T(128)}, u32[]{:S(2)}, u32[]{:S(2)}) collective-permute-start(s32[1]{0:T(128)} %add.55), channel_id=1, source_target_pairs={{0,8},{1,9},{2,10},{3,11},{4,12},{5,13},{6,14},{7,15},{16,24},{17,... | collective-permute-start | bytes 20 | tf_op jit(solution)/shard_map/ppermute | solution.py:23
  100.9 1.4 copy-start.1
  101.6 4.3 %copy-start.2 = (f32[2048]{0:T(1024)S(1)}, f32[2048]{0:T(1024)}, u32[]{:S(2)}) copy-start(f32[2048]{0:T(1024)} %param.17) | copy-start | bytes 24580
  106.1 26.1 %collective-permute-start.8 = (bf16[256,2048]{1,0:T(8,128)(2,1)S(1)}, bf16[256,2048]{1,0:T(8,128)(2,1)}, u32[]{:S(2)}, u32[]{:S(2)}) collective-permute-start(bf16[256,2048]{1,0:T(8,128)(2,1)S(1)} %multiply_convert_fusion), channel_id=1, source_target_pairs={{0,16},{16,0},{1,17},{17,1},{2,18},{18,2},{3,19},{19,3},{4,20},{20... | collective-permute-start | bytes 3145736 | tf_op jit(solution)/shard_map/ppermute | solution.py:190
  123.1 9.2 %copy-start.4 = (bf16[2048,1024]{1,0:T(8,128)(2,1)S(1)}, bf16[2048,1024]{1,0:T(8,128)(2,1)}, u32[]{:S(2)}) copy-start(bf16[2048,1024]{1,0:T(8,128)(2,1)} %all-gather.5.cloned.1.call-done) | copy-start | bytes 12582916
  126.7 12.4 %copy-start.3 = (s32[4,2]{0,1:T(2,128)S(1)}, s32[4,2]{0,1:T(2,128)}, u32[]{:S(2)}) copy-start(s32[4,2]{0,1:T(2,128)} %param.23) | copy-start | bytes 100
  126.7 18.3 %collective-permute-start.6 = (bf16[256,1024]{1,0:T(8,128)(2,1)S(1)}, bf16[256,1024]{1,0:T(8,128)(2,1)S(1)}, u32[]{:S(2)}, u32[]{:S(2)}) collective-permute-start(bf16[256,1024]{1,0:T(8,128)(2,1)S(1)} %convolution_convert_fusion.1), channel_id=1, source_target_pairs={{0,1},{1,2},{2,3},{3,4},{4,5},{5,6},{6,7},{7,8},{8,9},{9,10},{10,1... | collective-permute-start | bytes 1572872 | tf_op jit(solution)/shard_map/ppermute | solution.py:47
  128.9 19.6 %collective-permute-start.7 = (bf16[256,1024]{1,0:T(8,128)(2,1)S(1)}, bf16[256,1024]{1,0:T(8,128)(2,1)S(1)}, u32[]{:S(2)}, u32[]{:S(2)}) collective-permute-start(bf16[256,1024]{1,0:T(8,128)(2,1)S(1)} %convolution_convert_fusion.1), channel_id=1, source_target_pairs={{1,0},{2,1},{3,2},{4,3},{5,4},{6,5},{7,6},{8,7},{9,8},{10,9},{11,1... | collective-permute-start | bytes 1572872 | tf_op jit(solution)/shard_map/ppermute | solution.py:47
  135.6 21.9 %collective-permute-start.9 = (bf16[256,1024]{1,0:T(8,128)(2,1)}, bf16[256,1024]{1,0:T(8,128)(2,1)S(1)}, u32[]{:S(2)}, u32[]{:S(2)}) collective-permute-start(bf16[256,1024]{1,0:T(8,128)(2,1)} %convolution_convert_fusion), channel_id=1, source_target_pairs={{0,17},{1,18},{2,19},{3,20},{4,21},{5,22},{6,23},{7,24},{8,25},{9,... | collective-permute-start | bytes 1572872 | tf_op jit(solution)/shard_map/ppermute | solution.py:47
  138.5 27.6 %collective-permute-start.10 = (bf16[256,1024]{1,0:T(8,128)(2,1)}, bf16[256,1024]{1,0:T(8,128)(2,1)S(1)}, u32[]{:S(2)}, u32[]{:S(2)}) collective-permute-start(bf16[256,1024]{1,0:T(8,128)(2,1)} %convolution_convert_fusion), channel_id=1, source_target_pairs={{0,16},{1,17},{2,18},{3,19},{4,20},{5,21},{6,22},{7,23},{8,24},{9,... | collective-permute-start | bytes 1572872 | tf_op jit(solution)/shard_map/ppermute | solution.py:47
  140.0 33.6 %collective-permute-start.11 = (bf16[256,1024]{1,0:T(8,128)(2,1)}, bf16[256,1024]{1,0:T(8,128)(2,1)S(1)}, u32[]{:S(2)}, u32[]{:S(2)}) collective-permute-start(bf16[256,1024]{1,0:T(8,128)(2,1)} %convolution_convert_fusion), channel_id=1, source_target_pairs={{1,16},{2,17},{3,18},{4,19},{5,20},{6,21},{7,22},{8,23},{9,24},{10... | collective-permute-start | bytes 1572872 | tf_op jit(solution)/shard_map/ppermute | solution.py:47
Sparse Core Ops, SparseCore 0:
  9.5 62.1 all-gather.2
  73.9 49.1 all-gather.4

commit v11 on v10

--- a/solution.py
+++ b/solution.py
@@ -189,7 +189,8 @@
     if shared:
         partner_normed = lax.ppermute(normed, "groups", partners)
         partner_part = contract_rows(partner_normed, gathered_proj).astype(jnp.bfloat16)
-        other_pieces = [sent_to(partner_part, 1, 1), sent_to(partner_part, 1, 0), sent_to(partner_part, 1, -1)]
+        partner_sum = sent_to(partner_part, 1, 0)
+        other_pieces = [sent_to(partner_sum, 0, 1), partner_sum, sent_to(partner_sum, 0, -1)]
         own_sum = contract_rows(normed, gathered_proj).astype(jnp.bfloat16)
         mine_pieces = [sent_to(own_sum, 0, 1), own_sum, sent_to(own_sum, 0, -1)]
         near_pair = jnp.concatenate(mine_pieces + other_pieces, axis=0).reshape(

time: 202 us -> 188 us (0.931); the launches traced: 198 us -> 187 us
  waiting for transfers between devices: 89.8 us -> 81.8 us
  matrix products: 12.1 us -> 9.97 us
    ppermute x5, waiting for transfers between devices: 24.9 us -> 12.6 us  [sent_to(): return lax.ppermute(array, ('groups', 'ctx'), pairs)]
    ppermute x1, waiting for transfers between devices: 0.01 us -> 4.31 us  [on_device(): partner_normed = lax.ppermute(normed, 'groups', partners)]
    dot_general x3, matrix products: 10.5 us -> 8.3 us  [contract_rows(): return jnp.dot(left_side, weight_piece, preferred_element_type=jnp.float32)]
  transfers between devices with their start and end apart: 14 -> 14, of which waited for: 9 -> 9; matrix products, arithmetic and copies ran while one was open for 14% -> 11% of each run, Pallas kernels for 0% -> 0%
where the time goes in v11:
time: 188 us; the launch traced here: 187 us
  waiting for transfers between devices  81.8 us (44%)
  starting transfers between devices  45.6 us (24%)
  between operations  16.8 us (9%)
  Pallas kernels  16.6 us (9%)
  matrix products  9.97 us (5%)
  local copies, waits for them, and re-layouts  9.31 us (5%)
  other arithmetic  7.02 us (4%)
    ppermute x6, waiting for transfers between devices, passed_along(): return lax.ppermute(array, axis, pairs)  48.6 us
    ppermute x6, starting transfers between devices, passed_along(): return lax.ppermute(array, axis, pairs)  31.2 us
    pallas_call x1, Pallas kernels, coarse_attention(): pl.pallas_call(kernel, grid_spec=grid_spec, out_shape=jax.ShapeDtypeStruc...  16.6 us
    all_gather x1, waiting for transfers between devices, on_device(): gathered_proj = lax.all_gather(own_proj, 'ctx', axis=0, tiled=True)  15.4 us
    ppermute x5, starting transfers between devices, sent_to(): return lax.ppermute(array, ('groups', 'ctx'), pairs)  12.8 us
    ppermute x5, waiting for transfers between devices, sent_to(): return lax.ppermute(array, ('groups', 'ctx'), pairs)  12.6 us
    dot_general x3, matrix products, contract_rows(): return jnp.dot(left_side, weight_piece, preferred_element_type=jnp.float32)  8.3 us
    unnamed x18, local copies, waits for them, and re-layouts  7.49 us
  transfers between devices with their start and end apart: 14, of which 9 were waited for; matrix products, arithmetic and copies ran while one was open for 11% of the time, Pallas kernels for 0%

profile of v11, /device:TPU:20, one launch (start us, length us, event | category | flops | bytes accessed | tf_op | source)
XLA Modules:
  0.0 187.0 jit_solution(4990838487412964631)
XLA Ops:
  6.5 0.7 all-gather.3.cloned.1.call-update
  7.3 0.0 all-gather.5.cloned.1.call-start
  7.3 1.7 broadcast_select_fusion
  9.0 1.2 copy.18
  10.3 1.2 copy.19
  11.5 0.1 pad_maximum_fusion
  11.6 3.4 %collective-permute-start.4 = (bf16[2,256,1024]{1,2,0:T(8,128)(2,1)S(1)}, bf16[2,256,1024]{1,2,0:T(8,128)(2,1)}, u32[]{:S(2)}, u32[]{:S(2)}) collective-permute-start(bf16[2,256,1024]{1,2,0:T(8,128)(2,1)S(1)} %pad_maximum_fusion), channel_id=1, source_target_pairs={{0,2},{1,3},{2,4},{3,5},{4,6},{5,7},{6,8},{7,9},{8,10},{9,11},{10,... | collective-permute-start | bytes 3145736 | tf_op jit(solution)/shard_map/ppermute | solution.py:23
  15.1 1.9 %collective-permute-start.5 = (bf16[2,256,1024]{1,2,0:T(8,128)(2,1)S(1)}, bf16[2,256,1024]{1,2,0:T(8,128)(2,1)}, u32[]{:S(2)}, u32[]{:S(2)}) collective-permute-start(bf16[2,256,1024]{1,2,0:T(8,128)(2,1)S(1)} %pad_maximum_fusion), channel_id=1, source_target_pairs={{0,1},{1,2},{2,3},{3,4},{4,5},{5,6},{6,7},{7,8},{8,9},{9,10},{10,1... | collective-permute-start | bytes 3145736 | tf_op jit(solution)/shard_map/ppermute | solution.py:23
  17.0 3.5 %collective-permute-start = (s32[1]{0:T(128)}, s32[1]{0:T(128)}, u32[]{:S(2)}, u32[]{:S(2)}) collective-permute-start(s32[1]{0:T(128)} %param.22), channel_id=1, source_target_pairs={{0,1},{1,2},{2,3},{3,4},{4,5},{5,6},{6,7},{7,8},{8,9},{9,10},{10,1... | collective-permute-start | bytes 20 | tf_op jit(solution)/shard_map/ppermute | solution.py:23
  21.2 0.2 fusion.10
  21.5 42.4 %collective-permute-done = s32[1]{0:T(128)} collective-permute-done((s32[1]{0:T(128)}, s32[1]{0:T(128)}, u32[]{:S(2)}, u32[]{:S(2)}) %collective-permute-start) | collective-permute-done | bytes 36 | tf_op jit(solution)/shard_map/ppermute | solution.py:23
  64.4 16.8 %collective-permute-start.1 = (s32[1]{0:T(128)}, s32[1]{0:T(128)}, u32[]{:S(2)}, u32[]{:S(2)}) collective-permute-start(s32[1]{0:T(128)} %add.53), channel_id=1, source_target_pairs={{0,2},{1,3},{2,4},{3,5},{4,6},{5,7},{6,8},{7,9},{8,10},{9,11},{10,... | collective-permute-start | bytes 20 | tf_op jit(solution)/shard_map/ppermute | solution.py:23
  81.9 4.1 %collective-permute-start.2 = (s32[1]{0:T(128)}, s32[1]{0:T(128)}, u32[]{:S(2)}, u32[]{:S(2)}) collective-permute-start(s32[1]{0:T(128)} %add.54), channel_id=1, source_target_pairs={{0,4},{1,5},{2,6},{3,7},{4,8},{5,9},{6,10},{7,11},{8,12},{9,13},{1... | collective-permute-start | bytes 20 | tf_op jit(solution)/shard_map/ppermute | solution.py:23
  86.1 1.3 collective-permute-done.2
  88.0 1.3 collective-permute-start.3
  89.3 5.0 %collective-permute-done.3 = s32[1]{0:T(128)} collective-permute-done((s32[1]{0:T(128)}, s32[1]{0:T(128)}, u32[]{:S(2)}, u32[]{:S(2)}) %collective-permute-start.3) | collective-permute-done | bytes 36 | tf_op jit(solution)/shard_map/ppermute | solution.py:23
  94.9 1.7 maximum_maximum_fusion
  96.6 0.2 fusion.16
  96.8 1.0 fusion.11
  97.8 3.1 %fusion.17 = (f32[8,256]{1,0:T(8,128)S(1)}, f32[8,256,768]{1,2,0:T(8,128)S(1)}) fusion(f32[8,768,256]{2,1,0:T(8,128)S(1)} %fusion.11, pred[256,768]{0,1:T(8,128)(4,1)S(1)} %fusion.10), kind=kOutput, calls=%fused_computation.38 | output fusion | flops 9437951 | bytes 12787712 | tf_op jit(solution)/shard_map/sub | solution.py:63
  100.9 0.6 fusion.6
  101.6 0.7 copy-done.1
  102.3 3.6 %multiply_reduce_fusion = (f32[256]{0:T(256)S(1)}, f32[256,2048]{1,0:T(8,128)S(1)}) fusion(bf16[256,1024]{0,1:T(8,128)(2,1)S(1)} %bitcast.41, bf16[1024,2048]{1,0:T(8,128)(2,1)} %all-gather.3.cloned.1.call-done, bf16[256,2048]{1,0:T(8,128)(2,1)S(1)} %copy-done.1), kind=kOutput, calls=%fused_computation.12 | convolution fusion | flops 1075838720 | bytes 7865344 | tf_op jit(solution)/shard_map/dot_general | solution.py:79
  105.9 0.2 multiply_convert_fusion
  106.1 1.5 collective-permute-start.8
  107.7 15.4 %all-gather.5.cloned.1.call-done = bf16[2048,1024]{1,0:T(8,128)(2,1)} async-done(((bf16[128,1024]{1,0:T(8,128)(2,1)}), bf16[2048,1024]{1,0:T(8,128)(2,1)}) %all-gather.5.cloned.1.call-update) | async-done | bytes 4194320 | tf_op jit(solution)/shard_map/all_gather | solution.py:169
  123.1 4.3 %collective-permute-done.8 = bf16[256,2048]{1,0:T(8,128)(2,1)S(1)} collective-permute-done((bf16[256,2048]{1,0:T(8,128)(2,1)S(1)}, bf16[256,2048]{1,0:T(8,128)(2,1)S(1)}, u32[]{:S(2)}, u32[]{:S(2)}) %collective-permute-start.8) | collective-permute-done | bytes 1048608 | tf_op jit(solution)/shard_map/ppermute | solution.py:190
  127.4 3.4 %convolution_convert_fusion = bf16[256,1024]{1,0:T(8,128)(2,1)S(1)} fusion(bf16[256,2048]{1,0:T(8,128)(2,1)S(1)} %collective-permute-done.8, bf16[2048,1024]{1,0:T(8,128)(2,1)} %all-gather.5.cloned.1.call-done), kind=kOutput, calls=%fused_computation.14 | convolution fusion | flops 1074003968 | bytes 5767168 | tf_op jit(solution)/shard_map/dot_general | solution.py:79
  130.9 1.5 collective-permute-start.9
  132.4 1.3 convolution_convert_fusion.1
  133.7 1.9 %collective-permute-start.6 = (bf16[256,1024]{1,0:T(8,128)(2,1)S(1)}, bf16[256,1024]{1,0:T(8,128)(2,1)S(1)}, u32[]{:S(2)}, u32[]{:S(2)}) collective-permute-start(bf16[256,1024]{1,0:T(8,128)(2,1)S(1)} %convolution_convert_fusion.1), channel_id=1, source_target_pairs={{0,1},{1,2},{2,3},{3,4},{4,5},{5,6},{6,7},{7,8},{8,9},{9,10},{10,1... | collective-permute-start | bytes 1572872 | tf_op jit(solution)/shard_map/ppermute | solution.py:47
  135.6 3.6 %collective-permute-start.7 = (bf16[256,1024]{1,0:T(8,128)(2,1)S(1)}, bf16[256,1024]{1,0:T(8,128)(2,1)S(1)}, u32[]{:S(2)}, u32[]{:S(2)}) collective-permute-start(bf16[256,1024]{1,0:T(8,128)(2,1)S(1)} %convolution_convert_fusion.1), channel_id=1, source_target_pairs={{1,0},{2,1},{3,2},{4,3},{5,4},{6,5},{7,6},{8,7},{9,8},{10,9},{11,1... | collective-permute-start | bytes 1572872 | tf_op jit(solution)/shard_map/ppermute | solution.py:47
  139.3 1.6 collective-permute-done.9
  140.8 1.9 %collective-permute-start.10 = (bf16[256,1024]{1,0:T(8,128)(2,1)S(1)}, bf16[256,1024]{1,0:T(8,128)(2,1)S(1)}, u32[]{:S(2)}, u32[]{:S(2)}) collective-permute-start(bf16[256,1024]{1,0:T(8,128)(2,1)S(1)} %collective-permute-done.9), channel_id=1, source_target_pairs={{0,1},{1,2},{2,3},{3,4},{4,5},{5,6},{6,7},{7,8},{8,9},{9,10},{10,1... | collective-permute-start | bytes 1572872 | tf_op jit(solution)/shard_map/ppermute | solution.py:47
  142.8 0.1 copy.17
  142.9 0.1 reshape.70
  143.0 0.7 concatenate.10.prm
  143.6 3.8 %collective-permute-start.11 = (bf16[256,1024]{1,0:T(8,128)(2,1)S(1)}, bf16[256,1024]{1,0:T(8,128)(2,1)S(1)}, u32[]{:S(2)}, u32[]{:S(2)}) collective-permute-start(bf16[256,1024]{1,0:T(8,128)(2,1)S(1)} %collective-permute-done.9), channel_id=1, source_target_pairs={{1,0},{2,1},{3,2},{4,3},{5,4},{6,5},{7,6},{8,7},{9,8},{10,9},{11,1... | collective-permute-start | bytes 1572872 | tf_op jit(solution)/shard_map/ppermute | solution.py:47
  147.5 2.4 %collective-permute-done.6 = bf16[256,1024]{1,0:T(8,128)(2,1)S(1)} collective-permute-done((bf16[256,1024]{1,0:T(8,128)(2,1)S(1)}, bf16[256,1024]{1,0:T(8,128)(2,1)S(1)}, u32[]{:S(2)}, u32[]{:S(2)}) %collective-permute-start.6) | collective-permute-done | bytes 524320 | tf_op jit(solution)/shard_map/ppermute | solution.py:47
  149.8 0.8 constant_dynamic-update-slice_fusion.5
  150.6 0.8 constant_dynamic-update-slice_fusion.4
  151.5 2.5 %collective-permute-done.7 = bf16[256,1024]{1,0:T(8,128)(2,1)S(1)} collective-permute-done((bf16[256,1024]{1,0:T(8,128)(2,1)S(1)}, bf16[256,1024]{1,0:T(8,128)(2,1)S(1)}, u32[]{:S(2)}, u32[]{:S(2)}) %collective-permute-start.7) | collective-permute-done | bytes 524320 | tf_op jit(solution)/shard_map/ppermute | solution.py:47
  154.0 0.9 constant_dynamic-update-slice_fusion.3
  154.8 6.2 %collective-permute-done.10 = bf16[256,1024]{1,0:T(8,128)(2,1)S(1)} collective-permute-done((bf16[256,1024]{1,0:T(8,128)(2,1)S(1)}, bf16[256,1024]{1,0:T(8,128)(2,1)S(1)}, u32[]{:S(2)}, u32[]{:S(2)}) %collective-permute-start.10) | collective-permute-done | bytes 524320 | tf_op jit(solution)/shard_map/ppermute | solution.py:47
  161.1 0.9 constant_dynamic-update-slice_fusion.2
  161.9 0.8 constant_dynamic-update-slice_fusion.1
  162.8 0.8 constant_dynamic-update-slice_fusion
  163.6 16.6 %shard_map.118 = bf16[1024,1024]{1,0:T(8,128)(2,1)} custom-call(s32[12]{0:T(128)} %concatenate.10.prm, f32[8]{0:T(128)} %slopes_ref.1, bf16[1024,1024]{1,0:T(8,128)(2,1)} %q_ref.1, bf16[2,768,1024]{2,1,0:T(8,128)(2,1)} %bitcast.9.k_ref.v_ref, bf16[2,768,1024]{2,1,0:T(8,128)(2,1)} %bitcast.9.k_ref.v_ref), custom_call_target="tpu_custom_call" | custom-call | tf_op jit(solution)/shard_map/pallas_call | solution.py:132
  (19 shorter events, 0.1 us)
Async XLA Ops:
  6.5 90.3 %copy-start = (bf16[256,1024]{1,0:T(8,128)(2,1)S(1)}, bf16[256,1024]{1,0:T(8,128)(2,1)}, u32[]{:S(2)}) copy-start(bf16[256,1024]{1,0:T(8,128)(2,1)} %param.12) | copy-start | bytes 1572868
  6.5 95.1 %all-gather.3.cloned.1.call-start = ((), (), s32[]{:S(2)}) async-start(), calls=%async_computation | async-start | bytes 4456448 | tf_op jit(solution)/shard_map/all_gather | solution.py:157
  7.3 115.8 %all-gather.5.cloned.1.call-start = ((), (), s32[]{:S(2)}) async-start(), calls=%async_computation.1 | async-start | bytes 4456448 | tf_op jit(solution)/shard_map/all_gather | solution.py:169
  11.6 83.3 %collective-permute-start.4 = (bf16[2,256,1024]{1,2,0:T(8,128)(2,1)S(1)}, bf16[2,256,1024]{1,2,0:T(8,128)(2,1)}, u32[]{:S(2)}, u32[]{:S(2)}) collective-permute-start(bf16[2,256,1024]{1,2,0:T(8,128)(2,1)S(1)} %pad_maximum_fusion), channel_id=1, source_target_pairs={{0,2},{1,3},{2,4},{3,5},{4,6},{5,7},{6,8},{7,9},{8,10},{9,11},{10,... | collective-permute-start | bytes 3145736 | tf_op jit(solution)/shard_map/ppermute | solution.py:23
  15.1 79.8 %collective-permute-start.5 = (bf16[2,256,1024]{1,2,0:T(8,128)(2,1)S(1)}, bf16[2,256,1024]{1,2,0:T(8,128)(2,1)}, u32[]{:S(2)}, u32[]{:S(2)}) collective-permute-start(bf16[2,256,1024]{1,2,0:T(8,128)(2,1)S(1)} %pad_maximum_fusion), channel_id=1, source_target_pairs={{0,1},{1,2},{2,3},{3,4},{4,5},{5,6},{6,7},{7,8},{8,9},{9,10},{10,1... | collective-permute-start | bytes 3145736 | tf_op jit(solution)/shard_map/ppermute | solution.py:23
  17.0 46.8 %collective-permute-start = (s32[1]{0:T(128)}, s32[1]{0:T(128)}, u32[]{:S(2)}, u32[]{:S(2)}) collective-permute-start(s32[1]{0:T(128)} %param.22), channel_id=1, source_target_pairs={{0,1},{1,2},{2,3},{3,4},{4,5},{5,6},{6,7},{7,8},{8,9},{9,10},{10,1... | collective-permute-start | bytes 20 | tf_op jit(solution)/shard_map/ppermute | solution.py:23
  64.4 16.8 %collective-permute-start.1 = (s32[1]{0:T(128)}, s32[1]{0:T(128)}, u32[]{:S(2)}, u32[]{:S(2)}) collective-permute-start(s32[1]{0:T(128)} %add.53), channel_id=1, source_target_pairs={{0,2},{1,3},{2,4},{3,5},{4,6},{5,7},{6,8},{7,9},{8,10},{9,11},{10,... | collective-permute-start | bytes 20 | tf_op jit(solution)/shard_map/ppermute | solution.py:23
  81.9 5.4 %collective-permute-start.2 = (s32[1]{0:T(128)}, s32[1]{0:T(128)}, u32[]{:S(2)}, u32[]{:S(2)}) collective-permute-start(s32[1]{0:T(128)} %add.54), channel_id=1, source_target_pairs={{0,4},{1,5},{2,6},{3,7},{4,8},{5,9},{6,10},{7,11},{8,12},{9,13},{1... | collective-permute-start | bytes 20 | tf_op jit(solution)/shard_map/ppermute | solution.py:23
  88.0 6.3 %collective-permute-start.3 = (s32[1]{0:T(128)}, s32[1]{0:T(128)}, u32[]{:S(2)}, u32[]{:S(2)}) collective-permute-start(s32[1]{0:T(128)} %add.55), channel_id=1, source_target_pairs={{0,8},{1,9},{2,10},{3,11},{4,12},{5,13},{6,14},{7,15},{16,24},{17,... | collective-permute-start | bytes 20 | tf_op jit(solution)/shard_map/ppermute | solution.py:23
  100.9 1.4 copy-start.1
  101.6 4.3 %copy-start.2 = (f32[2048]{0:T(1024)S(1)}, f32[2048]{0:T(1024)}, u32[]{:S(2)}) copy-start(f32[2048]{0:T(1024)} %param.17) | copy-start | bytes 24580
  106.1 21.3 %collective-permute-start.8 = (bf16[256,2048]{1,0:T(8,128)(2,1)S(1)}, bf16[256,2048]{1,0:T(8,128)(2,1)S(1)}, u32[]{:S(2)}, u32[]{:S(2)}) collective-permute-start(bf16[256,2048]{1,0:T(8,128)(2,1)S(1)} %multiply_convert_fusion), channel_id=1, source_target_pairs={{0,16},{16,0},{1,17},{17,1},{2,18},{18,2},{3,19},{19,3},{4,20},{20... | collective-permute-start | bytes 3145736 | tf_op jit(solution)/shard_map/ppermute | solution.py:190
  123.1 9.3 %copy-start.4 = (bf16[2048,1024]{1,0:T(8,128)(2,1)S(1)}, bf16[2048,1024]{1,0:T(8,128)(2,1)}, u32[]{:S(2)}) copy-start(bf16[2048,1024]{1,0:T(8,128)(2,1)} %all-gather.5.cloned.1.call-done) | copy-start | bytes 12582916
  130.8 11.9 %copy-start.3 = (s32[4,2]{0,1:T(2,128)S(1)}, s32[4,2]{0,1:T(2,128)}, u32[]{:S(2)}) copy-start(s32[4,2]{0,1:T(2,128)} %param.23) | copy-start | bytes 100
  130.9 10.0 %collective-permute-start.9 = (bf16[256,1024]{1,0:T(8,128)(2,1)S(1)}, bf16[256,1024]{1,0:T(8,128)(2,1)S(1)}, u32[]{:S(2)}, u32[]{:S(2)}) collective-permute-start(bf16[256,1024]{1,0:T(8,128)(2,1)S(1)} %convolution_convert_fusion), channel_id=1, source_target_pairs={{0,16},{1,17},{2,18},{3,19},{4,20},{5,21},{6,22},{7,23},{8,24},{9,... | collective-permute-start | bytes 1572872 | tf_op jit(solution)/shard_map/ppermute | solution.py:47
  133.7 16.1 %collective-permute-start.6 = (bf16[256,1024]{1,0:T(8,128)(2,1)S(1)}, bf16[256,1024]{1,0:T(8,128)(2,1)S(1)}, u32[]{:S(2)}, u32[]{:S(2)}) collective-permute-start(bf16[256,1024]{1,0:T(8,128)(2,1)S(1)} %convolution_convert_fusion.1), channel_id=1, source_target_pairs={{0,1},{1,2},{2,3},{3,4},{4,5},{5,6},{6,7},{7,8},{8,9},{9,10},{10,1... | collective-permute-start | bytes 1572872 | tf_op jit(solution)/shard_map/ppermute | solution.py:47
  135.6 18.4 %collective-permute-start.7 = (bf16[256,1024]{1,0:T(8,128)(2,1)S(1)}, bf16[256,1024]{1,0:T(8,128)(2,1)S(1)}, u32[]{:S(2)}, u32[]{:S(2)}) collective-permute-start(bf16[256,1024]{1,0:T(8,128)(2,1)S(1)} %convolution_convert_fusion.1), channel_id=1, source_target_pairs={{1,0},{2,1},{3,2},{4,3},{5,4},{6,5},{7,6},{8,7},{9,8},{10,9},{11,1... | collective-permute-start | bytes 1572872 | tf_op jit(solution)/shard_map/ppermute | solution.py:47
  140.8 20.2 %collective-permute-start.10 = (bf16[256,1024]{1,0:T(8,128)(2,1)S(1)}, bf16[256,1024]{1,0:T(8,128)(2,1)S(1)}, u32[]{:S(2)}, u32[]{:S(2)}) collective-permute-start(bf16[256,1024]{1,0:T(8,128)(2,1)S(1)} %collective-permute-done.9), channel_id=1, source_target_pairs={{0,1},{1,2},{2,3},{3,4},{4,5},{5,6},{6,7},{7,8},{8,9},{9,10},{10,1... | collective-permute-start | bytes 1572872 | tf_op jit(solution)/shard_map/ppermute | solution.py:47
  143.6 19.1 %collective-permute-start.11 = (bf16[256,1024]{1,0:T(8,128)(2,1)S(1)}, bf16[256,1024]{1,0:T(8,128)(2,1)S(1)}, u32[]{:S(2)}, u32[]{:S(2)}) collective-permute-start(bf16[256,1024]{1,0:T(8,128)(2,1)S(1)} %collective-permute-done.9), channel_id=1, source_target_pairs={{1,0},{2,1},{3,2},{4,3},{5,4},{6,5},{7,6},{8,7},{9,8},{10,9},{11,1... | collective-permute-start | bytes 1572872 | tf_op jit(solution)/shard_map/ppermute | solution.py:47
Sparse Core Ops, SparseCore 0:
  9.5 62.1 all-gather.2
  73.9 49.1 all-gather.4

commit v12 on v11

--- a/solution.py
+++ b/solution.py
@@ -171,6 +171,7 @@
         stacked_proj = jnp.stack([key_proj, value_proj])
         gathered_proj = lax.all_gather(stacked_proj, "ctx", axis=1, tiled=True)
     own_pair = jnp.stack([sem_keys, sem_values])
+    full_out_proj, own_pair = lax.optimization_barrier((full_out_proj, own_pair))
     reach_shards = (W - 1 + rows_here - 1) // rows_here
     earlier = []
     for distance in range(1, reach_shards + 1):

time: 188 us -> 235 us (1.25)
  waiting for transfers between devices: 81.8 us -> 131 us
  local copies, waits for them, and re-layouts: 9.31 us -> 11.9 us
    all_gather x1, waiting for transfers between devices: 0.02 us -> 47.8 us  [on_device(): full_out_proj = lax.all_gather(out_proj, 'ctx', axis=0, tiled=True)]
    all_gather x1, waiting for transfers between devices: 15.4 us -> 0.01 us  [on_device(): gathered_proj = lax.all_gather(own_proj, 'ctx', axis=0, tiled=True)]
    ppermute x1, waiting for transfers between devices: 4.31 us -> 19.4 us  [on_device(): partner_normed = lax.ppermute(normed, 'groups', partners)]
    unnamed x18 -> x22, local copies, waits for them, and re-layouts: 7.49 us -> 10 us
  transfers between devices with their start and end apart: 14 -> 14, of which waited for: 9 -> 10; matrix products, arithmetic and copies ran while one was open for 11% -> 8% of each run, Pallas kernels for 0% -> 0%
where the time goes in v12:
time: 235 us; the launch traced here: 234 us
  waiting for transfers between devices  131 us (56%)
  starting transfers between devices  44.2 us (19%)
  between operations  17.1 us (7%)
  Pallas kernels  16.6 us (7%)
  local copies, waits for them, and re-layouts  11.9 us (5%)
  matrix products  7.76 us (3%)
  other arithmetic  5.36 us (2%)
    ppermute x6, waiting for transfers between devices, passed_along(): return lax.ppermute(array, axis, pairs)  50.5 us
    all_gather x1, waiting for transfers between devices, on_device(): full_out_proj = lax.all_gather(out_proj, 'ctx', axis=0, tiled=True)  47.8 us
    ppermute x6, starting transfers between devices, passed_along(): return lax.ppermute(array, axis, pairs)  29.8 us
    ppermute x1, waiting for transfers between devices, on_device(): partner_normed = lax.ppermute(normed, 'groups', partners)  19.4 us
    pallas_call x1, Pallas kernels, coarse_attention(): pl.pallas_call(kernel, grid_spec=grid_spec, out_shape=jax.ShapeDtypeStruc...  16.6 us
    ppermute x5, starting transfers between devices, sent_to(): return lax.ppermute(array, ('groups', 'ctx'), pairs)  12.8 us
    ppermute x5, waiting for transfers between devices, sent_to(): return lax.ppermute(array, ('groups', 'ctx'), pairs)  12.6 us
    unnamed x22, local copies, waits for them, and re-layouts  10 us
  transfers between devices with their start and end apart: 14, of which 10 were waited for; matrix products, arithmetic and copies ran while one was open for 8% of the time, Pallas kernels for 0%

profile of v12, /device:TPU:20, one launch (start us, length us, event | category | flops | bytes accessed | tf_op | source)
XLA Modules:
  0.0 233.9 jit_solution(1864642955462135272)
XLA Ops:
  6.5 0.7 all-gather.3.cloned.1.call-update
  7.3 1.7 broadcast_select_fusion
  9.0 1.2 copy.18
  10.3 1.2 copy.19
  11.5 0.1 pad_maximum_fusion
  11.6 47.8 %all-gather.3.cloned.1.call-done = bf16[1024,2048]{1,0:T(8,128)(2,1)} async-done(((bf16[64,2048]{1,0:T(8,128)(2,1)}), bf16[1024,2048]{1,0:T(8,128)(2,1)}) %all-gather.3.cloned.1.call-update) | async-done | bytes 4194320 | tf_op jit(solution)/shard_map/all_gather | solution.py:157
  59.4 3.4 %collective-permute-start.4 = (bf16[2,256,1024]{1,2,0:T(8,128)(2,1)S(1)}, bf16[2,256,1024]{1,2,0:T(8,128)(2,1)}, u32[]{:S(2)}, u32[]{:S(2)}) collective-permute-start(bf16[2,256,1024]{1,2,0:T(8,128)(2,1)S(1)} %pad_maximum_fusion), channel_id=1, source_target_pairs={{0,2},{1,3},{2,4},{3,5},{4,6},{5,7},{6,8},{7,9},{8,10},{9,11},{10,... | collective-permute-start | bytes 3145736 | tf_op jit(solution)/shard_map/ppermute | solution.py:23
  62.8 1.9 collective-permute-start.5
  64.8 2.6 %collective-permute-start = (s32[1]{0:T(128)}, s32[1]{0:T(128)}, u32[]{:S(2)}, u32[]{:S(2)}) collective-permute-start(s32[1]{0:T(128)} %param.22), channel_id=1, source_target_pairs={{0,1},{1,2},{2,3},{3,4},{4,5},{5,6},{6,7},{7,8},{8,9},{9,10},{10,1... | collective-permute-start | bytes 20 | tf_op jit(solution)/shard_map/ppermute | solution.py:23
  68.0 0.2 fusion.10
  68.2 43.7 %collective-permute-done = s32[1]{0:T(128)} collective-permute-done((s32[1]{0:T(128)}, s32[1]{0:T(128)}, u32[]{:S(2)}, u32[]{:S(2)}) %collective-permute-start) | collective-permute-done | bytes 36 | tf_op jit(solution)/shard_map/ppermute | solution.py:23
  112.6 16.8 %collective-permute-start.1 = (s32[1]{0:T(128)}, s32[1]{0:T(128)}, u32[]{:S(2)}, u32[]{:S(2)}) collective-permute-start(s32[1]{0:T(128)} %add.53), channel_id=1, source_target_pairs={{0,2},{1,3},{2,4},{3,5},{4,6},{5,7},{6,8},{7,9},{8,10},{9,11},{10,... | collective-permute-start | bytes 20 | tf_op jit(solution)/shard_map/ppermute | solution.py:23
  129.5 0.2 collective-permute-done.1
  130.3 3.8 %collective-permute-start.2 = (s32[1]{0:T(128)}, s32[1]{0:T(128)}, u32[]{:S(2)}, u32[]{:S(2)}) collective-permute-start(s32[1]{0:T(128)} %add.54), channel_id=1, source_target_pairs={{0,4},{1,5},{2,6},{3,7},{4,8},{5,9},{6,10},{7,11},{8,12},{9,13},{1... | collective-permute-start | bytes 20 | tf_op jit(solution)/shard_map/ppermute | solution.py:23
  134.1 1.6 collective-permute-done.2
  136.5 1.3 collective-permute-start.3
  137.8 5.0 %collective-permute-done.3 = s32[1]{0:T(128)} collective-permute-done((s32[1]{0:T(128)}, s32[1]{0:T(128)}, u32[]{:S(2)}, u32[]{:S(2)}) %collective-permute-start.3) | collective-permute-done | bytes 36 | tf_op jit(solution)/shard_map/ppermute | solution.py:23
  143.5 1.3 constant_dynamic-update-slice_fusion.2
  144.9 0.2 fusion.16
  145.2 1.0 fusion.11
  146.2 3.1 %fusion.17 = (f32[8,256]{1,0:T(8,128)S(1)}, f32[8,256,768]{1,2,0:T(8,128)S(1)}) fusion(f32[8,768,256]{2,1,0:T(8,128)S(1)} %fusion.11, pred[256,768]{0,1:T(8,128)(4,1)S(1)} %fusion.10), kind=kOutput, calls=%fused_computation.40 | output fusion | flops 9437951 | bytes 12787712 | tf_op jit(solution)/shard_map/sub | solution.py:63
  149.3 0.6 fusion.6
  149.9 1.5 copy-done.1
  151.5 0.3 copy-done.2
  151.8 1.4 multiply_reduce_fusion
  153.2 0.2 multiply_convert_fusion
  153.4 1.5 collective-permute-start.8
  155.0 19.4 %collective-permute-done.8 = bf16[256,2048]{1,0:T(8,128)(2,1)S(1)} collective-permute-done((bf16[256,2048]{1,0:T(8,128)(2,1)S(1)}, bf16[256,2048]{1,0:T(8,128)(2,1)S(1)}, u32[]{:S(2)}, u32[]{:S(2)}) %collective-permute-start.8) | collective-permute-done | bytes 1048608 | tf_op jit(solution)/shard_map/ppermute | solution.py:191
  174.3 3.4 %convolution_convert_fusion = bf16[256,1024]{1,0:T(8,128)(2,1)S(1)} fusion(bf16[256,2048]{1,0:T(8,128)(2,1)S(1)} %collective-permute-done.8, bf16[2048,1024]{1,0:T(8,128)(2,1)} %all-gather.5.cloned.1.call-done), kind=kOutput, calls=%fused_computation.13 | convolution fusion | flops 1074003968 | bytes 5767168 | tf_op jit(solution)/shard_map/dot_general | solution.py:79
  177.8 1.5 collective-permute-start.9
  179.3 1.3 convolution_convert_fusion.1
  180.6 1.9 collective-permute-start.6
  182.5 3.6 %collective-permute-start.7 = (bf16[256,1024]{1,0:T(8,128)(2,1)S(1)}, bf16[256,1024]{1,0:T(8,128)(2,1)S(1)}, u32[]{:S(2)}, u32[]{:S(2)}) collective-permute-start(bf16[256,1024]{1,0:T(8,128)(2,1)S(1)} %convolution_convert_fusion.1), channel_id=1, source_target_pairs={{1,0},{2,1},{3,2},{4,3},{5,4},{6,5},{7,6},{8,7},{9,8},{10,9},{11,1... | collective-permute-start | bytes 1572872 | tf_op jit(solution)/shard_map/ppermute | solution.py:47
  186.2 0.8 collective-permute-done.9
  187.0 1.9 collective-permute-start.10
  189.0 0.1 copy.17
  189.1 0.7 concatenate.10.prm
  189.8 3.8 %collective-permute-start.11 = (bf16[256,1024]{1,0:T(8,128)(2,1)S(1)}, bf16[256,1024]{1,0:T(8,128)(2,1)S(1)}, u32[]{:S(2)}, u32[]{:S(2)}) collective-permute-start(bf16[256,1024]{1,0:T(8,128)(2,1)S(1)} %collective-permute-done.9), channel_id=1, source_target_pairs={{1,0},{2,1},{3,2},{4,3},{5,4},{6,5},{7,6},{8,7},{9,8},{10,9},{11,1... | collective-permute-start | bytes 1572872 | tf_op jit(solution)/shard_map/ppermute | solution.py:47
  193.6 3.1 %collective-permute-done.6 = bf16[256,1024]{1,0:T(8,128)(2,1)S(1)} collective-permute-done((bf16[256,1024]{1,0:T(8,128)(2,1)S(1)}, bf16[256,1024]{1,0:T(8,128)(2,1)S(1)}, u32[]{:S(2)}, u32[]{:S(2)}) %collective-permute-start.6) | collective-permute-done | bytes 524320 | tf_op jit(solution)/shard_map/ppermute | solution.py:47
  196.7 0.8 constant_dynamic-update-slice_fusion.8
  197.6 0.8 constant_dynamic-update-slice_fusion.7
  198.4 4.2 %collective-permute-done.7 = bf16[256,1024]{1,0:T(8,128)(2,1)S(1)} collective-permute-done((bf16[256,1024]{1,0:T(8,128)(2,1)S(1)}, bf16[256,1024]{1,0:T(8,128)(2,1)S(1)}, u32[]{:S(2)}, u32[]{:S(2)}) %collective-permute-start.7) | collective-permute-done | bytes 524320 | tf_op jit(solution)/shard_map/ppermute | solution.py:47
  202.6 0.9 constant_dynamic-update-slice_fusion.6
  203.5 4.5 %collective-permute-done.10 = bf16[256,1024]{1,0:T(8,128)(2,1)S(1)} collective-permute-done((bf16[256,1024]{1,0:T(8,128)(2,1)S(1)}, bf16[256,1024]{1,0:T(8,128)(2,1)S(1)}, u32[]{:S(2)}, u32[]{:S(2)}) %collective-permute-start.10) | collective-permute-done | bytes 524320 | tf_op jit(solution)/shard_map/ppermute | solution.py:47
  208.0 0.8 constant_dynamic-update-slice_fusion.5
  208.8 0.8 constant_dynamic-update-slice_fusion.4
  209.7 0.8 constant_dynamic-update-slice_fusion.3
  210.5 16.6 %shard_map.118 = bf16[1024,1024]{1,0:T(8,128)(2,1)} custom-call(s32[12]{0:T(128)} %concatenate.10.prm, f32[8]{0:T(128)} %slopes_ref.1, bf16[1024,1024]{1,0:T(8,128)(2,1)} %q_ref.1, bf16[2,768,1024]{2,1,0:T(8,128)(2,1)} %bitcast.9.k_ref.v_ref, bf16[2,768,1024]{2,1,0:T(8,128)(2,1)} %bitcast.9.k_ref.v_ref), custom_call_target="tpu_custom_call" | custom-call | tf_op jit(solution)/shard_map/pallas_call | solution.py:132
  (23 shorter events, 0.3 us)
Async XLA Ops:
  6.5 138.6 %copy-start = (bf16[256,1024]{1,0:T(8,128)(2,1)S(1)}, bf16[256,1024]{1,0:T(8,128)(2,1)}, u32[]{:S(2)}) copy-start(bf16[256,1024]{1,0:T(8,128)(2,1)} %param.12) | copy-start | bytes 1572868
  6.5 52.9 %all-gather.3.cloned.1.call-start = ((), (), s32[]{:S(2)}) async-start(), calls=%async_computation | async-start | bytes 4456448 | tf_op jit(solution)/shard_map/all_gather | solution.py:157
  7.3 147.7 %all-gather.5.cloned.1.call-start = ((), (), s32[]{:S(2)}) async-start(), calls=%async_computation.1 | async-start | bytes 4456448 | tf_op jit(solution)/shard_map/all_gather | solution.py:169
  59.4 84.0 %collective-permute-start.4 = (bf16[2,256,1024]{1,2,0:T(8,128)(2,1)S(1)}, bf16[2,256,1024]{1,2,0:T(8,128)(2,1)}, u32[]{:S(2)}, u32[]{:S(2)}) collective-permute-start(bf16[2,256,1024]{1,2,0:T(8,128)(2,1)S(1)} %pad_maximum_fusion), channel_id=1, source_target_pairs={{0,2},{1,3},{2,4},{3,5},{4,6},{5,7},{6,8},{7,9},{8,10},{9,11},{10,... | collective-permute-start | bytes 3145736 | tf_op jit(solution)/shard_map/ppermute | solution.py:23
  62.8 81.9 %collective-permute-start.5 = (bf16[2,256,1024]{1,2,0:T(8,128)(2,1)S(1)}, bf16[2,256,1024]{1,2,0:T(8,128)(2,1)S(1)}, u32[]{:S(2)}, u32[]{:S(2)}) collective-permute-start(bf16[2,256,1024]{1,2,0:T(8,128)(2,1)S(1)} %pad_maximum_fusion), channel_id=1, source_target_pairs={{0,1},{1,2},{2,3},{3,4},{4,5},{5,6},{6,7},{7,8},{8,9},{9,10},{10,1... | collective-permute-start | bytes 3145736 | tf_op jit(solution)/shard_map/ppermute | solution.py:23
  64.8 47.2 %collective-permute-start = (s32[1]{0:T(128)}, s32[1]{0:T(128)}, u32[]{:S(2)}, u32[]{:S(2)}) collective-permute-start(s32[1]{0:T(128)} %param.22), channel_id=1, source_target_pairs={{0,1},{1,2},{2,3},{3,4},{4,5},{5,6},{6,7},{7,8},{8,9},{9,10},{10,1... | collective-permute-start | bytes 20 | tf_op jit(solution)/shard_map/ppermute | solution.py:23
  112.6 17.0 %collective-permute-start.1 = (s32[1]{0:T(128)}, s32[1]{0:T(128)}, u32[]{:S(2)}, u32[]{:S(2)}) collective-permute-start(s32[1]{0:T(128)} %add.53), channel_id=1, source_target_pairs={{0,2},{1,3},{2,4},{3,5},{4,6},{5,7},{6,8},{7,9},{8,10},{9,11},{10,... | collective-permute-start | bytes 20 | tf_op jit(solution)/shard_map/ppermute | solution.py:23
  130.3 5.4 %collective-permute-start.2 = (s32[1]{0:T(128)}, s32[1]{0:T(128)}, u32[]{:S(2)}, u32[]{:S(2)}) collective-permute-start(s32[1]{0:T(128)} %add.54), channel_id=1, source_target_pairs={{0,4},{1,5},{2,6},{3,7},{4,8},{5,9},{6,10},{7,11},{8,12},{9,13},{1... | collective-permute-start | bytes 20 | tf_op jit(solution)/shard_map/ppermute | solution.py:23
  136.5 6.3 %collective-permute-start.3 = (s32[1]{0:T(128)}, s32[1]{0:T(128)}, u32[]{:S(2)}, u32[]{:S(2)}) collective-permute-start(s32[1]{0:T(128)} %add.55), channel_id=1, source_target_pairs={{0,8},{1,9},{2,10},{3,11},{4,12},{5,13},{6,14},{7,15},{16,24},{17,... | collective-permute-start | bytes 20 | tf_op jit(solution)/shard_map/ppermute | solution.py:23
  149.3 2.2 copy-start.1
  149.3 2.5 %copy-start.2 = (bf16[256,2048]{1,0:T(8,128)(2,1)S(1)}, bf16[256,2048]{1,0:T(8,128)(2,1)}, u32[]{:S(2)}) copy-start(bf16[256,2048]{1,0:T(8,128)(2,1)} %param.15) | copy-start | bytes 3145732
  151.8 1.4 copy-start.3
  153.4 20.9 %collective-permute-start.8 = (bf16[256,2048]{1,0:T(8,128)(2,1)S(1)}, bf16[256,2048]{1,0:T(8,128)(2,1)S(1)}, u32[]{:S(2)}, u32[]{:S(2)}) collective-permute-start(bf16[256,2048]{1,0:T(8,128)(2,1)S(1)} %multiply_convert_fusion), channel_id=1, source_target_pairs={{0,16},{16,0},{1,17},{17,1},{2,18},{18,2},{3,19},{19,3},{4,20},{20... | collective-permute-start | bytes 3145736 | tf_op jit(solution)/shard_map/ppermute | solution.py:191
  155.0 24.4 %copy-start.5 = (bf16[2048,1024]{1,0:T(8,128)(2,1)S(1)}, bf16[2048,1024]{1,0:T(8,128)(2,1)}, u32[]{:S(2)}) copy-start(bf16[2048,1024]{1,0:T(8,128)(2,1)} %all-gather.5.cloned.1.call-done) | copy-start | bytes 12582916
  177.8 11.2 %copy-start.4 = (s32[4,2]{0,1:T(2,128)S(1)}, s32[4,2]{0,1:T(2,128)}, u32[]{:S(2)}) copy-start(s32[4,2]{0,1:T(2,128)} %param.23) | copy-start | bytes 100
  177.8 9.2 %collective-permute-start.9 = (bf16[256,1024]{1,0:T(8,128)(2,1)S(1)}, bf16[256,1024]{1,0:T(8,128)(2,1)S(1)}, u32[]{:S(2)}, u32[]{:S(2)}) collective-permute-start(bf16[256,1024]{1,0:T(8,128)(2,1)S(1)} %convolution_convert_fusion), channel_id=1, source_target_pairs={{0,16},{1,17},{2,18},{3,19},{4,20},{5,21},{6,22},{7,23},{8,24},{9,... | collective-permute-start | bytes 1572872 | tf_op jit(solution)/shard_map/ppermute | solution.py:47
  180.6 16.1 %collective-permute-start.6 = (bf16[256,1024]{1,0:T(8,128)(2,1)S(1)}, bf16[256,1024]{1,0:T(8,128)(2,1)S(1)}, u32[]{:S(2)}, u32[]{:S(2)}) collective-permute-start(bf16[256,1024]{1,0:T(8,128)(2,1)S(1)} %convolution_convert_fusion.1), channel_id=1, source_target_pairs={{0,1},{1,2},{2,3},{3,4},{4,5},{5,6},{6,7},{7,8},{8,9},{9,10},{10,1... | collective-permute-start | bytes 1572872 | tf_op jit(solution)/shard_map/ppermute | solution.py:47
  182.5 20.1 %collective-permute-start.7 = (bf16[256,1024]{1,0:T(8,128)(2,1)S(1)}, bf16[256,1024]{1,0:T(8,128)(2,1)S(1)}, u32[]{:S(2)}, u32[]{:S(2)}) collective-permute-start(bf16[256,1024]{1,0:T(8,128)(2,1)S(1)} %convolution_convert_fusion.1), channel_id=1, source_target_pairs={{1,0},{2,1},{3,2},{4,3},{5,4},{6,5},{7,6},{8,7},{9,8},{10,9},{11,1... | collective-permute-start | bytes 1572872 | tf_op jit(solution)/shard_map/ppermute | solution.py:47
  187.0 20.9 %collective-permute-start.10 = (bf16[256,1024]{1,0:T(8,128)(2,1)S(1)}, bf16[256,1024]{1,0:T(8,128)(2,1)S(1)}, u32[]{:S(2)}, u32[]{:S(2)}) collective-permute-start(bf16[256,1024]{1,0:T(8,128)(2,1)S(1)} %collective-permute-done.9), channel_id=1, source_target_pairs={{0,1},{1,2},{2,3},{3,4},{4,5},{5,6},{6,7},{7,8},{8,9},{9,10},{10,1... | collective-permute-start | bytes 1572872 | tf_op jit(solution)/shard_map/ppermute | solution.py:47
  189.8 19.8 %collective-permute-start.11 = (bf16[256,1024]{1,0:T(8,128)(2,1)S(1)}, bf16[256,1024]{1,0:T(8,128)(2,1)S(1)}, u32[]{:S(2)}, u32[]{:S(2)}) collective-permute-start(bf16[256,1024]{1,0:T(8,128)(2,1)S(1)} %collective-permute-done.9), channel_id=1, source_target_pairs={{1,0},{2,1},{3,2},{4,3},{5,4},{6,5},{7,6},{8,7},{9,8},{10,9},{11,1... | collective-permute-start | bytes 1572872 | tf_op jit(solution)/shard_map/ppermute | solution.py:47
Sparse Core Ops, SparseCore 0:
  9.5 49.8 all-gather.2
  61.6 61.0 all-gather.4

commit v13 on v11

--- a/solution.py
+++ b/solution.py
@@ -191,6 +191,7 @@
         partner_part = contract_rows(partner_normed, gathered_proj).astype(jnp.bfloat16)
         partner_sum = sent_to(partner_part, 1, 0)
         other_pieces = [sent_to(partner_sum, 0, 1), partner_sum, sent_to(partner_sum, 0, -1)]
+        partner_part, normed = lax.optimization_barrier((partner_part, normed))
         own_sum = contract_rows(normed, gathered_proj).astype(jnp.bfloat16)
         mine_pieces = [sent_to(own_sum, 0, 1), own_sum, sent_to(own_sum, 0, -1)]
         near_pair = jnp.concatenate(mine_pieces + other_pieces, axis=0).reshape(

time: 188 us -> 188 us (level)
  no operation moved by 1% of the time
where the time goes in v13:
time: 188 us; the launch traced here: 187 us
  waiting for transfers between devices  81.8 us (44%)
  starting transfers between devices  45.6 us (24%)
  between operations  16.8 us (9%)
  Pallas kernels  16.6 us (9%)
  matrix products  9.97 us (5%)
  local copies, waits for them, and re-layouts  9.31 us (5%)
  other arithmetic  7.02 us (4%)
    ppermute x6, waiting for transfers between devices, passed_along(): return lax.ppermute(array, axis, pairs)  48.6 us
    ppermute x6, starting transfers between devices, passed_along(): return lax.ppermute(array, axis, pairs)  31.2 us
    pallas_call x1, Pallas kernels, coarse_attention(): pl.pallas_call(kernel, grid_spec=grid_spec, out_shape=jax.ShapeDtypeStruc...  16.6 us
    all_gather x1, waiting for transfers between devices, on_device(): gathered_proj = lax.all_gather(own_proj, 'ctx', axis=0, tiled=True)  15.4 us
    ppermute x5, starting transfers between devices, sent_to(): return lax.ppermute(array, ('groups', 'ctx'), pairs)  12.8 us
    ppermute x5, waiting for transfers between devices, sent_to(): return lax.ppermute(array, ('groups', 'ctx'), pairs)  12.6 us
    dot_general x3, matrix products, contract_rows(): return jnp.dot(left_side, weight_piece, preferred_element_type=jnp.float32)  8.3 us
    unnamed x18, local copies, waits for them, and re-layouts  7.49 us
  transfers between devices with their start and end apart: 14, of which 9 were waited for; matrix products, arithmetic and copies ran while one was open for 11% of the time, Pallas kernels for 0%

profile of v13, /device:TPU:20, one launch (start us, length us, event | category | flops | bytes accessed | tf_op | source)
XLA Modules:
  0.0 187.0 jit_solution(4990838487412964631)
XLA Ops:
  6.5 0.7 all-gather.3.cloned.1.call-update
  7.3 0.0 all-gather.5.cloned.1.call-start
  7.3 1.7 broadcast_select_fusion
  9.0 1.2 copy.18
  10.3 1.2 copy.19
  11.5 0.1 pad_maximum_fusion
  11.6 3.4 %collective-permute-start.4 = (bf16[2,256,1024]{1,2,0:T(8,128)(2,1)S(1)}, bf16[2,256,1024]{1,2,0:T(8,128)(2,1)}, u32[]{:S(2)}, u32[]{:S(2)}) collective-permute-start(bf16[2,256,1024]{1,2,0:T(8,128)(2,1)S(1)} %pad_maximum_fusion), channel_id=1, source_target_pairs={{0,2},{1,3},{2,4},{3,5},{4,6},{5,7},{6,8},{7,9},{8,10},{9,11},{10,... | collective-permute-start | bytes 3145736 | tf_op jit(solution)/shard_map/ppermute | solution.py:23
  15.1 1.9 %collective-permute-start.5 = (bf16[2,256,1024]{1,2,0:T(8,128)(2,1)S(1)}, bf16[2,256,1024]{1,2,0:T(8,128)(2,1)}, u32[]{:S(2)}, u32[]{:S(2)}) collective-permute-start(bf16[2,256,1024]{1,2,0:T(8,128)(2,1)S(1)} %pad_maximum_fusion), channel_id=1, source_target_pairs={{0,1},{1,2},{2,3},{3,4},{4,5},{5,6},{6,7},{7,8},{8,9},{9,10},{10,1... | collective-permute-start | bytes 3145736 | tf_op jit(solution)/shard_map/ppermute | solution.py:23
  17.0 3.5 %collective-permute-start = (s32[1]{0:T(128)}, s32[1]{0:T(128)}, u32[]{:S(2)}, u32[]{:S(2)}) collective-permute-start(s32[1]{0:T(128)} %param.22), channel_id=1, source_target_pairs={{0,1},{1,2},{2,3},{3,4},{4,5},{5,6},{6,7},{7,8},{8,9},{9,10},{10,1... | collective-permute-start | bytes 20 | tf_op jit(solution)/shard_map/ppermute | solution.py:23
  21.2 0.2 fusion.10
  21.5 42.4 %collective-permute-done = s32[1]{0:T(128)} collective-permute-done((s32[1]{0:T(128)}, s32[1]{0:T(128)}, u32[]{:S(2)}, u32[]{:S(2)}) %collective-permute-start) | collective-permute-done | bytes 36 | tf_op jit(solution)/shard_map/ppermute | solution.py:23
  64.4 16.8 %collective-permute-start.1 = (s32[1]{0:T(128)}, s32[1]{0:T(128)}, u32[]{:S(2)}, u32[]{:S(2)}) collective-permute-start(s32[1]{0:T(128)} %add.53), channel_id=1, source_target_pairs={{0,2},{1,3},{2,4},{3,5},{4,6},{5,7},{6,8},{7,9},{8,10},{9,11},{10,... | collective-permute-start | bytes 20 | tf_op jit(solution)/shard_map/ppermute | solution.py:23
  81.9 4.1 %collective-permute-start.2 = (s32[1]{0:T(128)}, s32[1]{0:T(128)}, u32[]{:S(2)}, u32[]{:S(2)}) collective-permute-start(s32[1]{0:T(128)} %add.54), channel_id=1, source_target_pairs={{0,4},{1,5},{2,6},{3,7},{4,8},{5,9},{6,10},{7,11},{8,12},{9,13},{1... | collective-permute-start | bytes 20 | tf_op jit(solution)/shard_map/ppermute | solution.py:23
  86.1 1.3 collective-permute-done.2
  88.0 1.3 collective-permute-start.3
  89.3 5.0 %collective-permute-done.3 = s32[1]{0:T(128)} collective-permute-done((s32[1]{0:T(128)}, s32[1]{0:T(128)}, u32[]{:S(2)}, u32[]{:S(2)}) %collective-permute-start.3) | collective-permute-done | bytes 36 | tf_op jit(solution)/shard_map/ppermute | solution.py:23
  94.9 1.7 maximum_maximum_fusion
  96.6 0.2 fusion.16
  96.8 1.0 fusion.11
  97.8 3.1 %fusion.17 = (f32[8,256]{1,0:T(8,128)S(1)}, f32[8,256,768]{1,2,0:T(8,128)S(1)}) fusion(f32[8,768,256]{2,1,0:T(8,128)S(1)} %fusion.11, pred[256,768]{0,1:T(8,128)(4,1)S(1)} %fusion.10), kind=kOutput, calls=%fused_computation.38 | output fusion | flops 9437951 | bytes 12787712 | tf_op jit(solution)/shard_map/sub | solution.py:63
  100.9 0.6 fusion.6
  101.6 0.7 copy-done.1
  102.3 3.6 %multiply_reduce_fusion = (f32[256]{0:T(256)S(1)}, f32[256,2048]{1,0:T(8,128)S(1)}) fusion(bf16[256,1024]{0,1:T(8,128)(2,1)S(1)} %bitcast.41, bf16[1024,2048]{1,0:T(8,128)(2,1)} %all-gather.3.cloned.1.call-done, bf16[256,2048]{1,0:T(8,128)(2,1)S(1)} %copy-done.1), kind=kOutput, calls=%fused_computation.12 | convolution fusion | flops 1075838720 | bytes 7865344 | tf_op jit(solution)/shard_map/dot_general | solution.py:79
  105.9 0.2 multiply_convert_fusion
  106.1 1.5 collective-permute-start.6
  107.7 15.4 %all-gather.5.cloned.1.call-done = bf16[2048,1024]{1,0:T(8,128)(2,1)} async-done(((bf16[128,1024]{1,0:T(8,128)(2,1)}), bf16[2048,1024]{1,0:T(8,128)(2,1)}) %all-gather.5.cloned.1.call-update) | async-done | bytes 4194320 | tf_op jit(solution)/shard_map/all_gather | solution.py:169
  123.1 4.3 %collective-permute-done.6 = bf16[256,2048]{1,0:T(8,128)(2,1)S(1)} collective-permute-done((bf16[256,2048]{1,0:T(8,128)(2,1)S(1)}, bf16[256,2048]{1,0:T(8,128)(2,1)S(1)}, u32[]{:S(2)}, u32[]{:S(2)}) %collective-permute-start.6) | collective-permute-done | bytes 1048608 | tf_op jit(solution)/shard_map/ppermute | solution.py:190
  127.4 3.4 %convolution_convert_fusion.1 = bf16[256,1024]{1,0:T(8,128)(2,1)S(1)} fusion(bf16[256,2048]{1,0:T(8,128)(2,1)S(1)} %collective-permute-done.6, bf16[2048,1024]{1,0:T(8,128)(2,1)} %all-gather.5.cloned.1.call-done), kind=kOutput, calls=%fused_computation.15 | convolution fusion | flops 1074003968 | bytes 5767168 | tf_op jit(solution)/shard_map/dot_general | solution.py:79
  130.9 1.5 collective-permute-start.9
  132.4 1.3 convolution_convert_fusion
  133.7 1.9 %collective-permute-start.7 = (bf16[256,1024]{1,0:T(8,128)(2,1)S(1)}, bf16[256,1024]{1,0:T(8,128)(2,1)S(1)}, u32[]{:S(2)}, u32[]{:S(2)}) collective-permute-start(bf16[256,1024]{1,0:T(8,128)(2,1)S(1)} %convolution_convert_fusion), channel_id=1, source_target_pairs={{0,1},{1,2},{2,3},{3,4},{4,5},{5,6},{6,7},{7,8},{8,9},{9,10},{10,1... | collective-permute-start | bytes 1572872 | tf_op jit(solution)/shard_map/ppermute | solution.py:47
  135.6 3.6 %collective-permute-start.8 = (bf16[256,1024]{1,0:T(8,128)(2,1)S(1)}, bf16[256,1024]{1,0:T(8,128)(2,1)S(1)}, u32[]{:S(2)}, u32[]{:S(2)}) collective-permute-start(bf16[256,1024]{1,0:T(8,128)(2,1)S(1)} %convolution_convert_fusion), channel_id=1, source_target_pairs={{1,0},{2,1},{3,2},{4,3},{5,4},{6,5},{7,6},{8,7},{9,8},{10,9},{11,1... | collective-permute-start | bytes 1572872 | tf_op jit(solution)/shard_map/ppermute | solution.py:47
  139.3 1.6 collective-permute-done.9
  140.8 1.9 %collective-permute-start.10 = (bf16[256,1024]{1,0:T(8,128)(2,1)S(1)}, bf16[256,1024]{1,0:T(8,128)(2,1)S(1)}, u32[]{:S(2)}, u32[]{:S(2)}) collective-permute-start(bf16[256,1024]{1,0:T(8,128)(2,1)S(1)} %collective-permute-done.9), channel_id=1, source_target_pairs={{0,1},{1,2},{2,3},{3,4},{4,5},{5,6},{6,7},{7,8},{8,9},{9,10},{10,1... | collective-permute-start | bytes 1572872 | tf_op jit(solution)/shard_map/ppermute | solution.py:47
  142.8 0.1 copy.17
  142.9 0.1 reshape.70
  143.0 0.7 concatenate.10.prm
  143.6 3.8 %collective-permute-start.11 = (bf16[256,1024]{1,0:T(8,128)(2,1)S(1)}, bf16[256,1024]{1,0:T(8,128)(2,1)S(1)}, u32[]{:S(2)}, u32[]{:S(2)}) collective-permute-start(bf16[256,1024]{1,0:T(8,128)(2,1)S(1)} %collective-permute-done.9), channel_id=1, source_target_pairs={{1,0},{2,1},{3,2},{4,3},{5,4},{6,5},{7,6},{8,7},{9,8},{10,9},{11,1... | collective-permute-start | bytes 1572872 | tf_op jit(solution)/shard_map/ppermute | solution.py:47
  147.5 2.4 %collective-permute-done.7 = bf16[256,1024]{1,0:T(8,128)(2,1)S(1)} collective-permute-done((bf16[256,1024]{1,0:T(8,128)(2,1)S(1)}, bf16[256,1024]{1,0:T(8,128)(2,1)S(1)}, u32[]{:S(2)}, u32[]{:S(2)}) %collective-permute-start.7) | collective-permute-done | bytes 524320 | tf_op jit(solution)/shard_map/ppermute | solution.py:47
  149.8 0.8 constant_dynamic-update-slice_fusion.5
  150.6 0.8 constant_dynamic-update-slice_fusion.4
  151.5 2.5 %collective-permute-done.8 = bf16[256,1024]{1,0:T(8,128)(2,1)S(1)} collective-permute-done((bf16[256,1024]{1,0:T(8,128)(2,1)S(1)}, bf16[256,1024]{1,0:T(8,128)(2,1)S(1)}, u32[]{:S(2)}, u32[]{:S(2)}) %collective-permute-start.8) | collective-permute-done | bytes 524320 | tf_op jit(solution)/shard_map/ppermute | solution.py:47
  154.0 0.9 constant_dynamic-update-slice_fusion.3
  154.8 6.2 %collective-permute-done.10 = bf16[256,1024]{1,0:T(8,128)(2,1)S(1)} collective-permute-done((bf16[256,1024]{1,0:T(8,128)(2,1)S(1)}, bf16[256,1024]{1,0:T(8,128)(2,1)S(1)}, u32[]{:S(2)}, u32[]{:S(2)}) %collective-permute-start.10) | collective-permute-done | bytes 524320 | tf_op jit(solution)/shard_map/ppermute | solution.py:47
  161.1 0.9 constant_dynamic-update-slice_fusion.2
  161.9 0.8 constant_dynamic-update-slice_fusion.1
  162.8 0.8 constant_dynamic-update-slice_fusion
  163.6 16.6 %shard_map.118 = bf16[1024,1024]{1,0:T(8,128)(2,1)} custom-call(s32[12]{0:T(128)} %concatenate.10.prm, f32[8]{0:T(128)} %slopes_ref.1, bf16[1024,1024]{1,0:T(8,128)(2,1)} %q_ref.1, bf16[2,768,1024]{2,1,0:T(8,128)(2,1)} %bitcast.9.k_ref.v_ref, bf16[2,768,1024]{2,1,0:T(8,128)(2,1)} %bitcast.9.k_ref.v_ref), custom_call_target="tpu_custom_call" | custom-call | tf_op jit(solution)/shard_map/pallas_call | solution.py:132
  (19 shorter events, 0.1 us)
Async XLA Ops:
  6.5 90.3 %copy-start = (bf16[256,1024]{1,0:T(8,128)(2,1)S(1)}, bf16[256,1024]{1,0:T(8,128)(2,1)}, u32[]{:S(2)}) copy-start(bf16[256,1024]{1,0:T(8,128)(2,1)} %param.12) | copy-start | bytes 1572868
  6.5 95.1 %all-gather.3.cloned.1.call-start = ((), (), s32[]{:S(2)}) async-start(), calls=%async_computation | async-start | bytes 4456448 | tf_op jit(solution)/shard_map/all_gather | solution.py:157
  7.3 115.8 %all-gather.5.cloned.1.call-start = ((), (), s32[]{:S(2)}) async-start(), calls=%async_computation.1 | async-start | bytes 4456448 | tf_op jit(solution)/shard_map/all_gather | solution.py:169
  11.6 83.3 %collective-permute-start.4 = (bf16[2,256,1024]{1,2,0:T(8,128)(2,1)S(1)}, bf16[2,256,1024]{1,2,0:T(8,128)(2,1)}, u32[]{:S(2)}, u32[]{:S(2)}) collective-permute-start(bf16[2,256,1024]{1,2,0:T(8,128)(2,1)S(1)} %pad_maximum_fusion), channel_id=1, source_target_pairs={{0,2},{1,3},{2,4},{3,5},{4,6},{5,7},{6,8},{7,9},{8,10},{9,11},{10,... | collective-permute-start | bytes 3145736 | tf_op jit(solution)/shard_map/ppermute | solution.py:23
  15.1 79.8 %collective-permute-start.5 = (bf16[2,256,1024]{1,2,0:T(8,128)(2,1)S(1)}, bf16[2,256,1024]{1,2,0:T(8,128)(2,1)}, u32[]{:S(2)}, u32[]{:S(2)}) collective-permute-start(bf16[2,256,1024]{1,2,0:T(8,128)(2,1)S(1)} %pad_maximum_fusion), channel_id=1, source_target_pairs={{0,1},{1,2},{2,3},{3,4},{4,5},{5,6},{6,7},{7,8},{8,9},{9,10},{10,1... | collective-permute-start | bytes 3145736 | tf_op jit(solution)/shard_map/ppermute | solution.py:23
  17.0 46.8 %collective-permute-start = (s32[1]{0:T(128)}, s32[1]{0:T(128)}, u32[]{:S(2)}, u32[]{:S(2)}) collective-permute-start(s32[1]{0:T(128)} %param.22), channel_id=1, source_target_pairs={{0,1},{1,2},{2,3},{3,4},{4,5},{5,6},{6,7},{7,8},{8,9},{9,10},{10,1... | collective-permute-start | bytes 20 | tf_op jit(solution)/shard_map/ppermute | solution.py:23
  64.4 16.8 %collective-permute-start.1 = (s32[1]{0:T(128)}, s32[1]{0:T(128)}, u32[]{:S(2)}, u32[]{:S(2)}) collective-permute-start(s32[1]{0:T(128)} %add.53), channel_id=1, source_target_pairs={{0,2},{1,3},{2,4},{3,5},{4,6},{5,7},{6,8},{7,9},{8,10},{9,11},{10,... | collective-permute-start | bytes 20 | tf_op jit(solution)/shard_map/ppermute | solution.py:23
  81.9 5.4 %collective-permute-start.2 = (s32[1]{0:T(128)}, s32[1]{0:T(128)}, u32[]{:S(2)}, u32[]{:S(2)}) collective-permute-start(s32[1]{0:T(128)} %add.54), channel_id=1, source_target_pairs={{0,4},{1,5},{2,6},{3,7},{4,8},{5,9},{6,10},{7,11},{8,12},{9,13},{1... | collective-permute-start | bytes 20 | tf_op jit(solution)/shard_map/ppermute | solution.py:23
  88.0 6.3 %collective-permute-start.3 = (s32[1]{0:T(128)}, s32[1]{0:T(128)}, u32[]{:S(2)}, u32[]{:S(2)}) collective-permute-start(s32[1]{0:T(128)} %add.55), channel_id=1, source_target_pairs={{0,8},{1,9},{2,10},{3,11},{4,12},{5,13},{6,14},{7,15},{16,24},{17,... | collective-permute-start | bytes 20 | tf_op jit(solution)/shard_map/ppermute | solution.py:23
  100.9 1.4 copy-start.1
  101.6 4.3 %copy-start.2 = (f32[2048]{0:T(1024)S(1)}, f32[2048]{0:T(1024)}, u32[]{:S(2)}) copy-start(f32[2048]{0:T(1024)} %param.17) | copy-start | bytes 24580
  106.1 21.3 %collective-permute-start.6 = (bf16[256,2048]{1,0:T(8,128)(2,1)S(1)}, bf16[256,2048]{1,0:T(8,128)(2,1)S(1)}, u32[]{:S(2)}, u32[]{:S(2)}) collective-permute-start(bf16[256,2048]{1,0:T(8,128)(2,1)S(1)} %multiply_convert_fusion), channel_id=1, source_target_pairs={{0,16},{16,0},{1,17},{17,1},{2,18},{18,2},{3,19},{19,3},{4,20},{20... | collective-permute-start | bytes 3145736 | tf_op jit(solution)/shard_map/ppermute | solution.py:190
  123.1 9.3 %copy-start.4 = (bf16[2048,1024]{1,0:T(8,128)(2,1)S(1)}, bf16[2048,1024]{1,0:T(8,128)(2,1)}, u32[]{:S(2)}) copy-start(bf16[2048,1024]{1,0:T(8,128)(2,1)} %all-gather.5.cloned.1.call-done) | copy-start | bytes 12582916
  130.8 11.9 %copy-start.3 = (s32[4,2]{0,1:T(2,128)S(1)}, s32[4,2]{0,1:T(2,128)}, u32[]{:S(2)}) copy-start(s32[4,2]{0,1:T(2,128)} %param.23) | copy-start | bytes 100
  130.9 10.0 %collective-permute-start.9 = (bf16[256,1024]{1,0:T(8,128)(2,1)S(1)}, bf16[256,1024]{1,0:T(8,128)(2,1)S(1)}, u32[]{:S(2)}, u32[]{:S(2)}) collective-permute-start(bf16[256,1024]{1,0:T(8,128)(2,1)S(1)} %convolution_convert_fusion.1), channel_id=1, source_target_pairs={{0,16},{1,17},{2,18},{3,19},{4,20},{5,21},{6,22},{7,23},{8,24},{9,... | collective-permute-start | bytes 1572872 | tf_op jit(solution)/shard_map/ppermute | solution.py:47
  133.7 16.1 %collective-permute-start.7 = (bf16[256,1024]{1,0:T(8,128)(2,1)S(1)}, bf16[256,1024]{1,0:T(8,128)(2,1)S(1)}, u32[]{:S(2)}, u32[]{:S(2)}) collective-permute-start(bf16[256,1024]{1,0:T(8,128)(2,1)S(1)} %convolution_convert_fusion), channel_id=1, source_target_pairs={{0,1},{1,2},{2,3},{3,4},{4,5},{5,6},{6,7},{7,8},{8,9},{9,10},{10,1... | collective-permute-start | bytes 1572872 | tf_op jit(solution)/shard_map/ppermute | solution.py:47
  135.6 18.4 %collective-permute-start.8 = (bf16[256,1024]{1,0:T(8,128)(2,1)S(1)}, bf16[256,1024]{1,0:T(8,128)(2,1)S(1)}, u32[]{:S(2)}, u32[]{:S(2)}) collective-permute-start(bf16[256,1024]{1,0:T(8,128)(2,1)S(1)} %convolution_convert_fusion), channel_id=1, source_target_pairs={{1,0},{2,1},{3,2},{4,3},{5,4},{6,5},{7,6},{8,7},{9,8},{10,9},{11,1... | collective-permute-start | bytes 1572872 | tf_op jit(solution)/shard_map/ppermute | solution.py:47
  140.8 20.2 %collective-permute-start.10 = (bf16[256,1024]{1,0:T(8,128)(2,1)S(1)}, bf16[256,1024]{1,0:T(8,128)(2,1)S(1)}, u32[]{:S(2)}, u32[]{:S(2)}) collective-permute-start(bf16[256,1024]{1,0:T(8,128)(2,1)S(1)} %collective-permute-done.9), channel_id=1, source_target_pairs={{0,1},{1,2},{2,3},{3,4},{4,5},{5,6},{6,7},{7,8},{8,9},{9,10},{10,1... | collective-permute-start | bytes 1572872 | tf_op jit(solution)/shard_map/ppermute | solution.py:47
  143.6 19.1 %collective-permute-start.11 = (bf16[256,1024]{1,0:T(8,128)(2,1)S(1)}, bf16[256,1024]{1,0:T(8,128)(2,1)S(1)}, u32[]{:S(2)}, u32[]{:S(2)}) collective-permute-start(bf16[256,1024]{1,0:T(8,128)(2,1)S(1)} %collective-permute-done.9), channel_id=1, source_target_pairs={{1,0},{2,1},{3,2},{4,3},{5,4},{6,5},{7,6},{8,7},{9,8},{10,9},{11,1... | collective-permute-start | bytes 1572872 | tf_op jit(solution)/shard_map/ppermute | solution.py:47
Sparse Core Ops, SparseCore 0:
  9.5 62.1 all-gather.2
  73.9 49.1 all-gather.4

commit v14 on v11

--- a/solution.py
+++ b/solution.py
@@ -173,8 +173,10 @@
     own_pair = jnp.stack([sem_keys, sem_values])
     reach_shards = (W - 1 + rows_here - 1) // rows_here
     earlier = []
+    relayed = own_pair
     for distance in range(1, reach_shards + 1):
-        earlier.insert(0, passed_along(own_pair, "ctx", distance))
+        relayed = passed_along(relayed, "ctx", 1)
+        earlier.insert(0, relayed)
     window_pair = jnp.concatenate(earlier + [own_pair], axis=1)
     query_pos = jnp.arange(rows_here, dtype=jnp.int32)
     key_pos = jnp.arange(window_pair.shape[1], dtype=jnp.int32)

time: 188 us -> 181 us (0.963)
  waiting for transfers between devices: 81.8 us -> 70.8 us
  starting transfers between devices: 45.6 us -> 49.2 us
    ppermute x6, waiting for transfers between devices: 48.6 us -> 38.3 us  [passed_along(): return lax.ppermute(array, axis, pairs)]
    ppermute x1, waiting for transfers between devices: 4.31 us -> 0.24 us  [on_device(): partner_normed = lax.ppermute(normed, 'groups', partners)]
    ppermute x6, starting transfers between devices: 31.2 us -> 34.9 us  [passed_along(): return lax.ppermute(array, axis, pairs)]
    all_gather x1, waiting for transfers between devices: 15.4 us -> 18.9 us  [on_device(): gathered_proj = lax.all_gather(own_proj, 'ctx', axis=0, tiled=True)]
  transfers between devices with their start and end apart: 14 -> 14, of which waited for: 9 -> 8; matrix products, arithmetic and copies ran while one was open for 11% -> 12% of each run, Pallas kernels for 0% -> 0%
where the time goes in v14:
time: 181 us; the launch traced here: 179 us
  waiting for transfers between devices  70.8 us (39%)
  starting transfers between devices  49.2 us (27%)
  between operations  16.8 us (9%)
  Pallas kernels  16.6 us (9%)
  matrix products  10.1 us (6%)
  local copies, waits for them, and re-layouts  9.18 us (5%)
  other arithmetic  6.7 us (4%)
    ppermute x6, waiting for transfers between devices, passed_along(): return lax.ppermute(array, axis, pairs)  38.3 us
    ppermute x6, starting transfers between devices, passed_along(): return lax.ppermute(array, axis, pairs)  34.9 us
    all_gather x1, waiting for transfers between devices, on_device(): gathered_proj = lax.all_gather(own_proj, 'ctx', axis=0, tiled=True)  18.9 us
    pallas_call x1, Pallas kernels, coarse_attention(): pl.pallas_call(kernel, grid_spec=grid_spec, out_shape=jax.ShapeDtypeStruc...  16.6 us
    ppermute x5, starting transfers between devices, sent_to(): return lax.ppermute(array, ('groups', 'ctx'), pairs)  12.8 us
    ppermute x5, waiting for transfers between devices, sent_to(): return lax.ppermute(array, ('groups', 'ctx'), pairs)  12.6 us
    dot_general x3, matrix products, contract_rows(): return jnp.dot(left_side, weight_piece, preferred_element_type=jnp.float32)  8.44 us
    unnamed x18, local copies, waits for them, and re-layouts  7.36 us
  transfers between devices with their start and end apart: 14, of which 8 were waited for; matrix products, arithmetic and copies ran while one was open for 12% of the time, Pallas kernels for 0%

profile of v14, /device:TPU:20, one launch (start us, length us, event | category | flops | bytes accessed | tf_op | source)
XLA Modules:
  0.0 179.4 jit_solution(6537745838434984075)
XLA Ops:
  6.5 0.7 all-gather.3.cloned.1.call-update
  7.3 0.0 all-gather.5.cloned.1.call-start
  7.3 1.7 broadcast_select_fusion
  9.0 1.2 copy.18
  10.3 1.2 copy.19
  11.5 0.1 pad_maximum_fusion
  11.6 1.9 %collective-permute-start.4 = (bf16[2,256,1024]{1,2,0:T(8,128)(2,1)S(1)}, bf16[2,256,1024]{1,2,0:T(8,128)(2,1)S(1)}, u32[]{:S(2)}, u32[]{:S(2)}) collective-permute-start(bf16[2,256,1024]{1,2,0:T(8,128)(2,1)S(1)} %pad_maximum_fusion), channel_id=1, source_target_pairs={{0,1},{1,2},{2,3},{3,4},{4,5},{5,6},{6,7},{7,8},{8,9},{9,10},{10,1... | collective-permute-start | bytes 3145736 | tf_op jit(solution)/shard_map/ppermute | solution.py:23
  13.6 17.0 %collective-permute-done.4 = bf16[2,256,1024]{1,2,0:T(8,128)(2,1)S(1)} collective-permute-done((bf16[2,256,1024]{1,2,0:T(8,128)(2,1)S(1)}, bf16[2,256,1024]{1,2,0:T(8,128)(2,1)S(1)}, u32[]{:S(2)}, u32[]{:S(2)}) %collective-permute-start.4) | collective-permute-done | bytes 1048608 | tf_op jit(solution)/shard_map/ppermute | solution.py:23
  30.6 6.7 %collective-permute-start.5 = (bf16[2,256,1024]{1,2,0:T(8,128)(2,1)S(1)}, bf16[2,256,1024]{1,2,0:T(8,128)(2,1)}, u32[]{:S(2)}, u32[]{:S(2)}) collective-permute-start(bf16[2,256,1024]{1,2,0:T(8,128)(2,1)S(1)} %collective-permute-done.4), channel_id=1, source_target_pairs={{0,1},{1,2},{2,3},{3,4},{4,5},{5,6},{6,7},{7,8},{8,9},{9,10},{10,1... | collective-permute-start | bytes 3145736 | tf_op jit(solution)/shard_map/ppermute | solution.py:23
  37.2 5.3 %collective-permute-start = (s32[1]{0:T(128)}, s32[1]{0:T(128)}, u32[]{:S(2)}, u32[]{:S(2)}) collective-permute-start(s32[1]{0:T(128)} %param.22), channel_id=1, source_target_pairs={{0,1},{1,2},{2,3},{3,4},{4,5},{5,6},{6,7},{7,8},{8,9},{9,10},{10,1... | collective-permute-start | bytes 20 | tf_op jit(solution)/shard_map/ppermute | solution.py:23
  43.2 0.2 fusion.10
  43.5 14.6 %collective-permute-done = s32[1]{0:T(128)} collective-permute-done((s32[1]{0:T(128)}, s32[1]{0:T(128)}, u32[]{:S(2)}, u32[]{:S(2)}) %collective-permute-start) | collective-permute-done | bytes 36 | tf_op jit(solution)/shard_map/ppermute | solution.py:23
  58.7 15.6 %collective-permute-start.1 = (s32[1]{0:T(128)}, s32[1]{0:T(128)}, u32[]{:S(2)}, u32[]{:S(2)}) collective-permute-start(s32[1]{0:T(128)} %add.53), channel_id=1, source_target_pairs={{0,2},{1,3},{2,4},{3,5},{4,6},{5,7},{6,8},{7,9},{8,10},{9,11},{10,... | collective-permute-start | bytes 20 | tf_op jit(solution)/shard_map/ppermute | solution.py:23
  74.9 4.1 %collective-permute-start.2 = (s32[1]{0:T(128)}, s32[1]{0:T(128)}, u32[]{:S(2)}, u32[]{:S(2)}) collective-permute-start(s32[1]{0:T(128)} %add.54), channel_id=1, source_target_pairs={{0,4},{1,5},{2,6},{3,7},{4,8},{5,9},{6,10},{7,11},{8,12},{9,13},{1... | collective-permute-start | bytes 20 | tf_op jit(solution)/shard_map/ppermute | solution.py:23
  79.0 1.5 collective-permute-done.2
  81.2 1.3 collective-permute-start.3
  82.5 5.2 %collective-permute-done.3 = s32[1]{0:T(128)} collective-permute-done((s32[1]{0:T(128)}, s32[1]{0:T(128)}, u32[]{:S(2)}, u32[]{:S(2)}) %collective-permute-start.3) | collective-permute-done | bytes 36 | tf_op jit(solution)/shard_map/ppermute | solution.py:23
  88.3 1.3 maximum_maximum_fusion
  89.6 0.2 fusion.16
  89.8 1.0 fusion.11
  90.9 3.1 %fusion.17 = (f32[8,256]{1,0:T(8,128)S(1)}, f32[8,256,768]{1,2,0:T(8,128)S(1)}) fusion(f32[8,768,256]{2,1,0:T(8,128)S(1)} %fusion.11, pred[256,768]{0,1:T(8,128)(4,1)S(1)} %fusion.10), kind=kOutput, calls=%fused_computation.38 | output fusion | flops 9437951 | bytes 12787712 | tf_op jit(solution)/shard_map/sub | solution.py:63
  94.0 0.6 fusion.6
  94.6 0.0 all-gather.3.cloned.1.call-done
  94.7 0.5 copy-done.1
  95.2 3.6 %multiply_reduce_fusion = (f32[256]{0:T(256)S(1)}, f32[256,2048]{1,0:T(8,128)S(1)}) fusion(bf16[256,1024]{0,1:T(8,128)(2,1)S(1)} %bitcast.41, bf16[1024,2048]{1,0:T(8,128)(2,1)} %all-gather.3.cloned.1.call-done, bf16[256,2048]{1,0:T(8,128)(2,1)S(1)} %copy-done.1), kind=kOutput, calls=%fused_computation.12 | convolution fusion | flops 1075838720 | bytes 7865344 | tf_op jit(solution)/shard_map/dot_general | solution.py:79
  98.8 0.2 multiply_convert_fusion
  99.0 1.5 collective-permute-start.8
  100.6 18.9 %all-gather.5.cloned.1.call-done = bf16[2048,1024]{1,0:T(8,128)(2,1)} async-done(((bf16[128,1024]{1,0:T(8,128)(2,1)}), bf16[2048,1024]{1,0:T(8,128)(2,1)}) %all-gather.5.cloned.1.call-update) | async-done | bytes 4194320 | tf_op jit(solution)/shard_map/all_gather | solution.py:169
  119.4 0.2 collective-permute-done.8
  119.7 3.6 %convolution_convert_fusion = bf16[256,1024]{1,0:T(8,128)(2,1)S(1)} fusion(bf16[256,2048]{1,0:T(8,128)(2,1)S(1)} %collective-permute-done.8, bf16[2048,1024]{1,0:T(8,128)(2,1)} %all-gather.5.cloned.1.call-done), kind=kOutput, calls=%fused_computation.14 | convolution fusion | flops 1074003968 | bytes 5767168 | tf_op jit(solution)/shard_map/dot_general | solution.py:79
  123.3 1.5 collective-permute-start.9
  124.8 1.3 convolution_convert_fusion.1
  126.1 1.9 %collective-permute-start.6 = (bf16[256,1024]{1,0:T(8,128)(2,1)S(1)}, bf16[256,1024]{1,0:T(8,128)(2,1)S(1)}, u32[]{:S(2)}, u32[]{:S(2)}) collective-permute-start(bf16[256,1024]{1,0:T(8,128)(2,1)S(1)} %convolution_convert_fusion.1), channel_id=1, source_target_pairs={{0,1},{1,2},{2,3},{3,4},{4,5},{5,6},{6,7},{7,8},{8,9},{9,10},{10,1... | collective-permute-start | bytes 1572872 | tf_op jit(solution)/shard_map/ppermute | solution.py:47
  128.0 3.6 %collective-permute-start.7 = (bf16[256,1024]{1,0:T(8,128)(2,1)S(1)}, bf16[256,1024]{1,0:T(8,128)(2,1)S(1)}, u32[]{:S(2)}, u32[]{:S(2)}) collective-permute-start(bf16[256,1024]{1,0:T(8,128)(2,1)S(1)} %convolution_convert_fusion.1), channel_id=1, source_target_pairs={{1,0},{2,1},{3,2},{4,3},{5,4},{6,5},{7,6},{8,7},{9,8},{10,9},{11,1... | collective-permute-start | bytes 1572872 | tf_op jit(solution)/shard_map/ppermute | solution.py:47
  131.7 5.5 %collective-permute-done.9 = bf16[256,1024]{1,0:T(8,128)(2,1)S(1)} collective-permute-done((bf16[256,1024]{1,0:T(8,128)(2,1)S(1)}, bf16[256,1024]{1,0:T(8,128)(2,1)S(1)}, u32[]{:S(2)}, u32[]{:S(2)}) %collective-permute-start.9) | collective-permute-done | bytes 524320 | tf_op jit(solution)/shard_map/ppermute | solution.py:47
  137.2 1.9 %collective-permute-start.10 = (bf16[256,1024]{1,0:T(8,128)(2,1)S(1)}, bf16[256,1024]{1,0:T(8,128)(2,1)S(1)}, u32[]{:S(2)}, u32[]{:S(2)}) collective-permute-start(bf16[256,1024]{1,0:T(8,128)(2,1)S(1)} %collective-permute-done.9), channel_id=1, source_target_pairs={{0,1},{1,2},{2,3},{3,4},{4,5},{5,6},{6,7},{7,8},{8,9},{9,10},{10,1... | collective-permute-start | bytes 1572872 | tf_op jit(solution)/shard_map/ppermute | solution.py:47
  139.1 0.1 copy.17
  139.2 0.1 reshape.70
  139.3 0.7 concatenate.10.prm
  140.0 3.8 %collective-permute-start.11 = (bf16[256,1024]{1,0:T(8,128)(2,1)S(1)}, bf16[256,1024]{1,0:T(8,128)(2,1)S(1)}, u32[]{:S(2)}, u32[]{:S(2)}) collective-permute-start(bf16[256,1024]{1,0:T(8,128)(2,1)S(1)} %collective-permute-done.9), channel_id=1, source_target_pairs={{1,0},{2,1},{3,2},{4,3},{5,4},{6,5},{7,6},{8,7},{9,8},{10,9},{11,1... | collective-permute-start | bytes 1572872 | tf_op jit(solution)/shard_map/ppermute | solution.py:47
  143.8 0.8 constant_dynamic-update-slice_fusion.5
  144.6 0.8 constant_dynamic-update-slice_fusion.4
  145.5 0.9 constant_dynamic-update-slice_fusion.3
  146.3 7.1 %collective-permute-done.10 = bf16[256,1024]{1,0:T(8,128)(2,1)S(1)} collective-permute-done((bf16[256,1024]{1,0:T(8,128)(2,1)S(1)}, bf16[256,1024]{1,0:T(8,128)(2,1)S(1)}, u32[]{:S(2)}, u32[]{:S(2)}) %collective-permute-start.10) | collective-permute-done | bytes 524320 | tf_op jit(solution)/shard_map/ppermute | solution.py:47
  153.5 0.9 constant_dynamic-update-slice_fusion.2
  154.3 0.8 constant_dynamic-update-slice_fusion.1
  155.2 0.8 constant_dynamic-update-slice_fusion
  156.0 16.6 %shard_map.118 = bf16[1024,1024]{1,0:T(8,128)(2,1)} custom-call(s32[12]{0:T(128)} %concatenate.10.prm, f32[8]{0:T(128)} %slopes_ref.1, bf16[1024,1024]{1,0:T(8,128)(2,1)} %q_ref.1, bf16[2,768,1024]{2,1,0:T(8,128)(2,1)} %bitcast.9.k_ref.v_ref, bf16[2,768,1024]{2,1,0:T(8,128)(2,1)} %bitcast.9.k_ref.v_ref), custom_call_target="tpu_custom_call" | custom-call | tf_op jit(solution)/shard_map/pallas_call | solution.py:132
  (19 shorter events, 0.1 us)
Async XLA Ops:
  6.5 83.3 %copy-start = (bf16[256,1024]{1,0:T(8,128)(2,1)S(1)}, bf16[256,1024]{1,0:T(8,128)(2,1)}, u32[]{:S(2)}) copy-start(bf16[256,1024]{1,0:T(8,128)(2,1)} %param.12) | copy-start | bytes 1572868
  6.5 88.1 %all-gather.3.cloned.1.call-start = ((), (), s32[]{:S(2)}) async-start(), calls=%async_computation | async-start | bytes 4456448 | tf_op jit(solution)/shard_map/all_gather | solution.py:157
  7.3 112.2 %all-gather.5.cloned.1.call-start = ((), (), s32[]{:S(2)}) async-start(), calls=%async_computation.1 | async-start | bytes 4456448 | tf_op jit(solution)/shard_map/all_gather | solution.py:169
  11.6 18.9 %collective-permute-start.4 = (bf16[2,256,1024]{1,2,0:T(8,128)(2,1)S(1)}, bf16[2,256,1024]{1,2,0:T(8,128)(2,1)S(1)}, u32[]{:S(2)}, u32[]{:S(2)}) collective-permute-start(bf16[2,256,1024]{1,2,0:T(8,128)(2,1)S(1)} %pad_maximum_fusion), channel_id=1, source_target_pairs={{0,1},{1,2},{2,3},{3,4},{4,5},{5,6},{6,7},{7,8},{8,9},{9,10},{10,1... | collective-permute-start | bytes 3145736 | tf_op jit(solution)/shard_map/ppermute | solution.py:23
  30.6 57.7 %collective-permute-start.5 = (bf16[2,256,1024]{1,2,0:T(8,128)(2,1)S(1)}, bf16[2,256,1024]{1,2,0:T(8,128)(2,1)}, u32[]{:S(2)}, u32[]{:S(2)}) collective-permute-start(bf16[2,256,1024]{1,2,0:T(8,128)(2,1)S(1)} %collective-permute-done.4), channel_id=1, source_target_pairs={{0,1},{1,2},{2,3},{3,4},{4,5},{5,6},{6,7},{7,8},{8,9},{9,10},{10,1... | collective-permute-start | bytes 3145736 | tf_op jit(solution)/shard_map/ppermute | solution.py:23
  37.2 20.9 %collective-permute-start = (s32[1]{0:T(128)}, s32[1]{0:T(128)}, u32[]{:S(2)}, u32[]{:S(2)}) collective-permute-start(s32[1]{0:T(128)} %param.22), channel_id=1, source_target_pairs={{0,1},{1,2},{2,3},{3,4},{4,5},{5,6},{6,7},{7,8},{8,9},{9,10},{10,1... | collective-permute-start | bytes 20 | tf_op jit(solution)/shard_map/ppermute | solution.py:23
  58.7 15.6 %collective-permute-start.1 = (s32[1]{0:T(128)}, s32[1]{0:T(128)}, u32[]{:S(2)}, u32[]{:S(2)}) collective-permute-start(s32[1]{0:T(128)} %add.53), channel_id=1, source_target_pairs={{0,2},{1,3},{2,4},{3,5},{4,6},{5,7},{6,8},{7,9},{8,10},{9,11},{10,... | collective-permute-start | bytes 20 | tf_op jit(solution)/shard_map/ppermute | solution.py:23
  74.9 5.6 %collective-permute-start.2 = (s32[1]{0:T(128)}, s32[1]{0:T(128)}, u32[]{:S(2)}, u32[]{:S(2)}) collective-permute-start(s32[1]{0:T(128)} %add.54), channel_id=1, source_target_pairs={{0,4},{1,5},{2,6},{3,7},{4,8},{5,9},{6,10},{7,11},{8,12},{9,13},{1... | collective-permute-start | bytes 20 | tf_op jit(solution)/shard_map/ppermute | solution.py:23
  81.2 6.5 %collective-permute-start.3 = (s32[1]{0:T(128)}, s32[1]{0:T(128)}, u32[]{:S(2)}, u32[]{:S(2)}) collective-permute-start(s32[1]{0:T(128)} %add.55), channel_id=1, source_target_pairs={{0,8},{1,9},{2,10},{3,11},{4,12},{5,13},{6,14},{7,15},{16,24},{17,... | collective-permute-start | bytes 20 | tf_op jit(solution)/shard_map/ppermute | solution.py:23
  94.0 1.2 copy-start.1
  94.6 4.2 %copy-start.2 = (f32[2048]{0:T(1024)S(1)}, f32[2048]{0:T(1024)}, u32[]{:S(2)}) copy-start(f32[2048]{0:T(1024)} %param.17) | copy-start | bytes 24580
  99.0 20.6 %collective-permute-start.8 = (bf16[256,2048]{1,0:T(8,128)(2,1)S(1)}, bf16[256,2048]{1,0:T(8,128)(2,1)S(1)}, u32[]{:S(2)}, u32[]{:S(2)}) collective-permute-start(bf16[256,2048]{1,0:T(8,128)(2,1)S(1)} %multiply_convert_fusion), channel_id=1, source_target_pairs={{0,16},{16,0},{1,17},{17,1},{2,18},{18,2},{3,19},{19,3},{4,20},{20... | collective-permute-start | bytes 3145736 | tf_op jit(solution)/shard_map/ppermute | solution.py:192
  119.4 5.4 %copy-start.4 = (bf16[2048,1024]{1,0:T(8,128)(2,1)S(1)}, bf16[2048,1024]{1,0:T(8,128)(2,1)}, u32[]{:S(2)}) copy-start(bf16[2048,1024]{1,0:T(8,128)(2,1)} %all-gather.5.cloned.1.call-done) | copy-start | bytes 12582916
  123.3 15.8 %copy-start.3 = (s32[4,2]{0,1:T(2,128)S(1)}, s32[4,2]{0,1:T(2,128)}, u32[]{:S(2)}) copy-start(s32[4,2]{0,1:T(2,128)} %param.23) | copy-start | bytes 100
  123.3 13.9 %collective-permute-start.9 = (bf16[256,1024]{1,0:T(8,128)(2,1)S(1)}, bf16[256,1024]{1,0:T(8,128)(2,1)S(1)}, u32[]{:S(2)}, u32[]{:S(2)}) collective-permute-start(bf16[256,1024]{1,0:T(8,128)(2,1)S(1)} %convolution_convert_fusion), channel_id=1, source_target_pairs={{0,16},{1,17},{2,18},{3,19},{4,20},{5,21},{6,22},{7,23},{8,24},{9,... | collective-permute-start | bytes 1572872 | tf_op jit(solution)/shard_map/ppermute | solution.py:47
  126.1 17.7 %collective-permute-start.6 = (bf16[256,1024]{1,0:T(8,128)(2,1)S(1)}, bf16[256,1024]{1,0:T(8,128)(2,1)S(1)}, u32[]{:S(2)}, u32[]{:S(2)}) collective-permute-start(bf16[256,1024]{1,0:T(8,128)(2,1)S(1)} %convolution_convert_fusion.1), channel_id=1, source_target_pairs={{0,1},{1,2},{2,3},{3,4},{4,5},{5,6},{6,7},{7,8},{8,9},{9,10},{10,1... | collective-permute-start | bytes 1572872 | tf_op jit(solution)/shard_map/ppermute | solution.py:47
  128.0 17.4 %collective-permute-start.7 = (bf16[256,1024]{1,0:T(8,128)(2,1)S(1)}, bf16[256,1024]{1,0:T(8,128)(2,1)S(1)}, u32[]{:S(2)}, u32[]{:S(2)}) collective-permute-start(bf16[256,1024]{1,0:T(8,128)(2,1)S(1)} %convolution_convert_fusion.1), channel_id=1, source_target_pairs={{1,0},{2,1},{3,2},{4,3},{5,4},{6,5},{7,6},{8,7},{9,8},{10,9},{11,1... | collective-permute-start | bytes 1572872 | tf_op jit(solution)/shard_map/ppermute | solution.py:47
  137.2 16.3 %collective-permute-start.10 = (bf16[256,1024]{1,0:T(8,128)(2,1)S(1)}, bf16[256,1024]{1,0:T(8,128)(2,1)S(1)}, u32[]{:S(2)}, u32[]{:S(2)}) collective-permute-start(bf16[256,1024]{1,0:T(8,128)(2,1)S(1)} %collective-permute-done.9), channel_id=1, source_target_pairs={{0,1},{1,2},{2,3},{3,4},{4,5},{5,6},{6,7},{7,8},{8,9},{9,10},{10,1... | collective-permute-start | bytes 1572872 | tf_op jit(solution)/shard_map/ppermute | solution.py:47
  140.0 15.2 %collective-permute-start.11 = (bf16[256,1024]{1,0:T(8,128)(2,1)S(1)}, bf16[256,1024]{1,0:T(8,128)(2,1)S(1)}, u32[]{:S(2)}, u32[]{:S(2)}) collective-permute-start(bf16[256,1024]{1,0:T(8,128)(2,1)S(1)} %collective-permute-done.9), channel_id=1, source_target_pairs={{1,0},{2,1},{3,2},{4,3},{5,4},{6,5},{7,6},{8,7},{9,8},{10,9},{11,1... | collective-permute-start | bytes 1572872 | tf_op jit(solution)/shard_map/ppermute | solution.py:47
Sparse Core Ops, SparseCore 0:
  9.5 58.3 all-gather.2
  70.0 49.3 all-gather.4

commit v15 on v14

--- a/solution.py
+++ b/solution.py
@@ -191,8 +191,13 @@
     if shared:
         partner_normed = lax.ppermute(normed, "groups", partners)
         partner_part = contract_rows(partner_normed, gathered_proj).astype(jnp.bfloat16)
-        partner_sum = sent_to(partner_part, 1, 0)
-        other_pieces = [sent_to(partner_sum, 0, 1), partner_sum, sent_to(partner_sum, 0, -1)]
+        halves = [sent_to(part, 1, 0) for part in jnp.split(partner_part, 2, axis=0)]
+        partner_sum = jnp.concatenate(halves, axis=0)
+        other_pieces = [
+            jnp.concatenate([sent_to(part, 0, 1) for part in halves], axis=0),
+            partner_sum,
+            jnp.concatenate([sent_to(part, 0, -1) for part in halves], axis=0),
+        ]
         own_sum = contract_rows(normed, gathered_proj).astype(jnp.bfloat16)
         mine_pieces = [sent_to(own_sum, 0, 1), own_sum, sent_to(own_sum, 0, -1)]
         near_pair = jnp.concatenate(mine_pieces + other_pieces, axis=0).reshape(

time: 181 us -> 188 us (1.039)
  the two profiles are of different devices: /device:TPU:20 before, /device:TPU:1 now
where the time goes in v15:
time: 188 us
  waiting for transfers between devices  66.2 us (35%)
  starting transfers between devices  58.9 us (31%)
  between operations  16.8 us (9%)
  Pallas kernels  16.6 us (9%)
  matrix products  11.3 us (6%)
  local copies, waits for them, and re-layouts  11 us (6%)
  other arithmetic  6.71 us (4%)
    ppermute x6, starting transfers between devices, passed_along(): return lax.ppermute(array, axis, pairs)  38.7 us
    ppermute x6, waiting for transfers between devices, passed_along(): return lax.ppermute(array, axis, pairs)  29.9 us
    all_gather x1, waiting for transfers between devices, on_device(): gathered_proj = lax.all_gather(own_proj, 'ctx', axis=0, tiled=True)  26.7 us
    ppermute x8, starting transfers between devices, sent_to(): return lax.ppermute(array, ('groups', 'ctx'), pairs)  18.8 us
    pallas_call x1, Pallas kernels, coarse_attention(): pl.pallas_call(kernel, grid_spec=grid_spec, out_shape=jax.ShapeDtypeStruc...  16.6 us
    dot_general x3, matrix products, contract_rows(): return jnp.dot(left_side, weight_piece, preferred_element_type=jnp.float32)  9.65 us
    unnamed x21, local copies, waits for them, and re-layouts  9.25 us
    ppermute x8, waiting for transfers between devices, sent_to(): return lax.ppermute(array, ('groups', 'ctx'), pairs)  8.93 us
  transfers between devices with their start and end apart: 17, of which 7 were waited for; matrix products, arithmetic and copies ran while one was open for 15% of the time, Pallas kernels for 0%

profile of v15, /device:TPU:1, one launch (start us, length us, event | category | flops | bytes accessed | tf_op | source)
XLA Modules:
  0.0 187.5 jit_solution(16337762206920484516)
XLA Ops:
  6.5 0.7 all-gather.3.cloned.1.call-update
  7.3 1.7 broadcast_select_fusion
  9.0 1.2 copy.18
  10.3 1.2 copy.19
  11.5 0.1 pad_maximum_fusion
  11.6 4.5 %collective-permute-start.4 = (bf16[2,256,1024]{1,2,0:T(8,128)(2,1)S(1)}, bf16[2,256,1024]{1,2,0:T(8,128)(2,1)S(1)}, u32[]{:S(2)}, u32[]{:S(2)}) collective-permute-start(bf16[2,256,1024]{1,2,0:T(8,128)(2,1)S(1)} %pad_maximum_fusion), channel_id=1, source_target_pairs={{0,1},{1,2},{2,3},{3,4},{4,5},{5,6},{6,7},{7,8},{8,9},{9,10},{10,1... | collective-permute-start | bytes 3145736 | tf_op jit(solution)/shard_map/ppermute | solution.py:23
  16.2 14.5 %collective-permute-done.4 = bf16[2,256,1024]{1,2,0:T(8,128)(2,1)S(1)} collective-permute-done((bf16[2,256,1024]{1,2,0:T(8,128)(2,1)S(1)}, bf16[2,256,1024]{1,2,0:T(8,128)(2,1)S(1)}, u32[]{:S(2)}, u32[]{:S(2)}) %collective-permute-start.4) | collective-permute-done | bytes 1048608 | tf_op jit(solution)/shard_map/ppermute | solution.py:23
  30.7 4.4 %collective-permute-start.5 = (bf16[2,256,1024]{1,2,0:T(8,128)(2,1)S(1)}, bf16[2,256,1024]{1,2,0:T(8,128)(2,1)}, u32[]{:S(2)}, u32[]{:S(2)}) collective-permute-start(bf16[2,256,1024]{1,2,0:T(8,128)(2,1)S(1)} %collective-permute-done.4), channel_id=1, source_target_pairs={{0,1},{1,2},{2,3},{3,4},{4,5},{5,6},{6,7},{7,8},{8,9},{9,10},{10,1... | collective-permute-start | bytes 3145736 | tf_op jit(solution)/shard_map/ppermute | solution.py:23
  35.1 6.7 %collective-permute-start = (s32[1]{0:T(128)}, s32[1]{0:T(128)}, u32[]{:S(2)}, u32[]{:S(2)}) collective-permute-start(s32[1]{0:T(128)} %param.22), channel_id=1, source_target_pairs={{0,1},{1,2},{2,3},{3,4},{4,5},{5,6},{6,7},{7,8},{8,9},{9,10},{10,1... | collective-permute-start | bytes 20 | tf_op jit(solution)/shard_map/ppermute | solution.py:23
  42.5 0.2 fusion.10
  42.7 15.4 %collective-permute-done = s32[1]{0:T(128)} collective-permute-done((s32[1]{0:T(128)}, s32[1]{0:T(128)}, u32[]{:S(2)}, u32[]{:S(2)}) %collective-permute-start) | collective-permute-done | bytes 36 | tf_op jit(solution)/shard_map/ppermute | solution.py:23
  58.7 14.0 %collective-permute-start.1 = (s32[1]{0:T(128)}, s32[1]{0:T(128)}, u32[]{:S(2)}, u32[]{:S(2)}) collective-permute-start(s32[1]{0:T(128)} %add.53), channel_id=1, source_target_pairs={{0,2},{1,3},{2,4},{3,5},{4,6},{5,7},{6,8},{7,9},{8,10},{9,11},{10,... | collective-permute-start | bytes 20 | tf_op jit(solution)/shard_map/ppermute | solution.py:23
  73.3 4.0 %collective-permute-start.2 = (s32[1]{0:T(128)}, s32[1]{0:T(128)}, u32[]{:S(2)}, u32[]{:S(2)}) collective-permute-start(s32[1]{0:T(128)} %add.54), channel_id=1, source_target_pairs={{0,4},{1,5},{2,6},{3,7},{4,8},{5,9},{6,10},{7,11},{8,12},{9,13},{1... | collective-permute-start | bytes 20 | tf_op jit(solution)/shard_map/ppermute | solution.py:23
  77.9 5.2 %collective-permute-start.3 = (s32[1]{0:T(128)}, s32[1]{0:T(128)}, u32[]{:S(2)}, u32[]{:S(2)}) collective-permute-start(s32[1]{0:T(128)} %add.55), channel_id=1, source_target_pairs={{0,8},{1,9},{2,10},{3,11},{4,12},{5,13},{6,14},{7,15},{16,24},{17,... | collective-permute-start | bytes 20 | tf_op jit(solution)/shard_map/ppermute | solution.py:23
  83.7 1.3 maximum_maximum_fusion
  85.1 0.2 fusion.16
  85.3 1.0 fusion.11
  86.4 3.1 %fusion.18 = (f32[8,256]{1,0:T(8,128)S(1)}, f32[8,256,768]{1,2,0:T(8,128)S(1)}) fusion(f32[8,768,256]{2,1,0:T(8,128)S(1)} %fusion.11, pred[256,768]{0,1:T(8,128)(4,1)S(1)} %fusion.10), kind=kOutput, calls=%fused_computation.42 | output fusion | flops 9437951 | bytes 12787712 | tf_op jit(solution)/shard_map/sub | solution.py:63
  89.5 0.6 fusion.6
  90.1 0.5 copy-done.1
  90.7 3.6 %multiply_reduce_fusion = (f32[256]{0:T(256)S(1)}, f32[256,2048]{1,0:T(8,128)S(1)}) fusion(bf16[256,1024]{0,1:T(8,128)(2,1)S(1)} %bitcast.41, bf16[1024,2048]{1,0:T(8,128)(2,1)} %all-gather.3.cloned.1.call-done, bf16[256,2048]{1,0:T(8,128)(2,1)S(1)} %copy-done.1), kind=kOutput, calls=%fused_computation.12 | convolution fusion | flops 1075838720 | bytes 7865344 | tf_op jit(solution)/shard_map/dot_general | solution.py:79
  94.3 0.2 multiply_convert_fusion
  94.5 1.3 collective-permute-start.8
  95.8 26.7 %all-gather.5.cloned.1.call-done = bf16[2048,1024]{1,0:T(8,128)(2,1)} async-done(((bf16[128,1024]{1,0:T(8,128)(2,1)}), bf16[2048,1024]{1,0:T(8,128)(2,1)}) %all-gather.5.cloned.1.call-update) | async-done | bytes 4194320 | tf_op jit(solution)/shard_map/all_gather | solution.py:169
  122.4 3.6 %convolution_convert_fusion.1 = bf16[256,1024]{1,0:T(8,128)(2,1)S(1)} fusion(bf16[256,2048]{1,0:T(8,128)(2,1)S(1)} %multiply_convert_fusion, bf16[2048,1024]{1,0:T(8,128)(2,1)} %all-gather.5.cloned.1.call-done), kind=kOutput, calls=%fused_computation.15 | convolution fusion | flops 1074003968 | bytes 5767168 | tf_op jit(solution)/shard_map/dot_general | solution.py:79
  126.0 2.3 %collective-permute-start.6 = (bf16[256,1024]{1,0:T(8,128)(2,1)S(1)}, bf16[256,1024]{1,0:T(8,128)(2,1)S(1)}, u32[]{:S(2)}, u32[]{:S(2)}) collective-permute-start(bf16[256,1024]{1,0:T(8,128)(2,1)S(1)} %convolution_convert_fusion.1), channel_id=1, source_target_pairs={{0,1},{1,2},{2,3},{3,4},{4,5},{5,6},{6,7},{7,8},{8,9},{9,10},{10,1... | collective-permute-start | bytes 1572872 | tf_op jit(solution)/shard_map/ppermute | solution.py:47
  128.4 2.0 %collective-permute-start.7 = (bf16[256,1024]{1,0:T(8,128)(2,1)S(1)}, bf16[256,1024]{1,0:T(8,128)(2,1)S(1)}, u32[]{:S(2)}, u32[]{:S(2)}) collective-permute-start(bf16[256,1024]{1,0:T(8,128)(2,1)S(1)} %convolution_convert_fusion.1), channel_id=1, source_target_pairs={{1,0},{2,1},{3,2},{4,3},{5,4},{6,5},{7,6},{8,7},{9,8},{10,9},{11,1... | collective-permute-start | bytes 1572872 | tf_op jit(solution)/shard_map/ppermute | solution.py:47
  130.4 2.5 %convolution_convert_fusion = bf16[256,1024]{1,0:T(8,128)(2,1)S(1)} fusion(bf16[256,2048]{1,0:T(8,128)(2,1)} %collective-permute-done.8, bf16[2048,1024]{1,0:T(8,128)(2,1)S(1)} %copy-done.4), kind=kOutput, calls=%fused_computation.14 | convolution fusion | flops 1074003968 | bytes 5767168 | tf_op jit(solution)/shard_map/dot_general | solution.py:79
  133.0 1.3 collective-permute-start.9
  134.2 0.3 collective-permute-start.11
  134.7 0.7 concatenate.10.prm
  135.4 6.0 %collective-permute-done.9 = bf16[128,1024]{1,0:T(8,128)(2,1)S(1)} collective-permute-done((bf16[128,1024]{1,0:T(8,128)(2,1)S(1)}, bf16[128,1024]{1,0:T(8,128)(2,1)S(1)}, u32[]{:S(2)}, u32[]{:S(2)}) %collective-permute-start.9) | collective-permute-done | bytes 262176 | tf_op jit(solution)/shard_map/ppermute | solution.py:47
  141.4 4.4 %collective-permute-start.10 = (bf16[128,1024]{1,0:T(8,128)(2,1)S(1)}, bf16[128,1024]{1,0:T(8,128)(2,1)S(1)}, u32[]{:S(2)}, u32[]{:S(2)}) collective-permute-start(bf16[128,1024]{1,0:T(8,128)(2,1)S(1)} %collective-permute-done.9), channel_id=1, source_target_pairs={{0,1},{1,2},{2,3},{3,4},{4,5},{5,6},{6,7},{7,8},{8,9},{9,10},{10,1... | collective-permute-start | bytes 786440 | tf_op jit(solution)/shard_map/ppermute | solution.py:47
  145.8 0.8 constant_dynamic-update-slice_fusion.8
  146.7 4.6 %collective-permute-start.12 = (bf16[128,1024]{1,0:T(8,128)(2,1)S(1)}, bf16[128,1024]{1,0:T(8,128)(2,1)S(1)}, u32[]{:S(2)}, u32[]{:S(2)}) collective-permute-start(bf16[128,1024]{1,0:T(8,128)(2,1)S(1)} %collective-permute-done.11), channel_id=1, source_target_pairs={{0,1},{1,2},{2,3},{3,4},{4,5},{5,6},{6,7},{7,8},{8,9},{9,10},{10,1... | collective-permute-start | bytes 786440 | tf_op jit(solution)/shard_map/ppermute | solution.py:47
  151.2 0.8 constant_dynamic-update-slice_fusion.7
  152.1 0.8 constant_dynamic-update-slice_fusion.6
  152.9 1.9 %collective-permute-start.13 = (bf16[128,1024]{1,0:T(8,128)(2,1)S(1)}, bf16[128,1024]{1,0:T(8,128)(2,1)S(1)}, u32[]{:S(2)}, u32[]{:S(2)}) collective-permute-start(bf16[128,1024]{1,0:T(8,128)(2,1)S(1)} %collective-permute-done.9), channel_id=1, source_target_pairs={{1,0},{2,1},{3,2},{4,3},{5,4},{6,5},{7,6},{8,7},{9,8},{10,9},{11,1... | collective-permute-start | bytes 786440 | tf_op jit(solution)/shard_map/ppermute | solution.py:47
  154.8 2.1 %collective-permute-start.14 = (bf16[128,1024]{1,0:T(8,128)(2,1)S(1)}, bf16[128,1024]{1,0:T(8,128)(2,1)S(1)}, u32[]{:S(2)}, u32[]{:S(2)}) collective-permute-start(bf16[128,1024]{1,0:T(8,128)(2,1)S(1)} %collective-permute-done.11), channel_id=1, source_target_pairs={{1,0},{2,1},{3,2},{4,3},{5,4},{6,5},{7,6},{8,7},{9,8},{10,9},{11,1... | collective-permute-start | bytes 786440 | tf_op jit(solution)/shard_map/ppermute | solution.py:47
  156.9 0.7 constant_dynamic-update-slice_fusion.5
  157.6 0.7 constant_dynamic-update-slice_fusion.4
  158.4 0.7 constant_dynamic-update-slice_fusion.3
  159.1 0.7 constant_dynamic-update-slice_fusion.2
  159.8 0.8 collective-permute-done.13
  160.6 0.7 constant_dynamic-update-slice_fusion.1
  161.3 2.1 %collective-permute-done.14 = bf16[128,1024]{1,0:T(8,128)(2,1)S(1)} collective-permute-done((bf16[128,1024]{1,0:T(8,128)(2,1)S(1)}, bf16[128,1024]{1,0:T(8,128)(2,1)S(1)}, u32[]{:S(2)}, u32[]{:S(2)}) %collective-permute-start.14) | collective-permute-done | bytes 262176 | tf_op jit(solution)/shard_map/ppermute | solution.py:47
  163.4 0.7 constant_dynamic-update-slice_fusion
  164.1 16.6 %shard_map.118 = bf16[1024,1024]{1,0:T(8,128)(2,1)} custom-call(s32[12]{0:T(128)} %concatenate.10.prm, f32[8]{0:T(128)} %slopes_ref.1, bf16[1024,1024]{1,0:T(8,128)(2,1)} %q_ref.1, bf16[2,768,1024]{2,1,0:T(8,128)(2,1)} %bitcast.9.k_ref.v_ref, bf16[2,768,1024]{2,1,0:T(8,128)(2,1)} %bitcast.9.k_ref.v_ref), custom_call_target="tpu_custom_call" | custom-call | tf_op jit(solution)/shard_map/pallas_call | solution.py:132
  (29 shorter events, 0.4 us)
Async XLA Ops:
  6.5 78.8 %copy-start = (bf16[256,1024]{1,0:T(8,128)(2,1)S(1)}, bf16[256,1024]{1,0:T(8,128)(2,1)}, u32[]{:S(2)}) copy-start(bf16[256,1024]{1,0:T(8,128)(2,1)} %param.12) | copy-start | bytes 1572868
  6.5 83.6 %all-gather.3.cloned.1.call-start = ((), (), s32[]{:S(2)}) async-start(), calls=%async_computation | async-start | bytes 4456448 | tf_op jit(solution)/shard_map/all_gather | solution.py:157
  7.3 115.1 %all-gather.5.cloned.1.call-start = ((), (), s32[]{:S(2)}) async-start(), calls=%async_computation.1 | async-start | bytes 4456448 | tf_op jit(solution)/shard_map/all_gather | solution.py:169
  11.6 19.1 %collective-permute-start.4 = (bf16[2,256,1024]{1,2,0:T(8,128)(2,1)S(1)}, bf16[2,256,1024]{1,2,0:T(8,128)(2,1)S(1)}, u32[]{:S(2)}, u32[]{:S(2)}) collective-permute-start(bf16[2,256,1024]{1,2,0:T(8,128)(2,1)S(1)} %pad_maximum_fusion), channel_id=1, source_target_pairs={{0,1},{1,2},{2,3},{3,4},{4,5},{5,6},{6,7},{7,8},{8,9},{9,10},{10,1... | collective-permute-start | bytes 3145736 | tf_op jit(solution)/shard_map/ppermute | solution.py:23
  30.7 53.0 %collective-permute-start.5 = (bf16[2,256,1024]{1,2,0:T(8,128)(2,1)S(1)}, bf16[2,256,1024]{1,2,0:T(8,128)(2,1)}, u32[]{:S(2)}, u32[]{:S(2)}) collective-permute-start(bf16[2,256,1024]{1,2,0:T(8,128)(2,1)S(1)} %collective-permute-done.4), channel_id=1, source_target_pairs={{0,1},{1,2},{2,3},{3,4},{4,5},{5,6},{6,7},{7,8},{8,9},{9,10},{10,1... | collective-permute-start | bytes 3145736 | tf_op jit(solution)/shard_map/ppermute | solution.py:23
  35.1 23.0 %collective-permute-start = (s32[1]{0:T(128)}, s32[1]{0:T(128)}, u32[]{:S(2)}, u32[]{:S(2)}) collective-permute-start(s32[1]{0:T(128)} %param.22), channel_id=1, source_target_pairs={{0,1},{1,2},{2,3},{3,4},{4,5},{5,6},{6,7},{7,8},{8,9},{9,10},{10,1... | collective-permute-start | bytes 20 | tf_op jit(solution)/shard_map/ppermute | solution.py:23
  58.7 14.0 %collective-permute-start.1 = (s32[1]{0:T(128)}, s32[1]{0:T(128)}, u32[]{:S(2)}, u32[]{:S(2)}) collective-permute-start(s32[1]{0:T(128)} %add.53), channel_id=1, source_target_pairs={{0,2},{1,3},{2,4},{3,5},{4,6},{5,7},{6,8},{7,9},{8,10},{9,11},{10,... | collective-permute-start | bytes 20 | tf_op jit(solution)/shard_map/ppermute | solution.py:23
  73.3 4.0 %collective-permute-start.2 = (s32[1]{0:T(128)}, s32[1]{0:T(128)}, u32[]{:S(2)}, u32[]{:S(2)}) collective-permute-start(s32[1]{0:T(128)} %add.54), channel_id=1, source_target_pairs={{0,4},{1,5},{2,6},{3,7},{4,8},{5,9},{6,10},{7,11},{8,12},{9,13},{1... | collective-permute-start | bytes 20 | tf_op jit(solution)/shard_map/ppermute | solution.py:23
  77.9 5.2 %collective-permute-start.3 = (s32[1]{0:T(128)}, s32[1]{0:T(128)}, u32[]{:S(2)}, u32[]{:S(2)}) collective-permute-start(s32[1]{0:T(128)} %add.55), channel_id=1, source_target_pairs={{0,8},{1,9},{2,10},{3,11},{4,12},{5,13},{6,14},{7,15},{16,24},{17,... | collective-permute-start | bytes 20 | tf_op jit(solution)/shard_map/ppermute | solution.py:23
  89.4 1.2 copy-start.1
  90.1 4.2 %copy-start.2 = (f32[2048]{0:T(1024)S(1)}, f32[2048]{0:T(1024)}, u32[]{:S(2)}) copy-start(f32[2048]{0:T(1024)} %param.17) | copy-start | bytes 24580
  94.5 35.9 %collective-permute-start.8 = (bf16[256,2048]{1,0:T(8,128)(2,1)S(1)}, bf16[256,2048]{1,0:T(8,128)(2,1)}, u32[]{:S(2)}, u32[]{:S(2)}) collective-permute-start(bf16[256,2048]{1,0:T(8,128)(2,1)S(1)} %multiply_convert_fusion), channel_id=1, source_target_pairs={{0,16},{16,0},{1,17},{17,1},{2,18},{18,2},{3,19},{19,3},{4,20},{20... | collective-permute-start | bytes 3145736 | tf_op jit(solution)/shard_map/ppermute | solution.py:192
  122.4 8.0 %copy-start.4 = (bf16[2048,1024]{1,0:T(8,128)(2,1)S(1)}, bf16[2048,1024]{1,0:T(8,128)(2,1)}, u32[]{:S(2)}) copy-start(bf16[2048,1024]{1,0:T(8,128)(2,1)} %all-gather.5.cloned.1.call-done) | copy-start | bytes 12582916
  126.0 8.5 %copy-start.3 = (s32[4,2]{0,1:T(2,128)S(1)}, s32[4,2]{0,1:T(2,128)}, u32[]{:S(2)}) copy-start(s32[4,2]{0,1:T(2,128)} %param.23) | copy-start | bytes 100
  126.0 19.7 %collective-permute-start.6 = (bf16[256,1024]{1,0:T(8,128)(2,1)S(1)}, bf16[256,1024]{1,0:T(8,128)(2,1)S(1)}, u32[]{:S(2)}, u32[]{:S(2)}) collective-permute-start(bf16[256,1024]{1,0:T(8,128)(2,1)S(1)} %convolution_convert_fusion.1), channel_id=1, source_target_pairs={{0,1},{1,2},{2,3},{3,4},{4,5},{5,6},{6,7},{7,8},{8,9},{9,10},{10,1... | collective-permute-start | bytes 1572872 | tf_op jit(solution)/shard_map/ppermute | solution.py:47
  128.4 23.7 %collective-permute-start.7 = (bf16[256,1024]{1,0:T(8,128)(2,1)S(1)}, bf16[256,1024]{1,0:T(8,128)(2,1)S(1)}, u32[]{:S(2)}, u32[]{:S(2)}) collective-permute-start(bf16[256,1024]{1,0:T(8,128)(2,1)S(1)} %convolution_convert_fusion.1), channel_id=1, source_target_pairs={{1,0},{2,1},{3,2},{4,3},{5,4},{6,5},{7,6},{8,7},{9,8},{10,9},{11,1... | collective-permute-start | bytes 1572872 | tf_op jit(solution)/shard_map/ppermute | solution.py:47
  133.0 8.4 %collective-permute-start.9 = (bf16[128,1024]{1,0:T(8,128)(2,1)S(1)}, bf16[128,1024]{1,0:T(8,128)(2,1)S(1)}, u32[]{:S(2)}, u32[]{:S(2)}) collective-permute-start(bf16[128,1024]{1,0:T(8,128)(2,1)S(1)} %get-tuple-element.12), channel_id=1, source_target_pairs={{0,16},{1,17},{2,18},{3,19},{4,20},{5,21},{6,22},{7,23},{8,24},{9,... | collective-permute-start | bytes 786440 | tf_op jit(solution)/shard_map/ppermute | solution.py:47
  134.2 12.4 %collective-permute-start.11 = (bf16[128,1024]{1,0:T(8,128)(2,1)S(1)}, bf16[128,1024]{1,0:T(8,128)(2,1)S(1)}, u32[]{:S(2)}, u32[]{:S(2)}) collective-permute-start(bf16[128,1024]{1,0:T(8,128)(2,1)S(1)} %get-tuple-element.11), channel_id=1, source_target_pairs={{0,16},{1,17},{2,18},{3,19},{4,20},{5,21},{6,22},{7,23},{8,24},{9,... | collective-permute-start | bytes 786440 | tf_op jit(solution)/shard_map/ppermute | solution.py:47
  141.4 15.6 %collective-permute-start.10 = (bf16[128,1024]{1,0:T(8,128)(2,1)S(1)}, bf16[128,1024]{1,0:T(8,128)(2,1)S(1)}, u32[]{:S(2)}, u32[]{:S(2)}) collective-permute-start(bf16[128,1024]{1,0:T(8,128)(2,1)S(1)} %collective-permute-done.9), channel_id=1, source_target_pairs={{0,1},{1,2},{2,3},{3,4},{4,5},{5,6},{6,7},{7,8},{8,9},{9,10},{10,1... | collective-permute-start | bytes 786440 | tf_op jit(solution)/shard_map/ppermute | solution.py:47
  146.7 11.0 %collective-permute-start.12 = (bf16[128,1024]{1,0:T(8,128)(2,1)S(1)}, bf16[128,1024]{1,0:T(8,128)(2,1)S(1)}, u32[]{:S(2)}, u32[]{:S(2)}) collective-permute-start(bf16[128,1024]{1,0:T(8,128)(2,1)S(1)} %collective-permute-done.11), channel_id=1, source_target_pairs={{0,1},{1,2},{2,3},{3,4},{4,5},{5,6},{6,7},{7,8},{8,9},{9,10},{10,1... | collective-permute-start | bytes 786440 | tf_op jit(solution)/shard_map/ppermute | solution.py:47
  152.9 7.7 %collective-permute-start.13 = (bf16[128,1024]{1,0:T(8,128)(2,1)S(1)}, bf16[128,1024]{1,0:T(8,128)(2,1)S(1)}, u32[]{:S(2)}, u32[]{:S(2)}) collective-permute-start(bf16[128,1024]{1,0:T(8,128)(2,1)S(1)} %collective-permute-done.9), channel_id=1, source_target_pairs={{1,0},{2,1},{3,2},{4,3},{5,4},{6,5},{7,6},{8,7},{9,8},{10,9},{11,1... | collective-permute-start | bytes 786440 | tf_op jit(solution)/shard_map/ppermute | solution.py:47
  154.8 8.6 %collective-permute-start.14 = (bf16[128,1024]{1,0:T(8,128)(2,1)S(1)}, bf16[128,1024]{1,0:T(8,128)(2,1)S(1)}, u32[]{:S(2)}, u32[]{:S(2)}) collective-permute-start(bf16[128,1024]{1,0:T(8,128)(2,1)S(1)} %collective-permute-done.11), channel_id=1, source_target_pairs={{1,0},{2,1},{3,2},{4,3},{5,4},{6,5},{7,6},{8,7},{9,8},{10,9},{11,1... | collective-permute-start | bytes 786440 | tf_op jit(solution)/shard_map/ppermute | solution.py:47
Sparse Core Ops, SparseCore 0:
  9.5 59.5 all-gather.2
  71.2 51.1 all-gather.4

commit v16 on v14

--- a/solution.py
+++ b/solution.py
@@ -175,6 +175,8 @@
     earlier = []
     relayed = own_pair
     for distance in range(1, reach_shards + 1):
+        if distance == 2:
+            full_out_proj, relayed = lax.optimization_barrier((full_out_proj, relayed))
         relayed = passed_along(relayed, "ctx", 1)
         earlier.insert(0, relayed)
     window_pair = jnp.concatenate(earlier + [own_pair], axis=1)

time: 181 us -> 198 us (1.094)
  waiting for transfers between devices: 70.8 us -> 101 us
  starting transfers between devices: 49.2 us -> 38 us
  matrix products: 10.1 us -> 7.76 us
    all_gather x1, waiting for transfers between devices: 0.02 us -> 30.3 us  [on_device(): full_out_proj = lax.all_gather(out_proj, 'ctx', axis=0, tiled=True)]
    ppermute x1, waiting for transfers between devices: 0.24 us -> 20 us  [on_device(): partner_normed = lax.ppermute(normed, 'groups', partners)]
    all_gather x1, waiting for transfers between devices: 18.9 us -> 0.01 us  [on_device(): gathered_proj = lax.all_gather(own_proj, 'ctx', axis=0, tiled=True)]
    ppermute x6, starting transfers between devices: 34.9 us -> 23.6 us  [passed_along(): return lax.ppermute(array, axis, pairs)]
    dot_general x3, matrix products: 8.44 us -> 6.1 us  [contract_rows(): return jnp.dot(left_side, weight_piece, preferred_element_type=jnp.float32)]
    unnamed x18 -> x20, local copies, waits for them, and re-layouts: 7.36 us -> 8.7 us
  transfers between devices with their start and end apart: 14 -> 14, of which waited for: 8 -> 11; matrix products, arithmetic and copies ran while one was open for 12% -> 10% of each run, Pallas kernels for 0% -> 0%
where the time goes in v16:
time: 198 us; the launch traced here: 197 us
  waiting for transfers between devices  101 us (51%)
  starting transfers between devices  38 us (19%)
  between operations  17.1 us (9%)
  Pallas kernels  16.6 us (8%)
  local copies, waits for them, and re-layouts  10.5 us (5%)
  matrix products  7.76 us (4%)
  other arithmetic  6.7 us (3%)
    ppermute x6, waiting for transfers between devices, passed_along(): return lax.ppermute(array, axis, pairs)  36.8 us
    all_gather x1, waiting for transfers between devices, on_device(): full_out_proj = lax.all_gather(out_proj, 'ctx', axis=0, tiled=True)  30.3 us
    ppermute x6, starting transfers between devices, passed_along(): return lax.ppermute(array, axis, pairs)  23.6 us
    ppermute x1, waiting for transfers between devices, on_device(): partner_normed = lax.ppermute(normed, 'groups', partners)  20 us
    pallas_call x1, Pallas kernels, coarse_attention(): pl.pallas_call(kernel, grid_spec=grid_spec, out_shape=jax.ShapeDtypeStruc...  16.6 us
    ppermute x5, starting transfers between devices, sent_to(): return lax.ppermute(array, ('groups', 'ctx'), pairs)  12.8 us
    ppermute x5, waiting for transfers between devices, sent_to(): return lax.ppermute(array, ('groups', 'ctx'), pairs)  12.6 us
    unnamed x20, local copies, waits for them, and re-layouts  8.7 us
  transfers between devices with their start and end apart: 14, of which 11 were waited for; matrix products, arithmetic and copies ran while one was open for 10% of the time, Pallas kernels for 0%

profile of v16, /device:TPU:20, one launch (start us, length us, event | category | flops | bytes accessed | tf_op | source)
XLA Modules:
  0.0 197.1 jit_solution(7215110521258073539)
XLA Ops:
  6.5 0.7 all-gather.3.cloned.1.call-update
  7.3 1.7 broadcast_select_fusion
  9.0 1.2 copy.18
  10.3 1.2 copy.19
  11.5 0.1 pad_maximum_fusion
  11.6 1.9 collective-permute-start.4
  13.6 17.0 %collective-permute-done.4 = bf16[2,256,1024]{1,2,0:T(8,128)(2,1)S(1)} collective-permute-done((bf16[2,256,1024]{1,2,0:T(8,128)(2,1)S(1)}, bf16[2,256,1024]{1,2,0:T(8,128)(2,1)S(1)}, u32[]{:S(2)}, u32[]{:S(2)}) %collective-permute-start.4) | collective-permute-done | bytes 1048608 | tf_op jit(solution)/shard_map/ppermute | solution.py:23
  30.6 30.3 %all-gather.3.cloned.1.call-done = bf16[1024,2048]{1,0:T(8,128)(2,1)} async-done(((bf16[64,2048]{1,0:T(8,128)(2,1)}), bf16[1024,2048]{1,0:T(8,128)(2,1)}) %all-gather.3.cloned.1.call-update) | async-done | bytes 4194320 | tf_op jit(solution)/shard_map/all_gather | solution.py:157
  60.8 2.1 %collective-permute-start.5 = (bf16[2,256,1024]{1,2,0:T(8,128)(2,1)S(1)}, bf16[2,256,1024]{1,2,0:T(8,128)(2,1)}, u32[]{:S(2)}, u32[]{:S(2)}) collective-permute-start(bf16[2,256,1024]{1,2,0:T(8,128)(2,1)S(1)} %collective-permute-done.4), channel_id=1, source_target_pairs={{0,1},{1,2},{2,3},{3,4},{4,5},{5,6},{6,7},{7,8},{8,9},{9,10},{10,1... | collective-permute-start | bytes 3145736 | tf_op jit(solution)/shard_map/ppermute | solution.py:23
  63.0 3.3 %collective-permute-start = (s32[1]{0:T(128)}, s32[1]{0:T(128)}, u32[]{:S(2)}, u32[]{:S(2)}) collective-permute-start(s32[1]{0:T(128)} %param.22), channel_id=1, source_target_pairs={{0,1},{1,2},{2,3},{3,4},{4,5},{5,6},{6,7},{7,8},{8,9},{9,10},{10,1... | collective-permute-start | bytes 20 | tf_op jit(solution)/shard_map/ppermute | solution.py:23
  66.9 0.2 fusion.10
  67.2 12.7 %collective-permute-done = s32[1]{0:T(128)} collective-permute-done((s32[1]{0:T(128)}, s32[1]{0:T(128)}, u32[]{:S(2)}, u32[]{:S(2)}) %collective-permute-start) | collective-permute-done | bytes 36 | tf_op jit(solution)/shard_map/ppermute | solution.py:23
  80.5 11.2 %collective-permute-start.1 = (s32[1]{0:T(128)}, s32[1]{0:T(128)}, u32[]{:S(2)}, u32[]{:S(2)}) collective-permute-start(s32[1]{0:T(128)} %add.53), channel_id=1, source_target_pairs={{0,2},{1,3},{2,4},{3,5},{4,6},{5,7},{6,8},{7,9},{8,10},{9,11},{10,... | collective-permute-start | bytes 20 | tf_op jit(solution)/shard_map/ppermute | solution.py:23
  91.7 0.2 collective-permute-done.1
  92.6 3.8 %collective-permute-start.2 = (s32[1]{0:T(128)}, s32[1]{0:T(128)}, u32[]{:S(2)}, u32[]{:S(2)}) collective-permute-start(s32[1]{0:T(128)} %add.54), channel_id=1, source_target_pairs={{0,4},{1,5},{2,6},{3,7},{4,8},{5,9},{6,10},{7,11},{8,12},{9,13},{1... | collective-permute-start | bytes 20 | tf_op jit(solution)/shard_map/ppermute | solution.py:23
  96.4 1.9 collective-permute-done.2
  99.0 1.3 collective-permute-start.3
  100.3 5.0 %collective-permute-done.3 = s32[1]{0:T(128)} collective-permute-done((s32[1]{0:T(128)}, s32[1]{0:T(128)}, u32[]{:S(2)}, u32[]{:S(2)}) %collective-permute-start.3) | collective-permute-done | bytes 36 | tf_op jit(solution)/shard_map/ppermute | solution.py:23
  106.1 1.3 maximum_maximum_fusion
  107.4 0.2 fusion.16
  107.6 1.0 fusion.11
  108.7 3.1 %fusion.17 = (f32[8,256]{1,0:T(8,128)S(1)}, f32[8,256,768]{1,2,0:T(8,128)S(1)}) fusion(f32[8,768,256]{2,1,0:T(8,128)S(1)} %fusion.11, pred[256,768]{0,1:T(8,128)(4,1)S(1)} %fusion.10), kind=kOutput, calls=%fused_computation.38 | output fusion | flops 9437951 | bytes 12787712 | tf_op jit(solution)/shard_map/sub | solution.py:63
  111.8 0.6 fusion.6
  112.4 1.6 copy-done.1
  114.0 0.3 copy-done.2
  114.3 1.4 multiply_reduce_fusion
  115.7 0.2 multiply_convert_fusion
  115.9 1.6 collective-permute-start.8
  117.5 20.0 %collective-permute-done.8 = bf16[256,2048]{1,0:T(8,128)(2,1)S(1)} collective-permute-done((bf16[256,2048]{1,0:T(8,128)(2,1)S(1)}, bf16[256,2048]{1,0:T(8,128)(2,1)S(1)}, u32[]{:S(2)}, u32[]{:S(2)}) %collective-permute-start.8) | collective-permute-done | bytes 1048608 | tf_op jit(solution)/shard_map/ppermute | solution.py:194
  137.5 3.4 %convolution_convert_fusion = bf16[256,1024]{1,0:T(8,128)(2,1)S(1)} fusion(bf16[256,2048]{1,0:T(8,128)(2,1)S(1)} %collective-permute-done.8, bf16[2048,1024]{1,0:T(8,128)(2,1)} %all-gather.5.cloned.1.call-done), kind=kOutput, calls=%fused_computation.14 | convolution fusion | flops 1074003968 | bytes 5767168 | tf_op jit(solution)/shard_map/dot_general | solution.py:79
  141.0 1.5 collective-permute-start.9
  142.5 1.3 convolution_convert_fusion.1
  143.8 1.9 collective-permute-start.6
  145.7 3.6 %collective-permute-start.7 = (bf16[256,1024]{1,0:T(8,128)(2,1)S(1)}, bf16[256,1024]{1,0:T(8,128)(2,1)S(1)}, u32[]{:S(2)}, u32[]{:S(2)}) collective-permute-start(bf16[256,1024]{1,0:T(8,128)(2,1)S(1)} %convolution_convert_fusion.1), channel_id=1, source_target_pairs={{1,0},{2,1},{3,2},{4,3},{5,4},{6,5},{7,6},{8,7},{9,8},{10,9},{11,1... | collective-permute-start | bytes 1572872 | tf_op jit(solution)/shard_map/ppermute | solution.py:47
  149.4 1.1 collective-permute-done.9
  150.5 1.9 collective-permute-start.10
  152.6 0.7 concatenate.10.prm
  153.3 3.8 %collective-permute-start.11 = (bf16[256,1024]{1,0:T(8,128)(2,1)S(1)}, bf16[256,1024]{1,0:T(8,128)(2,1)S(1)}, u32[]{:S(2)}, u32[]{:S(2)}) collective-permute-start(bf16[256,1024]{1,0:T(8,128)(2,1)S(1)} %collective-permute-done.9), channel_id=1, source_target_pairs={{1,0},{2,1},{3,2},{4,3},{5,4},{6,5},{7,6},{8,7},{9,8},{10,9},{11,1... | collective-permute-start | bytes 1572872 | tf_op jit(solution)/shard_map/ppermute | solution.py:47
  157.1 2.8 %collective-permute-done.6 = bf16[256,1024]{1,0:T(8,128)(2,1)S(1)} collective-permute-done((bf16[256,1024]{1,0:T(8,128)(2,1)S(1)}, bf16[256,1024]{1,0:T(8,128)(2,1)S(1)}, u32[]{:S(2)}, u32[]{:S(2)}) %collective-permute-start.6) | collective-permute-done | bytes 524320 | tf_op jit(solution)/shard_map/ppermute | solution.py:47
  159.9 0.8 constant_dynamic-update-slice_fusion.5
  160.8 0.8 constant_dynamic-update-slice_fusion.4
  161.6 3.5 %collective-permute-done.7 = bf16[256,1024]{1,0:T(8,128)(2,1)S(1)} collective-permute-done((bf16[256,1024]{1,0:T(8,128)(2,1)S(1)}, bf16[256,1024]{1,0:T(8,128)(2,1)S(1)}, u32[]{:S(2)}, u32[]{:S(2)}) %collective-permute-start.7) | collective-permute-done | bytes 524320 | tf_op jit(solution)/shard_map/ppermute | solution.py:47
  165.1 0.9 constant_dynamic-update-slice_fusion.3
  166.0 5.2 %collective-permute-done.10 = bf16[256,1024]{1,0:T(8,128)(2,1)S(1)} collective-permute-done((bf16[256,1024]{1,0:T(8,128)(2,1)S(1)}, bf16[256,1024]{1,0:T(8,128)(2,1)S(1)}, u32[]{:S(2)}, u32[]{:S(2)}) %collective-permute-start.10) | collective-permute-done | bytes 524320 | tf_op jit(solution)/shard_map/ppermute | solution.py:47
  171.2 0.8 constant_dynamic-update-slice_fusion.2
  172.0 0.8 constant_dynamic-update-slice_fusion.1
  172.9 0.8 constant_dynamic-update-slice_fusion
  173.7 16.6 %shard_map.118 = bf16[1024,1024]{1,0:T(8,128)(2,1)} custom-call(s32[12]{0:T(128)} %concatenate.10.prm, f32[8]{0:T(128)} %slopes_ref.1, bf16[1024,1024]{1,0:T(8,128)(2,1)} %q_ref.1, bf16[2,768,1024]{2,1,0:T(8,128)(2,1)} %bitcast.9.k_ref.v_ref, bf16[2,768,1024]{2,1,0:T(8,128)(2,1)} %bitcast.9.k_ref.v_ref), custom_call_target="tpu_custom_call" | custom-call | tf_op jit(solution)/shard_map/pallas_call | solution.py:132
  (21 shorter events, 0.3 us)
Async XLA Ops:
  6.5 101.1 %copy-start = (bf16[256,1024]{1,0:T(8,128)(2,1)S(1)}, bf16[256,1024]{1,0:T(8,128)(2,1)}, u32[]{:S(2)}) copy-start(bf16[256,1024]{1,0:T(8,128)(2,1)} %param.12) | copy-start | bytes 1572868
  6.5 54.3 %all-gather.3.cloned.1.call-start = ((), (), s32[]{:S(2)}) async-start(), calls=%async_computation | async-start | bytes 4456448 | tf_op jit(solution)/shard_map/all_gather | solution.py:157
  7.3 110.2 %all-gather.5.cloned.1.call-start = ((), (), s32[]{:S(2)}) async-start(), calls=%async_computation.1 | async-start | bytes 4456448 | tf_op jit(solution)/shard_map/all_gather | solution.py:169
  11.6 18.9 %collective-permute-start.4 = (bf16[2,256,1024]{1,2,0:T(8,128)(2,1)S(1)}, bf16[2,256,1024]{1,2,0:T(8,128)(2,1)S(1)}, u32[]{:S(2)}, u32[]{:S(2)}) collective-permute-start(bf16[2,256,1024]{1,2,0:T(8,128)(2,1)S(1)} %pad_maximum_fusion), channel_id=1, source_target_pairs={{0,1},{1,2},{2,3},{3,4},{4,5},{5,6},{6,7},{7,8},{8,9},{9,10},{10,1... | collective-permute-start | bytes 3145736 | tf_op jit(solution)/shard_map/ppermute | solution.py:23
  60.8 45.2 %collective-permute-start.5 = (bf16[2,256,1024]{1,2,0:T(8,128)(2,1)S(1)}, bf16[2,256,1024]{1,2,0:T(8,128)(2,1)}, u32[]{:S(2)}, u32[]{:S(2)}) collective-permute-start(bf16[2,256,1024]{1,2,0:T(8,128)(2,1)S(1)} %collective-permute-done.4), channel_id=1, source_target_pairs={{0,1},{1,2},{2,3},{3,4},{4,5},{5,6},{6,7},{7,8},{8,9},{9,10},{10,1... | collective-permute-start | bytes 3145736 | tf_op jit(solution)/shard_map/ppermute | solution.py:23
  63.0 16.9 %collective-permute-start = (s32[1]{0:T(128)}, s32[1]{0:T(128)}, u32[]{:S(2)}, u32[]{:S(2)}) collective-permute-start(s32[1]{0:T(128)} %param.22), channel_id=1, source_target_pairs={{0,1},{1,2},{2,3},{3,4},{4,5},{5,6},{6,7},{7,8},{8,9},{9,10},{10,1... | collective-permute-start | bytes 20 | tf_op jit(solution)/shard_map/ppermute | solution.py:23
  80.5 11.4 %collective-permute-start.1 = (s32[1]{0:T(128)}, s32[1]{0:T(128)}, u32[]{:S(2)}, u32[]{:S(2)}) collective-permute-start(s32[1]{0:T(128)} %add.53), channel_id=1, source_target_pairs={{0,2},{1,3},{2,4},{3,5},{4,6},{5,7},{6,8},{7,9},{8,10},{9,11},{10,... | collective-permute-start | bytes 20 | tf_op jit(solution)/shard_map/ppermute | solution.py:23
  92.6 5.7 %collective-permute-start.2 = (s32[1]{0:T(128)}, s32[1]{0:T(128)}, u32[]{:S(2)}, u32[]{:S(2)}) collective-permute-start(s32[1]{0:T(128)} %add.54), channel_id=1, source_target_pairs={{0,4},{1,5},{2,6},{3,7},{4,8},{5,9},{6,10},{7,11},{8,12},{9,13},{1... | collective-permute-start | bytes 20 | tf_op jit(solution)/shard_map/ppermute | solution.py:23
  99.0 6.3 %collective-permute-start.3 = (s32[1]{0:T(128)}, s32[1]{0:T(128)}, u32[]{:S(2)}, u32[]{:S(2)}) collective-permute-start(s32[1]{0:T(128)} %add.55), channel_id=1, source_target_pairs={{0,8},{1,9},{2,10},{3,11},{4,12},{5,13},{6,14},{7,15},{16,24},{17,... | collective-permute-start | bytes 20 | tf_op jit(solution)/shard_map/ppermute | solution.py:23
  111.7 2.2 %copy-start.1 = (bf16[1024,2048]{1,0:T(8,128)(2,1)S(1)}, bf16[1024,2048]{1,0:T(8,128)(2,1)}, u32[]{:S(2)}) copy-start(bf16[1024,2048]{1,0:T(8,128)(2,1)} %all-gather.3.cloned.1.call-done) | copy-start | bytes 12582916
  111.8 2.5 %copy-start.2 = (bf16[256,2048]{1,0:T(8,128)(2,1)S(1)}, bf16[256,2048]{1,0:T(8,128)(2,1)}, u32[]{:S(2)}) copy-start(bf16[256,2048]{1,0:T(8,128)(2,1)} %param.15) | copy-start | bytes 3145732
  114.3 1.4 copy-start.3
  115.9 21.6 %collective-permute-start.8 = (bf16[256,2048]{1,0:T(8,128)(2,1)S(1)}, bf16[256,2048]{1,0:T(8,128)(2,1)S(1)}, u32[]{:S(2)}, u32[]{:S(2)}) collective-permute-start(bf16[256,2048]{1,0:T(8,128)(2,1)S(1)} %multiply_convert_fusion), channel_id=1, source_target_pairs={{0,16},{16,0},{1,17},{17,1},{2,18},{18,2},{3,19},{19,3},{4,20},{20... | collective-permute-start | bytes 3145736 | tf_op jit(solution)/shard_map/ppermute | solution.py:194
  117.5 25.0 %copy-start.5 = (bf16[2048,1024]{1,0:T(8,128)(2,1)S(1)}, bf16[2048,1024]{1,0:T(8,128)(2,1)}, u32[]{:S(2)}) copy-start(bf16[2048,1024]{1,0:T(8,128)(2,1)} %all-gather.5.cloned.1.call-done) | copy-start | bytes 12582916
  141.0 11.5 %copy-start.4 = (s32[4,2]{0,1:T(2,128)S(1)}, s32[4,2]{0,1:T(2,128)}, u32[]{:S(2)}) copy-start(s32[4,2]{0,1:T(2,128)} %param.23) | copy-start | bytes 100
  141.0 9.5 %collective-permute-start.9 = (bf16[256,1024]{1,0:T(8,128)(2,1)S(1)}, bf16[256,1024]{1,0:T(8,128)(2,1)S(1)}, u32[]{:S(2)}, u32[]{:S(2)}) collective-permute-start(bf16[256,1024]{1,0:T(8,128)(2,1)S(1)} %convolution_convert_fusion), channel_id=1, source_target_pairs={{0,16},{1,17},{2,18},{3,19},{4,20},{5,21},{6,22},{7,23},{8,24},{9,... | collective-permute-start | bytes 1572872 | tf_op jit(solution)/shard_map/ppermute | solution.py:47
  143.8 16.1 %collective-permute-start.6 = (bf16[256,1024]{1,0:T(8,128)(2,1)S(1)}, bf16[256,1024]{1,0:T(8,128)(2,1)S(1)}, u32[]{:S(2)}, u32[]{:S(2)}) collective-permute-start(bf16[256,1024]{1,0:T(8,128)(2,1)S(1)} %convolution_convert_fusion.1), channel_id=1, source_target_pairs={{0,1},{1,2},{2,3},{3,4},{4,5},{5,6},{6,7},{7,8},{8,9},{9,10},{10,1... | collective-permute-start | bytes 1572872 | tf_op jit(solution)/shard_map/ppermute | solution.py:47
  145.7 19.4 %collective-permute-start.7 = (bf16[256,1024]{1,0:T(8,128)(2,1)S(1)}, bf16[256,1024]{1,0:T(8,128)(2,1)S(1)}, u32[]{:S(2)}, u32[]{:S(2)}) collective-permute-start(bf16[256,1024]{1,0:T(8,128)(2,1)S(1)} %convolution_convert_fusion.1), channel_id=1, source_target_pairs={{1,0},{2,1},{3,2},{4,3},{5,4},{6,5},{7,6},{8,7},{9,8},{10,9},{11,1... | collective-permute-start | bytes 1572872 | tf_op jit(solution)/shard_map/ppermute | solution.py:47
  150.5 20.7 %collective-permute-start.10 = (bf16[256,1024]{1,0:T(8,128)(2,1)S(1)}, bf16[256,1024]{1,0:T(8,128)(2,1)S(1)}, u32[]{:S(2)}, u32[]{:S(2)}) collective-permute-start(bf16[256,1024]{1,0:T(8,128)(2,1)S(1)} %collective-permute-done.9), channel_id=1, source_target_pairs={{0,1},{1,2},{2,3},{3,4},{4,5},{5,6},{6,7},{7,8},{8,9},{9,10},{10,1... | collective-permute-start | bytes 1572872 | tf_op jit(solution)/shard_map/ppermute | solution.py:47
  153.3 19.6 %collective-permute-start.11 = (bf16[256,1024]{1,0:T(8,128)(2,1)S(1)}, bf16[256,1024]{1,0:T(8,128)(2,1)S(1)}, u32[]{:S(2)}, u32[]{:S(2)}) collective-permute-start(bf16[256,1024]{1,0:T(8,128)(2,1)S(1)} %collective-permute-done.9), channel_id=1, source_target_pairs={{1,0},{2,1},{3,2},{4,3},{5,4},{6,5},{7,6},{8,7},{9,8},{10,9},{11,1... | collective-permute-start | bytes 1572872 | tf_op jit(solution)/shard_map/ppermute | solution.py:47
Sparse Core Ops, SparseCore 0:
  9.5 51.2 all-gather.2
  63.0 50.2 all-gather.4

commit v17 on v16

--- a/solution.py
+++ b/solution.py
@@ -186,12 +186,12 @@
     key_global = device_index * rows_here - reach_shards * rows_here + key_pos
     allowed = (key_lag >= 0) & (key_lag < W) & (key_global[None, :] >= 0)
     sem_att = attend(sem_queries, window_pair[0], window_pair[1], allowed, 0.0).astype(jnp.bfloat16)
-    running, sem_att = lax.optimization_barrier((running, sem_att))
     projected = contract_rows(sem_att, full_out_proj)
     sem_stream = sem_inputs.astype(jnp.float32) + projected
     normed = normalize(sem_stream, norm_gain)
     if shared:
         partner_normed = lax.ppermute(normed, "groups", partners)
+        running, partner_normed = lax.optimization_barrier((running, partner_normed))
         partner_part = contract_rows(partner_normed, gathered_proj).astype(jnp.bfloat16)
         partner_sum = sent_to(partner_part, 1, 0)
         other_pieces = [sent_to(partner_sum, 0, 1), partner_sum, sent_to(partner_sum, 0, -1)]

time: 198 us -> 185 us (0.934)
  waiting for transfers between devices: 101 us -> 84.5 us
    ppermute x1, waiting for transfers between devices: 20 us -> 0.01 us  [on_device(): partner_normed = lax.ppermute(normed, 'groups', partners)]
    ppermute x6, waiting for transfers between devices: 36.8 us -> 41.1 us  [passed_along(): return lax.ppermute(array, axis, pairs)]
  transfers between devices with their start and end apart: 14 -> 14, of which waited for: 11 -> 10; matrix products, arithmetic and copies ran while one was open for 10% -> 11% of each run, Pallas kernels for 0% -> 0%
where the time goes in v17:
time: 185 us; the launch traced here: 183 us
  waiting for transfers between devices  84.5 us (46%)
  starting transfers between devices  39 us (21%)
  between operations  16.9 us (9%)
  Pallas kernels  16.6 us (9%)
  local copies, waits for them, and re-layouts  11.5 us (6%)
  matrix products  7.92 us (4%)
  other arithmetic  6.69 us (4%)
    ppermute x6, waiting for transfers between devices, passed_along(): return lax.ppermute(array, axis, pairs)  41.1 us
    all_gather x1, waiting for transfers between devices, on_device(): full_out_proj = lax.all_gather(out_proj, 'ctx', axis=0, tiled=True)  30.3 us
    ppermute x6, starting transfers between devices, passed_along(): return lax.ppermute(array, axis, pairs)  25.6 us
    pallas_call x1, Pallas kernels, coarse_attention(): pl.pallas_call(kernel, grid_spec=grid_spec, out_shape=jax.ShapeDtypeStruc...  16.6 us
    ppermute x5, waiting for transfers between devices, sent_to(): return lax.ppermute(array, ('groups', 'ctx'), pairs)  12.4 us
    ppermute x5, starting transfers between devices, sent_to(): return lax.ppermute(array, ('groups', 'ctx'), pairs)  11.9 us
    unnamed x20, local copies, waits for them, and re-layouts  9.7 us
    dot_general x3, matrix products, contract_rows(): return jnp.dot(left_side, weight_piece, preferred_element_type=jnp.float32)  6.25 us
  transfers between devices with their start and end apart: 14, of which 10 were waited for; matrix products, arithmetic and copies ran while one was open for 11% of the time, Pallas kernels for 0%

profile of v17, /device:TPU:20, one launch (start us, length us, event | category | flops | bytes accessed | tf_op | source)
XLA Modules:
  0.0 183.1 jit_solution(11191242295722009546)
XLA Ops:
  6.5 0.7 all-gather.3.cloned.1.call-update
  7.3 1.7 broadcast_select_fusion
  9.0 1.2 copy.19
  10.3 1.2 copy.18
  11.5 0.1 pad_maximum_fusion
  11.6 1.9 %collective-permute-start.4 = (bf16[2,256,1024]{1,2,0:T(8,128)(2,1)S(1)}, bf16[2,256,1024]{1,2,0:T(8,128)(2,1)S(1)}, u32[]{:S(2)}, u32[]{:S(2)}) collective-permute-start(bf16[2,256,1024]{1,2,0:T(8,128)(2,1)S(1)} %pad_maximum_fusion), channel_id=1, source_target_pairs={{0,1},{1,2},{2,3},{3,4},{4,5},{5,6},{6,7},{7,8},{8,9},{9,10},{10,1... | collective-permute-start | bytes 3145736 | tf_op jit(solution)/shard_map/ppermute | solution.py:23
  13.6 17.0 %collective-permute-done.4 = bf16[2,256,1024]{1,2,0:T(8,128)(2,1)S(1)} collective-permute-done((bf16[2,256,1024]{1,2,0:T(8,128)(2,1)S(1)}, bf16[2,256,1024]{1,2,0:T(8,128)(2,1)S(1)}, u32[]{:S(2)}, u32[]{:S(2)}) %collective-permute-start.4) | collective-permute-done | bytes 1048608 | tf_op jit(solution)/shard_map/ppermute | solution.py:23
  30.6 30.3 %all-gather.3.cloned.1.call-done = bf16[1024,2048]{1,0:T(8,128)(2,1)} async-done(((bf16[64,2048]{1,0:T(8,128)(2,1)}), bf16[1024,2048]{1,0:T(8,128)(2,1)}) %all-gather.3.cloned.1.call-update) | async-done | bytes 4194320 | tf_op jit(solution)/shard_map/all_gather | solution.py:157
  60.8 2.1 %collective-permute-start.5 = (bf16[2,256,1024]{1,2,0:T(8,128)(2,1)S(1)}, bf16[2,256,1024]{1,2,0:T(8,128)(2,1)}, u32[]{:S(2)}, u32[]{:S(2)}) collective-permute-start(bf16[2,256,1024]{1,2,0:T(8,128)(2,1)S(1)} %collective-permute-done.4), channel_id=1, source_target_pairs={{0,1},{1,2},{2,3},{3,4},{4,5},{5,6},{6,7},{7,8},{8,9},{9,10},{10,1... | collective-permute-start | bytes 3145736 | tf_op jit(solution)/shard_map/ppermute | solution.py:23
  63.0 0.2 fusion.10
  63.2 16.6 %collective-permute-done.5 = bf16[2,256,1024]{1,2,0:T(8,128)(2,1)} collective-permute-done((bf16[2,256,1024]{1,2,0:T(8,128)(2,1)S(1)}, bf16[2,256,1024]{1,2,0:T(8,128)(2,1)}, u32[]{:S(2)}, u32[]{:S(2)}) %collective-permute-start.5) | collective-permute-done | bytes 1048608 | tf_op jit(solution)/shard_map/ppermute | solution.py:23
  79.9 1.3 maximum_maximum_fusion
  81.2 0.2 fusion.16
  81.4 1.0 fusion.11
  82.5 3.1 %fusion.17 = (f32[8,256]{1,0:T(8,128)S(1)}, f32[8,256,768]{1,2,0:T(8,128)S(1)}) fusion(f32[8,768,256]{2,1,0:T(8,128)S(1)} %fusion.11, pred[256,768]{0,1:T(8,128)(4,1)S(1)} %fusion.10), kind=kOutput, calls=%fused_computation.38 | output fusion | flops 9437951 | bytes 12787712 | tf_op jit(solution)/shard_map/sub | solution.py:63
  85.6 0.6 fusion.6
  86.2 1.5 copy-done.1
  87.7 0.3 copy-done.2
  88.0 1.4 multiply_reduce_fusion
  89.4 0.2 multiply_convert_fusion
  89.7 1.5 collective-permute-start.6
  91.2 6.8 %collective-permute-start = (s32[1]{0:T(128)}, s32[1]{0:T(128)}, u32[]{:S(2)}, u32[]{:S(2)}) collective-permute-start(s32[1]{0:T(128)} %param.22), channel_id=1, source_target_pairs={{0,1},{1,2},{2,3},{3,4},{4,5},{5,6},{6,7},{7,8},{8,9},{9,10},{10,1... | collective-permute-start | bytes 20 | tf_op jit(solution)/shard_map/ppermute | solution.py:23
  98.6 0.4 collective-permute-done
  99.7 9.5 %collective-permute-start.1 = (s32[1]{0:T(128)}, s32[1]{0:T(128)}, u32[]{:S(2)}, u32[]{:S(2)}) collective-permute-start(s32[1]{0:T(128)} %add.53), channel_id=1, source_target_pairs={{0,2},{1,3},{2,4},{3,5},{4,6},{5,7},{6,8},{7,9},{8,10},{9,11},{10,... | collective-permute-start | bytes 20 | tf_op jit(solution)/shard_map/ppermute | solution.py:23
  109.2 0.2 collective-permute-done.1
  110.1 3.9 %collective-permute-start.2 = (s32[1]{0:T(128)}, s32[1]{0:T(128)}, u32[]{:S(2)}, u32[]{:S(2)}) collective-permute-start(s32[1]{0:T(128)} %add.54), channel_id=1, source_target_pairs={{0,4},{1,5},{2,6},{3,7},{4,8},{5,9},{6,10},{7,11},{8,12},{9,13},{1... | collective-permute-start | bytes 20 | tf_op jit(solution)/shard_map/ppermute | solution.py:23
  114.0 1.7 collective-permute-done.2
  116.3 1.3 collective-permute-start.3
  117.6 5.2 %collective-permute-done.3 = s32[1]{0:T(128)} collective-permute-done((s32[1]{0:T(128)}, s32[1]{0:T(128)}, u32[]{:S(2)}, u32[]{:S(2)}) %collective-permute-start.3) | collective-permute-done | bytes 36 | tf_op jit(solution)/shard_map/ppermute | solution.py:23
  123.4 3.6 %convolution_convert_fusion = bf16[256,1024]{1,0:T(8,128)(2,1)S(1)} fusion(bf16[256,2048]{1,0:T(8,128)(2,1)S(1)} %collective-permute-done.6, bf16[2048,1024]{1,0:T(8,128)(2,1)} %all-gather.5.cloned.1.call-done), kind=kOutput, calls=%fused_computation.14 | convolution fusion | flops 1074003968 | bytes 5767168 | tf_op jit(solution)/shard_map/dot_general | solution.py:79
  127.0 0.6 collective-permute-start.9
  127.7 1.3 convolution_convert_fusion.1
  129.0 1.9 %collective-permute-start.7 = (bf16[256,1024]{1,0:T(8,128)(2,1)S(1)}, bf16[256,1024]{1,0:T(8,128)(2,1)}, u32[]{:S(2)}, u32[]{:S(2)}) collective-permute-start(bf16[256,1024]{1,0:T(8,128)(2,1)S(1)} %convolution_convert_fusion.1), channel_id=1, source_target_pairs={{0,1},{1,2},{2,3},{3,4},{4,5},{5,6},{6,7},{7,8},{8,9},{9,10},{10,1... | collective-permute-start | bytes 1572872 | tf_op jit(solution)/shard_map/ppermute | solution.py:47
  130.9 3.6 %collective-permute-start.8 = (bf16[256,1024]{1,0:T(8,128)(2,1)S(1)}, bf16[256,1024]{1,0:T(8,128)(2,1)S(1)}, u32[]{:S(2)}, u32[]{:S(2)}) collective-permute-start(bf16[256,1024]{1,0:T(8,128)(2,1)S(1)} %convolution_convert_fusion.1), channel_id=1, source_target_pairs={{1,0},{2,1},{3,2},{4,3},{5,4},{6,5},{7,6},{8,7},{9,8},{10,9},{11,1... | collective-permute-start | bytes 1572872 | tf_op jit(solution)/shard_map/ppermute | solution.py:47
  134.5 1.7 collective-permute-done.9
  136.3 1.9 %collective-permute-start.10 = (bf16[256,1024]{1,0:T(8,128)(2,1)S(1)}, bf16[256,1024]{1,0:T(8,128)(2,1)S(1)}, u32[]{:S(2)}, u32[]{:S(2)}) collective-permute-start(bf16[256,1024]{1,0:T(8,128)(2,1)S(1)} %collective-permute-done.9), channel_id=1, source_target_pairs={{0,1},{1,2},{2,3},{3,4},{4,5},{5,6},{6,7},{7,8},{8,9},{9,10},{10,1... | collective-permute-start | bytes 1572872 | tf_op jit(solution)/shard_map/ppermute | solution.py:47
  138.2 0.1 copy.17
  138.4 3.8 %collective-permute-start.11 = (bf16[256,1024]{1,0:T(8,128)(2,1)S(1)}, bf16[256,1024]{1,0:T(8,128)(2,1)S(1)}, u32[]{:S(2)}, u32[]{:S(2)}) collective-permute-start(bf16[256,1024]{1,0:T(8,128)(2,1)S(1)} %collective-permute-done.9), channel_id=1, source_target_pairs={{1,0},{2,1},{3,2},{4,3},{5,4},{6,5},{7,6},{8,7},{9,8},{10,9},{11,1... | collective-permute-start | bytes 1572872 | tf_op jit(solution)/shard_map/ppermute | solution.py:47
  142.2 1.9 %constant_dynamic-update-slice_fusion.5 = bf16[1536,1024]{1,0:T(8,128)(2,1)} fusion(bf16[256,1024]{1,0:T(8,128)(2,1)} %collective-permute-done.7), kind=kLoop, calls=%fused_computation.31 | loop fusion | bytes 1048576
  144.1 0.8 constant_dynamic-update-slice_fusion.4
  144.9 7.2 %collective-permute-done.8 = bf16[256,1024]{1,0:T(8,128)(2,1)S(1)} collective-permute-done((bf16[256,1024]{1,0:T(8,128)(2,1)S(1)}, bf16[256,1024]{1,0:T(8,128)(2,1)S(1)}, u32[]{:S(2)}, u32[]{:S(2)}) %collective-permute-start.8) | collective-permute-done | bytes 524320 | tf_op jit(solution)/shard_map/ppermute | solution.py:47
  152.2 0.9 constant_dynamic-update-slice_fusion.3
  153.0 0.7 concatenate.10.prm
  153.7 3.5 %collective-permute-done.10 = bf16[256,1024]{1,0:T(8,128)(2,1)S(1)} collective-permute-done((bf16[256,1024]{1,0:T(8,128)(2,1)S(1)}, bf16[256,1024]{1,0:T(8,128)(2,1)S(1)}, u32[]{:S(2)}, u32[]{:S(2)}) %collective-permute-start.10) | collective-permute-done | bytes 524320 | tf_op jit(solution)/shard_map/ppermute | solution.py:47
  157.1 0.8 constant_dynamic-update-slice_fusion.2
  158.0 0.8 constant_dynamic-update-slice_fusion.1
  158.8 0.8 constant_dynamic-update-slice_fusion
  159.7 16.6 %shard_map.118 = bf16[1024,1024]{1,0:T(8,128)(2,1)} custom-call(s32[12]{0:T(128)} %concatenate.10.prm, f32[8]{0:T(128)} %slopes_ref.1, bf16[1024,1024]{1,0:T(8,128)(2,1)} %q_ref.1, bf16[2,768,1024]{2,1,0:T(8,128)(2,1)} %bitcast.9.k_ref.v_ref, bf16[2,768,1024]{2,1,0:T(8,128)(2,1)} %bitcast.9.k_ref.v_ref), custom_call_target="tpu_custom_call" | custom-call | tf_op jit(solution)/shard_map/pallas_call | solution.py:132
  (21 shorter events, 0.2 us)
Async XLA Ops:
  6.5 74.9 %copy-start = (bf16[256,1024]{1,0:T(8,128)(2,1)S(1)}, bf16[256,1024]{1,0:T(8,128)(2,1)}, u32[]{:S(2)}) copy-start(bf16[256,1024]{1,0:T(8,128)(2,1)} %param.12) | copy-start | bytes 1572868
  6.5 54.3 %all-gather.3.cloned.1.call-start = ((), (), s32[]{:S(2)}) async-start(), calls=%async_computation | async-start | bytes 4456448 | tf_op jit(solution)/shard_map/all_gather | solution.py:157
  7.3 116.2 %all-gather.5.cloned.1.call-start = ((), (), s32[]{:S(2)}) async-start(), calls=%async_computation.1 | async-start | bytes 4456448 | tf_op jit(solution)/shard_map/all_gather | solution.py:169
  11.6 18.9 %collective-permute-start.4 = (bf16[2,256,1024]{1,2,0:T(8,128)(2,1)S(1)}, bf16[2,256,1024]{1,2,0:T(8,128)(2,1)S(1)}, u32[]{:S(2)}, u32[]{:S(2)}) collective-permute-start(bf16[2,256,1024]{1,2,0:T(8,128)(2,1)S(1)} %pad_maximum_fusion), channel_id=1, source_target_pairs={{0,1},{1,2},{2,3},{3,4},{4,5},{5,6},{6,7},{7,8},{8,9},{9,10},{10,1... | collective-permute-start | bytes 3145736 | tf_op jit(solution)/shard_map/ppermute | solution.py:23
  60.8 19.0 %collective-permute-start.5 = (bf16[2,256,1024]{1,2,0:T(8,128)(2,1)S(1)}, bf16[2,256,1024]{1,2,0:T(8,128)(2,1)}, u32[]{:S(2)}, u32[]{:S(2)}) collective-permute-start(bf16[2,256,1024]{1,2,0:T(8,128)(2,1)S(1)} %collective-permute-done.4), channel_id=1, source_target_pairs={{0,1},{1,2},{2,3},{3,4},{4,5},{5,6},{6,7},{7,8},{8,9},{9,10},{10,1... | collective-permute-start | bytes 3145736 | tf_op jit(solution)/shard_map/ppermute | solution.py:23
  85.5 2.2 %copy-start.1 = (bf16[1024,2048]{1,0:T(8,128)(2,1)S(1)}, bf16[1024,2048]{1,0:T(8,128)(2,1)}, u32[]{:S(2)}) copy-start(bf16[1024,2048]{1,0:T(8,128)(2,1)} %all-gather.3.cloned.1.call-done) | copy-start | bytes 12582916
  85.6 2.5 %copy-start.2 = (bf16[256,2048]{1,0:T(8,128)(2,1)S(1)}, bf16[256,2048]{1,0:T(8,128)(2,1)}, u32[]{:S(2)}) copy-start(bf16[256,2048]{1,0:T(8,128)(2,1)} %param.15) | copy-start | bytes 3145732
  88.0 1.4 copy-start.3
  89.7 33.7 %collective-permute-start.6 = (bf16[256,2048]{1,0:T(8,128)(2,1)S(1)}, bf16[256,2048]{1,0:T(8,128)(2,1)S(1)}, u32[]{:S(2)}, u32[]{:S(2)}) collective-permute-start(bf16[256,2048]{1,0:T(8,128)(2,1)S(1)} %multiply_convert_fusion), channel_id=1, source_target_pairs={{0,16},{16,0},{1,17},{17,1},{2,18},{18,2},{3,19},{19,3},{4,20},{20... | collective-permute-start | bytes 3145736 | tf_op jit(solution)/shard_map/ppermute | solution.py:193
  91.2 7.8 %collective-permute-start = (s32[1]{0:T(128)}, s32[1]{0:T(128)}, u32[]{:S(2)}, u32[]{:S(2)}) collective-permute-start(s32[1]{0:T(128)} %param.22), channel_id=1, source_target_pairs={{0,1},{1,2},{2,3},{3,4},{4,5},{5,6},{6,7},{7,8},{8,9},{9,10},{10,1... | collective-permute-start | bytes 20 | tf_op jit(solution)/shard_map/ppermute | solution.py:23
  99.7 9.7 %collective-permute-start.1 = (s32[1]{0:T(128)}, s32[1]{0:T(128)}, u32[]{:S(2)}, u32[]{:S(2)}) collective-permute-start(s32[1]{0:T(128)} %add.53), channel_id=1, source_target_pairs={{0,2},{1,3},{2,4},{3,5},{4,6},{5,7},{6,8},{7,9},{8,10},{9,11},{10,... | collective-permute-start | bytes 20 | tf_op jit(solution)/shard_map/ppermute | solution.py:23
  110.1 5.6 %collective-permute-start.2 = (s32[1]{0:T(128)}, s32[1]{0:T(128)}, u32[]{:S(2)}, u32[]{:S(2)}) collective-permute-start(s32[1]{0:T(128)} %add.54), channel_id=1, source_target_pairs={{0,4},{1,5},{2,6},{3,7},{4,8},{5,9},{6,10},{7,11},{8,12},{9,13},{1... | collective-permute-start | bytes 20 | tf_op jit(solution)/shard_map/ppermute | solution.py:23
  116.3 6.5 %collective-permute-start.3 = (s32[1]{0:T(128)}, s32[1]{0:T(128)}, u32[]{:S(2)}, u32[]{:S(2)}) collective-permute-start(s32[1]{0:T(128)} %add.55), channel_id=1, source_target_pairs={{0,8},{1,9},{2,10},{3,11},{4,12},{5,13},{6,14},{7,15},{16,24},{17,... | collective-permute-start | bytes 20 | tf_op jit(solution)/shard_map/ppermute | solution.py:23
  123.4 4.2 %copy-start.5 = (bf16[2048,1024]{1,0:T(8,128)(2,1)S(1)}, bf16[2048,1024]{1,0:T(8,128)(2,1)}, u32[]{:S(2)}) copy-start(bf16[2048,1024]{1,0:T(8,128)(2,1)} %all-gather.5.cloned.1.call-done) | copy-start | bytes 12582916
  127.0 11.2 %copy-start.4 = (s32[4,2]{0,1:T(2,128)S(1)}, s32[4,2]{0,1:T(2,128)}, u32[]{:S(2)}) copy-start(s32[4,2]{0,1:T(2,128)} %param.23) | copy-start | bytes 100
  127.0 9.2 %collective-permute-start.9 = (bf16[256,1024]{1,0:T(8,128)(2,1)S(1)}, bf16[256,1024]{1,0:T(8,128)(2,1)S(1)}, u32[]{:S(2)}, u32[]{:S(2)}) collective-permute-start(bf16[256,1024]{1,0:T(8,128)(2,1)S(1)} %convolution_convert_fusion), channel_id=1, source_target_pairs={{0,16},{1,17},{2,18},{3,19},{4,20},{5,21},{6,22},{7,23},{8,24},{9,... | collective-permute-start | bytes 1572872 | tf_op jit(solution)/shard_map/ppermute | solution.py:47
  129.0 13.3 %collective-permute-start.7 = (bf16[256,1024]{1,0:T(8,128)(2,1)S(1)}, bf16[256,1024]{1,0:T(8,128)(2,1)}, u32[]{:S(2)}, u32[]{:S(2)}) collective-permute-start(bf16[256,1024]{1,0:T(8,128)(2,1)S(1)} %convolution_convert_fusion.1), channel_id=1, source_target_pairs={{0,1},{1,2},{2,3},{3,4},{4,5},{5,6},{6,7},{7,8},{8,9},{9,10},{10,1... | collective-permute-start | bytes 1572872 | tf_op jit(solution)/shard_map/ppermute | solution.py:47
  130.9 21.3 %collective-permute-start.8 = (bf16[256,1024]{1,0:T(8,128)(2,1)S(1)}, bf16[256,1024]{1,0:T(8,128)(2,1)S(1)}, u32[]{:S(2)}, u32[]{:S(2)}) collective-permute-start(bf16[256,1024]{1,0:T(8,128)(2,1)S(1)} %convolution_convert_fusion.1), channel_id=1, source_target_pairs={{1,0},{2,1},{3,2},{4,3},{5,4},{6,5},{7,6},{8,7},{9,8},{10,9},{11,1... | collective-permute-start | bytes 1572872 | tf_op jit(solution)/shard_map/ppermute | solution.py:47
  136.3 20.9 %collective-permute-start.10 = (bf16[256,1024]{1,0:T(8,128)(2,1)S(1)}, bf16[256,1024]{1,0:T(8,128)(2,1)S(1)}, u32[]{:S(2)}, u32[]{:S(2)}) collective-permute-start(bf16[256,1024]{1,0:T(8,128)(2,1)S(1)} %collective-permute-done.9), channel_id=1, source_target_pairs={{0,1},{1,2},{2,3},{3,4},{4,5},{5,6},{6,7},{7,8},{8,9},{9,10},{10,1... | collective-permute-start | bytes 1572872 | tf_op jit(solution)/shard_map/ppermute | solution.py:47
  138.4 20.4 %collective-permute-start.11 = (bf16[256,1024]{1,0:T(8,128)(2,1)S(1)}, bf16[256,1024]{1,0:T(8,128)(2,1)S(1)}, u32[]{:S(2)}, u32[]{:S(2)}) collective-permute-start(bf16[256,1024]{1,0:T(8,128)(2,1)S(1)} %collective-permute-done.9), channel_id=1, source_target_pairs={{1,0},{2,1},{3,2},{4,3},{5,4},{6,5},{7,6},{8,7},{9,8},{10,9},{11,1... | collective-permute-start | bytes 1572872 | tf_op jit(solution)/shard_map/ppermute | solution.py:47
Sparse Core Ops, SparseCore 0:
  9.5 51.2 all-gather.2
  63.0 50.2 all-gather.4
